TPU v7x, 1024 devices: a whole 4x8x16 slice. The times are simulated.
1024 devices in a mesh: gx: 16 (over x, y_hi, core), gy: 64 (over y_lo, z).
Axes of the slice: x: 4, y: 8 (y_hi: 2, y_lo: 4; y = y_hi * 4 + y_lo), z: 16, core: 2. Of those that a mesh axis runs over, the one named last changes fastest.
Arguments:
- potential: float32 [256, 1024, 256], P('gx', 'gy'), may hold values from -1 to 1
- charge: float32 [256, 1024, 256], P('gx', 'gy'), may hold values from -6 to 6
- region: int32 [256, 1024, 256], P('gx', 'gy'), may hold values from 0 to 16, as said below
- electrode_volts: float32 [16], replicated, may hold values from -2 to 2
Outputs:
- correction: float32 [256, 1024, 256], P('gx', 'gy')
Inputs may be any that keep to these rules, and one draw needn't show every extreme that they name: `region`: 0 marks a free cell; k marks a cell of electrode k, held at electrode_volts[k - 1]; about one cell in eight belongs to an electrode.
All inputs are finite; a program needn't handle non-finite values.
Results may differ from a plain program's by a relative error of at most 0.00002.
Values sent between devices are 32-bit elements; how exact they have to be, the bound alone decides.
No kernel may reach another device: no remote copies, remote signals or barrier semaphores. Data moves between devices by JAX's collectives and lax.ppermute only.
A program may use at most 64 MiB of HBM per device.

v0:
```python
import jax
import jax.numpy as jnp
from jax import lax
from jax.sharding import PartitionSpec as P

LEVELS = 4
COARSE_SWEEPS = 4


screen = 0.5


def extended(block, sides, width):
    for axis, dim in sides:
        count = lax.axis_size(axis)
        forward = [(i, i + 1) for i in range(count - 1)]
        backward = [(target, source) for source, target in forward]
        low = lax.ppermute(
            lax.slice_in_dim(block, block.shape[dim] - width, None, axis=dim), axis, forward
        )
        high = lax.ppermute(lax.slice_in_dim(block, 0, width, axis=dim), axis, backward)
        block = jnp.concatenate([low, block, high], axis=dim)
    return block


def shifted(block, axis, distance):
    devices = range(lax.axis_size(axis))
    route = [(i - distance, i) for i in devices if i - distance in devices]
    return lax.ppermute(block, axis, route)


def neighbour_sums(padded):
    interior = padded[1:-1, 1:-1]
    flat_sum = padded[2:, 1:-1] + padded[:-2, 1:-1] + padded[1:-1, 2:] + padded[1:-1, :-2]
    padded_z = jnp.pad(interior, ((0, 0), (0, 0), (1, 1)))
    vertical = padded_z[:, :, 2:] + padded_z[:, :, :-2]
    return (flat_sum, vertical)


def checker(span_x, span_y, span_z):
    index_x = jnp.arange(span_x, dtype=jnp.int32)[:, None, None]
    index_y = jnp.arange(span_y, dtype=jnp.int32)[None, :, None]
    index_z = jnp.arange(span_z, dtype=jnp.int32)[None, None, :]
    return (index_x + index_y + index_z) % 2


def whole_rims(iterate, wanted):
    return extended(iterate, (("gx", 0), ("gy", 1)), 1)


def half_sweep(iterate, source, divisor, weight, movable, colour, padder):
    flat_sum, vertical = neighbour_sums(padder(iterate, 1 - colour))
    renewed = (source + weight * flat_sum + vertical) / divisor
    span_x, span_y, span_z = iterate.shape
    update = checker(span_x, span_y, span_z) == colour
    if movable is not None:
        update = jnp.logical_and(update, movable)
    return jnp.where(update, renewed, iterate)


def full_sweep(iterate, source, divisor, weight, movable, padder):
    iterate = half_sweep(iterate, source, divisor, weight, movable, 0, padder)
    return half_sweep(iterate, source, divisor, weight, movable, 1, padder)


def restrict(values):
    paired = values.reshape(values.shape[0] // 2, 2, values.shape[1], values.shape[2])
    even_rows, odd_rows = (paired[:, 0], paired[:, 1])
    from_below = shifted(odd_rows[-1:], "gx", 1)
    before = jnp.concatenate([from_below, odd_rows[:-1]], axis=0)
    across = 0.25 * before + 0.5 * even_rows + 0.25 * odd_rows
    paired = across.reshape(across.shape[0], across.shape[1] // 2, 2, across.shape[2])
    even_rows, odd_rows = (paired[:, :, 0], paired[:, :, 1])
    from_below = shifted(odd_rows[:, -1:], "gy", 1)
    before = jnp.concatenate([from_below, odd_rows[:, :-1]], axis=1)
    return 0.25 * before + 0.5 * even_rows + 0.25 * odd_rows


def coarsen(values):
    paired = values.reshape(values.shape[0] // 2, 2, values.shape[1], values.shape[2])
    across = 0.5 * (paired[:, 0] + paired[:, 1])
    paired = across.reshape(across.shape[0], across.shape[1] // 2, 2, across.shape[2])
    return 0.5 * (paired[:, :, 0] + paired[:, :, 1])


def coarsest_solve(source, coefficient, weight, padder):
    divisor = 4.0 * weight + 2.0 + coefficient
    iterate = jnp.zeros_like(source)
    for sweep_index in range(COARSE_SWEEPS):
        iterate = full_sweep(iterate, source, divisor, weight, None, padder)
    return iterate


def solve_level(grid_level, source, coefficient, iterate, movable, padder):
    weight = 0.25**grid_level
    if grid_level == LEVELS - 1:
        return coarsest_solve(source, coefficient, weight, padder)
    divisor = 4.0 * weight + 2.0 + coefficient
    iterate = full_sweep(iterate, source, divisor, weight, movable, padder)
    flat_sum, vertical = neighbour_sums(whole_rims(iterate, 0))
    residual = source - (divisor * iterate - (weight * flat_sum + vertical))
    if movable is not None:
        residual = jnp.where(movable, residual, 0.0)
    coarse_source = restrict(residual)
    coarse_coefficient = coarsen(coefficient)
    coarse = solve_level(
        grid_level + 1,
        coarse_source,
        coarse_coefficient,
        jnp.zeros_like(coarse_source),
        None,
        padder,
    )
    lifted = jnp.repeat(jnp.repeat(coarse, 2, axis=0), 2, axis=1)
    if movable is not None:
        lifted = jnp.where(movable, lifted, 0.0)
    iterate = iterate + lifted
    iterate = full_sweep(iterate, source, divisor, weight, movable, padder)
    return iterate


def body(potential, charge, region, electrode_volts):
    movable = region == 0
    dirichlet = jnp.zeros_like(potential)
    for electrode in range(electrode_volts.shape[0]):
        dirichlet = dirichlet + jnp.where(
            region == electrode + 1, electrode_volts[electrode], jnp.float32(0.0)
        )
    flat_sum, vertical = neighbour_sums(whole_rims(potential, 0))
    source = (
        charge - (6.0 * potential - (flat_sum + vertical)) - screen * (jnp.exp(potential) - 1.0)
    )
    coefficient = screen * jnp.exp(potential)
    return solve_level(0, source, coefficient, dirichlet, movable, whole_rims)


def solution(mesh):
    placed = (P("gx", "gy", None), P("gx", "gy", None), P("gx", "gy", None), P())
    return jax.shard_map(
        body, mesh=mesh, in_specs=placed, out_specs=P("gx", "gy", None), check_vma=False
    )
```

profile of v0, /device:TPU:57, one launch (start us, length us, event | category | flops | bytes accessed | tf_op | source)
XLA Modules:
  0.0 566.1 jit_solution(6499397895903773911)
XLA Ops:
  2.0 11.3 %select_add_fusion.1 = f32[16,16,256]{2,1,0:T(8,128)S(1)} fusion(s32[16,16,256]{2,1,0:T(8,128)} %param.6, f32[]{:T(128)} %bitcast.15, f32[]{:T(128)} %bitcast.14, f32[]{:T(128)} %bitcast.13, f32[]{:T(128)} %bitcast.12, f32[]{:T(128)} %bitcast.11, f32[]{:T(128)} %bitcast.10, f32[]{:T(128)} %bitcast.9, f32[]{:T(128)} %bitcast.8, f32[]{:T(128)} %bitcast.7, ...), kind=kLoop, calls=%fused_computation.109 | loop fusion | flops 3080192 | bytes 524352 | tf_op jit(solution)/shard_map/add | solution.py:126
  13.2 5.9 %collective-permute-start.5 = (f32[1,16,256]{2,1,0:T(8,128)S(1)}, f32[1,16,256]{2,1,0:T(8,128)S(1)}, u32[]{:S(2)}, u32[]{:S(2)}) collective-permute-start(f32[1,16,256]{2,1,0:T(8,128)S(1)} %get-tuple-element.43), channel_id=1, source_target_pairs={{0,64},{64,128},{128,192},{192,256},{256,320},{320,384},{384,448},... | collective-permute-start | bytes 49160 | tf_op jit(solution)/shard_map/ppermute | solution.py:18
  21.1 4.2 collective-permute-start
  25.3 6.2 %collective-permute-start.1 = (f32[1,16,256]{2,1,0:T(8,128)S(1)}, f32[1,16,256]{2,1,0:T(8,128)S(1)}, u32[]{:S(2)}, u32[]{:S(2)}) collective-permute-start(f32[1,16,256]{2,1,0:T(8,128)S(1)} %get-tuple-element.42), channel_id=1, source_target_pairs={{0,64},{64,128},{128,192},{192,256},{256,320},{320,384},{384,448},... | collective-permute-start | bytes 49160 | tf_op jit(solution)/shard_map/ppermute | solution.py:18
  31.6 17.8 %collective-permute-start.6 = (f32[18,1,256]{2,1,0:T(1,128)S(1)}, f32[18,1,256]{2,1,0:T(1,128)S(1)}, u32[]{:S(2)}, u32[]{:S(2)}) collective-permute-start(f32[18,1,256]{2,1,0:T(1,128)S(1)} %get-tuple-element.27), channel_id=1, source_target_pairs={{1,0},{2,1},{3,2},{4,3},{5,4},{6,5},{7,6},{8,7},{9,8},{10,9},{11,1... | collective-permute-start | bytes 55304 | tf_op jit(solution)/shard_map/ppermute | solution.py:21
  51.5 5.6 collective-permute-start.2
  59.0 4.6 collective-permute-done.3
  64.3 4.4 collective-permute-start.9
  70.7 7.9 %collective-permute-done.8 = f32[1,16,256]{2,1,0:T(8,128)S(1)} collective-permute-done((f32[1,16,256]{2,1,0:T(8,128)S(1)}, f32[1,16,256]{2,1,0:T(8,128)S(1)}, u32[]{:S(2)}, u32[]{:S(2)}) %collective-permute-start.8) | collective-permute-done | bytes 16416 | tf_op jit(solution)/shard_map/ppermute | solution.py:21
  80.6 3.4 collective-permute-start.11
  88.8 8.4 %collective-permute-start.13 = (f32[1,16,256]{2,1,0:T(8,128)S(1)}, f32[1,16,256]{2,1,0:T(8,128)S(1)}, u32[]{:S(2)}, u32[]{:S(2)}) collective-permute-start(f32[1,16,256]{2,1,0:T(8,128)S(1)} %get-tuple-element.37), channel_id=1, source_target_pairs={{0,64},{64,128},{128,192},{192,256},{256,320},{320,384},{384,448},... | collective-permute-start | bytes 49160 | tf_op jit(solution)/shard_map/ppermute | solution.py:18
  99.2 7.9 %collective-permute-done.12 = f32[1,16,256]{2,1,0:T(8,128)S(1)} collective-permute-done((f32[1,16,256]{2,1,0:T(8,128)S(1)}, f32[1,16,256]{2,1,0:T(8,128)S(1)}, u32[]{:S(2)}, u32[]{:S(2)}) %collective-permute-start.12) | collective-permute-done | bytes 16416 | tf_op jit(solution)/shard_map/ppermute | solution.py:21
  107.2 3.8 collective-permute-start.14
  112.9 5.5 collective-permute-start.20
  126.6 4.7 collective-permute-done.17
  131.5 9.9 %collective-permute-start.23 = (f32[1,8,256]{2,1,0:T(8,128)S(1)}, f32[1,8,256]{2,1,0:T(8,128)S(1)}, u32[]{:S(2)}, u32[]{:S(2)}) collective-permute-start(f32[1,8,256]{2,1,0:T(8,128)S(1)} %get-tuple-element.67), channel_id=1, source_target_pairs={{0,64},{64,128},{128,192},{192,256},{256,320},{320,384},{384,448},... | collective-permute-start | bytes 24584 | tf_op jit(solution)/shard_map/ppermute | solution.py:18
  143.3 8.4 %collective-permute-start.47 = (f32[1,2,256]{2,1,0:T(2,128)S(1)}, f32[1,2,256]{2,1,0:T(2,128)S(1)}, u32[]{:S(2)}, u32[]{:S(2)}) collective-permute-start(f32[1,2,256]{2,1,0:T(2,128)S(1)} %broadcast.289), channel_id=1, source_target_pairs={{0,64},{64,128},{128,192},{192,256},{256,320},{320,384},{384,448},... | collective-permute-start | bytes 6152 | tf_op jit(solution)/shard_map/ppermute | solution.py:18
  153.7 8.4 %collective-permute-start.33 = (f32[1,4,256]{2,1,0:T(4,128)S(1)}, f32[1,4,256]{2,1,0:T(4,128)S(1)}, u32[]{:S(2)}, u32[]{:S(2)}) collective-permute-start(f32[1,4,256]{2,1,0:T(4,128)S(1)} %broadcast.281), channel_id=1, source_target_pairs={{0,64},{64,128},{128,192},{192,256},{256,320},{320,384},{384,448},... | collective-permute-start | bytes 12296 | tf_op jit(solution)/shard_map/ppermute | solution.py:18
  162.2 3.6 collective-permute-start.24
  172.5 5.8 %collective-permute-start.27 = (f32[1,8,256]{2,1,0:T(8,128)S(1)}, f32[1,8,256]{2,1,0:T(8,128)S(1)}, u32[]{:S(2)}, u32[]{:S(2)}) collective-permute-start(f32[1,8,256]{2,1,0:T(8,128)S(1)} %get-tuple-element.65), channel_id=1, source_target_pairs={{0,64},{64,128},{128,192},{192,256},{256,320},{320,384},{384,448},... | collective-permute-start | bytes 24584 | tf_op jit(solution)/shard_map/ppermute | solution.py:18
  180.3 5.5 collective-permute-start.34
  188.1 5.5 collective-permute-start.28
  200.2 4.0 collective-permute-start.30
  207.1 4.5 collective-permute-done.31
  211.7 10.1 %collective-permute-start.37 = (f32[1,4,256]{2,1,0:T(4,128)S(1)}, f32[1,4,256]{2,1,0:T(4,128)S(1)}, u32[]{:S(2)}, u32[]{:S(2)}) collective-permute-start(f32[1,4,256]{2,1,0:T(4,128)S(1)} %get-tuple-element.93), channel_id=1, source_target_pairs={{0,64},{64,128},{128,192},{192,256},{256,320},{320,384},{384,448},... | collective-permute-start | bytes 12296 | tf_op jit(solution)/shard_map/ppermute | solution.py:18
  223.8 7.8 %collective-permute-done.36 = f32[1,4,256]{2,1,0:T(4,128)S(1)} collective-permute-done((f32[1,4,256]{2,1,0:T(4,128)S(1)}, f32[1,4,256]{2,1,0:T(4,128)S(1)}, u32[]{:S(2)}, u32[]{:S(2)}) %collective-permute-start.36) | collective-permute-done | bytes 4128 | tf_op jit(solution)/shard_map/ppermute | solution.py:21
  233.6 3.4 collective-permute-start.39
  240.1 3.3 collective-permute-start.41
  247.4 3.4 collective-permute-start.49
  255.2 3.4 collective-permute-start.43
  258.6 3.1 collective-permute-done.43
  261.8 9.7 %collective-permute-start.44 = (f32[1,4,256]{2,1,0:T(4,128)S(1)}, f32[1,4,256]{2,1,0:T(4,128)S(1)}, u32[]{:S(2)}, u32[]{:S(2)}) collective-permute-start(f32[1,4,256]{2,1,0:T(4,128)S(1)} %get-tuple-element.87), channel_id=1, source_target_pairs={{0,64},{64,128},{128,192},{192,256},{256,320},{320,384},{384,448},... | collective-permute-start | bytes 12296 | tf_op jit(solution)/shard_map/ppermute | solution.py:29
  274.3 4.5 collective-permute-done.45
  278.9 10.1 %collective-permute-start.51 = (f32[1,2,256]{2,1,0:T(2,128)S(1)}, f32[1,2,256]{2,1,0:T(2,128)S(1)}, u32[]{:S(2)}, u32[]{:S(2)}) collective-permute-start(f32[1,2,256]{2,1,0:T(2,128)S(1)} %get-tuple-element.127), channel_id=1, source_target_pairs={{0,64},{64,128},{128,192},{192,256},{256,320},{320,384},{384,448},... | collective-permute-start | bytes 6152 | tf_op jit(solution)/shard_map/ppermute | solution.py:18
  291.0 7.8 %collective-permute-done.50 = f32[1,2,256]{2,1,0:T(2,128)S(1)} collective-permute-done((f32[1,2,256]{2,1,0:T(2,128)S(1)}, f32[1,2,256]{2,1,0:T(2,128)S(1)}, u32[]{:S(2)}, u32[]{:S(2)}) %collective-permute-start.50) | collective-permute-done | bytes 2080 | tf_op jit(solution)/shard_map/ppermute | solution.py:21
  300.7 3.4 collective-permute-start.53
  312.3 7.8 %collective-permute-done.54 = f32[1,2,256]{2,1,0:T(2,128)S(1)} collective-permute-done((f32[1,2,256]{2,1,0:T(2,128)S(1)}, f32[1,2,256]{2,1,0:T(2,128)S(1)}, u32[]{:S(2)}, u32[]{:S(2)}) %collective-permute-start.54) | collective-permute-done | bytes 2080 | tf_op jit(solution)/shard_map/ppermute | solution.py:21
  322.1 3.4 collective-permute-start.57
  333.7 7.8 %collective-permute-done.58 = f32[1,2,256]{2,1,0:T(2,128)S(1)} collective-permute-done((f32[1,2,256]{2,1,0:T(2,128)S(1)}, f32[1,2,256]{2,1,0:T(2,128)S(1)}, u32[]{:S(2)}, u32[]{:S(2)}) %collective-permute-start.58) | collective-permute-done | bytes 2080 | tf_op jit(solution)/shard_map/ppermute | solution.py:21
  343.4 3.4 collective-permute-start.61
  355.0 7.8 %collective-permute-done.62 = f32[1,2,256]{2,1,0:T(2,128)S(1)} collective-permute-done((f32[1,2,256]{2,1,0:T(2,128)S(1)}, f32[1,2,256]{2,1,0:T(2,128)S(1)}, u32[]{:S(2)}, u32[]{:S(2)}) %collective-permute-start.62) | collective-permute-done | bytes 2080 | tf_op jit(solution)/shard_map/ppermute | solution.py:21
  364.7 3.4 collective-permute-start.65
  376.3 7.8 %collective-permute-done.66 = f32[1,2,256]{2,1,0:T(2,128)S(1)} collective-permute-done((f32[1,2,256]{2,1,0:T(2,128)S(1)}, f32[1,2,256]{2,1,0:T(2,128)S(1)}, u32[]{:S(2)}, u32[]{:S(2)}) %collective-permute-start.66) | collective-permute-done | bytes 2080 | tf_op jit(solution)/shard_map/ppermute | solution.py:21
  386.0 3.4 collective-permute-start.69
  397.6 7.8 %collective-permute-done.70 = f32[1,2,256]{2,1,0:T(2,128)S(1)} collective-permute-done((f32[1,2,256]{2,1,0:T(2,128)S(1)}, f32[1,2,256]{2,1,0:T(2,128)S(1)}, u32[]{:S(2)}, u32[]{:S(2)}) %collective-permute-start.70) | collective-permute-done | bytes 2080 | tf_op jit(solution)/shard_map/ppermute | solution.py:21
  407.4 3.4 collective-permute-start.73
  419.0 7.8 %collective-permute-done.74 = f32[1,2,256]{2,1,0:T(2,128)S(1)} collective-permute-done((f32[1,2,256]{2,1,0:T(2,128)S(1)}, f32[1,2,256]{2,1,0:T(2,128)S(1)}, u32[]{:S(2)}, u32[]{:S(2)}) %collective-permute-start.74) | collective-permute-done | bytes 2080 | tf_op jit(solution)/shard_map/ppermute | solution.py:21
  428.7 3.4 collective-permute-start.77
  440.4 7.8 %collective-permute-done.78 = f32[1,4,256]{2,1,0:T(4,128)S(1)} collective-permute-done((f32[1,4,256]{2,1,0:T(4,128)S(1)}, f32[1,4,256]{2,1,0:T(4,128)S(1)}, u32[]{:S(2)}, u32[]{:S(2)}) %collective-permute-start.78) | collective-permute-done | bytes 4128 | tf_op jit(solution)/shard_map/ppermute | solution.py:21
  450.1 3.4 collective-permute-start.81
  461.7 7.8 %collective-permute-done.82 = f32[1,4,256]{2,1,0:T(4,128)S(1)} collective-permute-done((f32[1,4,256]{2,1,0:T(4,128)S(1)}, f32[1,4,256]{2,1,0:T(4,128)S(1)}, u32[]{:S(2)}, u32[]{:S(2)}) %collective-permute-start.82) | collective-permute-done | bytes 4128 | tf_op jit(solution)/shard_map/ppermute | solution.py:21
  471.5 3.4 collective-permute-start.85
  483.2 7.8 %collective-permute-done.86 = f32[1,8,256]{2,1,0:T(8,128)S(1)} collective-permute-done((f32[1,8,256]{2,1,0:T(8,128)S(1)}, f32[1,8,256]{2,1,0:T(8,128)S(1)}, u32[]{:S(2)}, u32[]{:S(2)}) %collective-permute-start.86) | collective-permute-done | bytes 8224 | tf_op jit(solution)/shard_map/ppermute | solution.py:21
  493.0 3.4 collective-permute-start.89
  496.4 3.1 collective-permute-done.89
  504.7 7.8 %collective-permute-done.90 = f32[1,8,256]{2,1,0:T(8,128)S(1)} collective-permute-done((f32[1,8,256]{2,1,0:T(8,128)S(1)}, f32[1,8,256]{2,1,0:T(8,128)S(1)}, u32[]{:S(2)}, u32[]{:S(2)}) %collective-permute-start.90) | collective-permute-done | bytes 8224 | tf_op jit(solution)/shard_map/ppermute | solution.py:21
  514.5 3.4 collective-permute-start.93
  517.9 3.1 collective-permute-done.93
  526.6 7.9 %collective-permute-done.94 = f32[1,16,256]{2,1,0:T(8,128)S(1)} collective-permute-done((f32[1,16,256]{2,1,0:T(8,128)S(1)}, f32[1,16,256]{2,1,0:T(8,128)S(1)}, u32[]{:S(2)}, u32[]{:S(2)}) %collective-permute-start.94) | collective-permute-done | bytes 16416 | tf_op jit(solution)/shard_map/ppermute | solution.py:21
  536.5 3.4 collective-permute-start.97
  539.9 3.2 collective-permute-done.97
  548.5 7.9 %collective-permute-done.98 = f32[1,16,256]{2,1,0:T(8,128)S(1)} collective-permute-done((f32[1,16,256]{2,1,0:T(8,128)S(1)}, f32[1,16,256]{2,1,0:T(8,128)S(1)}, u32[]{:S(2)}, u32[]{:S(2)}) %collective-permute-start.98) | collective-permute-done | bytes 16416 | tf_op jit(solution)/shard_map/ppermute | solution.py:21
  558.4 3.4 collective-permute-start.101
  561.8 3.2 collective-permute-done.101
  (290 shorter events, 189.8 us)
Async XLA Ops:
  13.2 18.3 %collective-permute-start.5 = (f32[1,16,256]{2,1,0:T(8,128)S(1)}, f32[1,16,256]{2,1,0:T(8,128)S(1)}, u32[]{:S(2)}, u32[]{:S(2)}) collective-permute-start(f32[1,16,256]{2,1,0:T(8,128)S(1)} %get-tuple-element.43), channel_id=1, source_target_pairs={{0,64},{64,128},{128,192},{192,256},{256,320},{320,384},{384,448},... | collective-permute-start | bytes 49160 | tf_op jit(solution)/shard_map/ppermute | solution.py:18
  19.2 12.3 %collective-permute-start.4 = (f32[1,16,256]{2,1,0:T(8,128)S(1)}, f32[1,16,256]{2,1,0:T(8,128)S(1)}, u32[]{:S(2)}, u32[]{:S(2)}) collective-permute-start(f32[1,16,256]{2,1,0:T(8,128)S(1)} %get-tuple-element.44), channel_id=1, source_target_pairs={{64,0},{128,64},{192,128},{256,192},{320,256},{384,320},{448,384},... | collective-permute-start | bytes 49160 | tf_op jit(solution)/shard_map/ppermute | solution.py:21
  21.1 30.3 %collective-permute-start = (f32[1,16,256]{2,1,0:T(8,128)S(1)}, f32[1,16,256]{2,1,0:T(8,128)S(1)}, u32[]{:S(2)}, u32[]{:S(2)}) collective-permute-start(f32[1,16,256]{2,1,0:T(8,128)S(1)} %get-tuple-element.41), channel_id=1, source_target_pairs={{64,0},{128,64},{192,128},{256,192},{320,256},{384,320},{448,384},... | collective-permute-start | bytes 49160 | tf_op jit(solution)/shard_map/ppermute | solution.py:21
  25.3 26.0 %collective-permute-start.1 = (f32[1,16,256]{2,1,0:T(8,128)S(1)}, f32[1,16,256]{2,1,0:T(8,128)S(1)}, u32[]{:S(2)}, u32[]{:S(2)}) collective-permute-start(f32[1,16,256]{2,1,0:T(8,128)S(1)} %get-tuple-element.42), channel_id=1, source_target_pairs={{0,64},{64,128},{128,192},{192,256},{256,320},{320,384},{384,448},... | collective-permute-start | bytes 49160 | tf_op jit(solution)/shard_map/ppermute | solution.py:18
  31.6 27.5 %collective-permute-start.6 = (f32[18,1,256]{2,1,0:T(1,128)S(1)}, f32[18,1,256]{2,1,0:T(1,128)S(1)}, u32[]{:S(2)}, u32[]{:S(2)}) collective-permute-start(f32[18,1,256]{2,1,0:T(1,128)S(1)} %get-tuple-element.27), channel_id=1, source_target_pairs={{1,0},{2,1},{3,2},{4,3},{5,4},{6,5},{7,6},{8,7},{9,8},{10,9},{11,1... | collective-permute-start | bytes 55304 | tf_op jit(solution)/shard_map/ppermute | solution.py:21
  49.4 9.6 %collective-permute-start.7 = (f32[18,1,256]{2,1,0:T(1,128)S(1)}, f32[18,1,256]{2,1,0:T(1,128)S(1)}, u32[]{:S(2)}, u32[]{:S(2)}) collective-permute-start(f32[18,1,256]{2,1,0:T(1,128)S(1)} %get-tuple-element.28), channel_id=1, source_target_pairs={{0,1},{1,2},{2,3},{3,4},{4,5},{5,6},{6,7},{7,8},{8,9},{9,10},{10,1... | collective-permute-start | bytes 55304 | tf_op jit(solution)/shard_map/ppermute | solution.py:18
  51.5 7.6 %collective-permute-start.2 = (f32[18,1,256]{2,1,0:T(1,128)S(1)}, f32[18,1,256]{2,1,0:T(1,128)S(1)}, u32[]{:S(2)}, u32[]{:S(2)}) collective-permute-start(f32[18,1,256]{2,1,0:T(1,128)S(1)} %get-tuple-element.25), channel_id=1, source_target_pairs={{1,0},{2,1},{3,2},{4,3},{5,4},{6,5},{7,6},{8,7},{9,8},{10,9},{11,1... | collective-permute-start | bytes 55304 | tf_op jit(solution)/shard_map/ppermute | solution.py:21
  57.1 6.6 %collective-permute-start.3 = (f32[18,1,256]{2,1,0:T(1,128)S(1)}, f32[18,1,256]{2,1,0:T(1,128)S(1)}, u32[]{:S(2)}, u32[]{:S(2)}) collective-permute-start(f32[18,1,256]{2,1,0:T(1,128)S(1)} %get-tuple-element.26), channel_id=1, source_target_pairs={{0,1},{1,2},{2,3},{3,4},{4,5},{5,6},{6,7},{7,8},{8,9},{9,10},{10,1... | collective-permute-start | bytes 55304 | tf_op jit(solution)/shard_map/ppermute | solution.py:18
  68.7 9.9 %collective-permute-start.8 = (f32[1,16,256]{2,1,0:T(8,128)S(1)}, f32[1,16,256]{2,1,0:T(8,128)S(1)}, u32[]{:S(2)}, u32[]{:S(2)}) collective-permute-start(f32[1,16,256]{2,1,0:T(8,128)S(1)} %get-tuple-element.40), channel_id=1, source_target_pairs={{64,0},{128,64},{192,128},{256,192},{320,256},{384,320},{448,384},... | collective-permute-start | bytes 49160 | tf_op jit(solution)/shard_map/ppermute | solution.py:21
  78.6 9.7 %collective-permute-start.10 = (f32[18,1,256]{2,1,0:T(1,128)S(1)}, f32[18,1,256]{2,1,0:T(1,128)S(1)}, u32[]{:S(2)}, u32[]{:S(2)}) collective-permute-start(f32[18,1,256]{2,1,0:T(1,128)S(1)} %get-tuple-element.23), channel_id=1, source_target_pairs={{1,0},{2,1},{3,2},{4,3},{5,4},{6,5},{7,6},{8,7},{9,8},{10,9},{11,1... | collective-permute-start | bytes 55304 | tf_op jit(solution)/shard_map/ppermute | solution.py:21
  80.6 7.8 %collective-permute-start.11 = (f32[18,1,256]{2,1,0:T(1,128)S(1)}, f32[18,1,256]{2,1,0:T(1,128)S(1)}, u32[]{:S(2)}, u32[]{:S(2)}) collective-permute-start(f32[18,1,256]{2,1,0:T(1,128)S(1)} %get-tuple-element.24), channel_id=1, source_target_pairs={{0,1},{1,2},{2,3},{3,4},{4,5},{5,6},{6,7},{7,8},{8,9},{9,10},{10,1... | collective-permute-start | bytes 55304 | tf_op jit(solution)/shard_map/ppermute | solution.py:18
  83.9 28.9 %collective-permute-start.19 = (f32[1,8,256]{2,1,0:T(8,128)S(1)}, f32[1,8,256]{2,1,0:T(8,128)S(1)}, u32[]{:S(2)}, u32[]{:S(2)}) collective-permute-start(f32[1,8,256]{2,1,0:T(8,128)S(1)} %broadcast.274), channel_id=1, source_target_pairs={{0,64},{64,128},{128,192},{192,256},{256,320},{320,384},{384,448},... | collective-permute-start | bytes 24584 | tf_op jit(solution)/shard_map/ppermute | solution.py:18
  86.4 26.4 %collective-permute-start.18 = (f32[1,8,256]{2,1,0:T(8,128)S(1)}, f32[1,8,256]{2,1,0:T(8,128)S(1)}, u32[]{:S(2)}, u32[]{:S(2)}) collective-permute-start(f32[1,8,256]{2,1,0:T(8,128)S(1)} %broadcast.274), channel_id=1, source_target_pairs={{64,0},{128,64},{192,128},{256,192},{320,256},{384,320},{448,384},... | collective-permute-start | bytes 24584 | tf_op jit(solution)/shard_map/ppermute | solution.py:21
  88.8 10.4 %collective-permute-start.13 = (f32[1,16,256]{2,1,0:T(8,128)S(1)}, f32[1,16,256]{2,1,0:T(8,128)S(1)}, u32[]{:S(2)}, u32[]{:S(2)}) collective-permute-start(f32[1,16,256]{2,1,0:T(8,128)S(1)} %get-tuple-element.37), channel_id=1, source_target_pairs={{0,64},{64,128},{128,192},{192,256},{256,320},{320,384},{384,448},... | collective-permute-start | bytes 49160 | tf_op jit(solution)/shard_map/ppermute | solution.py:18
  97.3 9.9 %collective-permute-start.12 = (f32[1,16,256]{2,1,0:T(8,128)S(1)}, f32[1,16,256]{2,1,0:T(8,128)S(1)}, u32[]{:S(2)}, u32[]{:S(2)}) collective-permute-start(f32[1,16,256]{2,1,0:T(8,128)S(1)} %get-tuple-element.38), channel_id=1, source_target_pairs={{64,0},{128,64},{192,128},{256,192},{320,256},{384,320},{448,384},... | collective-permute-start | bytes 49160 | tf_op jit(solution)/shard_map/ppermute | solution.py:21
  107.2 13.2 %collective-permute-start.14 = (f32[18,1,256]{2,1,0:T(1,128)S(1)}, f32[18,1,256]{2,1,0:T(1,128)S(1)}, u32[]{:S(2)}, u32[]{:S(2)}) collective-permute-start(f32[18,1,256]{2,1,0:T(1,128)S(1)} %get-tuple-element.21), channel_id=1, source_target_pairs={{1,0},{2,1},{3,2},{4,3},{5,4},{6,5},{7,6},{8,7},{9,8},{10,9},{11,1... | collective-permute-start | bytes 55304 | tf_op jit(solution)/shard_map/ppermute | solution.py:21
  110.9 9.4 %collective-permute-start.15 = (f32[18,1,256]{2,1,0:T(1,128)S(1)}, f32[18,1,256]{2,1,0:T(1,128)S(1)}, u32[]{:S(2)}, u32[]{:S(2)}) collective-permute-start(f32[18,1,256]{2,1,0:T(1,128)S(1)} %get-tuple-element.22), channel_id=1, source_target_pairs={{0,1},{1,2},{2,3},{3,4},{4,5},{5,6},{6,7},{7,8},{8,9},{9,10},{10,1... | collective-permute-start | bytes 55304 | tf_op jit(solution)/shard_map/ppermute | solution.py:18
  112.9 13.7 %collective-permute-start.20 = (f32[10,1,256]{2,1,0:T(1,128)S(1)}, f32[10,1,256]{2,1,0:T(1,128)S(1)}, u32[]{:S(2)}, u32[]{:S(2)}) collective-permute-start(f32[10,1,256]{2,1,0:T(1,128)S(1)} %get-tuple-element.57), channel_id=1, source_target_pairs={{1,0},{2,1},{3,2},{4,3},{5,4},{6,5},{7,6},{8,7},{9,8},{10,9},{11,1... | collective-permute-start | bytes 30728 | tf_op jit(solution)/shard_map/ppermute | solution.py:21
  118.4 8.2 %collective-permute-start.21 = (f32[10,1,256]{2,1,0:T(1,128)S(1)}, f32[10,1,256]{2,1,0:T(1,128)S(1)}, u32[]{:S(2)}, u32[]{:S(2)}) collective-permute-start(f32[10,1,256]{2,1,0:T(1,128)S(1)} %get-tuple-element.58), channel_id=1, source_target_pairs={{0,1},{1,2},{2,3},{3,4},{4,5},{5,6},{6,7},{7,8},{8,9},{9,10},{10,1... | collective-permute-start | bytes 30728 | tf_op jit(solution)/shard_map/ppermute | solution.py:18
  124.5 6.8 %collective-permute-start.17 = (f32[8,1,256]{2,1,0:T(1,128)S(1)}, f32[8,1,256]{2,1,0:T(1,128)S(1)}, u32[]{:S(2)}, u32[]{:S(2)}) collective-permute-start(f32[8,1,256]{2,1,0:T(1,128)S(1)} %slice.1274), channel_id=1, source_target_pairs={{0,1},{1,2},{2,3},{3,4},{4,5},{5,6},{6,7},{7,8},{8,9},{9,10},{10,1... | collective-permute-start | bytes 24584 | tf_op jit(solution)/shard_map/ppermute | solution.py:29
  131.5 30.7 %collective-permute-start.23 = (f32[1,8,256]{2,1,0:T(8,128)S(1)}, f32[1,8,256]{2,1,0:T(8,128)S(1)}, u32[]{:S(2)}, u32[]{:S(2)}) collective-permute-start(f32[1,8,256]{2,1,0:T(8,128)S(1)} %get-tuple-element.67), channel_id=1, source_target_pairs={{0,64},{64,128},{128,192},{192,256},{256,320},{320,384},{384,448},... | collective-permute-start | bytes 24584 | tf_op jit(solution)/shard_map/ppermute | solution.py:18
  141.3 20.8 %collective-permute-start.22 = (f32[1,8,256]{2,1,0:T(8,128)S(1)}, f32[1,8,256]{2,1,0:T(8,128)S(1)}, u32[]{:S(2)}, u32[]{:S(2)}) collective-permute-start(f32[1,8,256]{2,1,0:T(8,128)S(1)} %get-tuple-element.68), channel_id=1, source_target_pairs={{64,0},{128,64},{192,128},{256,192},{320,256},{384,320},{448,384},... | collective-permute-start | bytes 24584 | tf_op jit(solution)/shard_map/ppermute | solution.py:21
  143.3 93.6 %collective-permute-start.47 = (f32[1,2,256]{2,1,0:T(2,128)S(1)}, f32[1,2,256]{2,1,0:T(2,128)S(1)}, u32[]{:S(2)}, u32[]{:S(2)}) collective-permute-start(f32[1,2,256]{2,1,0:T(2,128)S(1)} %broadcast.289), channel_id=1, source_target_pairs={{0,64},{64,128},{128,192},{192,256},{256,320},{320,384},{384,448},... | collective-permute-start | bytes 6152 | tf_op jit(solution)/shard_map/ppermute | solution.py:18
  151.7 85.2 %collective-permute-start.46 = (f32[1,2,256]{2,1,0:T(2,128)S(1)}, f32[1,2,256]{2,1,0:T(2,128)S(1)}, u32[]{:S(2)}, u32[]{:S(2)}) collective-permute-start(f32[1,2,256]{2,1,0:T(2,128)S(1)} %broadcast.289), channel_id=1, source_target_pairs={{64,0},{128,64},{192,128},{256,192},{320,256},{384,320},{448,384},... | collective-permute-start | bytes 6152 | tf_op jit(solution)/shard_map/ppermute | solution.py:21
  153.7 24.6 %collective-permute-start.33 = (f32[1,4,256]{2,1,0:T(4,128)S(1)}, f32[1,4,256]{2,1,0:T(4,128)S(1)}, u32[]{:S(2)}, u32[]{:S(2)}) collective-permute-start(f32[1,4,256]{2,1,0:T(4,128)S(1)} %broadcast.281), channel_id=1, source_target_pairs={{0,64},{64,128},{128,192},{192,256},{256,320},{320,384},{384,448},... | collective-permute-start | bytes 12296 | tf_op jit(solution)/shard_map/ppermute | solution.py:18
  165.8 6.5 %collective-permute-start.25 = (f32[10,1,256]{2,1,0:T(1,128)S(1)}, f32[10,1,256]{2,1,0:T(1,128)S(1)}, u32[]{:S(2)}, u32[]{:S(2)}) collective-permute-start(f32[10,1,256]{2,1,0:T(1,128)S(1)} %get-tuple-element.56), channel_id=1, source_target_pairs={{0,1},{1,2},{2,3},{3,4},{4,5},{5,6},{6,7},{7,8},{8,9},{9,10},{10,1... | collective-permute-start | bytes 30728 | tf_op jit(solution)/shard_map/ppermute | solution.py:18
  167.8 12.5 %collective-permute-start.32 = (f32[1,4,256]{2,1,0:T(4,128)S(1)}, f32[1,4,256]{2,1,0:T(4,128)S(1)}, u32[]{:S(2)}, u32[]{:S(2)}) collective-permute-start(f32[1,4,256]{2,1,0:T(4,128)S(1)} %broadcast.281), channel_id=1, source_target_pairs={{64,0},{128,64},{192,128},{256,192},{320,256},{384,320},{448,384},... | collective-permute-start | bytes 12296 | tf_op jit(solution)/shard_map/ppermute | solution.py:21
  172.5 13.3 %collective-permute-start.27 = (f32[1,8,256]{2,1,0:T(8,128)S(1)}, f32[1,8,256]{2,1,0:T(8,128)S(1)}, u32[]{:S(2)}, u32[]{:S(2)}) collective-permute-start(f32[1,8,256]{2,1,0:T(8,128)S(1)} %get-tuple-element.65), channel_id=1, source_target_pairs={{0,64},{64,128},{128,192},{192,256},{256,320},{320,384},{384,448},... | collective-permute-start | bytes 24584 | tf_op jit(solution)/shard_map/ppermute | solution.py:18
  178.3 9.8 %collective-permute-start.26 = (f32[1,8,256]{2,1,0:T(8,128)S(1)}, f32[1,8,256]{2,1,0:T(8,128)S(1)}, u32[]{:S(2)}, u32[]{:S(2)}) collective-permute-start(f32[1,8,256]{2,1,0:T(8,128)S(1)} %get-tuple-element.66), channel_id=1, source_target_pairs={{64,0},{128,64},{192,128},{256,192},{320,256},{384,320},{448,384},... | collective-permute-start | bytes 24584 | tf_op jit(solution)/shard_map/ppermute | solution.py:21
  180.3 26.8 %collective-permute-start.34 = (f32[6,1,256]{2,1,0:T(1,128)S(1)}, f32[6,1,256]{2,1,0:T(1,128)S(1)}, u32[]{:S(2)}, u32[]{:S(2)}) collective-permute-start(f32[6,1,256]{2,1,0:T(1,128)S(1)} %get-tuple-element.81), channel_id=1, source_target_pairs={{1,0},{2,1},{3,2},{4,3},{5,4},{6,5},{7,6},{8,7},{9,8},{10,9},{11,1... | collective-permute-start | bytes 18440 | tf_op jit(solution)/shard_map/ppermute | solution.py:21
  188.1 7.5 %collective-permute-start.28 = (f32[10,1,256]{2,1,0:T(1,128)S(1)}, f32[10,1,256]{2,1,0:T(1,128)S(1)}, u32[]{:S(2)}, u32[]{:S(2)}) collective-permute-start(f32[10,1,256]{2,1,0:T(1,128)S(1)} %get-tuple-element.53), channel_id=1, source_target_pairs={{1,0},{2,1},{3,2},{4,3},{5,4},{6,5},{7,6},{8,7},{9,8},{10,9},{11,1... | collective-permute-start | bytes 30728 | tf_op jit(solution)/shard_map/ppermute | solution.py:21
  193.6 6.5 %collective-permute-start.29 = (f32[10,1,256]{2,1,0:T(1,128)S(1)}, f32[10,1,256]{2,1,0:T(1,128)S(1)}, u32[]{:S(2)}, u32[]{:S(2)}) collective-permute-start(f32[10,1,256]{2,1,0:T(1,128)S(1)} %get-tuple-element.54), channel_id=1, source_target_pairs={{0,1},{1,2},{2,3},{3,4},{4,5},{5,6},{6,7},{7,8},{8,9},{9,10},{10,1... | collective-permute-start | bytes 30728 | tf_op jit(solution)/shard_map/ppermute | solution.py:18
  195.6 11.6 %collective-permute-start.35 = (f32[6,1,256]{2,1,0:T(1,128)S(1)}, f32[6,1,256]{2,1,0:T(1,128)S(1)}, u32[]{:S(2)}, u32[]{:S(2)}) collective-permute-start(f32[6,1,256]{2,1,0:T(1,128)S(1)} %get-tuple-element.82), channel_id=1, source_target_pairs={{0,1},{1,2},{2,3},{3,4},{4,5},{5,6},{6,7},{7,8},{8,9},{9,10},{10,1... | collective-permute-start | bytes 18440 | tf_op jit(solution)/shard_map/ppermute | solution.py:18
  205.2 6.5 %collective-permute-start.31 = (f32[4,1,256]{2,1,0:T(1,128)S(1)}, f32[4,1,256]{2,1,0:T(1,128)S(1)}, u32[]{:S(2)}, u32[]{:S(2)}) collective-permute-start(f32[4,1,256]{2,1,0:T(1,128)S(1)} %slice.1290), channel_id=1, source_target_pairs={{0,1},{1,2},{2,3},{3,4},{4,5},{5,6},{6,7},{7,8},{8,9},{9,10},{10,1... | collective-permute-start | bytes 12296 | tf_op jit(solution)/shard_map/ppermute | solution.py:29
  211.7 12.1 %collective-permute-start.37 = (f32[1,4,256]{2,1,0:T(4,128)S(1)}, f32[1,4,256]{2,1,0:T(4,128)S(1)}, u32[]{:S(2)}, u32[]{:S(2)}) collective-permute-start(f32[1,4,256]{2,1,0:T(4,128)S(1)} %get-tuple-element.93), channel_id=1, source_target_pairs={{0,64},{64,128},{128,192},{192,256},{256,320},{320,384},{384,448},... | collective-permute-start | bytes 12296 | tf_op jit(solution)/shard_map/ppermute | solution.py:18
  221.9 9.7 %collective-permute-start.36 = (f32[1,4,256]{2,1,0:T(4,128)S(1)}, f32[1,4,256]{2,1,0:T(4,128)S(1)}, u32[]{:S(2)}, u32[]{:S(2)}) collective-permute-start(f32[1,4,256]{2,1,0:T(4,128)S(1)} %get-tuple-element.94), channel_id=1, source_target_pairs={{64,0},{128,64},{192,128},{256,192},{320,256},{384,320},{448,384},... | collective-permute-start | bytes 12296 | tf_op jit(solution)/shard_map/ppermute | solution.py:21
  233.6 6.5 %collective-permute-start.39 = (f32[6,1,256]{2,1,0:T(1,128)S(1)}, f32[6,1,256]{2,1,0:T(1,128)S(1)}, u32[]{:S(2)}, u32[]{:S(2)}) collective-permute-start(f32[6,1,256]{2,1,0:T(1,128)S(1)} %get-tuple-element.80), channel_id=1, source_target_pairs={{0,1},{1,2},{2,3},{3,4},{4,5},{5,6},{6,7},{7,8},{8,9},{9,10},{10,1... | collective-permute-start | bytes 18440 | tf_op jit(solution)/shard_map/ppermute | solution.py:18
  240.1 10.6 %collective-permute-start.41 = (f32[1,4,256]{2,1,0:T(4,128)S(1)}, f32[1,4,256]{2,1,0:T(4,128)S(1)}, u32[]{:S(2)}, u32[]{:S(2)}) collective-permute-start(f32[1,4,256]{2,1,0:T(4,128)S(1)} %get-tuple-element.91), channel_id=1, source_target_pairs={{0,64},{64,128},{128,192},{192,256},{256,320},{320,384},{384,448},... | collective-permute-start | bytes 12296 | tf_op jit(solution)/shard_map/ppermute | solution.py:18
  243.5 9.7 %collective-permute-start.40 = (f32[1,4,256]{2,1,0:T(4,128)S(1)}, f32[1,4,256]{2,1,0:T(4,128)S(1)}, u32[]{:S(2)}, u32[]{:S(2)}) collective-permute-start(f32[1,4,256]{2,1,0:T(4,128)S(1)} %get-tuple-element.92), channel_id=1, source_target_pairs={{64,0},{128,64},{192,128},{256,192},{320,256},{384,320},{448,384},... | collective-permute-start | bytes 12296 | tf_op jit(solution)/shard_map/ppermute | solution.py:21
  245.4 28.9 %collective-permute-start.48 = (f32[4,1,256]{2,1,0:T(1,128)S(1)}, f32[4,1,256]{2,1,0:T(1,128)S(1)}, u32[]{:S(2)}, u32[]{:S(2)}) collective-permute-start(f32[4,1,256]{2,1,0:T(1,128)S(1)} %get-tuple-element.113), channel_id=1, source_target_pairs={{1,0},{2,1},{3,2},{4,3},{5,4},{6,5},{7,6},{8,7},{9,8},{10,9},{11,1... | collective-permute-start | bytes 12296 | tf_op jit(solution)/shard_map/ppermute | solution.py:21
  247.4 27.0 %collective-permute-start.49 = (f32[4,1,256]{2,1,0:T(1,128)S(1)}, f32[4,1,256]{2,1,0:T(1,128)S(1)}, u32[]{:S(2)}, u32[]{:S(2)}) collective-permute-start(f32[4,1,256]{2,1,0:T(1,128)S(1)} %get-tuple-element.114), channel_id=1, source_target_pairs={{0,1},{1,2},{2,3},{3,4},{4,5},{5,6},{6,7},{7,8},{8,9},{9,10},{10,1... | collective-permute-start | bytes 12296 | tf_op jit(solution)/shard_map/ppermute | solution.py:18
  255.2 6.5 %collective-permute-start.43 = (f32[6,1,256]{2,1,0:T(1,128)S(1)}, f32[6,1,256]{2,1,0:T(1,128)S(1)}, u32[]{:S(2)}, u32[]{:S(2)}) collective-permute-start(f32[6,1,256]{2,1,0:T(1,128)S(1)} %get-tuple-element.78), channel_id=1, source_target_pairs={{0,1},{1,2},{2,3},{3,4},{4,5},{5,6},{6,7},{7,8},{8,9},{9,10},{10,1... | collective-permute-start | bytes 18440 | tf_op jit(solution)/shard_map/ppermute | solution.py:18
  261.8 10.5 %collective-permute-start.44 = (f32[1,4,256]{2,1,0:T(4,128)S(1)}, f32[1,4,256]{2,1,0:T(4,128)S(1)}, u32[]{:S(2)}, u32[]{:S(2)}) collective-permute-start(f32[1,4,256]{2,1,0:T(4,128)S(1)} %get-tuple-element.87), channel_id=1, source_target_pairs={{0,64},{64,128},{128,192},{192,256},{256,320},{320,384},{384,448},... | collective-permute-start | bytes 12296 | tf_op jit(solution)/shard_map/ppermute | solution.py:29
  278.9 12.1 %collective-permute-start.51 = (f32[1,2,256]{2,1,0:T(2,128)S(1)}, f32[1,2,256]{2,1,0:T(2,128)S(1)}, u32[]{:S(2)}, u32[]{:S(2)}) collective-permute-start(f32[1,2,256]{2,1,0:T(2,128)S(1)} %get-tuple-element.127), channel_id=1, source_target_pairs={{0,64},{64,128},{128,192},{192,256},{256,320},{320,384},{384,448},... | collective-permute-start | bytes 6152 | tf_op jit(solution)/shard_map/ppermute | solution.py:18
  289.1 9.7 %collective-permute-start.50 = (f32[1,2,256]{2,1,0:T(2,128)S(1)}, f32[1,2,256]{2,1,0:T(2,128)S(1)}, u32[]{:S(2)}, u32[]{:S(2)}) collective-permute-start(f32[1,2,256]{2,1,0:T(2,128)S(1)} %get-tuple-element.128), channel_id=1, source_target_pairs={{64,0},{128,64},{192,128},{256,192},{320,256},{384,320},{448,384},... | collective-permute-start | bytes 6152 | tf_op jit(solution)/shard_map/ppermute | solution.py:21
  300.7 6.5 %collective-permute-start.53 = (f32[4,1,256]{2,1,0:T(1,128)S(1)}, f32[4,1,256]{2,1,0:T(1,128)S(1)}, u32[]{:S(2)}, u32[]{:S(2)}) collective-permute-start(f32[4,1,256]{2,1,0:T(1,128)S(1)} %get-tuple-element.108), channel_id=1, source_target_pairs={{0,1},{1,2},{2,3},{3,4},{4,5},{5,6},{6,7},{7,8},{8,9},{9,10},{10,1... | collective-permute-start | bytes 12296 | tf_op jit(solution)/shard_map/ppermute | solution.py:18
  310.4 9.7 %collective-permute-start.54 = (f32[1,2,256]{2,1,0:T(2,128)S(1)}, f32[1,2,256]{2,1,0:T(2,128)S(1)}, u32[]{:S(2)}, u32[]{:S(2)}) collective-permute-start(f32[1,2,256]{2,1,0:T(2,128)S(1)} %get-tuple-element.126), channel_id=1, source_target_pairs={{64,0},{128,64},{192,128},{256,192},{320,256},{384,320},{448,384},... | collective-permute-start | bytes 6152 | tf_op jit(solution)/shard_map/ppermute | solution.py:21
  331.7 9.7 %collective-permute-start.58 = (f32[1,2,256]{2,1,0:T(2,128)S(1)}, f32[1,2,256]{2,1,0:T(2,128)S(1)}, u32[]{:S(2)}, u32[]{:S(2)}) collective-permute-start(f32[1,2,256]{2,1,0:T(2,128)S(1)} %get-tuple-element.124), channel_id=1, source_target_pairs={{64,0},{128,64},{192,128},{256,192},{320,256},{384,320},{448,384},... | collective-permute-start | bytes 6152 | tf_op jit(solution)/shard_map/ppermute | solution.py:21
  353.0 9.7 %collective-permute-start.62 = (f32[1,2,256]{2,1,0:T(2,128)S(1)}, f32[1,2,256]{2,1,0:T(2,128)S(1)}, u32[]{:S(2)}, u32[]{:S(2)}) collective-permute-start(f32[1,2,256]{2,1,0:T(2,128)S(1)} %get-tuple-element.122), channel_id=1, source_target_pairs={{64,0},{128,64},{192,128},{256,192},{320,256},{384,320},{448,384},... | collective-permute-start | bytes 6152 | tf_op jit(solution)/shard_map/ppermute | solution.py:21
  374.4 9.7 %collective-permute-start.66 = (f32[1,2,256]{2,1,0:T(2,128)S(1)}, f32[1,2,256]{2,1,0:T(2,128)S(1)}, u32[]{:S(2)}, u32[]{:S(2)}) collective-permute-start(f32[1,2,256]{2,1,0:T(2,128)S(1)} %get-tuple-element.120), channel_id=1, source_target_pairs={{64,0},{128,64},{192,128},{256,192},{320,256},{384,320},{448,384},... | collective-permute-start | bytes 6152 | tf_op jit(solution)/shard_map/ppermute | solution.py:21
  395.7 9.7 %collective-permute-start.70 = (f32[1,2,256]{2,1,0:T(2,128)S(1)}, f32[1,2,256]{2,1,0:T(2,128)S(1)}, u32[]{:S(2)}, u32[]{:S(2)}) collective-permute-start(f32[1,2,256]{2,1,0:T(2,128)S(1)} %get-tuple-element.118), channel_id=1, source_target_pairs={{64,0},{128,64},{192,128},{256,192},{320,256},{384,320},{448,384},... | collective-permute-start | bytes 6152 | tf_op jit(solution)/shard_map/ppermute | solution.py:21
  417.0 9.7 %collective-permute-start.74 = (f32[1,2,256]{2,1,0:T(2,128)S(1)}, f32[1,2,256]{2,1,0:T(2,128)S(1)}, u32[]{:S(2)}, u32[]{:S(2)}) collective-permute-start(f32[1,2,256]{2,1,0:T(2,128)S(1)} %get-tuple-element.116), channel_id=1, source_target_pairs={{64,0},{128,64},{192,128},{256,192},{320,256},{384,320},{448,384},... | collective-permute-start | bytes 6152 | tf_op jit(solution)/shard_map/ppermute | solution.py:21
  438.4 9.7 %collective-permute-start.78 = (f32[1,4,256]{2,1,0:T(4,128)S(1)}, f32[1,4,256]{2,1,0:T(4,128)S(1)}, u32[]{:S(2)}, u32[]{:S(2)}) collective-permute-start(f32[1,4,256]{2,1,0:T(4,128)S(1)} %get-tuple-element.86), channel_id=1, source_target_pairs={{64,0},{128,64},{192,128},{256,192},{320,256},{384,320},{448,384},... | collective-permute-start | bytes 12296 | tf_op jit(solution)/shard_map/ppermute | solution.py:21
  450.1 6.5 %collective-permute-start.81 = (f32[6,1,256]{2,1,0:T(1,128)S(1)}, f32[6,1,256]{2,1,0:T(1,128)S(1)}, u32[]{:S(2)}, u32[]{:S(2)}) collective-permute-start(f32[6,1,256]{2,1,0:T(1,128)S(1)} %get-tuple-element.76), channel_id=1, source_target_pairs={{0,1},{1,2},{2,3},{3,4},{4,5},{5,6},{6,7},{7,8},{8,9},{9,10},{10,1... | collective-permute-start | bytes 18440 | tf_op jit(solution)/shard_map/ppermute | solution.py:18
  459.8 9.7 %collective-permute-start.82 = (f32[1,4,256]{2,1,0:T(4,128)S(1)}, f32[1,4,256]{2,1,0:T(4,128)S(1)}, u32[]{:S(2)}, u32[]{:S(2)}) collective-permute-start(f32[1,4,256]{2,1,0:T(4,128)S(1)} %get-tuple-element.84), channel_id=1, source_target_pairs={{64,0},{128,64},{192,128},{256,192},{320,256},{384,320},{448,384},... | collective-permute-start | bytes 12296 | tf_op jit(solution)/shard_map/ppermute | solution.py:21
  471.5 6.5 %collective-permute-start.85 = (f32[6,1,256]{2,1,0:T(1,128)S(1)}, f32[6,1,256]{2,1,0:T(1,128)S(1)}, u32[]{:S(2)}, u32[]{:S(2)}) collective-permute-start(f32[6,1,256]{2,1,0:T(1,128)S(1)} %get-tuple-element.74), channel_id=1, source_target_pairs={{0,1},{1,2},{2,3},{3,4},{4,5},{5,6},{6,7},{7,8},{8,9},{9,10},{10,1... | collective-permute-start | bytes 18440 | tf_op jit(solution)/shard_map/ppermute | solution.py:18
  481.3 9.8 %collective-permute-start.86 = (f32[1,8,256]{2,1,0:T(8,128)S(1)}, f32[1,8,256]{2,1,0:T(8,128)S(1)}, u32[]{:S(2)}, u32[]{:S(2)}) collective-permute-start(f32[1,8,256]{2,1,0:T(8,128)S(1)} %get-tuple-element.62), channel_id=1, source_target_pairs={{64,0},{128,64},{192,128},{256,192},{320,256},{384,320},{448,384},... | collective-permute-start | bytes 24584 | tf_op jit(solution)/shard_map/ppermute | solution.py:21
  493.0 6.5 %collective-permute-start.89 = (f32[10,1,256]{2,1,0:T(1,128)S(1)}, f32[10,1,256]{2,1,0:T(1,128)S(1)}, u32[]{:S(2)}, u32[]{:S(2)}) collective-permute-start(f32[10,1,256]{2,1,0:T(1,128)S(1)} %get-tuple-element.52), channel_id=1, source_target_pairs={{0,1},{1,2},{2,3},{3,4},{4,5},{5,6},{6,7},{7,8},{8,9},{9,10},{10,1... | collective-permute-start | bytes 30728 | tf_op jit(solution)/shard_map/ppermute | solution.py:18
  502.8 9.8 %collective-permute-start.90 = (f32[1,8,256]{2,1,0:T(8,128)S(1)}, f32[1,8,256]{2,1,0:T(8,128)S(1)}, u32[]{:S(2)}, u32[]{:S(2)}) collective-permute-start(f32[1,8,256]{2,1,0:T(8,128)S(1)} %get-tuple-element.60), channel_id=1, source_target_pairs={{64,0},{128,64},{192,128},{256,192},{320,256},{384,320},{448,384},... | collective-permute-start | bytes 24584 | tf_op jit(solution)/shard_map/ppermute | solution.py:21
  514.5 6.5 %collective-permute-start.93 = (f32[10,1,256]{2,1,0:T(1,128)S(1)}, f32[10,1,256]{2,1,0:T(1,128)S(1)}, u32[]{:S(2)}, u32[]{:S(2)}) collective-permute-start(f32[10,1,256]{2,1,0:T(1,128)S(1)} %get-tuple-element.50), channel_id=1, source_target_pairs={{0,1},{1,2},{2,3},{3,4},{4,5},{5,6},{6,7},{7,8},{8,9},{9,10},{10,1... | collective-permute-start | bytes 30728 | tf_op jit(solution)/shard_map/ppermute | solution.py:18
  524.6 9.9 %collective-permute-start.94 = (f32[1,16,256]{2,1,0:T(8,128)S(1)}, f32[1,16,256]{2,1,0:T(8,128)S(1)}, u32[]{:S(2)}, u32[]{:S(2)}) collective-permute-start(f32[1,16,256]{2,1,0:T(8,128)S(1)} %get-tuple-element.32), channel_id=1, source_target_pairs={{64,0},{128,64},{192,128},{256,192},{320,256},{384,320},{448,384},... | collective-permute-start | bytes 49160 | tf_op jit(solution)/shard_map/ppermute | solution.py:21
  536.5 6.6 %collective-permute-start.97 = (f32[18,1,256]{2,1,0:T(1,128)S(1)}, f32[18,1,256]{2,1,0:T(1,128)S(1)}, u32[]{:S(2)}, u32[]{:S(2)}) collective-permute-start(f32[18,1,256]{2,1,0:T(1,128)S(1)} %get-tuple-element.20), channel_id=1, source_target_pairs={{0,1},{1,2},{2,3},{3,4},{4,5},{5,6},{6,7},{7,8},{8,9},{9,10},{10,1... | collective-permute-start | bytes 55304 | tf_op jit(solution)/shard_map/ppermute | solution.py:18
  546.6 9.9 %collective-permute-start.98 = (f32[1,16,256]{2,1,0:T(8,128)S(1)}, f32[1,16,256]{2,1,0:T(8,128)S(1)}, u32[]{:S(2)}, u32[]{:S(2)}) collective-permute-start(f32[1,16,256]{2,1,0:T(8,128)S(1)} %get-tuple-element.30), channel_id=1, source_target_pairs={{64,0},{128,64},{192,128},{256,192},{320,256},{384,320},{448,384},... | collective-permute-start | bytes 49160 | tf_op jit(solution)/shard_map/ppermute | solution.py:21
  558.4 6.6 %collective-permute-start.101 = (f32[18,1,256]{2,1,0:T(1,128)S(1)}, f32[18,1,256]{2,1,0:T(1,128)S(1)}, u32[]{:S(2)}, u32[]{:S(2)}) collective-permute-start(f32[18,1,256]{2,1,0:T(1,128)S(1)} %get-tuple-element.18), channel_id=1, source_target_pairs={{0,1},{1,2},{2,3},{3,4},{4,5},{5,6},{6,7},{7,8},{8,9},{9,10},{10,1... | collective-permute-start | bytes 55304 | tf_op jit(solution)/shard_map/ppermute | solution.py:18
  (41 other events, 249.4 us)
where the time goes:
time: 569 us; the launch traced here: 566 us
  starting transfers between devices  342 us (60%)
  waiting for transfers between devices  202 us (36%)
  other arithmetic  16.5 us (3%)
    ppermute x48, starting transfers between devices, extended(): lax.ppermute(lax.slice_in_dim(block, block.shape[dim] - width, None, axis...  191 us
    ppermute x48, waiting for transfers between devices, extended(): lax.ppermute(lax.slice_in_dim(block, 0, width, axis=dim), axis, backward)  130 us
    ppermute x48, starting transfers between devices, extended(): lax.ppermute(lax.slice_in_dim(block, 0, width, axis=dim), axis, backward)  128 us
    ppermute x48, waiting for transfers between devices, extended(): lax.ppermute(lax.slice_in_dim(block, block.shape[dim] - width, None, axis...  56.7 us
    ppermute x6, starting transfers between devices, shifted(): return lax.ppermute(block, axis, route)  22.3 us
    ppermute x6, waiting for transfers between devices, shifted(): return lax.ppermute(block, axis, route)  15.5 us
  transfers between devices with their start and end apart: 102, of which 42 were waited for; matrix products, arithmetic and copies ran while one was open for 0% of the time, Pallas kernels for 0%

commit v1 on v0

v1 whole, which is shorter than its diff:
```python
import jax
import jax.numpy as jnp
from jax import lax
from jax.sharding import PartitionSpec as P

screen = 0.5

HALO_FINE = 4
HALO_MID = 4
HALO_COARSE = 2


def shifted(block, axis, distance):
    count = lax.axis_size(axis)
    route = [(i, i + distance) for i in range(count) if 0 <= i + distance < count]
    return lax.ppermute(block, axis, route)


def exchange(block, width):
    block = jnp.concatenate(
        [shifted(block[-width:], "gx", 1), block, shifted(block[:width], "gx", -1)], axis=0
    )
    return jnp.concatenate(
        [shifted(block[:, -width:], "gy", 1), block, shifted(block[:, :width], "gy", -1)], axis=1
    )


def exchange_many(arrays, width):
    depth = arrays[0].shape[2]
    packed = exchange(jnp.concatenate(arrays, axis=2), width)
    return [packed[:, :, i * depth:(i + 1) * depth] for i in range(len(arrays))]


def inside(span_x, span_y, width):
    index_x = lax.axis_index("gx") * span_x - width + jnp.arange(span_x + 2 * width)
    index_y = lax.axis_index("gy") * span_y - width + jnp.arange(span_y + 2 * width)
    total_x = span_x * lax.axis_size("gx")
    total_y = span_y * lax.axis_size("gy")
    keep_x = (index_x >= 0) & (index_x < total_x)
    keep_y = (index_y >= 0) & (index_y < total_y)
    return (keep_x[:, None] & keep_y[None, :])[:, :, None]


def pad_plane(values):
    return jnp.pad(values, ((1, 1), (1, 1), (0, 0)))


def neighbour_sums(padded):
    interior = padded[1:-1, 1:-1]
    flat_sum = padded[2:, 1:-1] + padded[:-2, 1:-1] + padded[1:-1, 2:] + padded[1:-1, :-2]
    padded_z = jnp.pad(interior, ((0, 0), (0, 0), (1, 1)))
    vertical = padded_z[:, :, 2:] + padded_z[:, :, :-2]
    return (flat_sum, vertical)


def checker(span_x, span_y, span_z):
    index_x = jnp.arange(span_x, dtype=jnp.int32)[:, None, None]
    index_y = jnp.arange(span_y, dtype=jnp.int32)[None, :, None]
    index_z = jnp.arange(span_z, dtype=jnp.int32)[None, None, :]
    return (index_x + index_y + index_z) % 2


def half_sweep(iterate, source, divisor, weight, allowed, colour):
    flat_sum, vertical = neighbour_sums(pad_plane(iterate))
    renewed = (source + weight * flat_sum + vertical) / divisor
    span_x, span_y, span_z = iterate.shape
    update = jnp.logical_and(checker(span_x, span_y, span_z) == colour, allowed)
    return jnp.where(update, renewed, iterate)


def sweeps(iterate, source, divisor, weight, allowed, count):
    for _ in range(count):
        iterate = half_sweep(iterate, source, divisor, weight, allowed, 0)
        iterate = half_sweep(iterate, source, divisor, weight, allowed, 1)
    return iterate


def residual_of(iterate, source, divisor, weight, allowed):
    flat_sum, vertical = neighbour_sums(pad_plane(iterate))
    residual = source - (divisor * iterate - (weight * flat_sum + vertical))
    return jnp.where(allowed, residual, 0.0)


def restrict(values, width, span_x, span_y):
    rows = values[width - 1:width + span_x]
    before = rows[:-1].reshape(span_x // 2, 2, *rows.shape[1:])[:, 0]
    paired = rows[1:].reshape(span_x // 2, 2, *rows.shape[1:])
    across = 0.25 * before + 0.5 * paired[:, 0] + 0.25 * paired[:, 1]
    cols = across[:, width - 1:width + span_y]
    before = cols[:, :-1].reshape(cols.shape[0], span_y // 2, 2, cols.shape[2])[:, :, 0]
    paired = cols[:, 1:].reshape(cols.shape[0], span_y // 2, 2, cols.shape[2])
    return 0.25 * before + 0.5 * paired[:, :, 0] + 0.25 * paired[:, :, 1]


def coarsen(values):
    paired = values.reshape(values.shape[0] // 2, 2, values.shape[1], values.shape[2])
    across = 0.5 * (paired[:, 0] + paired[:, 1])
    paired = across.reshape(across.shape[0], across.shape[1] // 2, 2, across.shape[2])
    return 0.5 * (paired[:, :, 0] + paired[:, :, 1])


def lift(coarse):
    return jnp.repeat(jnp.repeat(coarse, 2, axis=0), 2, axis=1)


def interior(values, width):
    return values[width:values.shape[0] - width, width:values.shape[1] - width]


def descend(grid_level, source, coefficient, width):
    span_x, span_y = source.shape[0], source.shape[1]
    source, coefficient_ext = exchange_many([source, coefficient], width)
    weight = 0.25**grid_level
    divisor = 4.0 * weight + 2.0 + coefficient_ext
    allowed = inside(span_x, span_y, width)
    iterate = sweeps(jnp.zeros_like(source), source, divisor, weight, allowed, 1)
    residual = residual_of(iterate, source, divisor, weight, allowed)
    coarse_source = restrict(residual, width, span_x, span_y)
    coarse_coefficient = coarsen(interior(coefficient_ext, width))
    return iterate, source, divisor, weight, allowed, coarse_source, coarse_coefficient


def coarsest(source, coefficient, width):
    span_x, span_y = source.shape[0], source.shape[1]
    source, coefficient = exchange_many([source, coefficient], width)
    weight = 0.25**3
    divisor = 4.0 * weight + 2.0 + coefficient
    allowed = inside(span_x, span_y, width)
    iterate = jnp.zeros_like(source)
    plan = [(0, 1, 0), (1, 0), (1, 0), (1,)]
    for step, colours in enumerate(plan):
        if step > 0:
            iterate = exchange(interior(iterate, width), width)
        for colour in colours:
            iterate = half_sweep(iterate, source, divisor, weight, allowed, colour)
    return iterate


def body(potential, charge, region, electrode_volts):
    span_x, span_y = potential.shape[0], potential.shape[1]
    dirichlet = jnp.zeros_like(potential)
    for electrode in range(electrode_volts.shape[0]):
        dirichlet = dirichlet + jnp.where(
            region == electrode + 1, electrode_volts[electrode], jnp.float32(0.0)
        )
    width = HALO_FINE
    potential, charge, region_f, dirichlet = exchange_many(
        [potential, charge, region.astype(jnp.float32), dirichlet], width
    )
    movable = jnp.logical_and(region_f == 0.0, inside(span_x, span_y, width))
    flat_sum, vertical = neighbour_sums(pad_plane(potential))
    source = (
        charge - (6.0 * potential - (flat_sum + vertical)) - screen * (jnp.exp(potential) - 1.0)
    )
    coefficient = screen * jnp.exp(potential)
    divisor = 4.0 * 1.0 + 2.0 + coefficient
    iterate = sweeps(dirichlet, source, divisor, 1.0, movable, 1)
    residual = residual_of(iterate, source, divisor, 1.0, movable)
    source_1 = restrict(residual, width, span_x, span_y)
    coefficient_1 = coarsen(interior(coefficient, width))

    level_1 = descend(1, source_1, coefficient_1, HALO_MID)
    level_2 = descend(2, level_1[5], level_1[6], HALO_MID)
    iterate_3 = coarsest(level_2[5], level_2[6], HALO_COARSE)

    iterate_2, source_2, divisor_2, weight_2, allowed_2 = level_2[:5]
    iterate_2 = sweeps(iterate_2 + lift(iterate_3), source_2, divisor_2, weight_2, allowed_2, 1)
    iterate_2 = exchange(interior(iterate_2, HALO_MID), HALO_MID // 2)

    iterate_1, source_1, divisor_1, weight_1, allowed_1 = level_1[:5]
    iterate_1 = sweeps(iterate_1 + lift(iterate_2), source_1, divisor_1, weight_1, allowed_1, 1)
    lifted = lift(interior(iterate_1, HALO_MID // 2))

    iterate = iterate + jnp.where(movable, lifted, 0.0)
    iterate = sweeps(iterate, source, divisor, 1.0, movable, 1)
    return interior(iterate, width)


def solution(mesh):
    placed = (P("gx", "gy", None), P("gx", "gy", None), P("gx", "gy", None), P())
    return jax.shard_map(
        body, mesh=mesh, in_specs=placed, out_specs=P("gx", "gy", None), check_vma=False
    )
```

time: 569 us -> 266 us (0.47)
  the two profiles are of different devices: /device:TPU:57 before, /device:TPU:51 now
where the time goes in v1:
time: 266 us; the launch traced here: 264 us
  starting transfers between devices  123 us (46%)
  waiting for transfers between devices  73 us (27%)
  other arithmetic  46.7 us (18%)
  local copies, waits for them, and re-layouts  20.9 us (8%)
    ppermute x32, starting transfers between devices, shifted(): return lax.ppermute(block, axis, route)  123 us
    ppermute x32, waiting for transfers between devices, shifted(): return lax.ppermute(block, axis, route)  73 us
    select_n x18, other arithmetic, half_sweep(): return jnp.where(update, renewed, iterate)  15.5 us
    add x1, other arithmetic, body(): dirichlet + jnp.where(region == electrode + 1, electrode_volts[electrode]...  11.5 us
  transfers between devices with their start and end apart: 32, of which 18 were waited for; matrix products, arithmetic and copies ran while one was open for 3% of the time, Pallas kernels for 0%

profile of v1, /device:TPU:51, one launch (start us, length us, event | category | flops | bytes accessed | tf_op | source)
XLA Modules:
  0.0 264.2 jit_solution(9362600373541895440)
XLA Ops:
  0.0 1.9 fusion.255
  3.0 1.1 copy.35
  4.2 1.1 copy_convert_fusion
  5.3 11.5 %select_add_fusion = f32[16,16,256]{2,0,1:T(8,128)S(1)} fusion(s32[16,16,256]{2,1,0:T(8,128)} %param.6, f32[]{:T(128)} %bitcast.15, f32[]{:T(128)} %bitcast.14, f32[]{:T(128)} %bitcast.13, f32[]{:T(128)} %bitcast.12, f32[]{:T(128)} %bitcast.11, f32[]{:T(128)} %bitcast.10, f32[]{:T(128)} %bitcast.9, f32[]{:T(128)} %bitcast.8, f32[]{:T(128)} %bitcast.7, ...), kind=kLoop, calls=%fused_computation.206 | loop fusion | flops 3080192 | bytes 524352 | tf_op jit(solution)/shard_map/add | solution.py:143
  16.9 5.0 %collective-permute-start = (f32[4,16,1024]{2,0,1:T(4,128)S(1)}, f32[4,16,1024]{2,0,1:T(4,128)S(1)}, u32[]{:S(2)}, u32[]{:S(2)}) collective-permute-start(f32[4,16,1024]{2,0,1:T(4,128)S(1)} %get-tuple-element.17), channel_id=1, source_target_pairs={{0,64},{64,128},{128,192},{192,256},{256,320},{320,384},{384,448},... | collective-permute-start | bytes 786440 | tf_op jit(solution)/shard_map/ppermute | solution.py:16
  21.9 1.9 collective-permute-start.1
  26.4 1.4 collective-permute-done
  27.8 7.4 %collective-permute-done.1 = f32[4,16,1024]{2,0,1:T(4,128)S(1)} collective-permute-done((f32[4,16,1024]{2,0,1:T(4,128)S(1)}, f32[4,16,1024]{2,0,1:T(4,128)S(1)}, u32[]{:S(2)}, u32[]{:S(2)}) %collective-permute-start.1) | collective-permute-done | bytes 262176 | tf_op jit(solution)/shard_map/ppermute | solution.py:16
  35.4 4.0 %collective-permute-start.2 = (f32[24,4,1024]{2,0,1:T(8,128)S(1)}, f32[24,4,1024]{2,0,1:T(8,128)S(1)}, u32[]{:S(2)}, u32[]{:S(2)}) collective-permute-start(f32[24,4,1024]{2,0,1:T(8,128)S(1)} %get-tuple-element.15), channel_id=1, source_target_pairs={{0,1},{1,2},{2,3},{3,4},{4,5},{5,6},{6,7},{7,8},{8,9},{9,10},{10,1... | collective-permute-start | bytes 1179656 | tf_op jit(solution)/shard_map/ppermute | solution.py:16
  39.4 19.2 %collective-permute-start.3 = (f32[24,4,1024]{2,0,1:T(8,128)S(1)}, f32[24,4,1024]{2,0,1:T(8,128)S(1)}, u32[]{:S(2)}, u32[]{:S(2)}) collective-permute-start(f32[24,4,1024]{2,0,1:T(8,128)S(1)} %get-tuple-element.16), channel_id=1, source_target_pairs={{1,0},{2,1},{3,2},{4,3},{5,4},{6,5},{7,6},{8,7},{9,8},{10,9},{11,1... | collective-permute-start | bytes 1179656 | tf_op jit(solution)/shard_map/ppermute | solution.py:16
  59.4 2.6 collective-permute-done.2
  61.9 1.8 collective-permute-done.3
  63.7 1.4 pad_maximum_fusion
  65.2 1.6 fusion.9
  66.7 1.4 fusion.13
  68.2 1.3 broadcast_add_fusion
  70.8 1.2 reshape.369
  74.6 4.5 %collective-permute-start.4 = (f32[4,8,512]{2,0,1:T(4,128)S(1)}, f32[4,8,512]{2,0,1:T(4,128)S(1)}, u32[]{:S(2)}, u32[]{:S(2)}) collective-permute-start(f32[4,8,512]{2,0,1:T(4,128)S(1)} %get-tuple-element.47), channel_id=1, source_target_pairs={{0,64},{64,128},{128,192},{192,256},{256,320},{320,384},{384,448},... | collective-permute-start | bytes 196616 | tf_op jit(solution)/shard_map/ppermute | solution.py:16
  79.1 1.9 collective-permute-start.5
  81.8 7.7 %collective-permute-done.5 = f32[4,8,512]{2,0,1:T(4,128)S(1)} collective-permute-done((f32[4,8,512]{2,0,1:T(4,128)S(1)}, f32[4,8,512]{2,0,1:T(4,128)S(1)}, u32[]{:S(2)}, u32[]{:S(2)}) %collective-permute-start.5) | collective-permute-done | bytes 65568 | tf_op jit(solution)/shard_map/ppermute | solution.py:16
  89.6 1.9 collective-permute-start.6
  91.5 6.2 %collective-permute-start.7 = (f32[16,4,512]{2,0,1:T(8,128)S(1)}, f32[16,4,512]{2,0,1:T(8,128)S(1)}, u32[]{:S(2)}, u32[]{:S(2)}) collective-permute-start(f32[16,4,512]{2,0,1:T(8,128)S(1)} %get-tuple-element.38), channel_id=1, source_target_pairs={{1,0},{2,1},{3,2},{4,3},{5,4},{6,5},{7,6},{8,7},{9,8},{10,9},{11,1... | collective-permute-start | bytes 393224 | tf_op jit(solution)/shard_map/ppermute | solution.py:16
  98.2 1.5 collective-permute-done.7
  99.8 1.8 fusion.244
  104.8 4.1 %collective-permute-start.8 = (f32[4,4,512]{2,0,1:T(4,128)S(1)}, f32[4,4,512]{2,0,1:T(4,128)S(1)}, u32[]{:S(2)}, u32[]{:S(2)}) collective-permute-start(f32[4,4,512]{2,0,1:T(4,128)S(1)} %pad_maximum_fusion.21), channel_id=1, source_target_pairs={{0,64},{64,128},{128,192},{192,256},{256,320},{320,384},{384,448},... | collective-permute-start | bytes 98312 | tf_op jit(solution)/shard_map/ppermute | solution.py:16
  108.9 1.9 collective-permute-start.9
  111.7 7.3 %collective-permute-done.9 = f32[4,4,512]{2,0,1:T(4,128)S(1)} collective-permute-done((f32[4,4,512]{2,0,1:T(4,128)S(1)}, f32[4,4,512]{2,0,1:T(4,128)S(1)}, u32[]{:S(2)}, u32[]{:S(2)}) %collective-permute-start.9) | collective-permute-done | bytes 32800 | tf_op jit(solution)/shard_map/ppermute | solution.py:16
  119.0 1.9 collective-permute-start.10
  120.9 6.2 %collective-permute-start.11 = (f32[12,4,512]{2,0,1:T(8,128)S(1)}, f32[12,4,512]{2,0,1:T(8,128)S(1)}, u32[]{:S(2)}, u32[]{:S(2)}) collective-permute-start(f32[12,4,512]{2,0,1:T(8,128)S(1)} %pad_maximum_fusion.14), channel_id=1, source_target_pairs={{1,0},{2,1},{3,2},{4,3},{5,4},{6,5},{7,6},{8,7},{9,8},{10,9},{11,1... | collective-permute-start | bytes 294920 | tf_op jit(solution)/shard_map/ppermute | solution.py:16
  127.7 1.3 collective-permute-done.11
  131.9 1.5 reshape.377
  133.4 1.4 reshape.378
  135.8 2.8 %collective-permute-start.12 = (f32[2,2,512]{2,0,1:T(2,128)S(1)}, f32[2,2,512]{2,0,1:T(2,128)S(1)}, u32[]{:S(2)}, u32[]{:S(2)}) collective-permute-start(f32[2,2,512]{2,0,1:T(2,128)S(1)} %pad_maximum_fusion.27), channel_id=1, source_target_pairs={{0,64},{64,128},{128,192},{192,256},{256,320},{320,384},{384,448},... | collective-permute-start | bytes 24584 | tf_op jit(solution)/shard_map/ppermute | solution.py:16
  138.6 1.9 collective-permute-start.13
  140.6 7.8 %collective-permute-done.13 = f32[2,2,512]{2,0,1:T(2,128)S(1)} collective-permute-done((f32[2,2,512]{2,0,1:T(2,128)S(1)}, f32[2,2,512]{2,0,1:T(2,128)S(1)}, u32[]{:S(2)}, u32[]{:S(2)}) %collective-permute-start.13) | collective-permute-done | bytes 8224 | tf_op jit(solution)/shard_map/ppermute | solution.py:16
  148.4 1.9 collective-permute-start.14
  150.3 6.2 %collective-permute-start.15 = (f32[6,2,512]{2,0,1:T(8,128)S(1)}, f32[6,2,512]{2,0,1:T(8,128)S(1)}, u32[]{:S(2)}, u32[]{:S(2)}) collective-permute-start(f32[6,2,512]{2,0,1:T(8,128)S(1)} %pad_maximum_fusion.22), channel_id=1, source_target_pairs={{1,0},{2,1},{3,2},{4,3},{5,4},{6,5},{7,6},{8,7},{9,8},{10,9},{11,1... | collective-permute-start | bytes 73736 | tf_op jit(solution)/shard_map/ppermute | solution.py:16
  159.2 2.8 %collective-permute-start.16 = (f32[2,2,256]{2,0,1:T(2,128)S(1)}, f32[2,2,256]{2,0,1:T(2,128)S(1)}, u32[]{:S(2)}, u32[]{:S(2)}) collective-permute-start(f32[2,2,256]{2,0,1:T(2,128)S(1)} %divide_select_fusion.2), channel_id=1, source_target_pairs={{0,64},{64,128},{128,192},{192,256},{256,320},{320,384},{384,448},... | collective-permute-start | bytes 12296 | tf_op jit(solution)/shard_map/ppermute | solution.py:16
  162.1 1.9 collective-permute-start.17
  164.0 7.8 %collective-permute-done.17 = f32[2,2,256]{2,0,1:T(2,128)S(1)} collective-permute-done((f32[2,2,256]{2,0,1:T(2,128)S(1)}, f32[2,2,256]{2,0,1:T(2,128)S(1)}, u32[]{:S(2)}, u32[]{:S(2)}) %collective-permute-start.17) | collective-permute-done | bytes 4128 | tf_op jit(solution)/shard_map/ppermute | solution.py:16
  171.8 1.9 collective-permute-start.18
  173.7 6.1 %collective-permute-start.19 = (f32[6,2,256]{2,0,1:T(8,128)S(1)}, f32[6,2,256]{2,0,1:T(8,128)S(1)}, u32[]{:S(2)}, u32[]{:S(2)}) collective-permute-start(f32[6,2,256]{2,0,1:T(8,128)S(1)} %pad_maximum_fusion.24), channel_id=1, source_target_pairs={{1,0},{2,1},{3,2},{4,3},{5,4},{6,5},{7,6},{8,7},{9,8},{10,9},{11,1... | collective-permute-start | bytes 36872 | tf_op jit(solution)/shard_map/ppermute | solution.py:16
  181.6 2.8 %collective-permute-start.20 = (f32[2,2,256]{2,0,1:T(2,128)S(1)}, f32[2,2,256]{2,0,1:T(2,128)S(1)}, u32[]{:S(2)}, u32[]{:S(2)}) collective-permute-start(f32[2,2,256]{2,0,1:T(2,128)S(1)} %divide_select_fusion.1), channel_id=1, source_target_pairs={{0,64},{64,128},{128,192},{192,256},{256,320},{320,384},{384,448},... | collective-permute-start | bytes 12296 | tf_op jit(solution)/shard_map/ppermute | solution.py:16
  184.4 1.9 collective-permute-start.21
  186.3 7.8 %collective-permute-done.21 = f32[2,2,256]{2,0,1:T(2,128)S(1)} collective-permute-done((f32[2,2,256]{2,0,1:T(2,128)S(1)}, f32[2,2,256]{2,0,1:T(2,128)S(1)}, u32[]{:S(2)}, u32[]{:S(2)}) %collective-permute-start.21) | collective-permute-done | bytes 4128 | tf_op jit(solution)/shard_map/ppermute | solution.py:16
  194.1 1.9 collective-permute-start.22
  196.0 6.0 %collective-permute-start.23 = (f32[6,2,256]{2,0,1:T(8,128)S(1)}, f32[6,2,256]{2,0,1:T(8,128)S(1)}, u32[]{:S(2)}, u32[]{:S(2)}) collective-permute-start(f32[6,2,256]{2,0,1:T(8,128)S(1)} %pad_maximum_fusion.25), channel_id=1, source_target_pairs={{1,0},{2,1},{3,2},{4,3},{5,4},{6,5},{7,6},{8,7},{9,8},{10,9},{11,1... | collective-permute-start | bytes 36872 | tf_op jit(solution)/shard_map/ppermute | solution.py:16
  203.8 2.8 %collective-permute-start.24 = (f32[2,2,256]{2,0,1:T(2,128)S(1)}, f32[2,2,256]{2,0,1:T(2,128)S(1)}, u32[]{:S(2)}, u32[]{:S(2)}) collective-permute-start(f32[2,2,256]{2,0,1:T(2,128)S(1)} %divide_select_fusion), channel_id=1, source_target_pairs={{0,64},{64,128},{128,192},{192,256},{256,320},{320,384},{384,448},... | collective-permute-start | bytes 12296 | tf_op jit(solution)/shard_map/ppermute | solution.py:16
  206.7 1.9 collective-permute-start.25
  208.6 7.8 %collective-permute-done.25 = f32[2,2,256]{2,0,1:T(2,128)S(1)} collective-permute-done((f32[2,2,256]{2,0,1:T(2,128)S(1)}, f32[2,2,256]{2,0,1:T(2,128)S(1)}, u32[]{:S(2)}, u32[]{:S(2)}) %collective-permute-start.25) | collective-permute-done | bytes 4128 | tf_op jit(solution)/shard_map/ppermute | solution.py:16
  216.4 1.9 collective-permute-start.26
  218.3 6.2 %collective-permute-start.27 = (f32[6,2,256]{2,0,1:T(8,128)S(1)}, f32[6,2,256]{2,0,1:T(8,128)S(1)}, u32[]{:S(2)}, u32[]{:S(2)}) collective-permute-start(f32[6,2,256]{2,0,1:T(8,128)S(1)} %pad_maximum_fusion.26), channel_id=1, source_target_pairs={{1,0},{2,1},{3,2},{4,3},{5,4},{6,5},{7,6},{8,7},{9,8},{10,9},{11,1... | collective-permute-start | bytes 36872 | tf_op jit(solution)/shard_map/ppermute | solution.py:16
  226.7 1.6 reshape.381
  231.2 2.8 %collective-permute-start.28 = (f32[2,4,256]{2,0,1:T(2,128)S(1)}, f32[2,4,256]{2,0,1:T(2,128)S(1)}, u32[]{:S(2)}, u32[]{:S(2)}) collective-permute-start(f32[2,4,256]{2,0,1:T(2,128)S(1)} %get-tuple-element.41), channel_id=1, source_target_pairs={{0,64},{64,128},{128,192},{192,256},{256,320},{320,384},{384,448},... | collective-permute-start | bytes 24584 | tf_op jit(solution)/shard_map/ppermute | solution.py:16
  234.0 1.9 collective-permute-start.29
  235.9 7.8 %collective-permute-done.29 = f32[2,4,256]{2,0,1:T(2,128)S(1)} collective-permute-done((f32[2,4,256]{2,0,1:T(2,128)S(1)}, f32[2,4,256]{2,0,1:T(2,128)S(1)}, u32[]{:S(2)}, u32[]{:S(2)}) %collective-permute-start.29) | collective-permute-done | bytes 8224 | tf_op jit(solution)/shard_map/ppermute | solution.py:16
  243.8 1.9 collective-permute-start.30
  245.7 6.0 %collective-permute-start.31 = (f32[8,2,256]{2,0,1:T(8,128)S(1)}, f32[8,2,256]{2,0,1:T(8,128)S(1)}, u32[]{:S(2)}, u32[]{:S(2)}) collective-permute-start(f32[8,2,256]{2,0,1:T(8,128)S(1)} %get-tuple-element.67), channel_id=1, source_target_pairs={{1,0},{2,1},{3,2},{4,3},{5,4},{6,5},{7,6},{8,7},{9,8},{10,9},{11,1... | collective-permute-start | bytes 49160 | tf_op jit(solution)/shard_map/ppermute | solution.py:16
  251.8 1.5 compare_and_fusion.3
  254.8 1.3 slice_select_fusion.1
  256.8 1.9 reshape.385
  258.7 1.1 fusion.42
  259.9 1.7 fusion.22
  262.0 1.3 slice_select_fusion
  (156 shorter events, 33.1 us)
Async XLA Ops:
  16.9 10.9 %collective-permute-start = (f32[4,16,1024]{2,0,1:T(4,128)S(1)}, f32[4,16,1024]{2,0,1:T(4,128)S(1)}, u32[]{:S(2)}, u32[]{:S(2)}) collective-permute-start(f32[4,16,1024]{2,0,1:T(4,128)S(1)} %get-tuple-element.17), channel_id=1, source_target_pairs={{0,64},{64,128},{128,192},{192,256},{256,320},{320,384},{384,448},... | collective-permute-start | bytes 786440 | tf_op jit(solution)/shard_map/ppermute | solution.py:16
  21.9 13.3 %collective-permute-start.1 = (f32[4,16,1024]{2,0,1:T(4,128)S(1)}, f32[4,16,1024]{2,0,1:T(4,128)S(1)}, u32[]{:S(2)}, u32[]{:S(2)}) collective-permute-start(f32[4,16,1024]{2,0,1:T(4,128)S(1)} %get-tuple-element.18), channel_id=1, source_target_pairs={{64,0},{128,64},{192,128},{256,192},{320,256},{384,320},{448,384},... | collective-permute-start | bytes 786440 | tf_op jit(solution)/shard_map/ppermute | solution.py:16
  23.9 42.9 %copy-start.12 = (s32[24,24]{0,1:T(8,128)}, s32[24,24]{0,1:T(8,128)S(1)}, u32[]{:S(2)}) copy-start(s32[24,24]{0,1:T(8,128)S(1)} %iota_add_fusion) | copy-start | bytes 6916
  27.8 34.1 %copy-start.6 = (f32[4,16,1024]{2,0,1:T(4,128)}, f32[4,16,1024]{2,0,1:T(4,128)S(1)}, u32[]{:S(2)}) copy-start(f32[4,16,1024]{2,0,1:T(4,128)S(1)} %collective-permute-done) | copy-start | bytes 786436
  35.2 26.7 %copy-start.7 = (f32[4,16,1024]{2,0,1:T(4,128)}, f32[4,16,1024]{2,0,1:T(4,128)S(1)}, u32[]{:S(2)}) copy-start(f32[4,16,1024]{2,0,1:T(4,128)S(1)} %collective-permute-done.1) | copy-start | bytes 786436
  35.4 26.6 %collective-permute-start.2 = (f32[24,4,1024]{2,0,1:T(8,128)S(1)}, f32[24,4,1024]{2,0,1:T(8,128)S(1)}, u32[]{:S(2)}, u32[]{:S(2)}) collective-permute-start(f32[24,4,1024]{2,0,1:T(8,128)S(1)} %get-tuple-element.15), channel_id=1, source_target_pairs={{0,1},{1,2},{2,3},{3,4},{4,5},{5,6},{6,7},{7,8},{8,9},{9,10},{10,1... | collective-permute-start | bytes 1179656 | tf_op jit(solution)/shard_map/ppermute | solution.py:16
  39.4 24.3 %collective-permute-start.3 = (f32[24,4,1024]{2,0,1:T(8,128)S(1)}, f32[24,4,1024]{2,0,1:T(8,128)S(1)}, u32[]{:S(2)}, u32[]{:S(2)}) collective-permute-start(f32[24,4,1024]{2,0,1:T(8,128)S(1)} %get-tuple-element.16), channel_id=1, source_target_pairs={{1,0},{2,1},{3,2},{4,3},{5,4},{6,5},{7,6},{8,7},{9,8},{10,9},{11,1... | collective-permute-start | bytes 1179656 | tf_op jit(solution)/shard_map/ppermute | solution.py:16
  66.7 2.7 %copy-start = (f32[24,24,256]{2,0,1:T(8,128)}, f32[24,24,256]{2,0,1:T(8,128)S(1)}, u32[]{:S(2)}) copy-start(f32[24,24,256]{2,0,1:T(8,128)S(1)} %get-tuple-element.8) | copy-start | bytes 1769476
  66.7 2.7 %copy-start.4 = (pred[24,24,256]{2,0,1:T(8,128)(4,1)}, pred[24,24,256]{2,0,1:T(8,128)(4,1)S(1)}, u32[]{:S(2)}) copy-start(pred[24,24,256]{2,0,1:T(8,128)(4,1)S(1)} %get-tuple-element.9) | copy-start | bytes 442372
  68.2 1.3 copy-start.2
  74.6 7.2 %collective-permute-start.4 = (f32[4,8,512]{2,0,1:T(4,128)S(1)}, f32[4,8,512]{2,0,1:T(4,128)S(1)}, u32[]{:S(2)}, u32[]{:S(2)}) collective-permute-start(f32[4,8,512]{2,0,1:T(4,128)S(1)} %get-tuple-element.47), channel_id=1, source_target_pairs={{0,64},{64,128},{128,192},{192,256},{256,320},{320,384},{384,448},... | collective-permute-start | bytes 196616 | tf_op jit(solution)/shard_map/ppermute | solution.py:16
  79.1 10.4 %collective-permute-start.5 = (f32[4,8,512]{2,0,1:T(4,128)S(1)}, f32[4,8,512]{2,0,1:T(4,128)S(1)}, u32[]{:S(2)}, u32[]{:S(2)}) collective-permute-start(f32[4,8,512]{2,0,1:T(4,128)S(1)} %get-tuple-element.48), channel_id=1, source_target_pairs={{64,0},{128,64},{192,128},{256,192},{320,256},{384,320},{448,384},... | collective-permute-start | bytes 196616 | tf_op jit(solution)/shard_map/ppermute | solution.py:16
  89.6 13.0 %copy-start.15 = (pred[16,16]{0,1:T(8,128)(4,1)S(1)}, pred[16,16]{0,1:T(8,128)(4,1)}, u32[]{:S(2)}) copy-start(pred[16,16]{0,1:T(8,128)(4,1)} %broadcast_and_fusion.2) | copy-start | bytes 772
  89.6 8.6 %collective-permute-start.6 = (f32[16,4,512]{2,0,1:T(8,128)S(1)}, f32[16,4,512]{2,0,1:T(8,128)S(1)}, u32[]{:S(2)}, u32[]{:S(2)}) collective-permute-start(f32[16,4,512]{2,0,1:T(8,128)S(1)} %get-tuple-element.37), channel_id=1, source_target_pairs={{0,1},{1,2},{2,3},{3,4},{4,5},{5,6},{6,7},{7,8},{8,9},{9,10},{10,1... | collective-permute-start | bytes 393224 | tf_op jit(solution)/shard_map/ppermute | solution.py:16
  91.5 8.2 %collective-permute-start.7 = (f32[16,4,512]{2,0,1:T(8,128)S(1)}, f32[16,4,512]{2,0,1:T(8,128)S(1)}, u32[]{:S(2)}, u32[]{:S(2)}) collective-permute-start(f32[16,4,512]{2,0,1:T(8,128)S(1)} %get-tuple-element.38), channel_id=1, source_target_pairs={{1,0},{2,1},{3,2},{4,3},{5,4},{6,5},{7,6},{8,7},{9,8},{10,9},{11,1... | collective-permute-start | bytes 393224 | tf_op jit(solution)/shard_map/ppermute | solution.py:16
  104.6 25.5 %copy-start.8 = (s32[12,12]{0,1:T(8,128)S(1)}, s32[12,12]{0,1:T(8,128)}, u32[]{:S(2)}) copy-start(s32[12,12]{0,1:T(8,128)} %iota_add_fusion.1) | copy-start | bytes 1732
  104.6 25.5 %copy-start.14 = (pred[12,12]{0,1:T(8,128)(4,1)S(1)}, pred[12,12]{0,1:T(8,128)(4,1)}, u32[]{:S(2)}) copy-start(pred[12,12]{0,1:T(8,128)(4,1)} %broadcast_and_fusion.1) | copy-start | bytes 436
  104.8 6.8 %collective-permute-start.8 = (f32[4,4,512]{2,0,1:T(4,128)S(1)}, f32[4,4,512]{2,0,1:T(4,128)S(1)}, u32[]{:S(2)}, u32[]{:S(2)}) collective-permute-start(f32[4,4,512]{2,0,1:T(4,128)S(1)} %pad_maximum_fusion.21), channel_id=1, source_target_pairs={{0,64},{64,128},{128,192},{192,256},{256,320},{320,384},{384,448},... | collective-permute-start | bytes 98312 | tf_op jit(solution)/shard_map/ppermute | solution.py:16
  108.9 10.0 %collective-permute-start.9 = (f32[4,4,512]{2,0,1:T(4,128)S(1)}, f32[4,4,512]{2,0,1:T(4,128)S(1)}, u32[]{:S(2)}, u32[]{:S(2)}) collective-permute-start(f32[4,4,512]{2,0,1:T(4,128)S(1)} %pad_maximum_fusion.21), channel_id=1, source_target_pairs={{64,0},{128,64},{192,128},{256,192},{320,256},{384,320},{448,384},... | collective-permute-start | bytes 98312 | tf_op jit(solution)/shard_map/ppermute | solution.py:16
  119.0 8.7 %collective-permute-start.10 = (f32[12,4,512]{2,0,1:T(8,128)S(1)}, f32[12,4,512]{2,0,1:T(8,128)S(1)}, u32[]{:S(2)}, u32[]{:S(2)}) collective-permute-start(f32[12,4,512]{2,0,1:T(8,128)S(1)} %pad_maximum_fusion.14), channel_id=1, source_target_pairs={{0,1},{1,2},{2,3},{3,4},{4,5},{5,6},{6,7},{7,8},{8,9},{9,10},{10,1... | collective-permute-start | bytes 294920 | tf_op jit(solution)/shard_map/ppermute | solution.py:16
  120.9 8.1 %collective-permute-start.11 = (f32[12,4,512]{2,0,1:T(8,128)S(1)}, f32[12,4,512]{2,0,1:T(8,128)S(1)}, u32[]{:S(2)}, u32[]{:S(2)}) collective-permute-start(f32[12,4,512]{2,0,1:T(8,128)S(1)} %pad_maximum_fusion.14), channel_id=1, source_target_pairs={{1,0},{2,1},{3,2},{4,3},{5,4},{6,5},{7,6},{8,7},{9,8},{10,9},{11,1... | collective-permute-start | bytes 294920 | tf_op jit(solution)/shard_map/ppermute | solution.py:16
  129.1 6.7 %copy-start.16 = (f32[2,2,256]{2,0,1:T(2,128)S(1)}, f32[2,2,256]{2,0,1:T(2,128)}, u32[]{:S(2)}) copy-start(f32[2,2,256]{2,0,1:T(2,128)} %fusion.233) | copy-start | bytes 12292
  130.4 0.7 copy-start.5
  131.1 98.2 %copy-start.9 = (s32[12,12]{0,1:T(8,128)S(1)}, s32[12,12]{0,1:T(8,128)}, u32[]{:S(2)}) copy-start(s32[12,12]{0,1:T(8,128)} %iota_add_fusion.1) | copy-start | bytes 1732
  135.8 4.7 %collective-permute-start.12 = (f32[2,2,512]{2,0,1:T(2,128)S(1)}, f32[2,2,512]{2,0,1:T(2,128)S(1)}, u32[]{:S(2)}, u32[]{:S(2)}) collective-permute-start(f32[2,2,512]{2,0,1:T(2,128)S(1)} %pad_maximum_fusion.27), channel_id=1, source_target_pairs={{0,64},{64,128},{128,192},{192,256},{256,320},{320,384},{384,448},... | collective-permute-start | bytes 24584 | tf_op jit(solution)/shard_map/ppermute | solution.py:16
  138.6 9.8 %collective-permute-start.13 = (f32[2,2,512]{2,0,1:T(2,128)S(1)}, f32[2,2,512]{2,0,1:T(2,128)S(1)}, u32[]{:S(2)}, u32[]{:S(2)}) collective-permute-start(f32[2,2,512]{2,0,1:T(2,128)S(1)} %pad_maximum_fusion.27), channel_id=1, source_target_pairs={{64,0},{128,64},{192,128},{256,192},{320,256},{384,320},{448,384},... | collective-permute-start | bytes 24584 | tf_op jit(solution)/shard_map/ppermute | solution.py:16
  148.4 8.9 %collective-permute-start.14 = (f32[6,2,512]{2,0,1:T(8,128)S(1)}, f32[6,2,512]{2,0,1:T(8,128)S(1)}, u32[]{:S(2)}, u32[]{:S(2)}) collective-permute-start(f32[6,2,512]{2,0,1:T(8,128)S(1)} %pad_maximum_fusion.22), channel_id=1, source_target_pairs={{0,1},{1,2},{2,3},{3,4},{4,5},{5,6},{6,7},{7,8},{8,9},{9,10},{10,1... | collective-permute-start | bytes 73736 | tf_op jit(solution)/shard_map/ppermute | solution.py:16
  150.3 7.2 %collective-permute-start.15 = (f32[6,2,512]{2,0,1:T(8,128)S(1)}, f32[6,2,512]{2,0,1:T(8,128)S(1)}, u32[]{:S(2)}, u32[]{:S(2)}) collective-permute-start(f32[6,2,512]{2,0,1:T(8,128)S(1)} %pad_maximum_fusion.22), channel_id=1, source_target_pairs={{1,0},{2,1},{3,2},{4,3},{5,4},{6,5},{7,6},{8,7},{9,8},{10,9},{11,1... | collective-permute-start | bytes 73736 | tf_op jit(solution)/shard_map/ppermute | solution.py:16
  158.3 93.4 %copy-start.10 = (s32[16,16]{0,1:T(8,128)S(1)}, s32[16,16]{0,1:T(8,128)}, u32[]{:S(2)}) copy-start(s32[16,16]{0,1:T(8,128)} %iota_add_fusion.2) | copy-start | bytes 3076
  159.2 4.7 %collective-permute-start.16 = (f32[2,2,256]{2,0,1:T(2,128)S(1)}, f32[2,2,256]{2,0,1:T(2,128)S(1)}, u32[]{:S(2)}, u32[]{:S(2)}) collective-permute-start(f32[2,2,256]{2,0,1:T(2,128)S(1)} %divide_select_fusion.2), channel_id=1, source_target_pairs={{0,64},{64,128},{128,192},{192,256},{256,320},{320,384},{384,448},... | collective-permute-start | bytes 12296 | tf_op jit(solution)/shard_map/ppermute | solution.py:16
  162.1 9.7 %collective-permute-start.17 = (f32[2,2,256]{2,0,1:T(2,128)S(1)}, f32[2,2,256]{2,0,1:T(2,128)S(1)}, u32[]{:S(2)}, u32[]{:S(2)}) collective-permute-start(f32[2,2,256]{2,0,1:T(2,128)S(1)} %divide_select_fusion.2), channel_id=1, source_target_pairs={{64,0},{128,64},{192,128},{256,192},{320,256},{384,320},{448,384},... | collective-permute-start | bytes 12296 | tf_op jit(solution)/shard_map/ppermute | solution.py:16
  171.8 8.0 %collective-permute-start.18 = (f32[6,2,256]{2,0,1:T(8,128)S(1)}, f32[6,2,256]{2,0,1:T(8,128)S(1)}, u32[]{:S(2)}, u32[]{:S(2)}) collective-permute-start(f32[6,2,256]{2,0,1:T(8,128)S(1)} %pad_maximum_fusion.24), channel_id=1, source_target_pairs={{0,1},{1,2},{2,3},{3,4},{4,5},{5,6},{6,7},{7,8},{8,9},{9,10},{10,1... | collective-permute-start | bytes 36872 | tf_op jit(solution)/shard_map/ppermute | solution.py:16
  173.7 6.9 %collective-permute-start.19 = (f32[6,2,256]{2,0,1:T(8,128)S(1)}, f32[6,2,256]{2,0,1:T(8,128)S(1)}, u32[]{:S(2)}, u32[]{:S(2)}) collective-permute-start(f32[6,2,256]{2,0,1:T(8,128)S(1)} %pad_maximum_fusion.24), channel_id=1, source_target_pairs={{1,0},{2,1},{3,2},{4,3},{5,4},{6,5},{7,6},{8,7},{9,8},{10,9},{11,1... | collective-permute-start | bytes 36872 | tf_op jit(solution)/shard_map/ppermute | solution.py:16
  181.6 4.7 %collective-permute-start.20 = (f32[2,2,256]{2,0,1:T(2,128)S(1)}, f32[2,2,256]{2,0,1:T(2,128)S(1)}, u32[]{:S(2)}, u32[]{:S(2)}) collective-permute-start(f32[2,2,256]{2,0,1:T(2,128)S(1)} %divide_select_fusion.1), channel_id=1, source_target_pairs={{0,64},{64,128},{128,192},{192,256},{256,320},{320,384},{384,448},... | collective-permute-start | bytes 12296 | tf_op jit(solution)/shard_map/ppermute | solution.py:16
  184.4 9.7 %collective-permute-start.21 = (f32[2,2,256]{2,0,1:T(2,128)S(1)}, f32[2,2,256]{2,0,1:T(2,128)S(1)}, u32[]{:S(2)}, u32[]{:S(2)}) collective-permute-start(f32[2,2,256]{2,0,1:T(2,128)S(1)} %divide_select_fusion.1), channel_id=1, source_target_pairs={{64,0},{128,64},{192,128},{256,192},{320,256},{384,320},{448,384},... | collective-permute-start | bytes 12296 | tf_op jit(solution)/shard_map/ppermute | solution.py:16
  194.1 8.0 %collective-permute-start.22 = (f32[6,2,256]{2,0,1:T(8,128)S(1)}, f32[6,2,256]{2,0,1:T(8,128)S(1)}, u32[]{:S(2)}, u32[]{:S(2)}) collective-permute-start(f32[6,2,256]{2,0,1:T(8,128)S(1)} %pad_maximum_fusion.25), channel_id=1, source_target_pairs={{0,1},{1,2},{2,3},{3,4},{4,5},{5,6},{6,7},{7,8},{8,9},{9,10},{10,1... | collective-permute-start | bytes 36872 | tf_op jit(solution)/shard_map/ppermute | solution.py:16
  196.0 6.9 %collective-permute-start.23 = (f32[6,2,256]{2,0,1:T(8,128)S(1)}, f32[6,2,256]{2,0,1:T(8,128)S(1)}, u32[]{:S(2)}, u32[]{:S(2)}) collective-permute-start(f32[6,2,256]{2,0,1:T(8,128)S(1)} %pad_maximum_fusion.25), channel_id=1, source_target_pairs={{1,0},{2,1},{3,2},{4,3},{5,4},{6,5},{7,6},{8,7},{9,8},{10,9},{11,1... | collective-permute-start | bytes 36872 | tf_op jit(solution)/shard_map/ppermute | solution.py:16
  203.8 4.7 %collective-permute-start.24 = (f32[2,2,256]{2,0,1:T(2,128)S(1)}, f32[2,2,256]{2,0,1:T(2,128)S(1)}, u32[]{:S(2)}, u32[]{:S(2)}) collective-permute-start(f32[2,2,256]{2,0,1:T(2,128)S(1)} %divide_select_fusion), channel_id=1, source_target_pairs={{0,64},{64,128},{128,192},{192,256},{256,320},{320,384},{384,448},... | collective-permute-start | bytes 12296 | tf_op jit(solution)/shard_map/ppermute | solution.py:16
  206.7 9.7 %collective-permute-start.25 = (f32[2,2,256]{2,0,1:T(2,128)S(1)}, f32[2,2,256]{2,0,1:T(2,128)S(1)}, u32[]{:S(2)}, u32[]{:S(2)}) collective-permute-start(f32[2,2,256]{2,0,1:T(2,128)S(1)} %divide_select_fusion), channel_id=1, source_target_pairs={{64,0},{128,64},{192,128},{256,192},{320,256},{384,320},{448,384},... | collective-permute-start | bytes 12296 | tf_op jit(solution)/shard_map/ppermute | solution.py:16
  216.4 8.2 %collective-permute-start.26 = (f32[6,2,256]{2,0,1:T(8,128)S(1)}, f32[6,2,256]{2,0,1:T(8,128)S(1)}, u32[]{:S(2)}, u32[]{:S(2)}) collective-permute-start(f32[6,2,256]{2,0,1:T(8,128)S(1)} %pad_maximum_fusion.26), channel_id=1, source_target_pairs={{0,1},{1,2},{2,3},{3,4},{4,5},{5,6},{6,7},{7,8},{8,9},{9,10},{10,1... | collective-permute-start | bytes 36872 | tf_op jit(solution)/shard_map/ppermute | solution.py:16
  218.3 6.9 %collective-permute-start.27 = (f32[6,2,256]{2,0,1:T(8,128)S(1)}, f32[6,2,256]{2,0,1:T(8,128)S(1)}, u32[]{:S(2)}, u32[]{:S(2)}) collective-permute-start(f32[6,2,256]{2,0,1:T(8,128)S(1)} %pad_maximum_fusion.26), channel_id=1, source_target_pairs={{1,0},{2,1},{3,2},{4,3},{5,4},{6,5},{7,6},{8,7},{9,8},{10,9},{11,1... | collective-permute-start | bytes 36872 | tf_op jit(solution)/shard_map/ppermute | solution.py:16
  231.2 4.8 %collective-permute-start.28 = (f32[2,4,256]{2,0,1:T(2,128)S(1)}, f32[2,4,256]{2,0,1:T(2,128)S(1)}, u32[]{:S(2)}, u32[]{:S(2)}) collective-permute-start(f32[2,4,256]{2,0,1:T(2,128)S(1)} %get-tuple-element.41), channel_id=1, source_target_pairs={{0,64},{64,128},{128,192},{192,256},{256,320},{320,384},{384,448},... | collective-permute-start | bytes 24584 | tf_op jit(solution)/shard_map/ppermute | solution.py:16
  234.0 9.8 %collective-permute-start.29 = (f32[2,4,256]{2,0,1:T(2,128)S(1)}, f32[2,4,256]{2,0,1:T(2,128)S(1)}, u32[]{:S(2)}, u32[]{:S(2)}) collective-permute-start(f32[2,4,256]{2,0,1:T(2,128)S(1)} %get-tuple-element.42), channel_id=1, source_target_pairs={{64,0},{128,64},{192,128},{256,192},{320,256},{384,320},{448,384},... | collective-permute-start | bytes 24584 | tf_op jit(solution)/shard_map/ppermute | solution.py:16
  243.8 9.5 %collective-permute-start.30 = (f32[8,2,256]{2,0,1:T(8,128)S(1)}, f32[8,2,256]{2,0,1:T(8,128)S(1)}, u32[]{:S(2)}, u32[]{:S(2)}) collective-permute-start(f32[8,2,256]{2,0,1:T(8,128)S(1)} %get-tuple-element.66), channel_id=1, source_target_pairs={{0,1},{1,2},{2,3},{3,4},{4,5},{5,6},{6,7},{7,8},{8,9},{9,10},{10,1... | collective-permute-start | bytes 49160 | tf_op jit(solution)/shard_map/ppermute | solution.py:16
  245.7 7.6 %collective-permute-start.31 = (f32[8,2,256]{2,0,1:T(8,128)S(1)}, f32[8,2,256]{2,0,1:T(8,128)S(1)}, u32[]{:S(2)}, u32[]{:S(2)}) collective-permute-start(f32[8,2,256]{2,0,1:T(8,128)S(1)} %get-tuple-element.67), channel_id=1, source_target_pairs={{1,0},{2,1},{3,2},{4,3},{5,4},{6,5},{7,6},{8,7},{9,8},{10,9},{11,1... | collective-permute-start | bytes 49160 | tf_op jit(solution)/shard_map/ppermute | solution.py:16
  253.4 1.3 copy-start.11
  254.5 4.2 %copy-start.3 = (f32[24,24,256]{2,0,1:T(8,128)S(1)}, f32[24,24,256]{2,0,1:T(8,128)}, u32[]{:S(2)}) copy-start(f32[24,24,256]{2,0,1:T(8,128)} %copy-done.2) | copy-start | bytes 1769476
  254.7 5.1 %copy-start.1 = (f32[24,24,256]{2,0,1:T(8,128)S(1)}, f32[24,24,256]{2,0,1:T(8,128)}, u32[]{:S(2)}) copy-start(f32[24,24,256]{2,0,1:T(8,128)} %copy-done) | copy-start | bytes 1769476
  254.7 5.1 %copy-start.13 = (s32[24,24]{0,1:T(8,128)S(1)}, s32[24,24]{0,1:T(8,128)}, u32[]{:S(2)}) copy-start(s32[24,24]{0,1:T(8,128)} %copy-done.12) | copy-start | bytes 6916

commit v2 on v1

--- a/solution.py
+++ b/solution.py
@@ -1,6 +1,8 @@
 import jax
 import jax.numpy as jnp
 from jax import lax
+from jax.experimental import pallas as pl
+from jax.experimental.pallas import tpu as pltpu
 from jax.sharding import PartitionSpec as P
 
 screen = 0.5
@@ -25,19 +27,40 @@
     )
 
 
-def exchange_many(arrays, width):
+def exchange_y(block, width):
+    return jnp.concatenate(
+        [shifted(block[:, -width:], "gy", 1), block, shifted(block[:, :width], "gy", -1)], axis=1
+    )
+
+
+def gather_x(block):
+    count, index = lax.axis_size("gx"), lax.axis_index("gx")
+    step = 1
+    while step < count:
+        other = lax.ppermute(block, "gx", [(i, i ^ step) for i in range(count)])
+        lower = (index & step) == 0
+        block = jnp.where(
+            lower, jnp.concatenate([block, other], axis=0), jnp.concatenate([other, block], axis=0)
+        )
+        step *= 2
+    return block
+
+
+def exchange_many(arrays, width, exchanger=exchange):
     depth = arrays[0].shape[2]
-    packed = exchange(jnp.concatenate(arrays, axis=2), width)
+    packed = exchanger(jnp.concatenate(arrays, axis=2), width)
     return [packed[:, :, i * depth:(i + 1) * depth] for i in range(len(arrays))]
 
 
-def inside(span_x, span_y, width):
+def inside(span_x, span_y, width, whole_x=False):
+    index_y = lax.axis_index("gy") * span_y - width + jnp.arange(span_y + 2 * width)
+    total_y = span_y * lax.axis_size("gy")
+    keep_y = (index_y >= 0) & (index_y < total_y)
+    if whole_x:
+        return jnp.broadcast_to(keep_y[None, :, None], (span_x, span_y + 2 * width, 1))
     index_x = lax.axis_index("gx") * span_x - width + jnp.arange(span_x + 2 * width)
-    index_y = lax.axis_index("gy") * span_y - width + jnp.arange(span_y + 2 * width)
     total_x = span_x * lax.axis_size("gx")
-    total_y = span_y * lax.axis_size("gy")
     keep_x = (index_x >= 0) & (index_x < total_x)
-    keep_y = (index_y >= 0) & (index_y < total_y)
     return (keep_x[:, None] & keep_y[None, :])[:, :, None]
 
 
@@ -81,12 +104,12 @@
     return jnp.where(allowed, residual, 0.0)
 
 
-def restrict(values, width, span_x, span_y):
-    rows = values[width - 1:width + span_x]
+def restrict(values, width_x, width_y, span_x, span_y):
+    rows = values[width_x - 1:width_x + span_x]
     before = rows[:-1].reshape(span_x // 2, 2, *rows.shape[1:])[:, 0]
     paired = rows[1:].reshape(span_x // 2, 2, *rows.shape[1:])
     across = 0.25 * before + 0.5 * paired[:, 0] + 0.25 * paired[:, 1]
-    cols = across[:, width - 1:width + span_y]
+    cols = across[:, width_y - 1:width_y + span_y]
     before = cols[:, :-1].reshape(cols.shape[0], span_y // 2, 2, cols.shape[2])[:, :, 0]
     paired = cols[:, 1:].reshape(cols.shape[0], span_y // 2, 2, cols.shape[2])
     return 0.25 * before + 0.5 * paired[:, :, 0] + 0.25 * paired[:, :, 1]
@@ -115,38 +138,78 @@
     allowed = inside(span_x, span_y, width)
     iterate = sweeps(jnp.zeros_like(source), source, divisor, weight, allowed, 1)
     residual = residual_of(iterate, source, divisor, weight, allowed)
-    coarse_source = restrict(residual, width, span_x, span_y)
+    coarse_source = restrict(residual, width, width, span_x, span_y)
     coarse_coefficient = coarsen(interior(coefficient_ext, width))
     return iterate, source, divisor, weight, allowed, coarse_source, coarse_coefficient
 
 
-def coarsest(source, coefficient, width):
-    span_x, span_y = source.shape[0], source.shape[1]
-    source, coefficient = exchange_many([source, coefficient], width)
+def descend_whole_x(grid_level, source, coefficient, width):
+    span_y = source.shape[1]
+    source, coefficient = exchange_many([source, coefficient], width, exchange_y)
+    span_x = source.shape[0]
+    weight = 0.25**grid_level
+    divisor = 4.0 * weight + 2.0 + coefficient
+    allowed = inside(span_x, span_y, width, whole_x=True)
+    iterate = sweeps(jnp.zeros_like(source), source, divisor, weight, allowed, 1)
+    residual = residual_of(iterate, source, divisor, weight, allowed)
+    residual = jnp.pad(residual, ((1, 0), (0, 0), (0, 0)))
+    coarse_source = restrict(residual, 1, width, span_x, span_y)
+    coarse_coefficient = coarsen(coefficient[:, width:width + span_y])
+    return iterate, source, divisor, weight, allowed, coarse_source, coarse_coefficient
+
+
+def coarsest_whole_x(source, coefficient, width):
+    span_y = source.shape[1]
+    source, coefficient = exchange_many([source, coefficient], width, exchange_y)
+    span_x = source.shape[0]
     weight = 0.25**3
     divisor = 4.0 * weight + 2.0 + coefficient
-    allowed = inside(span_x, span_y, width)
+    allowed = inside(span_x, span_y, width, whole_x=True)
     iterate = jnp.zeros_like(source)
     plan = [(0, 1, 0), (1, 0), (1, 0), (1,)]
     for step, colours in enumerate(plan):
         if step > 0:
-            iterate = exchange(interior(iterate, width), width)
+            iterate = exchange_y(iterate[:, width:width + span_y], width)
         for colour in colours:
             iterate = half_sweep(iterate, source, divisor, weight, allowed, colour)
     return iterate
 
 
+def x_window(values, start, length, margin):
+    padded = jnp.pad(values, ((margin, margin), (0, 0), (0, 0)))
+    return lax.dynamic_slice_in_dim(padded, start, length, axis=0)
+
+
+def dirichlet_kernel(volts_ref, potential_ref, charge_ref, region_ref, packed_ref):
+    region = region_ref[...]
+    total = jnp.zeros(region.shape, jnp.float32)
+    for electrode in range(volts_ref.shape[0]):
+        total = total + jnp.where(region == electrode + 1, volts_ref[electrode], jnp.float32(0.0))
+    depth = region.shape[2]
+    packed_ref[:, :, 0:depth] = potential_ref[...]
+    packed_ref[:, :, depth:2 * depth] = charge_ref[...]
+    packed_ref[:, :, 2 * depth:3 * depth] = region.astype(jnp.float32)
+    packed_ref[:, :, 3 * depth:4 * depth] = total
+
+
+def packed_inputs(potential, charge, region, electrode_volts):
+    span_x, span_y, depth = potential.shape
+    vmem = pl.BlockSpec(memory_space=pltpu.VMEM)
+    return pl.pallas_call(
+        dirichlet_kernel,
+        out_shape=jax.ShapeDtypeStruct((span_x, span_y, 4 * depth), jnp.float32),
+        in_specs=[pl.BlockSpec(memory_space=pltpu.SMEM), vmem, vmem, vmem],
+        out_specs=vmem,
+    )(electrode_volts, potential, charge, region)
+
+
 def body(potential, charge, region, electrode_volts):
-    span_x, span_y = potential.shape[0], potential.shape[1]
-    dirichlet = jnp.zeros_like(potential)
-    for electrode in range(electrode_volts.shape[0]):
-        dirichlet = dirichlet + jnp.where(
-            region == electrode + 1, electrode_volts[electrode], jnp.float32(0.0)
-        )
+    span_x, span_y, depth = potential.shape
     width = HALO_FINE
-    potential, charge, region_f, dirichlet = exchange_many(
-        [potential, charge, region.astype(jnp.float32), dirichlet], width
-    )
+    packed = exchange(packed_inputs(potential, charge, region, electrode_volts), width)
+    potential, charge, region_f, dirichlet = [
+        packed[:, :, i * depth:(i + 1) * depth] for i in range(4)
+    ]
     movable = jnp.logical_and(region_f == 0.0, inside(span_x, span_y, width))
     flat_sum, vertical = neighbour_sums(pad_plane(potential))
     source = (
@@ -156,16 +219,21 @@
     divisor = 4.0 * 1.0 + 2.0 + coefficient
     iterate = sweeps(dirichlet, source, divisor, 1.0, movable, 1)
     residual = residual_of(iterate, source, divisor, 1.0, movable)
-    source_1 = restrict(residual, width, span_x, span_y)
+    source_1 = restrict(residual, width, width, span_x, span_y)
     coefficient_1 = coarsen(interior(coefficient, width))
 
     level_1 = descend(1, source_1, coefficient_1, HALO_MID)
-    level_2 = descend(2, level_1[5], level_1[6], HALO_MID)
-    iterate_3 = coarsest(level_2[5], level_2[6], HALO_COARSE)
+    source_2, coefficient_2 = level_1[5], level_1[6]
+    span_x2 = source_2.shape[0]
+    whole = gather_x(jnp.concatenate([source_2, coefficient_2], axis=2))
+    level_2 = descend_whole_x(2, whole[:, :, :depth], whole[:, :, depth:], HALO_MID)
+    iterate_3 = coarsest_whole_x(level_2[5], level_2[6], HALO_COARSE)
 
     iterate_2, source_2, divisor_2, weight_2, allowed_2 = level_2[:5]
     iterate_2 = sweeps(iterate_2 + lift(iterate_3), source_2, divisor_2, weight_2, allowed_2, 1)
-    iterate_2 = exchange(interior(iterate_2, HALO_MID), HALO_MID // 2)
+    rim = HALO_MID // 2
+    iterate_2 = exchange_y(iterate_2[:, HALO_MID:HALO_MID + source_2.shape[1] - 2 * HALO_MID], rim)
+    iterate_2 = x_window(iterate_2, lax.axis_index("gx") * span_x2, span_x2 + 2 * rim, rim)
 
     iterate_1, source_1, divisor_1, weight_1, allowed_1 = level_1[:5]
     iterate_1 = sweeps(iterate_1 + lift(iterate_2), source_1, divisor_1, weight_1, allowed_1, 1)

time: 266 us -> 218 us (0.82)
  the two profiles are of different devices: /device:TPU:51 before, /device:TPU:16 now
where the time goes in v2:
time: 218 us; the launch traced here: 217 us
  starting transfers between devices  116 us (53%)
  waiting for transfers between devices  57.9 us (27%)
  other arithmetic  25.5 us (12%)
  local copies, waits for them, and re-layouts  13.8 us (6%)
  Pallas kernels  2.59 us (1%)
    ppermute x20, starting transfers between devices, shifted(): return lax.ppermute(block, axis, route)  82.5 us
    ppermute x20, waiting for transfers between devices, shifted(): return lax.ppermute(block, axis, route)  47.6 us
    ppermute x4, starting transfers between devices, gather_x(): other = lax.ppermute(block, 'gx', [(i, i ^ step) for i in range(count)])  33.7 us
    select_n x18, other arithmetic, half_sweep(): return jnp.where(update, renewed, iterate)  12.5 us
    ppermute x4, waiting for transfers between devices, gather_x(): other = lax.ppermute(block, 'gx', [(i, i ^ step) for i in range(count)])  10.3 us
  transfers between devices with their start and end apart: 24, of which 22 were waited for; matrix products, arithmetic and copies ran while one was open for 1% of the time, Pallas kernels for 0%

profile of v2, /device:TPU:16, one launch (start us, length us, event | category | flops | bytes accessed | tf_op | source)
XLA Modules:
  0.0 217.2 jit_solution(10722262584166062036)
XLA Ops:
  0.0 2.6 %shard_map.46 = f32[16,16,1024]{2,1,0:T(8,128)} custom-call(f32[16]{0:T(128)} %volts_ref.1, f32[16,16,256]{2,1,0:T(8,128)} %potential_ref.1, f32[16,16,256]{2,1,0:T(8,128)} %charge_ref.1, s32[16,16,256]{2,1,0:T(8,128)} %region_ref.1), custom_call_target="tpu_custom_call" | custom-call | tf_op jit(solution)/shard_map/pallas_call | solution.py:198
  2.6 1.2 fusion.253
  3.8 1.3 collective-permute-start.1
  5.1 3.0 %collective-permute-start = (f32[4,16,1024]{2,1,0:T(8,128)S(1)}, f32[4,16,1024]{2,1,0:T(8,128)S(1)}, u32[]{:S(2)}, u32[]{:S(2)}) collective-permute-start(f32[4,16,1024]{2,1,0:T(8,128)S(1)} %get-tuple-element.17), channel_id=1, source_target_pairs={{0,64},{64,128},{128,192},{192,256},{256,320},{320,384},{384,448},... | collective-permute-start | bytes 786440 | tf_op jit(solution)/shard_map/ppermute | solution.py:18
  8.2 1.0 collective-permute-done
  9.4 18.1 %collective-permute-start.3 = (f32[24,4,1024]{2,1,0:T(4,128)S(1)}, f32[24,4,1024]{2,1,0:T(4,128)S(1)}, u32[]{:S(2)}, u32[]{:S(2)}) collective-permute-start(f32[24,4,1024]{2,1,0:T(4,128)S(1)} %get-tuple-element.16), channel_id=1, source_target_pairs={{1,0},{2,1},{3,2},{4,3},{5,4},{6,5},{7,6},{8,7},{9,8},{10,9},{11,1... | collective-permute-start | bytes 1179656 | tf_op jit(solution)/shard_map/ppermute | solution.py:18
  27.5 1.9 collective-permute-start.2
  29.6 4.4 %collective-permute-done.3 = f32[24,4,1024]{2,1,0:T(4,128)S(1)} collective-permute-done((f32[24,4,1024]{2,1,0:T(4,128)S(1)}, f32[24,4,1024]{2,1,0:T(4,128)S(1)}, u32[]{:S(2)}, u32[]{:S(2)}) %collective-permute-start.3) | collective-permute-done | bytes 393248 | tf_op jit(solution)/shard_map/ppermute | solution.py:18
  34.0 5.3 %collective-permute-done.2 = f32[24,4,1024]{2,1,0:T(4,128)S(1)} collective-permute-done((f32[24,4,1024]{2,1,0:T(4,128)S(1)}, f32[24,4,1024]{2,1,0:T(4,128)S(1)}, u32[]{:S(2)}, u32[]{:S(2)}) %collective-permute-start.2) | collective-permute-done | bytes 393248 | tf_op jit(solution)/shard_map/ppermute | solution.py:18
  39.8 1.6 fusion.58
  41.4 1.5 fusion.62
  42.9 1.3 broadcast_add_fusion
  44.8 1.3 collective-permute-start.5
  46.1 13.6 %collective-permute-start.4 = (f32[4,8,512]{2,0,1:T(4,128)S(1)}, f32[4,8,512]{2,0,1:T(4,128)S(1)}, u32[]{:S(2)}, u32[]{:S(2)}) collective-permute-start(f32[4,8,512]{2,0,1:T(4,128)S(1)} %get-tuple-element.62), channel_id=1, source_target_pairs={{0,64},{64,128},{128,192},{192,256},{256,320},{320,384},{384,448},... | collective-permute-start | bytes 196616 | tf_op jit(solution)/shard_map/ppermute | solution.py:18
  59.8 0.8 collective-permute-done.4
  60.6 1.9 collective-permute-start.7
  62.6 3.9 %collective-permute-start.6 = (f32[16,4,512]{2,0,1:T(8,128)S(1)}, f32[16,4,512]{2,0,1:T(8,128)S(1)}, u32[]{:S(2)}, u32[]{:S(2)}) collective-permute-start(f32[16,4,512]{2,0,1:T(8,128)S(1)} %get-tuple-element.44), channel_id=1, source_target_pairs={{0,1},{1,2},{2,3},{3,4},{4,5},{5,6},{6,7},{7,8},{8,9},{9,10},{10,1... | collective-permute-start | bytes 393224 | tf_op jit(solution)/shard_map/ppermute | solution.py:18
  66.5 1.0 collective-permute-done.7
  67.5 4.3 %collective-permute-done.6 = f32[16,4,512]{2,0,1:T(8,128)S(1)} collective-permute-done((f32[16,4,512]{2,0,1:T(8,128)S(1)}, f32[16,4,512]{2,0,1:T(8,128)S(1)}, u32[]{:S(2)}, u32[]{:S(2)}) %collective-permute-start.6) | collective-permute-done | bytes 131104 | tf_op jit(solution)/shard_map/ppermute | solution.py:18
  71.9 1.1 fusion.256
  74.6 12.1 %collective-permute-start.8 = (f32[4,4,512]{2,0,1:T(4,128)S(1)}, f32[4,4,512]{2,0,1:T(4,128)S(1)}, u32[]{:S(2)}, u32[]{:S(2)}) collective-permute-start(f32[4,4,512]{2,0,1:T(4,128)S(1)} %pad_maximum_fusion.13), channel_id=1, source_target_pairs={{0,64},{64,0},{128,192},{192,128},{256,320},{320,256},{384,448},{4... | collective-permute-start | bytes 98312 | tf_op jit(solution)/shard_map/ppermute | solution.py:40
  86.7 0.8 collective-permute-done.8
  87.6 8.9 %collective-permute-start.9 = (f32[8,4,512]{2,0,1:T(8,128)S(1)}, f32[8,4,512]{2,0,1:T(8,128)S(1)}, u32[]{:S(2)}, u32[]{:S(2)}) collective-permute-start(f32[8,4,512]{2,0,1:T(8,128)S(1)} %maximum_select_fusion.3), channel_id=1, source_target_pairs={{0,128},{64,192},{128,0},{192,64},{256,384},{320,448},{384,256},{4... | collective-permute-start | bytes 196616 | tf_op jit(solution)/shard_map/ppermute | solution.py:40
  96.5 2.4 %collective-permute-done.9 = f32[8,4,512]{2,0,1:T(8,128)S(1)} collective-permute-done((f32[8,4,512]{2,0,1:T(8,128)S(1)}, f32[8,4,512]{2,0,1:T(8,128)S(1)}, u32[]{:S(2)}, u32[]{:S(2)}) %collective-permute-start.9) | collective-permute-done | bytes 65568 | tf_op jit(solution)/shard_map/ppermute | solution.py:40
  98.9 7.7 %collective-permute-start.10 = (f32[16,4,512]{2,0,1:T(8,128)S(1)}, f32[16,4,512]{2,0,1:T(8,128)S(1)}, u32[]{:S(2)}, u32[]{:S(2)}) collective-permute-start(f32[16,4,512]{2,0,1:T(8,128)S(1)} %maximum_select_fusion.2), channel_id=1, source_target_pairs={{0,256},{64,320},{128,384},{192,448},{256,0},{320,64},{384,128},{4... | collective-permute-start | bytes 393224 | tf_op jit(solution)/shard_map/ppermute | solution.py:40
  106.7 2.9 %collective-permute-done.10 = f32[16,4,512]{2,0,1:T(8,128)S(1)} collective-permute-done((f32[16,4,512]{2,0,1:T(8,128)S(1)}, f32[16,4,512]{2,0,1:T(8,128)S(1)}, u32[]{:S(2)}, u32[]{:S(2)}) %collective-permute-start.10) | collective-permute-done | bytes 131104 | tf_op jit(solution)/shard_map/ppermute | solution.py:40
  109.6 4.9 %collective-permute-start.11 = (f32[32,4,512]{2,0,1:T(8,128)S(1)}, f32[32,4,512]{2,0,1:T(8,128)S(1)}, u32[]{:S(2)}, u32[]{:S(2)}) collective-permute-start(f32[32,4,512]{2,0,1:T(8,128)S(1)} %maximum_select_fusion.1), channel_id=1, source_target_pairs={{0,512},{64,576},{128,640},{192,704},{256,768},{320,832},{384,896}... | collective-permute-start | bytes 786440 | tf_op jit(solution)/shard_map/ppermute | solution.py:40
  115.2 4.2 %collective-permute-done.11 = f32[32,4,512]{2,0,1:T(8,128)S(1)} collective-permute-done((f32[32,4,512]{2,0,1:T(8,128)S(1)}, f32[32,4,512]{2,0,1:T(8,128)S(1)}, u32[]{:S(2)}, u32[]{:S(2)}) %collective-permute-start.11) | collective-permute-done | bytes 262176 | tf_op jit(solution)/shard_map/ppermute | solution.py:40
  119.4 2.7 %collective-permute-start.13 = (f32[64,4,512]{2,0,1:T(8,128)S(1)}, f32[64,4,512]{2,0,1:T(8,128)S(1)}, u32[]{:S(2)}, u32[]{:S(2)}) collective-permute-start(f32[64,4,512]{2,0,1:T(8,128)S(1)} %maximum_select_fusion), channel_id=1, source_target_pairs={{1,0},{2,1},{3,2},{4,3},{5,4},{6,5},{7,6},{8,7},{9,8},{10,9},{11,1... | collective-permute-start | bytes 1572872 | tf_op jit(solution)/shard_map/ppermute | solution.py:18
  122.1 3.2 %collective-permute-start.12 = (f32[64,4,512]{2,0,1:T(8,128)S(1)}, f32[64,4,512]{2,0,1:T(8,128)}, u32[]{:S(2)}, u32[]{:S(2)}) collective-permute-start(f32[64,4,512]{2,0,1:T(8,128)S(1)} %maximum_select_fusion), channel_id=1, source_target_pairs={{0,1},{1,2},{2,3},{3,4},{4,5},{5,6},{6,7},{7,8},{8,9},{9,10},{10,1... | collective-permute-start | bytes 1572872 | tf_op jit(solution)/shard_map/ppermute | solution.py:18
  126.2 6.0 %collective-permute-done.13 = f32[64,4,512]{2,0,1:T(8,128)S(1)} collective-permute-done((f32[64,4,512]{2,0,1:T(8,128)S(1)}, f32[64,4,512]{2,0,1:T(8,128)S(1)}, u32[]{:S(2)}, u32[]{:S(2)}) %collective-permute-start.13) | collective-permute-done | bytes 524320 | tf_op jit(solution)/shard_map/ppermute | solution.py:18
  132.2 0.8 copy-done.13
  133.0 4.9 %collective-permute-done.12 = f32[64,4,512]{2,0,1:T(8,128)} collective-permute-done((f32[64,4,512]{2,0,1:T(8,128)S(1)}, f32[64,4,512]{2,0,1:T(8,128)}, u32[]{:S(2)}, u32[]{:S(2)}) %collective-permute-start.12) | collective-permute-done | bytes 524320 | tf_op jit(solution)/shard_map/ppermute | solution.py:18
  137.8 1.4 pad_maximum_fusion.1
  139.2 0.9 fusion.40
  140.2 0.9 fusion.8
  141.1 0.9 copy-done.2
  142.0 1.2 fusion.16
  143.1 1.4 reshape.302
  144.5 1.0 pad_slice_fusion.70
  145.5 2.6 %reshape.301 = f32[32,2,12,256]{3,1,0,2:T(2,128)} reshape(f32[64,12,256]{2,0,1:T(8,128)} %pad_slice_fusion.70) | data formatting | bytes 1572864 | tf_op jit(solution)/shard_map/reshape | solution.py:109
  148.0 1.9 fusion.95
  150.1 1.9 collective-permute-start.15
  152.0 4.1 %collective-permute-start.14 = (f32[32,2,512]{2,0,1:T(8,128)S(1)}, f32[32,2,512]{2,0,1:T(8,128)S(1)}, u32[]{:S(2)}, u32[]{:S(2)}) collective-permute-start(f32[32,2,512]{2,0,1:T(8,128)S(1)} %pad_maximum_fusion.11), channel_id=1, source_target_pairs={{0,1},{1,2},{2,3},{3,4},{4,5},{5,6},{6,7},{7,8},{8,9},{9,10},{10,1... | collective-permute-start | bytes 393224 | tf_op jit(solution)/shard_map/ppermute | solution.py:18
  157.0 4.0 %collective-permute-done.14 = f32[32,2,512]{2,0,1:T(8,128)S(1)} collective-permute-done((f32[32,2,512]{2,0,1:T(8,128)S(1)}, f32[32,2,512]{2,0,1:T(8,128)S(1)}, u32[]{:S(2)}, u32[]{:S(2)}) %collective-permute-start.14) | collective-permute-done | bytes 131104 | tf_op jit(solution)/shard_map/ppermute | solution.py:18
  161.8 1.9 collective-permute-start.17
  163.7 3.9 %collective-permute-start.16 = (f32[32,2,256]{2,0,1:T(8,128)S(1)}, f32[32,2,256]{2,0,1:T(8,128)S(1)}, u32[]{:S(2)}, u32[]{:S(2)}) collective-permute-start(f32[32,2,256]{2,0,1:T(8,128)S(1)} %slice_select_fusion.4), channel_id=1, source_target_pairs={{0,1},{1,2},{2,3},{3,4},{4,5},{5,6},{6,7},{7,8},{8,9},{9,10},{10,1... | collective-permute-start | bytes 196616 | tf_op jit(solution)/shard_map/ppermute | solution.py:18
  168.0 4.0 %collective-permute-done.16 = f32[32,2,256]{2,0,1:T(8,128)S(1)} collective-permute-done((f32[32,2,256]{2,0,1:T(8,128)S(1)}, f32[32,2,256]{2,0,1:T(8,128)S(1)}, u32[]{:S(2)}, u32[]{:S(2)}) %collective-permute-start.16) | collective-permute-done | bytes 65568 | tf_op jit(solution)/shard_map/ppermute | solution.py:18
  172.5 1.9 collective-permute-start.19
  174.5 3.9 %collective-permute-start.18 = (f32[32,2,256]{2,0,1:T(8,128)S(1)}, f32[32,2,256]{2,0,1:T(8,128)S(1)}, u32[]{:S(2)}, u32[]{:S(2)}) collective-permute-start(f32[32,2,256]{2,0,1:T(8,128)S(1)} %slice_select_fusion.3), channel_id=1, source_target_pairs={{0,1},{1,2},{2,3},{3,4},{4,5},{5,6},{6,7},{7,8},{8,9},{9,10},{10,1... | collective-permute-start | bytes 196616 | tf_op jit(solution)/shard_map/ppermute | solution.py:18
  178.7 4.0 %collective-permute-done.18 = f32[32,2,256]{2,0,1:T(8,128)S(1)} collective-permute-done((f32[32,2,256]{2,0,1:T(8,128)S(1)}, f32[32,2,256]{2,0,1:T(8,128)S(1)}, u32[]{:S(2)}, u32[]{:S(2)}) %collective-permute-start.18) | collective-permute-done | bytes 65568 | tf_op jit(solution)/shard_map/ppermute | solution.py:18
  183.2 1.9 collective-permute-start.21
  185.2 3.9 %collective-permute-start.20 = (f32[32,2,256]{2,0,1:T(8,128)S(1)}, f32[32,2,256]{2,0,1:T(8,128)S(1)}, u32[]{:S(2)}, u32[]{:S(2)}) collective-permute-start(f32[32,2,256]{2,0,1:T(8,128)S(1)} %slice_select_fusion.2), channel_id=1, source_target_pairs={{0,1},{1,2},{2,3},{3,4},{4,5},{5,6},{6,7},{7,8},{8,9},{9,10},{10,1... | collective-permute-start | bytes 196616 | tf_op jit(solution)/shard_map/ppermute | solution.py:18
  189.4 4.0 %collective-permute-done.20 = f32[32,2,256]{2,0,1:T(8,128)S(1)} collective-permute-done((f32[32,2,256]{2,0,1:T(8,128)S(1)}, f32[32,2,256]{2,0,1:T(8,128)S(1)}, u32[]{:S(2)}, u32[]{:S(2)}) %collective-permute-start.20) | collective-permute-done | bytes 65568 | tf_op jit(solution)/shard_map/ppermute | solution.py:18
  193.8 0.9 broadcast_in_dim.36
  194.7 2.0 reshape.306
  196.7 1.1 bitcast_add_fusion
  197.8 0.9 fusion.24
  198.7 0.9 fusion.32
  199.6 2.1 collective-permute-start.22
  201.7 6.0 %collective-permute-start.23 = (f32[64,2,256]{2,0,1:T(8,128)S(1)}, f32[64,2,256]{2,0,1:T(8,128)S(1)}, u32[]{:S(2)}, u32[]{:S(2)}) collective-permute-start(f32[64,2,256]{2,0,1:T(8,128)S(1)} %get-tuple-element.19), channel_id=1, source_target_pairs={{1,0},{2,1},{3,2},{4,3},{5,4},{6,5},{7,6},{8,7},{9,8},{10,9},{11,1... | collective-permute-start | bytes 393224 | tf_op jit(solution)/shard_map/ppermute | solution.py:18
  208.7 1.5 collective-permute-done.23
  212.9 1.8 fusion.71
  215.2 2.0 slice_select_fusion
  (144 shorter events, 12.6 us)
Async XLA Ops:
  2.6 6.6 %copy-start.1 = (f32[16,16,1024]{2,1,0:T(8,128)S(1)}, f32[16,16,1024]{2,1,0:T(8,128)}, u32[]{:S(2)}) copy-start(f32[16,16,1024]{2,1,0:T(8,128)} %shard_map.46) | copy-start | bytes 3145732
  3.8 4.4 %collective-permute-start.1 = (f32[4,16,1024]{2,1,0:T(8,128)S(1)}, f32[4,16,1024]{2,1,0:T(8,128)S(1)}, u32[]{:S(2)}, u32[]{:S(2)}) collective-permute-start(f32[4,16,1024]{2,1,0:T(8,128)S(1)} %get-tuple-element.18), channel_id=1, source_target_pairs={{64,0},{128,64},{192,128},{256,192},{320,256},{384,320},{448,384},... | collective-permute-start | bytes 786440 | tf_op jit(solution)/shard_map/ppermute | solution.py:18
  5.1 4.2 %collective-permute-start = (f32[4,16,1024]{2,1,0:T(8,128)S(1)}, f32[4,16,1024]{2,1,0:T(8,128)S(1)}, u32[]{:S(2)}, u32[]{:S(2)}) collective-permute-start(f32[4,16,1024]{2,1,0:T(8,128)S(1)} %get-tuple-element.17), channel_id=1, source_target_pairs={{0,64},{64,128},{128,192},{192,256},{256,320},{320,384},{384,448},... | collective-permute-start | bytes 786440 | tf_op jit(solution)/shard_map/ppermute | solution.py:18
  8.2 33.2 %copy-start.16 = (s32[24,24]{1,0:T(8,128)}, s32[24,24]{1,0:T(8,128)S(1)}, u32[]{:S(2)}) copy-start(s32[24,24]{1,0:T(8,128)S(1)} %iota_add_fusion.1) | copy-start | bytes 6916
  9.4 24.6 %collective-permute-start.3 = (f32[24,4,1024]{2,1,0:T(4,128)S(1)}, f32[24,4,1024]{2,1,0:T(4,128)S(1)}, u32[]{:S(2)}, u32[]{:S(2)}) collective-permute-start(f32[24,4,1024]{2,1,0:T(4,128)S(1)} %get-tuple-element.16), channel_id=1, source_target_pairs={{1,0},{2,1},{3,2},{4,3},{5,4},{6,5},{7,6},{8,7},{9,8},{10,9},{11,1... | collective-permute-start | bytes 1179656 | tf_op jit(solution)/shard_map/ppermute | solution.py:18
  27.5 11.8 %collective-permute-start.2 = (f32[24,4,1024]{2,1,0:T(4,128)S(1)}, f32[24,4,1024]{2,1,0:T(4,128)S(1)}, u32[]{:S(2)}, u32[]{:S(2)}) collective-permute-start(f32[24,4,1024]{2,1,0:T(4,128)S(1)} %get-tuple-element.15), channel_id=1, source_target_pairs={{0,1},{1,2},{2,3},{3,4},{4,5},{5,6},{6,7},{7,8},{8,9},{9,10},{10,1... | collective-permute-start | bytes 1179656 | tf_op jit(solution)/shard_map/ppermute | solution.py:18
  29.5 43.8 %copy-start.18 = (pred[16,16]{0,1:T(8,128)(4,1)}, pred[16,16]{0,1:T(8,128)(4,1)S(1)}, u32[]{:S(2)}) copy-start(pred[16,16]{0,1:T(8,128)(4,1)S(1)} %broadcast_and_fusion.1) | copy-start | bytes 772
  39.7 3.2 %copy-start = (f32[24,24,1024]{2,1,0:T(8,128)}, f32[24,24,1024]{2,1,0:T(8,128)S(1)}, u32[]{:S(2)}) copy-start(f32[24,24,1024]{2,1,0:T(8,128)S(1)} %pad_maximum_fusion) | copy-start | bytes 7077892
  41.4 2.8 %copy-start.6 = (pred[24,24,256]{2,1,0:T(8,128)(4,1)}, pred[24,24,256]{2,1,0:T(8,128)(4,1)S(1)}, u32[]{:S(2)}) copy-start(pred[24,24,256]{2,1,0:T(8,128)(4,1)S(1)} %get-tuple-element.9) | copy-start | bytes 442372
  42.9 1.3 copy-start.4
  44.8 14.9 %collective-permute-start.5 = (f32[4,8,512]{2,0,1:T(4,128)S(1)}, f32[4,8,512]{2,0,1:T(4,128)S(1)}, u32[]{:S(2)}, u32[]{:S(2)}) collective-permute-start(f32[4,8,512]{2,0,1:T(4,128)S(1)} %get-tuple-element.63), channel_id=1, source_target_pairs={{64,0},{128,64},{192,128},{256,192},{320,256},{384,320},{448,384},... | collective-permute-start | bytes 196616 | tf_op jit(solution)/shard_map/ppermute | solution.py:18
  46.1 14.4 %collective-permute-start.4 = (f32[4,8,512]{2,0,1:T(4,128)S(1)}, f32[4,8,512]{2,0,1:T(4,128)S(1)}, u32[]{:S(2)}, u32[]{:S(2)}) collective-permute-start(f32[4,8,512]{2,0,1:T(4,128)S(1)} %get-tuple-element.62), channel_id=1, source_target_pairs={{0,64},{64,128},{128,192},{192,256},{256,320},{320,384},{384,448},... | collective-permute-start | bytes 196616 | tf_op jit(solution)/shard_map/ppermute | solution.py:18
  60.6 6.9 %collective-permute-start.7 = (f32[16,4,512]{2,0,1:T(8,128)S(1)}, f32[16,4,512]{2,0,1:T(8,128)S(1)}, u32[]{:S(2)}, u32[]{:S(2)}) collective-permute-start(f32[16,4,512]{2,0,1:T(8,128)S(1)} %get-tuple-element.45), channel_id=1, source_target_pairs={{1,0},{2,1},{3,2},{4,3},{5,4},{6,5},{7,6},{8,7},{9,8},{10,9},{11,1... | collective-permute-start | bytes 393224 | tf_op jit(solution)/shard_map/ppermute | solution.py:18
  62.6 9.3 %collective-permute-start.6 = (f32[16,4,512]{2,0,1:T(8,128)S(1)}, f32[16,4,512]{2,0,1:T(8,128)S(1)}, u32[]{:S(2)}, u32[]{:S(2)}) collective-permute-start(f32[16,4,512]{2,0,1:T(8,128)S(1)} %get-tuple-element.44), channel_id=1, source_target_pairs={{0,1},{1,2},{2,3},{3,4},{4,5},{5,6},{6,7},{7,8},{8,9},{9,10},{10,1... | collective-permute-start | bytes 393224 | tf_op jit(solution)/shard_map/ppermute | solution.py:18
  73.4 0.7 copy-start.9
  74.6 12.9 %collective-permute-start.8 = (f32[4,4,512]{2,0,1:T(4,128)S(1)}, f32[4,4,512]{2,0,1:T(4,128)S(1)}, u32[]{:S(2)}, u32[]{:S(2)}) collective-permute-start(f32[4,4,512]{2,0,1:T(4,128)S(1)} %pad_maximum_fusion.13), channel_id=1, source_target_pairs={{0,64},{64,0},{128,192},{192,128},{256,320},{320,256},{384,448},{4... | collective-permute-start | bytes 98312 | tf_op jit(solution)/shard_map/ppermute | solution.py:40
  87.6 11.4 %collective-permute-start.9 = (f32[8,4,512]{2,0,1:T(8,128)S(1)}, f32[8,4,512]{2,0,1:T(8,128)S(1)}, u32[]{:S(2)}, u32[]{:S(2)}) collective-permute-start(f32[8,4,512]{2,0,1:T(8,128)S(1)} %maximum_select_fusion.3), channel_id=1, source_target_pairs={{0,128},{64,192},{128,0},{192,64},{256,384},{320,448},{384,256},{4... | collective-permute-start | bytes 196616 | tf_op jit(solution)/shard_map/ppermute | solution.py:40
  98.9 10.7 %collective-permute-start.10 = (f32[16,4,512]{2,0,1:T(8,128)S(1)}, f32[16,4,512]{2,0,1:T(8,128)S(1)}, u32[]{:S(2)}, u32[]{:S(2)}) collective-permute-start(f32[16,4,512]{2,0,1:T(8,128)S(1)} %maximum_select_fusion.2), channel_id=1, source_target_pairs={{0,256},{64,320},{128,384},{192,448},{256,0},{320,64},{384,128},{4... | collective-permute-start | bytes 393224 | tf_op jit(solution)/shard_map/ppermute | solution.py:40
  109.6 9.8 %collective-permute-start.11 = (f32[32,4,512]{2,0,1:T(8,128)S(1)}, f32[32,4,512]{2,0,1:T(8,128)S(1)}, u32[]{:S(2)}, u32[]{:S(2)}) collective-permute-start(f32[32,4,512]{2,0,1:T(8,128)S(1)} %maximum_select_fusion.1), channel_id=1, source_target_pairs={{0,512},{64,576},{128,640},{192,704},{256,768},{320,832},{384,896}... | collective-permute-start | bytes 786440 | tf_op jit(solution)/shard_map/ppermute | solution.py:40
  114.6 25.6 %copy-start.22 = (pred[12]{0:T(512)(128)(4,1)}, pred[12]{0:T(512)(128)(4,1)S(1)}, u32[]{:S(2)}) copy-start(pred[12]{0:T(512)(128)(4,1)S(1)} %compare_and_fusion.9) | copy-start | bytes 40
  119.4 12.7 %collective-permute-start.13 = (f32[64,4,512]{2,0,1:T(8,128)S(1)}, f32[64,4,512]{2,0,1:T(8,128)S(1)}, u32[]{:S(2)}, u32[]{:S(2)}) collective-permute-start(f32[64,4,512]{2,0,1:T(8,128)S(1)} %maximum_select_fusion), channel_id=1, source_target_pairs={{1,0},{2,1},{3,2},{4,3},{5,4},{6,5},{7,6},{8,7},{9,8},{10,9},{11,1... | collective-permute-start | bytes 1572872 | tf_op jit(solution)/shard_map/ppermute | solution.py:18
  122.1 15.7 %collective-permute-start.12 = (f32[64,4,512]{2,0,1:T(8,128)S(1)}, f32[64,4,512]{2,0,1:T(8,128)}, u32[]{:S(2)}, u32[]{:S(2)}) collective-permute-start(f32[64,4,512]{2,0,1:T(8,128)S(1)} %maximum_select_fusion), channel_id=1, source_target_pairs={{0,1},{1,2},{2,3},{3,4},{4,5},{5,6},{6,7},{7,8},{8,9},{9,10},{10,1... | collective-permute-start | bytes 1572872 | tf_op jit(solution)/shard_map/ppermute | solution.py:18
  132.2 0.8 copy-start.13
  141.1 0.9 copy-start.2
  145.5 2.6 %copy-start.8 = (f32[32,2,12,256]{3,1,0,2:T(2,128)S(1)}, f32[32,2,12,256]{3,1,0,2:T(2,128)}, u32[]{:S(2)}) copy-start(f32[32,2,12,256]{3,1,0,2:T(2,128)} %reshape.302) | copy-start | bytes 2359300
  148.0 8.1 %copy-start.14 = (s32[32,6]{0,1:T(8,128)S(1)}, s32[32,6]{0,1:T(8,128)}, u32[]{:S(2)}) copy-start(s32[32,6]{0,1:T(8,128)} %iota_add_fusion.4) | copy-start | bytes 2308
  148.0 8.1 %copy-start.20 = (pred[6]{0:T(512)(128)(4,1)S(1)}, pred[6]{0:T(512)(128)(4,1)}, u32[]{:S(2)}) copy-start(pred[6]{0:T(512)(128)(4,1)} %compare_and_fusion.8) | copy-start | bytes 22
  150.1 6.9 %collective-permute-start.15 = (f32[32,2,512]{2,0,1:T(8,128)S(1)}, f32[32,2,512]{2,0,1:T(8,128)S(1)}, u32[]{:S(2)}, u32[]{:S(2)}) collective-permute-start(f32[32,2,512]{2,0,1:T(8,128)S(1)} %pad_maximum_fusion.11), channel_id=1, source_target_pairs={{1,0},{2,1},{3,2},{4,3},{5,4},{6,5},{7,6},{8,7},{9,8},{10,9},{11,1... | collective-permute-start | bytes 393224 | tf_op jit(solution)/shard_map/ppermute | solution.py:18
  152.0 9.0 %collective-permute-start.14 = (f32[32,2,512]{2,0,1:T(8,128)S(1)}, f32[32,2,512]{2,0,1:T(8,128)S(1)}, u32[]{:S(2)}, u32[]{:S(2)}) collective-permute-start(f32[32,2,512]{2,0,1:T(8,128)S(1)} %pad_maximum_fusion.11), channel_id=1, source_target_pairs={{0,1},{1,2},{2,3},{3,4},{4,5},{5,6},{6,7},{7,8},{8,9},{9,10},{10,1... | collective-permute-start | bytes 393224 | tf_op jit(solution)/shard_map/ppermute | solution.py:18
  161.8 6.2 %collective-permute-start.17 = (f32[32,2,256]{2,0,1:T(8,128)S(1)}, f32[32,2,256]{2,0,1:T(8,128)S(1)}, u32[]{:S(2)}, u32[]{:S(2)}) collective-permute-start(f32[32,2,256]{2,0,1:T(8,128)S(1)} %slice_select_fusion.4), channel_id=1, source_target_pairs={{1,0},{2,1},{3,2},{4,3},{5,4},{6,5},{7,6},{8,7},{9,8},{10,9},{11,1... | collective-permute-start | bytes 196616 | tf_op jit(solution)/shard_map/ppermute | solution.py:18
  163.7 8.3 %collective-permute-start.16 = (f32[32,2,256]{2,0,1:T(8,128)S(1)}, f32[32,2,256]{2,0,1:T(8,128)S(1)}, u32[]{:S(2)}, u32[]{:S(2)}) collective-permute-start(f32[32,2,256]{2,0,1:T(8,128)S(1)} %slice_select_fusion.4), channel_id=1, source_target_pairs={{0,1},{1,2},{2,3},{3,4},{4,5},{5,6},{6,7},{7,8},{8,9},{9,10},{10,1... | collective-permute-start | bytes 196616 | tf_op jit(solution)/shard_map/ppermute | solution.py:18
  172.5 20.9 %copy-start.15 = (s32[32,6]{0,1:T(8,128)S(1)}, s32[32,6]{0,1:T(8,128)}, u32[]{:S(2)}) copy-start(s32[32,6]{0,1:T(8,128)} %iota_add_fusion.4) | copy-start | bytes 2308
  172.5 20.9 %copy-start.21 = (pred[6]{0:T(512)(128)(4,1)S(1)}, pred[6]{0:T(512)(128)(4,1)}, u32[]{:S(2)}) copy-start(pred[6]{0:T(512)(128)(4,1)} %compare_and_fusion.8) | copy-start | bytes 22
  172.5 6.2 %collective-permute-start.19 = (f32[32,2,256]{2,0,1:T(8,128)S(1)}, f32[32,2,256]{2,0,1:T(8,128)S(1)}, u32[]{:S(2)}, u32[]{:S(2)}) collective-permute-start(f32[32,2,256]{2,0,1:T(8,128)S(1)} %slice_select_fusion.3), channel_id=1, source_target_pairs={{1,0},{2,1},{3,2},{4,3},{5,4},{6,5},{7,6},{8,7},{9,8},{10,9},{11,1... | collective-permute-start | bytes 196616 | tf_op jit(solution)/shard_map/ppermute | solution.py:18
  174.5 8.3 %collective-permute-start.18 = (f32[32,2,256]{2,0,1:T(8,128)S(1)}, f32[32,2,256]{2,0,1:T(8,128)S(1)}, u32[]{:S(2)}, u32[]{:S(2)}) collective-permute-start(f32[32,2,256]{2,0,1:T(8,128)S(1)} %slice_select_fusion.3), channel_id=1, source_target_pairs={{0,1},{1,2},{2,3},{3,4},{4,5},{5,6},{6,7},{7,8},{8,9},{9,10},{10,1... | collective-permute-start | bytes 196616 | tf_op jit(solution)/shard_map/ppermute | solution.py:18
  183.2 6.2 %collective-permute-start.21 = (f32[32,2,256]{2,0,1:T(8,128)S(1)}, f32[32,2,256]{2,0,1:T(8,128)S(1)}, u32[]{:S(2)}, u32[]{:S(2)}) collective-permute-start(f32[32,2,256]{2,0,1:T(8,128)S(1)} %slice_select_fusion.2), channel_id=1, source_target_pairs={{1,0},{2,1},{3,2},{4,3},{5,4},{6,5},{7,6},{8,7},{9,8},{10,9},{11,1... | collective-permute-start | bytes 196616 | tf_op jit(solution)/shard_map/ppermute | solution.py:18
  185.2 8.3 %collective-permute-start.20 = (f32[32,2,256]{2,0,1:T(8,128)S(1)}, f32[32,2,256]{2,0,1:T(8,128)S(1)}, u32[]{:S(2)}, u32[]{:S(2)}) collective-permute-start(f32[32,2,256]{2,0,1:T(8,128)S(1)} %slice_select_fusion.2), channel_id=1, source_target_pairs={{0,1},{1,2},{2,3},{3,4},{4,5},{5,6},{6,7},{7,8},{8,9},{9,10},{10,1... | collective-permute-start | bytes 196616 | tf_op jit(solution)/shard_map/ppermute | solution.py:18
  193.7 2.9 %copy-start.3 = (f32[64,12,256]{2,0,1:T(8,128)S(1)}, f32[64,12,256]{2,0,1:T(8,128)}, u32[]{:S(2)}) copy-start(f32[64,12,256]{2,0,1:T(8,128)} %copy-done.2) | copy-start | bytes 2359300
  193.8 4.0 %copy-start.23 = (pred[12]{0:T(512)(128)(4,1)S(1)}, pred[12]{0:T(512)(128)(4,1)}, u32[]{:S(2)}) copy-start(pred[12]{0:T(512)(128)(4,1)} %copy-done.22) | copy-start | bytes 40
  198.7 9.1 %copy-start.19 = (pred[16,16]{0,1:T(8,128)(4,1)S(1)}, pred[16,16]{0,1:T(8,128)(4,1)}, u32[]{:S(2)}) copy-start(pred[16,16]{0,1:T(8,128)(4,1)} %copy-done.18) | copy-start | bytes 772
  199.6 10.8 %copy-start.10 = (f32[16,16,256]{2,0,1:T(8,128)S(1)}, f32[16,16,256]{2,0,1:T(8,128)}, u32[]{:S(2)}) copy-start(f32[16,16,256]{2,0,1:T(8,128)} %copy-done.9) | copy-start | bytes 786436
  199.6 9.1 %collective-permute-start.22 = (f32[64,2,256]{2,0,1:T(8,128)S(1)}, f32[64,2,256]{2,0,1:T(8,128)S(1)}, u32[]{:S(2)}, u32[]{:S(2)}) collective-permute-start(f32[64,2,256]{2,0,1:T(8,128)S(1)} %get-tuple-element.20), channel_id=1, source_target_pairs={{0,1},{1,2},{2,3},{3,4},{4,5},{5,6},{6,7},{7,8},{8,9},{9,10},{10,1... | collective-permute-start | bytes 393224 | tf_op jit(solution)/shard_map/ppermute | solution.py:18
  201.7 8.5 %collective-permute-start.23 = (f32[64,2,256]{2,0,1:T(8,128)S(1)}, f32[64,2,256]{2,0,1:T(8,128)S(1)}, u32[]{:S(2)}, u32[]{:S(2)}) collective-permute-start(f32[64,2,256]{2,0,1:T(8,128)S(1)} %get-tuple-element.19), channel_id=1, source_target_pairs={{1,0},{2,1},{3,2},{4,3},{5,4},{6,5},{7,6},{8,7},{9,8},{10,9},{11,1... | collective-permute-start | bytes 393224 | tf_op jit(solution)/shard_map/ppermute | solution.py:18
  210.4 1.0 copy-start.11
  210.5 1.0 copy-start.12
  211.7 1.1 copy-start.5
  211.7 1.1 copy-start.7
  212.0 0.8 copy-start.17

commit v3 on v2

v3 whole, which is shorter than its diff:
```python
import jax
import jax.numpy as jnp
from jax import lax
from jax.experimental import pallas as pl
from jax.experimental.pallas import tpu as pltpu
from jax.sharding import PartitionSpec as P

screen = 0.5

HALO_0 = 4
HALO_1 = 14
HALO_2 = 5
HALO_3 = 9


def shifted(block, axis, distance):
    count = lax.axis_size(axis)
    route = [(i, i + distance) for i in range(count) if 0 <= i + distance < count]
    if not route:
        return jnp.zeros_like(block)
    return lax.ppermute(block, axis, route)


def along(block, width, axis, dim):
    span = block.shape[dim]
    reach = -(-width // span)
    part = width - (reach - 1) * span
    low = [shifted(lax.slice_in_dim(block, span - part, span, axis=dim), axis, reach)]
    low += [shifted(block, axis, d) for d in range(reach - 1, 0, -1)]
    high = [shifted(block, axis, -d) for d in range(1, reach)]
    high += [shifted(lax.slice_in_dim(block, 0, part, axis=dim), axis, -reach)]
    return jnp.concatenate(low + [block] + high, axis=dim)


def exchange(block, width):
    return along(along(block, width, "gx", 0), width, "gy", 1)


def exchange_y(block, width):
    return jnp.concatenate(
        [shifted(block[:, -width:], "gy", 1), block, shifted(block[:, :width], "gy", -1)], axis=1
    )


def gather_x(block):
    count, index = lax.axis_size("gx"), lax.axis_index("gx")
    step = 1
    while step < count:
        other = lax.ppermute(block, "gx", [(i, i ^ step) for i in range(count)])
        lower = (index & step) == 0
        block = jnp.where(
            lower, jnp.concatenate([block, other], axis=0), jnp.concatenate([other, block], axis=0)
        )
        step *= 2
    return block


def exchange_many(arrays, width, exchanger=exchange):
    depth = arrays[0].shape[2]
    packed = exchanger(jnp.concatenate(arrays, axis=2), width)
    return [packed[:, :, i * depth:(i + 1) * depth] for i in range(len(arrays))]


def inside(span_x, span_y, width, whole_x=False):
    index_y = lax.axis_index("gy") * span_y - width + jnp.arange(span_y + 2 * width)
    total_y = span_y * lax.axis_size("gy")
    keep_y = (index_y >= 0) & (index_y < total_y)
    if whole_x:
        return jnp.broadcast_to(keep_y[None, :, None], (span_x, span_y + 2 * width, 1))
    index_x = lax.axis_index("gx") * span_x - width + jnp.arange(span_x + 2 * width)
    total_x = span_x * lax.axis_size("gx")
    keep_x = (index_x >= 0) & (index_x < total_x)
    return (keep_x[:, None] & keep_y[None, :])[:, :, None]


def pad_plane(values):
    return jnp.pad(values, ((1, 1), (1, 1), (0, 0)))


def neighbour_sums(padded):
    interior = padded[1:-1, 1:-1]
    flat_sum = padded[2:, 1:-1] + padded[:-2, 1:-1] + padded[1:-1, 2:] + padded[1:-1, :-2]
    padded_z = jnp.pad(interior, ((0, 0), (0, 0), (1, 1)))
    vertical = padded_z[:, :, 2:] + padded_z[:, :, :-2]
    return (flat_sum, vertical)


def checker(span_x, span_y, span_z):
    index_x = jnp.arange(span_x, dtype=jnp.int32)[:, None, None]
    index_y = jnp.arange(span_y, dtype=jnp.int32)[None, :, None]
    index_z = jnp.arange(span_z, dtype=jnp.int32)[None, None, :]
    return (index_x + index_y + index_z) % 2


def half_sweep(iterate, source, divisor, weight, allowed, colour):
    flat_sum, vertical = neighbour_sums(pad_plane(iterate))
    renewed = (source + weight * flat_sum + vertical) / divisor
    span_x, span_y, span_z = iterate.shape
    update = jnp.logical_and(checker(span_x, span_y, span_z) == colour, allowed)
    return jnp.where(update, renewed, iterate)


def sweeps(iterate, source, divisor, weight, allowed, count):
    for _ in range(count):
        iterate = half_sweep(iterate, source, divisor, weight, allowed, 0)
        iterate = half_sweep(iterate, source, divisor, weight, allowed, 1)
    return iterate


def residual_of(iterate, source, divisor, weight, allowed):
    flat_sum, vertical = neighbour_sums(pad_plane(iterate))
    residual = source - (divisor * iterate - (weight * flat_sum + vertical))
    return jnp.where(allowed, residual, 0.0)


def restrict(values, width, rim, span_x, span_y):
    low = width - 2 * rim - 1
    rows = values[low:width + span_x + 2 * rim]
    count = span_x // 2 + 2 * rim
    before = rows[:-1].reshape(count, 2, *rows.shape[1:])[:, 0]
    paired = rows[1:].reshape(count, 2, *rows.shape[1:])
    across = 0.25 * before + 0.5 * paired[:, 0] + 0.25 * paired[:, 1]
    cols = across[:, low:width + span_y + 2 * rim]
    count_y = span_y // 2 + 2 * rim
    before = cols[:, :-1].reshape(count, count_y, 2, cols.shape[2])[:, :, 0]
    paired = cols[:, 1:].reshape(count, count_y, 2, cols.shape[2])
    return 0.25 * before + 0.5 * paired[:, :, 0] + 0.25 * paired[:, :, 1]


def coarsen(values):
    paired = values.reshape(values.shape[0] // 2, 2, values.shape[1], values.shape[2])
    across = 0.5 * (paired[:, 0] + paired[:, 1])
    paired = across.reshape(across.shape[0], across.shape[1] // 2, 2, across.shape[2])
    return 0.5 * (paired[:, :, 0] + paired[:, :, 1])


def lift(coarse):
    return jnp.repeat(jnp.repeat(coarse, 2, axis=0), 2, axis=1)


def interior(values, width):
    return values[width:values.shape[0] - width, width:values.shape[1] - width]


def trimmed(values, cut):
    return values[cut:values.shape[0] - cut, cut:values.shape[1] - cut]


def dirichlet_kernel(volts_ref, potential_ref, charge_ref, region_ref, packed_ref):
    region = region_ref[...]
    total = jnp.zeros(region.shape, jnp.float32)
    for electrode in range(volts_ref.shape[0]):
        total = total + jnp.where(region == electrode + 1, volts_ref[electrode], jnp.float32(0.0))
    depth = region.shape[2]
    packed_ref[:, :, 0:depth] = potential_ref[...]
    packed_ref[:, :, depth:2 * depth] = charge_ref[...]
    packed_ref[:, :, 2 * depth:3 * depth] = region.astype(jnp.float32)
    packed_ref[:, :, 3 * depth:4 * depth] = total


def packed_inputs(potential, charge, region, electrode_volts):
    span_x, span_y, depth = potential.shape
    vmem = pl.BlockSpec(memory_space=pltpu.VMEM)
    return pl.pallas_call(
        dirichlet_kernel,
        out_shape=jax.ShapeDtypeStruct((span_x, span_y, 4 * depth), jnp.float32),
        in_specs=[pl.BlockSpec(memory_space=pltpu.SMEM), vmem, vmem, vmem],
        out_specs=vmem,
    )(electrode_volts, potential, charge, region)


def body(potential, charge, region, electrode_volts):
    span_x, span_y, depth = potential.shape
    packed = exchange(packed_inputs(potential, charge, region, electrode_volts), HALO_0)
    potential, charge, region_f, dirichlet = [
        packed[:, :, i * depth:(i + 1) * depth] for i in range(4)
    ]
    movable = jnp.logical_and(region_f == 0.0, inside(span_x, span_y, HALO_0))
    flat_sum, vertical = neighbour_sums(pad_plane(potential))
    source_0 = (
        charge - (6.0 * potential - (flat_sum + vertical)) - screen * (jnp.exp(potential) - 1.0)
    )
    coefficient_0 = screen * jnp.exp(potential)
    divisor_0 = 4.0 * 1.0 + 2.0 + coefficient_0
    iterate_0 = sweeps(dirichlet, source_0, divisor_0, 1.0, movable, 1)
    residual = residual_of(iterate_0, source_0, divisor_0, 1.0, movable)
    source_1 = restrict(residual, HALO_0, 0, span_x, span_y)
    coefficient_1 = coarsen(interior(coefficient_0, HALO_0))

    span_x1, span_y1 = span_x // 2, span_y // 2
    source_1, coefficient_1 = exchange_many([source_1, coefficient_1], HALO_1)
    weight_1 = 0.25
    divisor_1 = 4.0 * weight_1 + 2.0 + coefficient_1
    allowed_1 = inside(span_x1, span_y1, HALO_1)
    iterate_1 = sweeps(jnp.zeros_like(source_1), source_1, divisor_1, weight_1, allowed_1, 1)
    residual = residual_of(iterate_1, source_1, divisor_1, weight_1, allowed_1)
    source_2 = restrict(residual, HALO_1, HALO_2, span_x1, span_y1)
    keep = HALO_1 - 2 * HALO_2
    coefficient_2 = coarsen(trimmed(coefficient_1, keep))

    span_x2, span_y2 = span_x1 // 2, span_y1 // 2
    weight_2 = 0.25**2
    divisor_2 = 4.0 * weight_2 + 2.0 + coefficient_2
    allowed_2 = inside(span_x2, span_y2, HALO_2)
    iterate_2 = sweeps(jnp.zeros_like(source_2), source_2, divisor_2, weight_2, allowed_2, 1)
    residual = residual_of(iterate_2, source_2, divisor_2, weight_2, allowed_2)
    source_3 = restrict(residual, HALO_2, 0, span_x2, span_y2)
    coefficient_3 = coarsen(interior(coefficient_2, HALO_2))

    span_x3, span_y3 = span_x2 // 2, span_y2 // 2
    source_3, coefficient_3 = exchange_many([source_3, coefficient_3], HALO_3)
    weight_3 = 0.25**3
    divisor_3 = 4.0 * weight_3 + 2.0 + coefficient_3
    allowed_3 = inside(span_x3, span_y3, HALO_3)
    iterate_3 = sweeps(jnp.zeros_like(source_3), source_3, divisor_3, weight_3, allowed_3, 4)

    cut = HALO_2 - 4
    iterate_2 = trimmed(iterate_2, cut) + lift(trimmed(iterate_3, HALO_3 - 2))
    iterate_2 = sweeps(
        iterate_2, trimmed(source_2, cut), trimmed(divisor_2, cut), weight_2, trimmed(allowed_2, cut), 1
    )
    cut = HALO_1 - 4
    iterate_1 = trimmed(iterate_1, cut) + lift(trimmed(iterate_2, 2))
    iterate_1 = sweeps(
        iterate_1, trimmed(source_1, cut), trimmed(divisor_1, cut), weight_1, trimmed(allowed_1, cut), 1
    )
    lifted = lift(trimmed(iterate_1, 2))
    iterate_0 = iterate_0 + jnp.where(movable, lifted, 0.0)
    iterate_0 = sweeps(iterate_0, source_0, divisor_0, 1.0, movable, 1)
    return interior(iterate_0, HALO_0)


def solution(mesh):
    placed = (P("gx", "gy", None), P("gx", "gy", None), P("gx", "gy", None), P())
    return jax.shard_map(
        body, mesh=mesh, in_specs=placed, out_specs=P("gx", "gy", None), check_vma=False
    )
```

time: 218 us -> 276 us (1.27)
  the two profiles are of different devices: /device:TPU:16 before, /device:TPU:56 now
where the time goes in v3:
time: 276 us; the launch traced here: 275 us
  starting transfers between devices  141 us (51%)
  waiting for transfers between devices  70.2 us (25%)
  other arithmetic  37.8 us (14%)
  local copies, waits for them, and re-layouts  21.7 us (8%)
    ppermute x32, starting transfers between devices, shifted(): return lax.ppermute(block, axis, route)  141 us
    ppermute x32, waiting for transfers between devices, shifted(): return lax.ppermute(block, axis, route)  70.2 us
    select_n x17, other arithmetic, half_sweep(): return jnp.where(update, renewed, iterate)  17.4 us
  transfers between devices with their start and end apart: 32, of which 14 were waited for; matrix products, arithmetic and copies ran while one was open for 4% of the time, Pallas kernels for 0%

profile of v3, /device:TPU:56, one launch (start us, length us, event | category | flops | bytes accessed | tf_op | source)
XLA Modules:
  0.0 274.7 jit_solution(14549939109249628435)
XLA Ops:
  0.0 2.5 shard_map.46
  2.5 1.2 fusion.245
  3.7 1.9 collective-permute-start
  5.6 7.5 %collective-permute-start.1 = (f32[4,16,1024]{2,1,0:T(8,128)S(1)}, f32[4,16,1024]{2,1,0:T(8,128)S(1)}, u32[]{:S(2)}, u32[]{:S(2)}) collective-permute-start(f32[4,16,1024]{2,1,0:T(8,128)S(1)} %get-tuple-element.27), channel_id=1, source_target_pairs={{64,0},{128,64},{192,128},{256,192},{320,256},{384,320},{448,384},... | collective-permute-start | bytes 786440 | tf_op jit(solution)/shard_map/ppermute | solution.py:21
  15.8 2.0 collective-permute-done
  18.5 4.3 %collective-permute-start.2 = (f32[24,4,1024]{2,1,0:T(4,128)S(1)}, f32[24,4,1024]{2,1,0:T(4,128)S(1)}, u32[]{:S(2)}, u32[]{:S(2)}) collective-permute-start(f32[24,4,1024]{2,1,0:T(4,128)S(1)} %get-tuple-element.21), channel_id=1, source_target_pairs={{0,1},{1,2},{2,3},{3,4},{4,5},{5,6},{6,7},{7,8},{8,9},{9,10},{10,1... | collective-permute-start | bytes 1179656 | tf_op jit(solution)/shard_map/ppermute | solution.py:21
  22.8 16.6 %collective-permute-start.3 = (f32[24,4,1024]{2,1,0:T(4,128)S(1)}, f32[24,4,1024]{2,1,0:T(4,128)S(1)}, u32[]{:S(2)}, u32[]{:S(2)}) collective-permute-start(f32[24,4,1024]{2,1,0:T(4,128)S(1)} %get-tuple-element.22), channel_id=1, source_target_pairs={{1,0},{2,1},{3,2},{4,3},{5,4},{6,5},{7,6},{8,7},{9,8},{10,9},{11,1... | collective-permute-start | bytes 1179656 | tf_op jit(solution)/shard_map/ppermute | solution.py:21
  41.5 2.7 %collective-permute-done.2 = f32[24,4,1024]{2,1,0:T(4,128)S(1)} collective-permute-done((f32[24,4,1024]{2,1,0:T(4,128)S(1)}, f32[24,4,1024]{2,1,0:T(4,128)S(1)}, u32[]{:S(2)}, u32[]{:S(2)}) %collective-permute-start.2) | collective-permute-done | bytes 393248 | tf_op jit(solution)/shard_map/ppermute | solution.py:21
  44.2 1.8 collective-permute-done.3
  46.6 1.6 fusion.32
  48.2 1.5 fusion.36
  49.6 1.3 broadcast_add_fusion
  51.6 4.8 %collective-permute-start.5 = (f32[8,8,512]{2,0,1:T(8,128)S(1)}, f32[8,8,512]{2,0,1:T(8,128)S(1)}, u32[]{:S(2)}, u32[]{:S(2)}) collective-permute-start(f32[8,8,512]{2,0,1:T(8,128)S(1)} %pad_maximum_fusion.6), channel_id=1, source_target_pairs={{0,64},{64,128},{128,192},{192,256},{256,320},{320,384},{384,448},... | collective-permute-start | bytes 393224 | tf_op jit(solution)/shard_map/ppermute | solution.py:21
  56.4 4.6 %collective-permute-start.6 = (f32[8,8,512]{2,0,1:T(8,128)S(1)}, f32[8,8,512]{2,0,1:T(8,128)S(1)}, u32[]{:S(2)}, u32[]{:S(2)}) collective-permute-start(f32[8,8,512]{2,0,1:T(8,128)S(1)} %pad_maximum_fusion.6), channel_id=1, source_target_pairs={{64,0},{128,64},{192,128},{256,192},{320,256},{384,320},{448,384},... | collective-permute-start | bytes 393224 | tf_op jit(solution)/shard_map/ppermute | solution.py:21
  61.1 6.9 %collective-permute-start.4 = (f32[6,8,512]{2,0,1:T(8,128)S(1)}, f32[6,8,512]{2,0,1:T(8,128)S(1)}, u32[]{:S(2)}, u32[]{:S(2)}) collective-permute-start(f32[6,8,512]{2,0,1:T(8,128)S(1)} %get-tuple-element.72), channel_id=1, source_target_pairs={{0,128},{64,192},{128,256},{192,320},{256,384},{320,448},{384,512}... | collective-permute-start | bytes 294920 | tf_op jit(solution)/shard_map/ppermute | solution.py:21
  68.0 2.9 %collective-permute-start.7 = (f32[6,8,512]{2,0,1:T(8,128)S(1)}, f32[6,8,512]{2,0,1:T(8,128)S(1)}, u32[]{:S(2)}, u32[]{:S(2)}) collective-permute-start(f32[6,8,512]{2,0,1:T(8,128)S(1)} %get-tuple-element.71), channel_id=1, source_target_pairs={{128,0},{192,64},{256,128},{320,192},{384,256},{448,320},{512,384}... | collective-permute-start | bytes 294920 | tf_op jit(solution)/shard_map/ppermute | solution.py:21
  71.5 2.6 collective-permute-done.4
  74.0 10.0 %collective-permute-done.7 = f32[6,8,512]{2,0,1:T(8,128)S(1)} collective-permute-done((f32[6,8,512]{2,0,1:T(8,128)S(1)}, f32[6,8,512]{2,0,1:T(8,128)S(1)}, u32[]{:S(2)}, u32[]{:S(2)}) %collective-permute-start.7) | collective-permute-done | bytes 98336 | tf_op jit(solution)/shard_map/ppermute | solution.py:21
  85.2 1.9 collective-permute-start.8
  87.3 1.9 collective-permute-start.10
  90.7 6.2 %collective-permute-start.9 = (f32[36,8,512]{2,1,0:T(8,128)S(1)}, f32[36,8,512]{2,1,0:T(8,128)S(1)}, u32[]{:S(2)}, u32[]{:S(2)}) collective-permute-start(f32[36,8,512]{2,1,0:T(8,128)S(1)} %copy.79), channel_id=1, source_target_pairs={{1,0},{2,1},{3,2},{4,3},{5,4},{6,5},{7,6},{8,7},{9,8},{10,9},{11,1... | collective-permute-start | bytes 1769480 | tf_op jit(solution)/shard_map/ppermute | solution.py:21
  97.4 5.0 %collective-permute-start.11 = (f32[36,6,512]{2,0,1:T(8,128)S(1)}, f32[36,6,512]{2,0,1:T(8,128)S(1)}, u32[]{:S(2)}, u32[]{:S(2)}) collective-permute-start(f32[36,6,512]{2,0,1:T(8,128)S(1)} %get-tuple-element.31), channel_id=1, source_target_pairs={{2,0},{3,1},{4,2},{5,3},{6,4},{7,5},{8,6},{9,7},{10,8},{11,9},{12,... | collective-permute-start | bytes 1327112 | tf_op jit(solution)/shard_map/ppermute | solution.py:21
  102.4 23.3 %collective-permute-done.10 = f32[36,6,512]{2,0,1:T(8,128)S(1)} collective-permute-done((f32[36,6,512]{2,0,1:T(8,128)S(1)}, f32[36,6,512]{2,0,1:T(8,128)S(1)}, u32[]{:S(2)}, u32[]{:S(2)}) %collective-permute-start.10) | collective-permute-done | bytes 442400 | tf_op jit(solution)/shard_map/ppermute | solution.py:21
  125.8 1.2 fusion.248
  127.0 1.2 fusion.249
  128.3 1.1 collective-permute-done.11
  130.5 2.6 reshape.445
  133.1 2.0 fusion.141
  137.5 1.3 mul.278
  138.8 1.4 fusion.260
  140.2 2.3 fusion.13
  142.6 3.0 %slice_add_fusion = (f32[36,36,256]{2,0,1:T(8,128)}, f32[36,36,256]{2,0,1:T(8,128)S(1)}) fusion(f32[36,36,512]{2,0,1:T(8,128)S(1)} %constant_dynamic-update-slice_fusion, f32[36,36,256]{2,0,1:T(8,128)S(1)} %fusion.13, pred[36,36]{0,1:T(8,128)(4,1)S(1)} %copy-done.19, s32[36,36]{0,1:T(8,128)S(1)} %copy-done.18), kind=kLoop, calls=%fused_computation.33 | loop fusion | flops 7962624 | bytes 6642000 | tf_op jit(solution)/shard_map/add | solution.py:193
  145.6 1.6 fusion.9
  151.4 1.3 collective-permute-start.12
  152.7 1.9 collective-permute-start.13
  154.6 6.7 %collective-permute-start.14 = (f32[2,2,512]{2,1,0:T(2,128)S(1)}, f32[2,2,512]{2,1,0:T(2,128)S(1)}, u32[]{:S(2)}, u32[]{:S(2)}) collective-permute-start(f32[2,2,512]{2,1,0:T(2,128)S(1)} %pad_maximum_fusion.7), channel_id=1, source_target_pairs={{0,192},{64,256},{128,320},{192,384},{256,448},{320,512},{384,576}... | collective-permute-start | bytes 24584 | tf_op jit(solution)/shard_map/ppermute | solution.py:21
  161.4 1.9 collective-permute-start.15
  163.3 2.0 collective-permute-start.16
  165.3 7.4 %collective-permute-start.17 = (f32[2,2,512]{2,1,0:T(2,128)S(1)}, f32[2,2,512]{2,1,0:T(2,128)S(1)}, u32[]{:S(2)}, u32[]{:S(2)}) collective-permute-start(f32[2,2,512]{2,1,0:T(2,128)S(1)} %pad_maximum_fusion.7), channel_id=1, source_target_pairs={{64,0},{128,64},{192,128},{256,192},{320,256},{384,320},{448,384},... | collective-permute-start | bytes 24584 | tf_op jit(solution)/shard_map/ppermute | solution.py:21
  172.8 1.9 collective-permute-start.18
  174.8 1.3 collective-permute-start.19
  176.1 1.3 collective-permute-start.20
  177.4 1.3 collective-permute-start.21
  178.8 4.4 %collective-permute-done.18 = f32[2,2,512]{2,1,0:T(2,128)S(1)} collective-permute-done((f32[2,2,512]{2,1,0:T(2,128)S(1)}, f32[2,2,512]{2,1,0:T(2,128)S(1)}, u32[]{:S(2)}, u32[]{:S(2)}) %collective-permute-start.18) | collective-permute-done | bytes 8224 | tf_op jit(solution)/shard_map/ppermute | solution.py:21
  183.2 1.4 collective-permute-done.19
  184.6 4.4 %collective-permute-done.21 = f32[1,2,512]{2,1,0:T(2,128)S(1)} collective-permute-done((f32[1,2,512]{2,1,0:T(2,128)S(1)}, f32[1,2,512]{2,1,0:T(2,128)S(1)}, u32[]{:S(2)}, u32[]{:S(2)}) %collective-permute-start.21) | collective-permute-done | bytes 4128 | tf_op jit(solution)/shard_map/ppermute | solution.py:21
  189.0 5.4 %collective-permute-start.23 = (f32[20,2,512]{2,1,0:T(2,128)S(1)}, f32[20,2,512]{2,1,0:T(2,128)S(1)}, u32[]{:S(2)}, u32[]{:S(2)}) collective-permute-start(f32[20,2,512]{2,1,0:T(2,128)S(1)} %constant_dynamic-update-slice_fusion.5), channel_id=1, source_target_pairs={{0,4},{1,5},{2,6},{3,7},{4,8},{5,9},{6,10},{7,11},{8,12},{9,13},{1... | collective-permute-start | bytes 245768 | tf_op jit(solution)/shard_map/ppermute | solution.py:21
  194.4 2.5 collective-permute-start.24
  196.9 10.0 %collective-permute-start.25 = (f32[20,2,512]{2,1,0:T(2,128)S(1)}, f32[20,2,512]{2,1,0:T(2,128)S(1)}, u32[]{:S(2)}, u32[]{:S(2)}) collective-permute-start(f32[20,2,512]{2,1,0:T(2,128)S(1)} %constant_dynamic-update-slice_fusion.5), channel_id=1, source_target_pairs={{0,2},{1,3},{2,4},{3,5},{4,6},{5,7},{6,8},{7,9},{8,10},{9,11},{10,... | collective-permute-start | bytes 245768 | tf_op jit(solution)/shard_map/ppermute | solution.py:21
  206.9 5.2 %collective-permute-start.22 = (f32[20,1,512]{2,1,0:T(1,128)S(1)}, f32[20,1,512]{2,1,0:T(1,128)S(1)}, u32[]{:S(2)}, u32[]{:S(2)}) collective-permute-start(f32[20,1,512]{2,1,0:T(1,128)S(1)} %get-tuple-element.74), channel_id=1, source_target_pairs={{0,5},{1,6},{2,7},{3,8},{4,9},{5,10},{6,11},{7,12},{8,13},{9,14},{... | collective-permute-start | bytes 122888 | tf_op jit(solution)/shard_map/ppermute | solution.py:21
  212.1 7.6 %collective-permute-start.31 = (f32[20,1,512]{2,1,0:T(1,128)S(1)}, f32[20,1,512]{2,1,0:T(1,128)S(1)}, u32[]{:S(2)}, u32[]{:S(2)}) collective-permute-start(f32[20,1,512]{2,1,0:T(1,128)S(1)} %get-tuple-element.73), channel_id=1, source_target_pairs={{5,0},{6,1},{7,2},{8,3},{9,4},{10,5},{11,6},{12,7},{13,8},{14,9},{... | collective-permute-start | bytes 122888 | tf_op jit(solution)/shard_map/ppermute | solution.py:21
  220.0 3.1 %collective-permute-done.22 = f32[20,1,512]{2,1,0:T(1,128)S(1)} collective-permute-done((f32[20,1,512]{2,1,0:T(1,128)S(1)}, f32[20,1,512]{2,1,0:T(1,128)S(1)}, u32[]{:S(2)}, u32[]{:S(2)}) %collective-permute-start.22) | collective-permute-done | bytes 40992 | tf_op jit(solution)/shard_map/ppermute | solution.py:21
  223.1 3.7 %collective-permute-start.26 = (f32[20,2,512]{2,1,0:T(2,128)S(1)}, f32[20,2,512]{2,1,0:T(2,128)S(1)}, u32[]{:S(2)}, u32[]{:S(2)}) collective-permute-start(f32[20,2,512]{2,1,0:T(2,128)S(1)} %constant_dynamic-update-slice_fusion.5), channel_id=1, source_target_pairs={{0,1},{1,2},{2,3},{3,4},{4,5},{5,6},{6,7},{7,8},{8,9},{9,10},{10,1... | collective-permute-start | bytes 245768 | tf_op jit(solution)/shard_map/ppermute | solution.py:21
  226.8 4.8 %collective-permute-start.27 = (f32[20,2,512]{2,1,0:T(2,128)S(1)}, f32[20,2,512]{2,1,0:T(2,128)S(1)}, u32[]{:S(2)}, u32[]{:S(2)}) collective-permute-start(f32[20,2,512]{2,1,0:T(2,128)S(1)} %constant_dynamic-update-slice_fusion.5), channel_id=1, source_target_pairs={{1,0},{2,1},{3,2},{4,3},{5,4},{6,5},{7,6},{8,7},{9,8},{10,9},{11,1... | collective-permute-start | bytes 245768 | tf_op jit(solution)/shard_map/ppermute | solution.py:21
  231.6 5.2 %collective-permute-start.28 = (f32[20,2,512]{2,1,0:T(2,128)S(1)}, f32[20,2,512]{2,1,0:T(2,128)S(1)}, u32[]{:S(2)}, u32[]{:S(2)}) collective-permute-start(f32[20,2,512]{2,1,0:T(2,128)S(1)} %constant_dynamic-update-slice_fusion.5), channel_id=1, source_target_pairs={{2,0},{3,1},{4,2},{5,3},{6,4},{7,5},{8,6},{9,7},{10,8},{11,9},{12,... | collective-permute-start | bytes 245768 | tf_op jit(solution)/shard_map/ppermute | solution.py:21
  236.8 2.9 %collective-permute-start.29 = (f32[20,2,512]{2,1,0:T(2,128)S(1)}, f32[20,2,512]{2,1,0:T(2,128)S(1)}, u32[]{:S(2)}, u32[]{:S(2)}) collective-permute-start(f32[20,2,512]{2,1,0:T(2,128)S(1)} %constant_dynamic-update-slice_fusion.5), channel_id=1, source_target_pairs={{3,0},{4,1},{5,2},{6,3},{7,4},{8,5},{9,6},{10,7},{11,8},{12,9},{13... | collective-permute-start | bytes 245768 | tf_op jit(solution)/shard_map/ppermute | solution.py:21
  239.8 2.1 collective-permute-start.30
  242.2 8.7 %collective-permute-done.29 = f32[20,2,512]{2,1,0:T(2,128)S(1)} collective-permute-done((f32[20,2,512]{2,1,0:T(2,128)S(1)}, f32[20,2,512]{2,1,0:T(2,128)S(1)}, u32[]{:S(2)}, u32[]{:S(2)}) %collective-permute-start.29) | collective-permute-done | bytes 81952 | tf_op jit(solution)/shard_map/ppermute | solution.py:21
  250.9 4.2 %collective-permute-done.30 = f32[20,2,512]{2,1,0:T(2,128)S(1)} collective-permute-done((f32[20,2,512]{2,1,0:T(2,128)S(1)}, f32[20,2,512]{2,1,0:T(2,128)S(1)}, u32[]{:S(2)}, u32[]{:S(2)}) %collective-permute-start.30) | collective-permute-done | bytes 81952 | tf_op jit(solution)/shard_map/ppermute | solution.py:21
  255.1 3.1 %concatenate.35 = f32[20,20,512]{2,1,0:T(8,128)S(1)} concatenate(f32[20,1,512]{2,1,0:T(1,128)S(1)} %collective-permute-done.22, f32[20,2,512]{2,1,0:T(2,128)S(1)} %collective-permute-done.23, f32[20,2,512]{2,1,0:T(2,128)S(1)} %collective-permute-done.24, f32[20,2,512]{2,1,0:T(2,128)S(1)} %collective-permute-done.25, f32[20,2,512]{2,1,0:T(2,128)S(1)} %collective-permute-done.26, ...), dimensions={1} | concatenate | bytes 1638400 | tf_op jit(solution)/shard_map/concatenate | solution.py:32
  264.9 1.1 slice_select_fusion.2
  267.3 1.4 fusion.146
  270.4 1.8 fusion.45
  272.7 2.0 slice_select_fusion
  (208 shorter events, 28.4 us)
Async XLA Ops:
  2.5 15.8 %copy-start.4 = (f32[16,16,1024]{2,1,0:T(8,128)S(1)}, f32[16,16,1024]{2,1,0:T(8,128)}, u32[]{:S(2)}) copy-start(f32[16,16,1024]{2,1,0:T(8,128)} %shard_map.46) | copy-start | bytes 3145732
  3.7 14.1 %collective-permute-start = (f32[4,16,1024]{2,1,0:T(8,128)S(1)}, f32[4,16,1024]{2,1,0:T(8,128)S(1)}, u32[]{:S(2)}, u32[]{:S(2)}) collective-permute-start(f32[4,16,1024]{2,1,0:T(8,128)S(1)} %get-tuple-element.26), channel_id=1, source_target_pairs={{0,64},{64,128},{128,192},{192,256},{256,320},{320,384},{384,448},... | collective-permute-start | bytes 786440 | tf_op jit(solution)/shard_map/ppermute | solution.py:21
  5.6 12.7 %collective-permute-start.1 = (f32[4,16,1024]{2,1,0:T(8,128)S(1)}, f32[4,16,1024]{2,1,0:T(8,128)S(1)}, u32[]{:S(2)}, u32[]{:S(2)}) collective-permute-start(f32[4,16,1024]{2,1,0:T(8,128)S(1)} %get-tuple-element.27), channel_id=1, source_target_pairs={{64,0},{128,64},{192,128},{256,192},{320,256},{384,320},{448,384},... | collective-permute-start | bytes 786440 | tf_op jit(solution)/shard_map/ppermute | solution.py:21
  13.3 9.5 %copy-start.28 = (pred[36]{0:T(512)(128)(4,1)}, pred[36]{0:T(512)(128)(4,1)S(1)}, u32[]{:S(2)}) copy-start(pred[36]{0:T(512)(128)(4,1)S(1)} %get-tuple-element.83) | copy-start | bytes 112
  13.3 9.5 %copy-start.30 = (pred[36]{0:T(512)(128)(4,1)}, pred[36]{0:T(512)(128)(4,1)S(1)}, u32[]{:S(2)}) copy-start(pred[36]{0:T(512)(128)(4,1)S(1)} %get-tuple-element.84) | copy-start | bytes 112
  18.5 25.8 %collective-permute-start.2 = (f32[24,4,1024]{2,1,0:T(4,128)S(1)}, f32[24,4,1024]{2,1,0:T(4,128)S(1)}, u32[]{:S(2)}, u32[]{:S(2)}) collective-permute-start(f32[24,4,1024]{2,1,0:T(4,128)S(1)} %get-tuple-element.21), channel_id=1, source_target_pairs={{0,1},{1,2},{2,3},{3,4},{4,5},{5,6},{6,7},{7,8},{8,9},{9,10},{10,1... | collective-permute-start | bytes 1179656 | tf_op jit(solution)/shard_map/ppermute | solution.py:21
  22.8 23.2 %collective-permute-start.3 = (f32[24,4,1024]{2,1,0:T(4,128)S(1)}, f32[24,4,1024]{2,1,0:T(4,128)S(1)}, u32[]{:S(2)}, u32[]{:S(2)}) collective-permute-start(f32[24,4,1024]{2,1,0:T(4,128)S(1)} %get-tuple-element.22), channel_id=1, source_target_pairs={{1,0},{2,1},{3,2},{4,3},{5,4},{6,5},{7,6},{8,7},{9,8},{10,9},{11,1... | collective-permute-start | bytes 1179656 | tf_op jit(solution)/shard_map/ppermute | solution.py:21
  39.3 7.1 %copy-start.21 = (s32[12,12]{1,0:T(8,128)}, s32[12,12]{1,0:T(8,128)S(1)}, u32[]{:S(2)}) copy-start(s32[12,12]{1,0:T(8,128)S(1)} %iota_add_fusion.4) | copy-start | bytes 1732
  40.7 7.5 %copy-start.16 = (s32[24,24]{1,0:T(8,128)}, s32[24,24]{1,0:T(8,128)S(1)}, u32[]{:S(2)}) copy-start(s32[24,24]{1,0:T(8,128)S(1)} %iota_add_fusion.2) | copy-start | bytes 6916
  46.5 3.1 %copy-start = (f32[24,24,1024]{2,1,0:T(8,128)}, f32[24,24,1024]{2,1,0:T(8,128)S(1)}, u32[]{:S(2)}) copy-start(f32[24,24,1024]{2,1,0:T(8,128)S(1)} %pad_maximum_fusion) | copy-start | bytes 7077892
  48.1 2.8 %copy-start.10 = (pred[24,24,256]{2,1,0:T(8,128)(4,1)}, pred[24,24,256]{2,1,0:T(8,128)(4,1)S(1)}, u32[]{:S(2)}) copy-start(pred[24,24,256]{2,1,0:T(8,128)(4,1)S(1)} %get-tuple-element.13) | copy-start | bytes 442372
  49.6 1.3 copy-start.6
  51.6 32.5 %collective-permute-start.5 = (f32[8,8,512]{2,0,1:T(8,128)S(1)}, f32[8,8,512]{2,0,1:T(8,128)S(1)}, u32[]{:S(2)}, u32[]{:S(2)}) collective-permute-start(f32[8,8,512]{2,0,1:T(8,128)S(1)} %pad_maximum_fusion.6), channel_id=1, source_target_pairs={{0,64},{64,128},{128,192},{192,256},{256,320},{320,384},{384,448},... | collective-permute-start | bytes 393224 | tf_op jit(solution)/shard_map/ppermute | solution.py:21
  56.4 27.6 %collective-permute-start.6 = (f32[8,8,512]{2,0,1:T(8,128)S(1)}, f32[8,8,512]{2,0,1:T(8,128)S(1)}, u32[]{:S(2)}, u32[]{:S(2)}) collective-permute-start(f32[8,8,512]{2,0,1:T(8,128)S(1)} %pad_maximum_fusion.6), channel_id=1, source_target_pairs={{64,0},{128,64},{192,128},{256,192},{320,256},{384,320},{448,384},... | collective-permute-start | bytes 393224 | tf_op jit(solution)/shard_map/ppermute | solution.py:21
  61.1 13.0 %collective-permute-start.4 = (f32[6,8,512]{2,0,1:T(8,128)S(1)}, f32[6,8,512]{2,0,1:T(8,128)S(1)}, u32[]{:S(2)}, u32[]{:S(2)}) collective-permute-start(f32[6,8,512]{2,0,1:T(8,128)S(1)} %get-tuple-element.72), channel_id=1, source_target_pairs={{0,128},{64,192},{128,256},{192,320},{256,384},{320,448},{384,512}... | collective-permute-start | bytes 294920 | tf_op jit(solution)/shard_map/ppermute | solution.py:21
  68.0 16.1 %collective-permute-start.7 = (f32[6,8,512]{2,0,1:T(8,128)S(1)}, f32[6,8,512]{2,0,1:T(8,128)S(1)}, u32[]{:S(2)}, u32[]{:S(2)}) collective-permute-start(f32[6,8,512]{2,0,1:T(8,128)S(1)} %get-tuple-element.71), channel_id=1, source_target_pairs={{128,0},{192,64},{256,128},{320,192},{384,256},{448,320},{512,384}... | collective-permute-start | bytes 294920 | tf_op jit(solution)/shard_map/ppermute | solution.py:21
  84.8 2.4 copy-start.1
  85.2 40.5 %collective-permute-start.8 = (f32[36,8,512]{2,1,0:T(8,128)S(1)}, f32[36,8,512]{2,1,0:T(8,128)S(1)}, u32[]{:S(2)}, u32[]{:S(2)}) collective-permute-start(f32[36,8,512]{2,1,0:T(8,128)S(1)} %copy.79), channel_id=1, source_target_pairs={{0,1},{1,2},{2,3},{3,4},{4,5},{5,6},{6,7},{7,8},{8,9},{9,10},{10,1... | collective-permute-start | bytes 1769480 | tf_op jit(solution)/shard_map/ppermute | solution.py:21
  87.3 38.4 %collective-permute-start.10 = (f32[36,6,512]{2,0,1:T(8,128)S(1)}, f32[36,6,512]{2,0,1:T(8,128)S(1)}, u32[]{:S(2)}, u32[]{:S(2)}) collective-permute-start(f32[36,6,512]{2,0,1:T(8,128)S(1)} %get-tuple-element.32), channel_id=1, source_target_pairs={{0,2},{1,3},{2,4},{3,5},{4,6},{5,7},{6,8},{7,9},{8,10},{9,11},{10,... | collective-permute-start | bytes 1327112 | tf_op jit(solution)/shard_map/ppermute | solution.py:21
  90.7 36.3 %copy-start.2 = (f32[36,8,512]{2,0,1:T(8,128)S(1)}, f32[36,8,512]{2,0,1:T(8,128)}, u32[]{:S(2)}) copy-start(f32[36,8,512]{2,0,1:T(8,128)} %copy-done.1) | copy-start | bytes 1769476
  90.7 36.3 %collective-permute-start.9 = (f32[36,8,512]{2,1,0:T(8,128)S(1)}, f32[36,8,512]{2,1,0:T(8,128)S(1)}, u32[]{:S(2)}, u32[]{:S(2)}) collective-permute-start(f32[36,8,512]{2,1,0:T(8,128)S(1)} %copy.79), channel_id=1, source_target_pairs={{1,0},{2,1},{3,2},{4,3},{5,4},{6,5},{7,6},{8,7},{9,8},{10,9},{11,1... | collective-permute-start | bytes 1769480 | tf_op jit(solution)/shard_map/ppermute | solution.py:21
  97.4 31.9 %collective-permute-start.11 = (f32[36,6,512]{2,0,1:T(8,128)S(1)}, f32[36,6,512]{2,0,1:T(8,128)S(1)}, u32[]{:S(2)}, u32[]{:S(2)}) collective-permute-start(f32[36,6,512]{2,0,1:T(8,128)S(1)} %get-tuple-element.31), channel_id=1, source_target_pairs={{2,0},{3,1},{4,2},{5,3},{6,4},{7,5},{8,6},{9,7},{10,8},{11,9},{12,... | collective-permute-start | bytes 1327112 | tf_op jit(solution)/shard_map/ppermute | solution.py:21
  138.8 1.5 copy-start.18
  138.8 1.5 copy-start.19
  145.6 1.6 copy-start.5
  149.2 1.0 copy-start.9
  149.2 1.0 copy-start.20
  149.3 1.0 copy-start.25
  150.2 1.1 copy-start.26
  150.2 1.1 copy-start.27
  150.6 69.1 %copy-start.32 = (pred[12]{0:T(512)(128)(4,1)S(1)}, pred[12]{0:T(512)(128)(4,1)}, u32[]{:S(2)}) copy-start(pred[12]{0:T(512)(128)(4,1)} %slice.961) | copy-start | bytes 40
  150.6 69.1 %copy-start.33 = (pred[12]{0:T(512)(128)(4,1)S(1)}, pred[12]{0:T(512)(128)(4,1)}, u32[]{:S(2)}) copy-start(pred[12]{0:T(512)(128)(4,1)} %slice.962) | copy-start | bytes 40
  150.6 69.2 %copy-start.31 = (pred[36]{0:T(512)(128)(4,1)S(1)}, pred[36]{0:T(512)(128)(4,1)}, u32[]{:S(2)}) copy-start(pred[36]{0:T(512)(128)(4,1)} %copy-done.30) | copy-start | bytes 112
  150.6 69.3 %copy-start.29 = (pred[36]{0:T(512)(128)(4,1)S(1)}, pred[36]{0:T(512)(128)(4,1)}, u32[]{:S(2)}) copy-start(pred[36]{0:T(512)(128)(4,1)} %copy-done.28) | copy-start | bytes 112
  151.4 13.9 %collective-permute-start.12 = (f32[1,2,512]{2,1,0:T(2,128)S(1)}, f32[1,2,512]{2,1,0:T(2,128)S(1)}, u32[]{:S(2)}, u32[]{:S(2)}) collective-permute-start(f32[1,2,512]{2,1,0:T(2,128)S(1)} %get-tuple-element.78), channel_id=1, source_target_pairs={{0,320},{64,384},{128,448},{192,512},{256,576},{320,640},{384,704}... | collective-permute-start | bytes 12296 | tf_op jit(solution)/shard_map/ppermute | solution.py:21
  152.7 20.1 %collective-permute-start.13 = (f32[2,2,512]{2,1,0:T(2,128)S(1)}, f32[2,2,512]{2,1,0:T(2,128)S(1)}, u32[]{:S(2)}, u32[]{:S(2)}) collective-permute-start(f32[2,2,512]{2,1,0:T(2,128)S(1)} %pad_maximum_fusion.7), channel_id=1, source_target_pairs={{0,256},{64,320},{128,384},{192,448},{256,512},{320,576},{384,640}... | collective-permute-start | bytes 24584 | tf_op jit(solution)/shard_map/ppermute | solution.py:21
  154.6 20.1 %collective-permute-start.14 = (f32[2,2,512]{2,1,0:T(2,128)S(1)}, f32[2,2,512]{2,1,0:T(2,128)S(1)}, u32[]{:S(2)}, u32[]{:S(2)}) collective-permute-start(f32[2,2,512]{2,1,0:T(2,128)S(1)} %pad_maximum_fusion.7), channel_id=1, source_target_pairs={{0,192},{64,256},{128,320},{192,384},{256,448},{320,512},{384,576}... | collective-permute-start | bytes 24584 | tf_op jit(solution)/shard_map/ppermute | solution.py:21
  161.4 14.7 %collective-permute-start.15 = (f32[2,2,512]{2,1,0:T(2,128)S(1)}, f32[2,2,512]{2,1,0:T(2,128)S(1)}, u32[]{:S(2)}, u32[]{:S(2)}) collective-permute-start(f32[2,2,512]{2,1,0:T(2,128)S(1)} %pad_maximum_fusion.7), channel_id=1, source_target_pairs={{0,128},{64,192},{128,256},{192,320},{256,384},{320,448},{384,512}... | collective-permute-start | bytes 24584 | tf_op jit(solution)/shard_map/ppermute | solution.py:21
  163.3 14.1 %collective-permute-start.16 = (f32[2,2,512]{2,1,0:T(2,128)S(1)}, f32[2,2,512]{2,1,0:T(2,128)S(1)}, u32[]{:S(2)}, u32[]{:S(2)}) collective-permute-start(f32[2,2,512]{2,1,0:T(2,128)S(1)} %pad_maximum_fusion.7), channel_id=1, source_target_pairs={{0,64},{64,128},{128,192},{192,256},{256,320},{320,384},{384,448},... | collective-permute-start | bytes 24584 | tf_op jit(solution)/shard_map/ppermute | solution.py:21
  165.3 13.4 %collective-permute-start.17 = (f32[2,2,512]{2,1,0:T(2,128)S(1)}, f32[2,2,512]{2,1,0:T(2,128)S(1)}, u32[]{:S(2)}, u32[]{:S(2)}) collective-permute-start(f32[2,2,512]{2,1,0:T(2,128)S(1)} %pad_maximum_fusion.7), channel_id=1, source_target_pairs={{64,0},{128,64},{192,128},{256,192},{320,256},{384,320},{448,384},... | collective-permute-start | bytes 24584 | tf_op jit(solution)/shard_map/ppermute | solution.py:21
  172.8 10.4 %collective-permute-start.18 = (f32[2,2,512]{2,1,0:T(2,128)S(1)}, f32[2,2,512]{2,1,0:T(2,128)S(1)}, u32[]{:S(2)}, u32[]{:S(2)}) collective-permute-start(f32[2,2,512]{2,1,0:T(2,128)S(1)} %pad_maximum_fusion.7), channel_id=1, source_target_pairs={{128,0},{192,64},{256,128},{320,192},{384,256},{448,320},{512,384}... | collective-permute-start | bytes 24584 | tf_op jit(solution)/shard_map/ppermute | solution.py:21
  174.8 9.8 %collective-permute-start.19 = (f32[2,2,512]{2,1,0:T(2,128)S(1)}, f32[2,2,512]{2,1,0:T(2,128)S(1)}, u32[]{:S(2)}, u32[]{:S(2)}) collective-permute-start(f32[2,2,512]{2,1,0:T(2,128)S(1)} %pad_maximum_fusion.7), channel_id=1, source_target_pairs={{192,0},{256,64},{320,128},{384,192},{448,256},{512,320},{576,384}... | collective-permute-start | bytes 24584 | tf_op jit(solution)/shard_map/ppermute | solution.py:21
  176.1 8.5 %collective-permute-start.20 = (f32[2,2,512]{2,1,0:T(2,128)S(1)}, f32[2,2,512]{2,1,0:T(2,128)S(1)}, u32[]{:S(2)}, u32[]{:S(2)}) collective-permute-start(f32[2,2,512]{2,1,0:T(2,128)S(1)} %pad_maximum_fusion.7), channel_id=1, source_target_pairs={{256,0},{320,64},{384,128},{448,192},{512,256},{576,320},{640,384}... | collective-permute-start | bytes 24584 | tf_op jit(solution)/shard_map/ppermute | solution.py:21
  177.4 11.5 %collective-permute-start.21 = (f32[1,2,512]{2,1,0:T(2,128)S(1)}, f32[1,2,512]{2,1,0:T(2,128)S(1)}, u32[]{:S(2)}, u32[]{:S(2)}) collective-permute-start(f32[1,2,512]{2,1,0:T(2,128)S(1)} %get-tuple-element.77), channel_id=1, source_target_pairs={{320,0},{384,64},{448,128},{512,192},{576,256},{640,320},{704,384}... | collective-permute-start | bytes 12296 | tf_op jit(solution)/shard_map/ppermute | solution.py:21
  189.0 42.6 %collective-permute-start.23 = (f32[20,2,512]{2,1,0:T(2,128)S(1)}, f32[20,2,512]{2,1,0:T(2,128)S(1)}, u32[]{:S(2)}, u32[]{:S(2)}) collective-permute-start(f32[20,2,512]{2,1,0:T(2,128)S(1)} %constant_dynamic-update-slice_fusion.5), channel_id=1, source_target_pairs={{0,4},{1,5},{2,6},{3,7},{4,8},{5,9},{6,10},{7,11},{8,12},{9,13},{1... | collective-permute-start | bytes 245768 | tf_op jit(solution)/shard_map/ppermute | solution.py:21
  194.4 42.4 %collective-permute-start.24 = (f32[20,2,512]{2,1,0:T(2,128)S(1)}, f32[20,2,512]{2,1,0:T(2,128)S(1)}, u32[]{:S(2)}, u32[]{:S(2)}) collective-permute-start(f32[20,2,512]{2,1,0:T(2,128)S(1)} %constant_dynamic-update-slice_fusion.5), channel_id=1, source_target_pairs={{0,3},{1,4},{2,5},{3,6},{4,7},{5,8},{6,9},{7,10},{8,11},{9,12},{10... | collective-permute-start | bytes 245768 | tf_op jit(solution)/shard_map/ppermute | solution.py:21
  196.9 42.8 %collective-permute-start.25 = (f32[20,2,512]{2,1,0:T(2,128)S(1)}, f32[20,2,512]{2,1,0:T(2,128)S(1)}, u32[]{:S(2)}, u32[]{:S(2)}) collective-permute-start(f32[20,2,512]{2,1,0:T(2,128)S(1)} %constant_dynamic-update-slice_fusion.5), channel_id=1, source_target_pairs={{0,2},{1,3},{2,4},{3,5},{4,6},{5,7},{6,8},{7,9},{8,10},{9,11},{10,... | collective-permute-start | bytes 245768 | tf_op jit(solution)/shard_map/ppermute | solution.py:21
  206.9 16.1 %collective-permute-start.22 = (f32[20,1,512]{2,1,0:T(1,128)S(1)}, f32[20,1,512]{2,1,0:T(1,128)S(1)}, u32[]{:S(2)}, u32[]{:S(2)}) collective-permute-start(f32[20,1,512]{2,1,0:T(1,128)S(1)} %get-tuple-element.74), channel_id=1, source_target_pairs={{0,5},{1,6},{2,7},{3,8},{4,9},{5,10},{6,11},{7,12},{8,13},{9,14},{... | collective-permute-start | bytes 122888 | tf_op jit(solution)/shard_map/ppermute | solution.py:21
  212.1 14.7 %collective-permute-start.31 = (f32[20,1,512]{2,1,0:T(1,128)S(1)}, f32[20,1,512]{2,1,0:T(1,128)S(1)}, u32[]{:S(2)}, u32[]{:S(2)}) collective-permute-start(f32[20,1,512]{2,1,0:T(1,128)S(1)} %get-tuple-element.73), channel_id=1, source_target_pairs={{5,0},{6,1},{7,2},{8,3},{9,4},{10,5},{11,6},{12,7},{13,8},{14,9},{... | collective-permute-start | bytes 122888 | tf_op jit(solution)/shard_map/ppermute | solution.py:21
  223.1 19.1 %collective-permute-start.26 = (f32[20,2,512]{2,1,0:T(2,128)S(1)}, f32[20,2,512]{2,1,0:T(2,128)S(1)}, u32[]{:S(2)}, u32[]{:S(2)}) collective-permute-start(f32[20,2,512]{2,1,0:T(2,128)S(1)} %constant_dynamic-update-slice_fusion.5), channel_id=1, source_target_pairs={{0,1},{1,2},{2,3},{3,4},{4,5},{5,6},{6,7},{7,8},{8,9},{9,10},{10,1... | collective-permute-start | bytes 245768 | tf_op jit(solution)/shard_map/ppermute | solution.py:21
  226.8 15.4 %collective-permute-start.27 = (f32[20,2,512]{2,1,0:T(2,128)S(1)}, f32[20,2,512]{2,1,0:T(2,128)S(1)}, u32[]{:S(2)}, u32[]{:S(2)}) collective-permute-start(f32[20,2,512]{2,1,0:T(2,128)S(1)} %constant_dynamic-update-slice_fusion.5), channel_id=1, source_target_pairs={{1,0},{2,1},{3,2},{4,3},{5,4},{6,5},{7,6},{8,7},{9,8},{10,9},{11,1... | collective-permute-start | bytes 245768 | tf_op jit(solution)/shard_map/ppermute | solution.py:21
  231.6 10.6 %collective-permute-start.28 = (f32[20,2,512]{2,1,0:T(2,128)S(1)}, f32[20,2,512]{2,1,0:T(2,128)S(1)}, u32[]{:S(2)}, u32[]{:S(2)}) collective-permute-start(f32[20,2,512]{2,1,0:T(2,128)S(1)} %constant_dynamic-update-slice_fusion.5), channel_id=1, source_target_pairs={{2,0},{3,1},{4,2},{5,3},{6,4},{7,5},{8,6},{9,7},{10,8},{11,9},{12,... | collective-permute-start | bytes 245768 | tf_op jit(solution)/shard_map/ppermute | solution.py:21
  236.8 14.1 %collective-permute-start.29 = (f32[20,2,512]{2,1,0:T(2,128)S(1)}, f32[20,2,512]{2,1,0:T(2,128)S(1)}, u32[]{:S(2)}, u32[]{:S(2)}) collective-permute-start(f32[20,2,512]{2,1,0:T(2,128)S(1)} %constant_dynamic-update-slice_fusion.5), channel_id=1, source_target_pairs={{3,0},{4,1},{5,2},{6,3},{7,4},{8,5},{9,6},{10,7},{11,8},{12,9},{13... | collective-permute-start | bytes 245768 | tf_op jit(solution)/shard_map/ppermute | solution.py:21
  239.8 15.3 %collective-permute-start.30 = (f32[20,2,512]{2,1,0:T(2,128)S(1)}, f32[20,2,512]{2,1,0:T(2,128)S(1)}, u32[]{:S(2)}, u32[]{:S(2)}) collective-permute-start(f32[20,2,512]{2,1,0:T(2,128)S(1)} %constant_dynamic-update-slice_fusion.5), channel_id=1, source_target_pairs={{4,0},{5,1},{6,2},{7,3},{8,4},{9,5},{10,6},{11,7},{12,8},{13,9},{1... | collective-permute-start | bytes 245768 | tf_op jit(solution)/shard_map/ppermute | solution.py:21
  263.2 1.1 copy-start.15
  263.3 1.1 copy-start.22
  264.6 2.6 copy-start.3
  264.7 2.6 copy-start.12
  264.7 2.6 copy-start.13
  264.7 2.6 copy-start.24
  267.2 1.7 copy-start.14
  269.2 1.1 copy-start.7
  269.2 1.1 copy-start.11
  269.5 0.9 copy-start.17
  (2 other events, 1.3 us)

commit v4 on v2

--- a/solution.py
+++ b/solution.py
@@ -35,14 +35,19 @@
 
 def gather_x(block):
     count, index = lax.axis_size("gx"), lax.axis_index("gx")
-    step = 1
-    while step < count:
-        other = lax.ppermute(block, "gx", [(i, i ^ step) for i in range(count)])
-        lower = (index & step) == 0
-        block = jnp.where(
-            lower, jnp.concatenate([block, other], axis=0), jnp.concatenate([other, block], axis=0)
+    group = 1
+    while group < count:
+        size = min(4, count // group)
+        received = [block] + [
+            lax.ppermute(block, "gx", [(i, i ^ (m * group)) for i in range(count)])
+            for m in range(1, size)
+        ]
+        stacked = jnp.stack(received)
+        own = (index // group) % size
+        block = jnp.concatenate(
+            [lax.dynamic_index_in_dim(stacked, q ^ own, keepdims=False) for q in range(size)], axis=0
         )
-        step *= 2
+        group *= size
     return block
 
 

time: 218 us -> 218 us (level)
  the two profiles are of different devices: /device:TPU:16 before, /device:TPU:10 now
where the time goes in v4:
time: 218 us; the launch traced here: 216 us
  starting transfers between devices  101 us (46%)
  waiting for transfers between devices  72.4 us (33%)
  other arithmetic  25.5 us (12%)
  local copies, waits for them, and re-layouts  14 us (6%)
  Pallas kernels  2.56 us (1%)
    ppermute x20, starting transfers between devices, shifted(): return lax.ppermute(block, axis, route)  79.5 us
    ppermute x20, waiting for transfers between devices, shifted(): return lax.ppermute(block, axis, route)  67.9 us
    ppermute x6, starting transfers between devices, gather_x(): lax.ppermute(block, 'gx', [(i, i ^ m * group) for i in range(count)])  21.3 us
    select_n x18, other arithmetic, half_sweep(): return jnp.where(update, renewed, iterate)  12.5 us
    ppermute x6, waiting for transfers between devices, gather_x(): lax.ppermute(block, 'gx', [(i, i ^ m * group) for i in range(count)])  4.46 us
  transfers between devices with their start and end apart: 26, of which 22 were waited for; matrix products, arithmetic and copies ran while one was open for 1% of the time, Pallas kernels for 0%

profile of v4, /device:TPU:10, one launch (start us, length us, event | category | flops | bytes accessed | tf_op | source)
XLA Modules:
  0.0 216.5 jit_solution(6816128713417960618)
XLA Ops:
  0.0 2.6 %shard_map.46 = f32[16,16,1024]{2,1,0:T(8,128)} custom-call(f32[16]{0:T(128)} %volts_ref.1, f32[16,16,256]{2,1,0:T(8,128)} %potential_ref.1, f32[16,16,256]{2,1,0:T(8,128)} %charge_ref.1, s32[16,16,256]{2,1,0:T(8,128)} %region_ref.1), custom_call_target="tpu_custom_call" | custom-call | tf_op jit(solution)/shard_map/pallas_call | solution.py:203
  2.6 1.2 fusion.256
  3.7 6.2 %collective-permute-start.1 = (f32[4,16,1024]{2,1,0:T(8,128)S(1)}, f32[4,16,1024]{2,1,0:T(8,128)S(1)}, u32[]{:S(2)}, u32[]{:S(2)}) collective-permute-start(f32[4,16,1024]{2,1,0:T(8,128)S(1)} %get-tuple-element.18), channel_id=1, source_target_pairs={{64,0},{128,64},{192,128},{256,192},{320,256},{384,320},{448,384},... | collective-permute-start | bytes 786440 | tf_op jit(solution)/shard_map/ppermute | solution.py:18
  10.0 1.9 collective-permute-start
  12.0 7.1 %collective-permute-done.1 = f32[4,16,1024]{2,1,0:T(8,128)S(1)} collective-permute-done((f32[4,16,1024]{2,1,0:T(8,128)S(1)}, f32[4,16,1024]{2,1,0:T(8,128)S(1)}, u32[]{:S(2)}, u32[]{:S(2)}) %collective-permute-start.1) | collective-permute-done | bytes 262176 | tf_op jit(solution)/shard_map/ppermute | solution.py:18
  19.1 6.2 %collective-permute-done = f32[4,16,1024]{2,1,0:T(8,128)S(1)} collective-permute-done((f32[4,16,1024]{2,1,0:T(8,128)S(1)}, f32[4,16,1024]{2,1,0:T(8,128)S(1)}, u32[]{:S(2)}, u32[]{:S(2)}) %collective-permute-start) | collective-permute-done | bytes 262176 | tf_op jit(solution)/shard_map/ppermute | solution.py:18
  25.5 18.7 %collective-permute-start.3 = (f32[24,4,1024]{2,1,0:T(4,128)S(1)}, f32[24,4,1024]{2,1,0:T(4,128)S(1)}, u32[]{:S(2)}, u32[]{:S(2)}) collective-permute-start(f32[24,4,1024]{2,1,0:T(4,128)S(1)} %get-tuple-element.16), channel_id=1, source_target_pairs={{1,0},{2,1},{3,2},{4,3},{5,4},{6,5},{7,6},{8,7},{9,8},{10,9},{11,1... | collective-permute-start | bytes 1179656 | tf_op jit(solution)/shard_map/ppermute | solution.py:18
  44.1 1.9 collective-permute-start.2
  46.2 3.7 %collective-permute-done.3 = f32[24,4,1024]{2,1,0:T(4,128)S(1)} collective-permute-done((f32[24,4,1024]{2,1,0:T(4,128)S(1)}, f32[24,4,1024]{2,1,0:T(4,128)S(1)}, u32[]{:S(2)}, u32[]{:S(2)}) %collective-permute-start.3) | collective-permute-done | bytes 393248 | tf_op jit(solution)/shard_map/ppermute | solution.py:18
  49.9 6.3 %collective-permute-done.2 = f32[24,4,1024]{2,1,0:T(4,128)S(1)} collective-permute-done((f32[24,4,1024]{2,1,0:T(4,128)S(1)}, f32[24,4,1024]{2,1,0:T(4,128)S(1)}, u32[]{:S(2)}, u32[]{:S(2)}) %collective-permute-start.2) | collective-permute-done | bytes 393248 | tf_op jit(solution)/shard_map/ppermute | solution.py:18
  56.7 1.6 fusion.58
  58.3 1.5 fusion.62
  59.8 1.3 broadcast_add_fusion
  61.7 5.2 %collective-permute-start.5 = (f32[4,8,512]{2,0,1:T(4,128)S(1)}, f32[4,8,512]{2,0,1:T(4,128)S(1)}, u32[]{:S(2)}, u32[]{:S(2)}) collective-permute-start(f32[4,8,512]{2,0,1:T(4,128)S(1)} %get-tuple-element.73), channel_id=1, source_target_pairs={{64,0},{128,64},{192,128},{256,192},{320,256},{384,320},{448,384},... | collective-permute-start | bytes 196616 | tf_op jit(solution)/shard_map/ppermute | solution.py:18
  67.0 1.9 collective-permute-start.4
  69.0 8.4 %collective-permute-done.4 = f32[4,8,512]{2,0,1:T(4,128)S(1)} collective-permute-done((f32[4,8,512]{2,0,1:T(4,128)S(1)}, f32[4,8,512]{2,0,1:T(4,128)S(1)}, u32[]{:S(2)}, u32[]{:S(2)}) %collective-permute-start.4) | collective-permute-done | bytes 65568 | tf_op jit(solution)/shard_map/ppermute | solution.py:18
  77.4 1.9 collective-permute-start.7
  79.4 3.9 %collective-permute-start.6 = (f32[16,4,512]{2,0,1:T(8,128)S(1)}, f32[16,4,512]{2,0,1:T(8,128)S(1)}, u32[]{:S(2)}, u32[]{:S(2)}) collective-permute-start(f32[16,4,512]{2,0,1:T(8,128)S(1)} %get-tuple-element.48), channel_id=1, source_target_pairs={{0,1},{1,2},{2,3},{3,4},{4,5},{5,6},{6,7},{7,8},{8,9},{9,10},{10,1... | collective-permute-start | bytes 393224 | tf_op jit(solution)/shard_map/ppermute | solution.py:18
  83.3 1.0 collective-permute-done.7
  84.3 4.0 %collective-permute-done.6 = f32[16,4,512]{2,0,1:T(8,128)S(1)} collective-permute-done((f32[16,4,512]{2,0,1:T(8,128)S(1)}, f32[16,4,512]{2,0,1:T(8,128)S(1)}, u32[]{:S(2)}, u32[]{:S(2)}) %collective-permute-start.6) | collective-permute-done | bytes 131104 | tf_op jit(solution)/shard_map/ppermute | solution.py:18
  88.4 1.1 fusion.259
  91.1 1.9 collective-permute-start.10
  93.1 2.9 %collective-permute-start.9 = (f32[4,4,512]{2,0,1:T(4,128)S(1)}, f32[4,4,512]{2,0,1:T(4,128)S(1)}, u32[]{:S(2)}, u32[]{:S(2)}) collective-permute-start(f32[4,4,512]{2,0,1:T(4,128)S(1)} %get-tuple-element.77), channel_id=1, source_target_pairs={{0,128},{64,192},{128,0},{192,64},{256,384},{320,448},{384,256},{4... | collective-permute-start | bytes 98312 | tf_op jit(solution)/shard_map/ppermute | solution.py:42
  95.9 6.7 %collective-permute-start.8 = (f32[4,4,512]{2,0,1:T(4,128)S(1)}, f32[4,4,512]{2,0,1:T(4,128)S(1)}, u32[]{:S(2)}, u32[]{:S(2)}) collective-permute-start(f32[4,4,512]{2,0,1:T(4,128)S(1)} %get-tuple-element.77), channel_id=1, source_target_pairs={{0,64},{64,0},{128,192},{192,128},{256,320},{320,256},{384,448},{4... | collective-permute-start | bytes 98312 | tf_op jit(solution)/shard_map/ppermute | solution.py:42
  103.6 2.5 %collective-permute-start.13 = (f32[16,4,512]{2,0,1:T(8,128)S(1)}, f32[16,4,512]{2,0,1:T(8,128)S(1)}, u32[]{:S(2)}, u32[]{:S(2)}) collective-permute-start(f32[16,4,512]{2,0,1:T(8,128)S(1)} %get-tuple-element.67), channel_id=1, source_target_pairs={{0,768},{64,832},{128,896},{192,960},{256,512},{320,576},{384,640}... | collective-permute-start | bytes 393224 | tf_op jit(solution)/shard_map/ppermute | solution.py:42
  106.1 1.9 collective-permute-start.12
  108.0 5.4 %collective-permute-start.11 = (f32[16,4,512]{2,0,1:T(8,128)S(1)}, f32[16,4,512]{2,0,1:T(8,128)S(1)}, u32[]{:S(2)}, u32[]{:S(2)}) collective-permute-start(f32[16,4,512]{2,0,1:T(8,128)S(1)} %get-tuple-element.67), channel_id=1, source_target_pairs={{0,256},{64,320},{128,384},{192,448},{256,0},{320,64},{384,128},{4... | collective-permute-start | bytes 393224 | tf_op jit(solution)/shard_map/ppermute | solution.py:42
  113.5 2.3 %collective-permute-done.12 = f32[16,4,512]{2,0,1:T(8,128)S(1)} collective-permute-done((f32[16,4,512]{2,0,1:T(8,128)S(1)}, f32[16,4,512]{2,0,1:T(8,128)S(1)}, u32[]{:S(2)}, u32[]{:S(2)}) %collective-permute-start.12) | collective-permute-done | bytes 131104 | tf_op jit(solution)/shard_map/ppermute | solution.py:42
  115.8 1.9 collective-permute-done.11
  117.9 1.9 collective-permute-start.15
  119.8 4.1 %collective-permute-start.14 = (f32[64,4,512]{2,0,1:T(8,128)S(1)}, f32[64,4,512]{2,0,1:T(8,128)}, u32[]{:S(2)}, u32[]{:S(2)}) collective-permute-start(f32[64,4,512]{2,0,1:T(8,128)S(1)} %pad_maximum_fusion.4), channel_id=1, source_target_pairs={{0,1},{1,2},{2,3},{3,4},{4,5},{5,6},{6,7},{7,8},{8,9},{9,10},{10,1... | collective-permute-start | bytes 1572872 | tf_op jit(solution)/shard_map/ppermute | solution.py:18
  124.9 8.0 %collective-permute-done.15 = f32[64,4,512]{2,0,1:T(8,128)S(1)} collective-permute-done((f32[64,4,512]{2,0,1:T(8,128)S(1)}, f32[64,4,512]{2,0,1:T(8,128)S(1)}, u32[]{:S(2)}, u32[]{:S(2)}) %collective-permute-start.15) | collective-permute-done | bytes 524320 | tf_op jit(solution)/shard_map/ppermute | solution.py:18
  133.7 3.3 %collective-permute-done.14 = f32[64,4,512]{2,0,1:T(8,128)} collective-permute-done((f32[64,4,512]{2,0,1:T(8,128)S(1)}, f32[64,4,512]{2,0,1:T(8,128)}, u32[]{:S(2)}, u32[]{:S(2)}) %collective-permute-start.14) | collective-permute-done | bytes 524320 | tf_op jit(solution)/shard_map/ppermute | solution.py:18
  137.0 1.4 pad_maximum_fusion.1
  138.4 0.9 fusion.40
  139.4 0.9 fusion.8
  140.3 0.9 copy-done.2
  141.2 1.2 fusion.16
  142.3 1.4 reshape.302
  143.7 1.0 pad_slice_fusion.70
  144.7 2.6 %reshape.301 = f32[32,2,12,256]{3,1,0,2:T(2,128)} reshape(f32[64,12,256]{2,0,1:T(8,128)} %pad_slice_fusion.70) | data formatting | bytes 1572864 | tf_op jit(solution)/shard_map/reshape | solution.py:114
  147.3 1.9 fusion.95
  149.3 1.9 collective-permute-start.17
  151.3 3.9 %collective-permute-start.16 = (f32[32,2,512]{2,0,1:T(8,128)S(1)}, f32[32,2,512]{2,0,1:T(8,128)S(1)}, u32[]{:S(2)}, u32[]{:S(2)}) collective-permute-start(f32[32,2,512]{2,0,1:T(8,128)S(1)} %pad_maximum_fusion.15), channel_id=1, source_target_pairs={{0,1},{1,2},{2,3},{3,4},{4,5},{5,6},{6,7},{7,8},{8,9},{9,10},{10,1... | collective-permute-start | bytes 393224 | tf_op jit(solution)/shard_map/ppermute | solution.py:18
  156.2 4.0 %collective-permute-done.16 = f32[32,2,512]{2,0,1:T(8,128)S(1)} collective-permute-done((f32[32,2,512]{2,0,1:T(8,128)S(1)}, f32[32,2,512]{2,0,1:T(8,128)S(1)}, u32[]{:S(2)}, u32[]{:S(2)}) %collective-permute-start.16) | collective-permute-done | bytes 131104 | tf_op jit(solution)/shard_map/ppermute | solution.py:18
  161.0 1.9 collective-permute-start.19
  163.0 3.9 %collective-permute-start.18 = (f32[32,2,256]{2,0,1:T(8,128)S(1)}, f32[32,2,256]{2,0,1:T(8,128)S(1)}, u32[]{:S(2)}, u32[]{:S(2)}) collective-permute-start(f32[32,2,256]{2,0,1:T(8,128)S(1)} %slice_select_fusion.4), channel_id=1, source_target_pairs={{0,1},{1,2},{2,3},{3,4},{4,5},{5,6},{6,7},{7,8},{8,9},{9,10},{10,1... | collective-permute-start | bytes 196616 | tf_op jit(solution)/shard_map/ppermute | solution.py:18
  167.2 4.0 %collective-permute-done.18 = f32[32,2,256]{2,0,1:T(8,128)S(1)} collective-permute-done((f32[32,2,256]{2,0,1:T(8,128)S(1)}, f32[32,2,256]{2,0,1:T(8,128)S(1)}, u32[]{:S(2)}, u32[]{:S(2)}) %collective-permute-start.18) | collective-permute-done | bytes 65568 | tf_op jit(solution)/shard_map/ppermute | solution.py:18
  171.8 1.9 collective-permute-start.21
  173.7 3.9 %collective-permute-start.20 = (f32[32,2,256]{2,0,1:T(8,128)S(1)}, f32[32,2,256]{2,0,1:T(8,128)S(1)}, u32[]{:S(2)}, u32[]{:S(2)}) collective-permute-start(f32[32,2,256]{2,0,1:T(8,128)S(1)} %slice_select_fusion.3), channel_id=1, source_target_pairs={{0,1},{1,2},{2,3},{3,4},{4,5},{5,6},{6,7},{7,8},{8,9},{9,10},{10,1... | collective-permute-start | bytes 196616 | tf_op jit(solution)/shard_map/ppermute | solution.py:18
  177.9 4.0 %collective-permute-done.20 = f32[32,2,256]{2,0,1:T(8,128)S(1)} collective-permute-done((f32[32,2,256]{2,0,1:T(8,128)S(1)}, f32[32,2,256]{2,0,1:T(8,128)S(1)}, u32[]{:S(2)}, u32[]{:S(2)}) %collective-permute-start.20) | collective-permute-done | bytes 65568 | tf_op jit(solution)/shard_map/ppermute | solution.py:18
  182.5 1.9 collective-permute-start.23
  184.4 3.9 %collective-permute-start.22 = (f32[32,2,256]{2,0,1:T(8,128)S(1)}, f32[32,2,256]{2,0,1:T(8,128)S(1)}, u32[]{:S(2)}, u32[]{:S(2)}) collective-permute-start(f32[32,2,256]{2,0,1:T(8,128)S(1)} %slice_select_fusion.2), channel_id=1, source_target_pairs={{0,1},{1,2},{2,3},{3,4},{4,5},{5,6},{6,7},{7,8},{8,9},{9,10},{10,1... | collective-permute-start | bytes 196616 | tf_op jit(solution)/shard_map/ppermute | solution.py:18
  188.6 4.0 %collective-permute-done.22 = f32[32,2,256]{2,0,1:T(8,128)S(1)} collective-permute-done((f32[32,2,256]{2,0,1:T(8,128)S(1)}, f32[32,2,256]{2,0,1:T(8,128)S(1)}, u32[]{:S(2)}, u32[]{:S(2)}) %collective-permute-start.22) | collective-permute-done | bytes 65568 | tf_op jit(solution)/shard_map/ppermute | solution.py:18
  193.0 0.9 broadcast_in_dim.36
  193.9 2.0 reshape.306
  195.9 1.1 bitcast_add_fusion
  197.0 0.9 fusion.24
  198.0 0.9 fusion.32
  198.9 2.1 collective-permute-start.24
  201.0 6.3 %collective-permute-start.25 = (f32[64,2,256]{2,0,1:T(8,128)S(1)}, f32[64,2,256]{2,0,1:T(8,128)S(1)}, u32[]{:S(2)}, u32[]{:S(2)}) collective-permute-start(f32[64,2,256]{2,0,1:T(8,128)S(1)} %get-tuple-element.19), channel_id=1, source_target_pairs={{1,0},{2,1},{3,2},{4,3},{5,4},{6,5},{7,6},{8,7},{9,8},{10,9},{11,1... | collective-permute-start | bytes 393224 | tf_op jit(solution)/shard_map/ppermute | solution.py:18
  208.0 1.5 collective-permute-done.25
  212.1 1.8 fusion.71
  214.4 2.0 slice_select_fusion
  (150 shorter events, 13.7 us)
Async XLA Ops:
  2.6 22.7 %copy-start.1 = (f32[16,16,1024]{2,1,0:T(8,128)S(1)}, f32[16,16,1024]{2,1,0:T(8,128)}, u32[]{:S(2)}) copy-start(f32[16,16,1024]{2,1,0:T(8,128)} %shard_map.46) | copy-start | bytes 3145732
  3.7 15.4 %collective-permute-start.1 = (f32[4,16,1024]{2,1,0:T(8,128)S(1)}, f32[4,16,1024]{2,1,0:T(8,128)S(1)}, u32[]{:S(2)}, u32[]{:S(2)}) collective-permute-start(f32[4,16,1024]{2,1,0:T(8,128)S(1)} %get-tuple-element.18), channel_id=1, source_target_pairs={{64,0},{128,64},{192,128},{256,192},{320,256},{384,320},{448,384},... | collective-permute-start | bytes 786440 | tf_op jit(solution)/shard_map/ppermute | solution.py:18
  10.0 15.3 %collective-permute-start = (f32[4,16,1024]{2,1,0:T(8,128)S(1)}, f32[4,16,1024]{2,1,0:T(8,128)S(1)}, u32[]{:S(2)}, u32[]{:S(2)}) collective-permute-start(f32[4,16,1024]{2,1,0:T(8,128)S(1)} %get-tuple-element.17), channel_id=1, source_target_pairs={{0,64},{64,128},{128,192},{192,256},{256,320},{320,384},{384,448},... | collective-permute-start | bytes 786440 | tf_op jit(solution)/shard_map/ppermute | solution.py:18
  12.0 46.3 %copy-start.16 = (s32[24,24]{1,0:T(8,128)}, s32[24,24]{1,0:T(8,128)S(1)}, u32[]{:S(2)}) copy-start(s32[24,24]{1,0:T(8,128)S(1)} %iota_add_fusion.1) | copy-start | bytes 6916
  25.5 24.4 %collective-permute-start.3 = (f32[24,4,1024]{2,1,0:T(4,128)S(1)}, f32[24,4,1024]{2,1,0:T(4,128)S(1)}, u32[]{:S(2)}, u32[]{:S(2)}) collective-permute-start(f32[24,4,1024]{2,1,0:T(4,128)S(1)} %get-tuple-element.16), channel_id=1, source_target_pairs={{1,0},{2,1},{3,2},{4,3},{5,4},{6,5},{7,6},{8,7},{9,8},{10,9},{11,1... | collective-permute-start | bytes 1179656 | tf_op jit(solution)/shard_map/ppermute | solution.py:18
  44.1 12.1 %collective-permute-start.2 = (f32[24,4,1024]{2,1,0:T(4,128)S(1)}, f32[24,4,1024]{2,1,0:T(4,128)S(1)}, u32[]{:S(2)}, u32[]{:S(2)}) collective-permute-start(f32[24,4,1024]{2,1,0:T(4,128)S(1)} %get-tuple-element.15), channel_id=1, source_target_pairs={{0,1},{1,2},{2,3},{3,4},{4,5},{5,6},{6,7},{7,8},{8,9},{9,10},{10,1... | collective-permute-start | bytes 1179656 | tf_op jit(solution)/shard_map/ppermute | solution.py:18
  46.1 43.7 %copy-start.18 = (pred[16,16]{0,1:T(8,128)(4,1)}, pred[16,16]{0,1:T(8,128)(4,1)S(1)}, u32[]{:S(2)}) copy-start(pred[16,16]{0,1:T(8,128)(4,1)S(1)} %broadcast_and_fusion.1) | copy-start | bytes 772
  56.6 3.1 %copy-start = (f32[24,24,1024]{2,1,0:T(8,128)}, f32[24,24,1024]{2,1,0:T(8,128)S(1)}, u32[]{:S(2)}) copy-start(f32[24,24,1024]{2,1,0:T(8,128)S(1)} %pad_maximum_fusion) | copy-start | bytes 7077892
  58.3 2.7 %copy-start.6 = (pred[24,24,256]{2,1,0:T(8,128)(4,1)}, pred[24,24,256]{2,1,0:T(8,128)(4,1)S(1)}, u32[]{:S(2)}) copy-start(pred[24,24,256]{2,1,0:T(8,128)(4,1)S(1)} %get-tuple-element.9) | copy-start | bytes 442372
  59.8 1.3 copy-start.4
  61.7 7.2 %collective-permute-start.5 = (f32[4,8,512]{2,0,1:T(4,128)S(1)}, f32[4,8,512]{2,0,1:T(4,128)S(1)}, u32[]{:S(2)}, u32[]{:S(2)}) collective-permute-start(f32[4,8,512]{2,0,1:T(4,128)S(1)} %get-tuple-element.73), channel_id=1, source_target_pairs={{64,0},{128,64},{192,128},{256,192},{320,256},{384,320},{448,384},... | collective-permute-start | bytes 196616 | tf_op jit(solution)/shard_map/ppermute | solution.py:18
  67.0 10.4 %collective-permute-start.4 = (f32[4,8,512]{2,0,1:T(4,128)S(1)}, f32[4,8,512]{2,0,1:T(4,128)S(1)}, u32[]{:S(2)}, u32[]{:S(2)}) collective-permute-start(f32[4,8,512]{2,0,1:T(4,128)S(1)} %get-tuple-element.72), channel_id=1, source_target_pairs={{0,64},{64,128},{128,192},{192,256},{256,320},{320,384},{384,448},... | collective-permute-start | bytes 196616 | tf_op jit(solution)/shard_map/ppermute | solution.py:18
  77.4 6.9 %collective-permute-start.7 = (f32[16,4,512]{2,0,1:T(8,128)S(1)}, f32[16,4,512]{2,0,1:T(8,128)S(1)}, u32[]{:S(2)}, u32[]{:S(2)}) collective-permute-start(f32[16,4,512]{2,0,1:T(8,128)S(1)} %get-tuple-element.49), channel_id=1, source_target_pairs={{1,0},{2,1},{3,2},{4,3},{5,4},{6,5},{7,6},{8,7},{9,8},{10,9},{11,1... | collective-permute-start | bytes 393224 | tf_op jit(solution)/shard_map/ppermute | solution.py:18
  79.4 9.0 %collective-permute-start.6 = (f32[16,4,512]{2,0,1:T(8,128)S(1)}, f32[16,4,512]{2,0,1:T(8,128)S(1)}, u32[]{:S(2)}, u32[]{:S(2)}) collective-permute-start(f32[16,4,512]{2,0,1:T(8,128)S(1)} %get-tuple-element.48), channel_id=1, source_target_pairs={{0,1},{1,2},{2,3},{3,4},{4,5},{5,6},{6,7},{7,8},{8,9},{9,10},{10,1... | collective-permute-start | bytes 393224 | tf_op jit(solution)/shard_map/ppermute | solution.py:18
  89.9 0.8 copy-start.9
  91.1 12.1 %collective-permute-start.10 = (f32[4,4,512]{2,0,1:T(4,128)S(1)}, f32[4,4,512]{2,0,1:T(4,128)S(1)}, u32[]{:S(2)}, u32[]{:S(2)}) collective-permute-start(f32[4,4,512]{2,0,1:T(4,128)S(1)} %get-tuple-element.77), channel_id=1, source_target_pairs={{0,192},{64,128},{128,64},{192,0},{256,448},{320,384},{384,320},{4... | collective-permute-start | bytes 98312 | tf_op jit(solution)/shard_map/ppermute | solution.py:42
  93.1 10.2 %collective-permute-start.9 = (f32[4,4,512]{2,0,1:T(4,128)S(1)}, f32[4,4,512]{2,0,1:T(4,128)S(1)}, u32[]{:S(2)}, u32[]{:S(2)}) collective-permute-start(f32[4,4,512]{2,0,1:T(4,128)S(1)} %get-tuple-element.77), channel_id=1, source_target_pairs={{0,128},{64,192},{128,0},{192,64},{256,384},{320,448},{384,256},{4... | collective-permute-start | bytes 98312 | tf_op jit(solution)/shard_map/ppermute | solution.py:42
  95.9 7.6 %collective-permute-start.8 = (f32[4,4,512]{2,0,1:T(4,128)S(1)}, f32[4,4,512]{2,0,1:T(4,128)S(1)}, u32[]{:S(2)}, u32[]{:S(2)}) collective-permute-start(f32[4,4,512]{2,0,1:T(4,128)S(1)} %get-tuple-element.77), channel_id=1, source_target_pairs={{0,64},{64,0},{128,192},{192,128},{256,320},{320,256},{384,448},{4... | collective-permute-start | bytes 98312 | tf_op jit(solution)/shard_map/ppermute | solution.py:42
  103.6 9.9 %collective-permute-start.13 = (f32[16,4,512]{2,0,1:T(8,128)S(1)}, f32[16,4,512]{2,0,1:T(8,128)S(1)}, u32[]{:S(2)}, u32[]{:S(2)}) collective-permute-start(f32[16,4,512]{2,0,1:T(8,128)S(1)} %get-tuple-element.67), channel_id=1, source_target_pairs={{0,768},{64,832},{128,896},{192,960},{256,512},{320,576},{384,640}... | collective-permute-start | bytes 393224 | tf_op jit(solution)/shard_map/ppermute | solution.py:42
  106.1 9.7 %collective-permute-start.12 = (f32[16,4,512]{2,0,1:T(8,128)S(1)}, f32[16,4,512]{2,0,1:T(8,128)S(1)}, u32[]{:S(2)}, u32[]{:S(2)}) collective-permute-start(f32[16,4,512]{2,0,1:T(8,128)S(1)} %get-tuple-element.67), channel_id=1, source_target_pairs={{0,512},{64,576},{128,640},{192,704},{256,768},{320,832},{384,896}... | collective-permute-start | bytes 393224 | tf_op jit(solution)/shard_map/ppermute | solution.py:42
  108.0 9.7 %collective-permute-start.11 = (f32[16,4,512]{2,0,1:T(8,128)S(1)}, f32[16,4,512]{2,0,1:T(8,128)S(1)}, u32[]{:S(2)}, u32[]{:S(2)}) collective-permute-start(f32[16,4,512]{2,0,1:T(8,128)S(1)} %get-tuple-element.67), channel_id=1, source_target_pairs={{0,256},{64,320},{128,384},{192,448},{256,0},{320,64},{384,128},{4... | collective-permute-start | bytes 393224 | tf_op jit(solution)/shard_map/ppermute | solution.py:42
  113.5 25.9 %copy-start.22 = (pred[12]{0:T(512)(128)(4,1)}, pred[12]{0:T(512)(128)(4,1)S(1)}, u32[]{:S(2)}) copy-start(pred[12]{0:T(512)(128)(4,1)S(1)} %compare_and_fusion.9) | copy-start | bytes 40
  117.9 15.0 %collective-permute-start.15 = (f32[64,4,512]{2,0,1:T(8,128)S(1)}, f32[64,4,512]{2,0,1:T(8,128)S(1)}, u32[]{:S(2)}, u32[]{:S(2)}) collective-permute-start(f32[64,4,512]{2,0,1:T(8,128)S(1)} %pad_maximum_fusion.4), channel_id=1, source_target_pairs={{1,0},{2,1},{3,2},{4,3},{5,4},{6,5},{7,6},{8,7},{9,8},{10,9},{11,1... | collective-permute-start | bytes 1572872 | tf_op jit(solution)/shard_map/ppermute | solution.py:18
  119.8 17.2 %collective-permute-start.14 = (f32[64,4,512]{2,0,1:T(8,128)S(1)}, f32[64,4,512]{2,0,1:T(8,128)}, u32[]{:S(2)}, u32[]{:S(2)}) collective-permute-start(f32[64,4,512]{2,0,1:T(8,128)S(1)} %pad_maximum_fusion.4), channel_id=1, source_target_pairs={{0,1},{1,2},{2,3},{3,4},{4,5},{5,6},{6,7},{7,8},{8,9},{9,10},{10,1... | collective-permute-start | bytes 1572872 | tf_op jit(solution)/shard_map/ppermute | solution.py:18
  132.9 0.8 copy-start.13
  140.3 0.9 copy-start.2
  144.7 2.6 %copy-start.8 = (f32[32,2,12,256]{3,1,0,2:T(2,128)S(1)}, f32[32,2,12,256]{3,1,0,2:T(2,128)}, u32[]{:S(2)}) copy-start(f32[32,2,12,256]{3,1,0,2:T(2,128)} %reshape.302) | copy-start | bytes 2359300
  147.3 7.9 %copy-start.14 = (s32[32,6]{0,1:T(8,128)S(1)}, s32[32,6]{0,1:T(8,128)}, u32[]{:S(2)}) copy-start(s32[32,6]{0,1:T(8,128)} %iota_add_fusion.4) | copy-start | bytes 2308
  147.3 7.9 %copy-start.20 = (pred[6]{0:T(512)(128)(4,1)S(1)}, pred[6]{0:T(512)(128)(4,1)}, u32[]{:S(2)}) copy-start(pred[6]{0:T(512)(128)(4,1)} %compare_and_fusion.8) | copy-start | bytes 22
  149.3 6.9 %collective-permute-start.17 = (f32[32,2,512]{2,0,1:T(8,128)S(1)}, f32[32,2,512]{2,0,1:T(8,128)S(1)}, u32[]{:S(2)}, u32[]{:S(2)}) collective-permute-start(f32[32,2,512]{2,0,1:T(8,128)S(1)} %pad_maximum_fusion.15), channel_id=1, source_target_pairs={{1,0},{2,1},{3,2},{4,3},{5,4},{6,5},{7,6},{8,7},{9,8},{10,9},{11,1... | collective-permute-start | bytes 393224 | tf_op jit(solution)/shard_map/ppermute | solution.py:18
  151.3 9.0 %collective-permute-start.16 = (f32[32,2,512]{2,0,1:T(8,128)S(1)}, f32[32,2,512]{2,0,1:T(8,128)S(1)}, u32[]{:S(2)}, u32[]{:S(2)}) collective-permute-start(f32[32,2,512]{2,0,1:T(8,128)S(1)} %pad_maximum_fusion.15), channel_id=1, source_target_pairs={{0,1},{1,2},{2,3},{3,4},{4,5},{5,6},{6,7},{7,8},{8,9},{9,10},{10,1... | collective-permute-start | bytes 393224 | tf_op jit(solution)/shard_map/ppermute | solution.py:18
  161.0 6.2 %collective-permute-start.19 = (f32[32,2,256]{2,0,1:T(8,128)S(1)}, f32[32,2,256]{2,0,1:T(8,128)S(1)}, u32[]{:S(2)}, u32[]{:S(2)}) collective-permute-start(f32[32,2,256]{2,0,1:T(8,128)S(1)} %slice_select_fusion.4), channel_id=1, source_target_pairs={{1,0},{2,1},{3,2},{4,3},{5,4},{6,5},{7,6},{8,7},{9,8},{10,9},{11,1... | collective-permute-start | bytes 196616 | tf_op jit(solution)/shard_map/ppermute | solution.py:18
  163.0 8.3 %collective-permute-start.18 = (f32[32,2,256]{2,0,1:T(8,128)S(1)}, f32[32,2,256]{2,0,1:T(8,128)S(1)}, u32[]{:S(2)}, u32[]{:S(2)}) collective-permute-start(f32[32,2,256]{2,0,1:T(8,128)S(1)} %slice_select_fusion.4), channel_id=1, source_target_pairs={{0,1},{1,2},{2,3},{3,4},{4,5},{5,6},{6,7},{7,8},{8,9},{9,10},{10,1... | collective-permute-start | bytes 196616 | tf_op jit(solution)/shard_map/ppermute | solution.py:18
  171.8 20.9 %copy-start.15 = (s32[32,6]{0,1:T(8,128)S(1)}, s32[32,6]{0,1:T(8,128)}, u32[]{:S(2)}) copy-start(s32[32,6]{0,1:T(8,128)} %iota_add_fusion.4) | copy-start | bytes 2308
  171.8 20.9 %copy-start.21 = (pred[6]{0:T(512)(128)(4,1)S(1)}, pred[6]{0:T(512)(128)(4,1)}, u32[]{:S(2)}) copy-start(pred[6]{0:T(512)(128)(4,1)} %compare_and_fusion.8) | copy-start | bytes 22
  171.8 6.2 %collective-permute-start.21 = (f32[32,2,256]{2,0,1:T(8,128)S(1)}, f32[32,2,256]{2,0,1:T(8,128)S(1)}, u32[]{:S(2)}, u32[]{:S(2)}) collective-permute-start(f32[32,2,256]{2,0,1:T(8,128)S(1)} %slice_select_fusion.3), channel_id=1, source_target_pairs={{1,0},{2,1},{3,2},{4,3},{5,4},{6,5},{7,6},{8,7},{9,8},{10,9},{11,1... | collective-permute-start | bytes 196616 | tf_op jit(solution)/shard_map/ppermute | solution.py:18
  173.7 8.3 %collective-permute-start.20 = (f32[32,2,256]{2,0,1:T(8,128)S(1)}, f32[32,2,256]{2,0,1:T(8,128)S(1)}, u32[]{:S(2)}, u32[]{:S(2)}) collective-permute-start(f32[32,2,256]{2,0,1:T(8,128)S(1)} %slice_select_fusion.3), channel_id=1, source_target_pairs={{0,1},{1,2},{2,3},{3,4},{4,5},{5,6},{6,7},{7,8},{8,9},{9,10},{10,1... | collective-permute-start | bytes 196616 | tf_op jit(solution)/shard_map/ppermute | solution.py:18
  182.5 6.2 %collective-permute-start.23 = (f32[32,2,256]{2,0,1:T(8,128)S(1)}, f32[32,2,256]{2,0,1:T(8,128)S(1)}, u32[]{:S(2)}, u32[]{:S(2)}) collective-permute-start(f32[32,2,256]{2,0,1:T(8,128)S(1)} %slice_select_fusion.2), channel_id=1, source_target_pairs={{1,0},{2,1},{3,2},{4,3},{5,4},{6,5},{7,6},{8,7},{9,8},{10,9},{11,1... | collective-permute-start | bytes 196616 | tf_op jit(solution)/shard_map/ppermute | solution.py:18
  184.4 8.3 %collective-permute-start.22 = (f32[32,2,256]{2,0,1:T(8,128)S(1)}, f32[32,2,256]{2,0,1:T(8,128)S(1)}, u32[]{:S(2)}, u32[]{:S(2)}) collective-permute-start(f32[32,2,256]{2,0,1:T(8,128)S(1)} %slice_select_fusion.2), channel_id=1, source_target_pairs={{0,1},{1,2},{2,3},{3,4},{4,5},{5,6},{6,7},{7,8},{8,9},{9,10},{10,1... | collective-permute-start | bytes 196616 | tf_op jit(solution)/shard_map/ppermute | solution.py:18
  193.0 3.0 %copy-start.3 = (f32[64,12,256]{2,0,1:T(8,128)S(1)}, f32[64,12,256]{2,0,1:T(8,128)}, u32[]{:S(2)}) copy-start(f32[64,12,256]{2,0,1:T(8,128)} %copy-done.2) | copy-start | bytes 2359300
  193.0 4.1 %copy-start.23 = (pred[12]{0:T(512)(128)(4,1)S(1)}, pred[12]{0:T(512)(128)(4,1)}, u32[]{:S(2)}) copy-start(pred[12]{0:T(512)(128)(4,1)} %copy-done.22) | copy-start | bytes 40
  198.0 9.3 %copy-start.19 = (pred[16,16]{0,1:T(8,128)(4,1)S(1)}, pred[16,16]{0,1:T(8,128)(4,1)}, u32[]{:S(2)}) copy-start(pred[16,16]{0,1:T(8,128)(4,1)} %copy-done.18) | copy-start | bytes 772
  198.9 10.8 %copy-start.10 = (f32[16,16,256]{2,0,1:T(8,128)S(1)}, f32[16,16,256]{2,0,1:T(8,128)}, u32[]{:S(2)}) copy-start(f32[16,16,256]{2,0,1:T(8,128)} %copy-done.9) | copy-start | bytes 786436
  198.9 9.1 %collective-permute-start.24 = (f32[64,2,256]{2,0,1:T(8,128)S(1)}, f32[64,2,256]{2,0,1:T(8,128)S(1)}, u32[]{:S(2)}, u32[]{:S(2)}) collective-permute-start(f32[64,2,256]{2,0,1:T(8,128)S(1)} %get-tuple-element.20), channel_id=1, source_target_pairs={{0,1},{1,2},{2,3},{3,4},{4,5},{5,6},{6,7},{7,8},{8,9},{9,10},{10,1... | collective-permute-start | bytes 393224 | tf_op jit(solution)/shard_map/ppermute | solution.py:18
  201.0 8.5 %collective-permute-start.25 = (f32[64,2,256]{2,0,1:T(8,128)S(1)}, f32[64,2,256]{2,0,1:T(8,128)S(1)}, u32[]{:S(2)}, u32[]{:S(2)}) collective-permute-start(f32[64,2,256]{2,0,1:T(8,128)S(1)} %get-tuple-element.19), channel_id=1, source_target_pairs={{1,0},{2,1},{3,2},{4,3},{5,4},{6,5},{7,6},{8,7},{9,8},{10,9},{11,1... | collective-permute-start | bytes 393224 | tf_op jit(solution)/shard_map/ppermute | solution.py:18
  209.7 1.0 copy-start.11
  209.7 1.0 copy-start.12
  210.9 1.1 copy-start.5
  210.9 1.1 copy-start.7
  211.3 0.8 copy-start.17

commit v5 on v4

--- a/solution.py
+++ b/solution.py
@@ -9,12 +9,14 @@
 
 HALO_FINE = 4
 HALO_MID = 4
-HALO_COARSE = 2
+HALO_COARSE = 4
 
 
 def shifted(block, axis, distance):
     count = lax.axis_size(axis)
     route = [(i, i + distance) for i in range(count) if 0 <= i + distance < count]
+    if not route:
+        return jnp.zeros_like(block)
     return lax.ppermute(block, axis, route)
 
 
@@ -25,6 +27,17 @@
     return jnp.concatenate(
         [shifted(block[:, -width:], "gy", 1), block, shifted(block[:, :width], "gy", -1)], axis=1
     )
+
+
+def along(block, width, axis, dim):
+    span = block.shape[dim]
+    reach = -(-width // span)
+    part = width - (reach - 1) * span
+    low = [shifted(lax.slice_in_dim(block, span - part, span, axis=dim), axis, reach)]
+    low += [shifted(block, axis, d) for d in range(reach - 1, 0, -1)]
+    high = [shifted(block, axis, -d) for d in range(1, reach)]
+    high += [shifted(lax.slice_in_dim(block, 0, part, axis=dim), axis, -reach)]
+    return jnp.concatenate(low + [block] + high, axis=dim)
 
 
 def exchange_y(block, width):
@@ -165,19 +178,21 @@
 
 def coarsest_whole_x(source, coefficient, width):
     span_y = source.shape[1]
-    source, coefficient = exchange_many([source, coefficient], width, exchange_y)
+    exchanger = lambda block, rim: along(block, rim, "gy", 1)
+    source, coefficient = exchange_many([source, coefficient], width, exchanger)
     span_x = source.shape[0]
     weight = 0.25**3
     divisor = 4.0 * weight + 2.0 + coefficient
     allowed = inside(span_x, span_y, width, whole_x=True)
     iterate = jnp.zeros_like(source)
-    plan = [(0, 1, 0), (1, 0), (1, 0), (1,)]
+    plan = [(0, 1, 0, 1, 0), (1, 0, 1)]
     for step, colours in enumerate(plan):
         if step > 0:
-            iterate = exchange_y(iterate[:, width:width + span_y], width)
+            iterate = exchanger(iterate[:, width:width + span_y], width)
         for colour in colours:
             iterate = half_sweep(iterate, source, divisor, weight, allowed, colour)
-    return iterate
+    cut = width - 2
+    return iterate[:, cut:iterate.shape[1] - cut]
 
 
 def x_window(values, start, length, margin):

time: 218 us -> 214 us (0.982)
  the two profiles are of different devices: /device:TPU:10 before, /device:TPU:8 now
where the time goes in v5:
time: 214 us; the launch traced here: 213 us
  starting transfers between devices  122 us (57%)
  waiting for transfers between devices  44.7 us (21%)
  other arithmetic  28.2 us (13%)
  local copies, waits for them, and re-layouts  13.5 us (6%)
  Pallas kernels  2.56 us (1%)
    ppermute x20, starting transfers between devices, shifted(): return lax.ppermute(block, axis, route)  91.6 us
    ppermute x20, waiting for transfers between devices, shifted(): return lax.ppermute(block, axis, route)  33.8 us
    ppermute x6, starting transfers between devices, gather_x(): lax.ppermute(block, 'gx', [(i, i ^ m * group) for i in range(count)])  30.9 us
    select_n x18, other arithmetic, half_sweep(): return jnp.where(update, renewed, iterate)  15 us
    ppermute x6, waiting for transfers between devices, gather_x(): lax.ppermute(block, 'gx', [(i, i ^ m * group) for i in range(count)])  10.9 us
  transfers between devices with their start and end apart: 26, of which 16 were waited for; matrix products, arithmetic and copies ran while one was open for 1% of the time, Pallas kernels for 0%

profile of v5, /device:TPU:8, one launch (start us, length us, event | category | flops | bytes accessed | tf_op | source)
XLA Modules:
  0.0 212.8 jit_solution(7075850211307191399)
XLA Ops:
  0.0 2.6 %shard_map.46 = f32[16,16,1024]{2,1,0:T(8,128)} custom-call(f32[16]{0:T(128)} %volts_ref.1, f32[16,16,256]{2,1,0:T(8,128)} %potential_ref.1, f32[16,16,256]{2,1,0:T(8,128)} %charge_ref.1, s32[16,16,256]{2,1,0:T(8,128)} %region_ref.1), custom_call_target="tpu_custom_call" | custom-call | tf_op jit(solution)/shard_map/pallas_call | solution.py:218
  2.6 1.2 fusion.255
  3.7 1.8 collective-permute-start
  5.5 1.3 collective-permute-start.1
  6.9 6.7 %collective-permute-done.1 = f32[4,16,1024]{2,1,0:T(8,128)S(1)} collective-permute-done((f32[4,16,1024]{2,1,0:T(8,128)S(1)}, f32[4,16,1024]{2,1,0:T(8,128)S(1)}, u32[]{:S(2)}, u32[]{:S(2)}) %collective-permute-start.1) | collective-permute-done | bytes 262176 | tf_op jit(solution)/shard_map/ppermute | solution.py:20
  13.8 4.3 %collective-permute-start.2 = (f32[24,4,1024]{2,1,0:T(4,128)S(1)}, f32[24,4,1024]{2,1,0:T(4,128)S(1)}, u32[]{:S(2)}, u32[]{:S(2)}) collective-permute-start(f32[24,4,1024]{2,1,0:T(4,128)S(1)} %get-tuple-element.15), channel_id=1, source_target_pairs={{0,1},{1,2},{2,3},{3,4},{4,5},{5,6},{6,7},{7,8},{8,9},{9,10},{10,1... | collective-permute-start | bytes 1179656 | tf_op jit(solution)/shard_map/ppermute | solution.py:20
  18.1 16.6 %collective-permute-start.3 = (f32[24,4,1024]{2,1,0:T(4,128)S(1)}, f32[24,4,1024]{2,1,0:T(4,128)S(1)}, u32[]{:S(2)}, u32[]{:S(2)}) collective-permute-start(f32[24,4,1024]{2,1,0:T(4,128)S(1)} %get-tuple-element.16), channel_id=1, source_target_pairs={{1,0},{2,1},{3,2},{4,3},{5,4},{6,5},{7,6},{8,7},{9,8},{10,9},{11,1... | collective-permute-start | bytes 1179656 | tf_op jit(solution)/shard_map/ppermute | solution.py:20
  34.9 3.7 %collective-permute-done.2 = f32[24,4,1024]{2,1,0:T(4,128)S(1)} collective-permute-done((f32[24,4,1024]{2,1,0:T(4,128)S(1)}, f32[24,4,1024]{2,1,0:T(4,128)S(1)}, u32[]{:S(2)}, u32[]{:S(2)}) %collective-permute-start.2) | collective-permute-done | bytes 393248 | tf_op jit(solution)/shard_map/ppermute | solution.py:20
  38.5 1.5 collective-permute-done.3
  40.5 1.6 fusion.58
  42.1 1.5 fusion.62
  43.6 1.3 broadcast_add_fusion
  45.5 10.9 %collective-permute-start.4 = (f32[4,8,512]{2,0,1:T(4,128)S(1)}, f32[4,8,512]{2,0,1:T(4,128)S(1)}, u32[]{:S(2)}, u32[]{:S(2)}) collective-permute-start(f32[4,8,512]{2,0,1:T(4,128)S(1)} %get-tuple-element.68), channel_id=1, source_target_pairs={{0,64},{64,128},{128,192},{192,256},{256,320},{320,384},{384,448},... | collective-permute-start | bytes 196616 | tf_op jit(solution)/shard_map/ppermute | solution.py:20
  56.5 1.3 collective-permute-start.5
  57.8 1.9 collective-permute-done.5
  59.8 1.9 collective-permute-start.6
  61.7 6.5 %collective-permute-start.7 = (f32[16,4,512]{2,0,1:T(8,128)S(1)}, f32[16,4,512]{2,0,1:T(8,128)S(1)}, u32[]{:S(2)}, u32[]{:S(2)}) collective-permute-start(f32[16,4,512]{2,0,1:T(8,128)S(1)} %get-tuple-element.57), channel_id=1, source_target_pairs={{1,0},{2,1},{3,2},{4,3},{5,4},{6,5},{7,6},{8,7},{9,8},{10,9},{11,1... | collective-permute-start | bytes 393224 | tf_op jit(solution)/shard_map/ppermute | solution.py:20
  68.2 1.7 collective-permute-done.6
  69.9 0.8 collective-permute-done.7
  70.8 1.1 fusion.259
  72.3 0.7 copy-done.9
  73.5 8.4 %collective-permute-start.8 = (f32[4,4,512]{2,0,1:T(4,128)S(1)}, f32[4,4,512]{2,0,1:T(4,128)S(1)}, u32[]{:S(2)}, u32[]{:S(2)}) collective-permute-start(f32[4,4,512]{2,0,1:T(4,128)S(1)} %get-tuple-element.73), channel_id=1, source_target_pairs={{0,64},{64,0},{128,192},{192,128},{256,320},{320,256},{384,448},{4... | collective-permute-start | bytes 98312 | tf_op jit(solution)/shard_map/ppermute | solution.py:55
  81.9 10.2 %collective-permute-start.9 = (f32[4,4,512]{2,0,1:T(4,128)S(1)}, f32[4,4,512]{2,0,1:T(4,128)S(1)}, u32[]{:S(2)}, u32[]{:S(2)}) collective-permute-start(f32[4,4,512]{2,0,1:T(4,128)S(1)} %get-tuple-element.73), channel_id=1, source_target_pairs={{0,128},{64,192},{128,0},{192,64},{256,384},{320,448},{384,256},{4... | collective-permute-start | bytes 98312 | tf_op jit(solution)/shard_map/ppermute | solution.py:55
  92.1 1.9 collective-permute-start.10
  94.3 7.2 %collective-permute-done.10 = f32[4,4,512]{2,0,1:T(4,128)S(1)} collective-permute-done((f32[4,4,512]{2,0,1:T(4,128)S(1)}, f32[4,4,512]{2,0,1:T(4,128)S(1)}, u32[]{:S(2)}, u32[]{:S(2)}) %collective-permute-start.10) | collective-permute-done | bytes 32800 | tf_op jit(solution)/shard_map/ppermute | solution.py:55
  101.6 3.1 %collective-permute-start.11 = (f32[16,4,512]{2,0,1:T(8,128)S(1)}, f32[16,4,512]{2,0,1:T(8,128)S(1)}, u32[]{:S(2)}, u32[]{:S(2)}) collective-permute-start(f32[16,4,512]{2,0,1:T(8,128)S(1)} %get-tuple-element.63), channel_id=1, source_target_pairs={{0,256},{64,320},{128,384},{192,448},{256,0},{320,64},{384,128},{4... | collective-permute-start | bytes 393224 | tf_op jit(solution)/shard_map/ppermute | solution.py:55
  104.7 1.9 collective-permute-start.12
  106.6 5.4 %collective-permute-start.13 = (f32[16,4,512]{2,0,1:T(8,128)S(1)}, f32[16,4,512]{2,0,1:T(8,128)S(1)}, u32[]{:S(2)}, u32[]{:S(2)}) collective-permute-start(f32[16,4,512]{2,0,1:T(8,128)S(1)} %get-tuple-element.63), channel_id=1, source_target_pairs={{0,768},{64,832},{128,896},{192,960},{256,512},{320,576},{384,640}... | collective-permute-start | bytes 393224 | tf_op jit(solution)/shard_map/ppermute | solution.py:55
  112.6 0.7 collective-permute-done.12
  113.4 2.7 %collective-permute-done.13 = f32[16,4,512]{2,0,1:T(8,128)S(1)} collective-permute-done((f32[16,4,512]{2,0,1:T(8,128)S(1)}, f32[16,4,512]{2,0,1:T(8,128)S(1)}, u32[]{:S(2)}, u32[]{:S(2)}) %collective-permute-start.13) | collective-permute-done | bytes 131104 | tf_op jit(solution)/shard_map/ppermute | solution.py:55
  116.2 1.9 collective-permute-start.14
  118.1 6.3 %collective-permute-start.15 = (f32[64,4,512]{2,0,1:T(8,128)S(1)}, f32[64,4,512]{2,0,1:T(8,128)}, u32[]{:S(2)}, u32[]{:S(2)}) collective-permute-start(f32[64,4,512]{2,0,1:T(8,128)S(1)} %pad_maximum_fusion.4), channel_id=1, source_target_pairs={{1,0},{2,1},{3,2},{4,3},{5,4},{6,5},{7,6},{8,7},{9,8},{10,9},{11,1... | collective-permute-start | bytes 1572872 | tf_op jit(solution)/shard_map/ppermute | solution.py:20
  125.5 8.8 %collective-permute-done.14 = f32[64,4,512]{2,0,1:T(8,128)S(1)} collective-permute-done((f32[64,4,512]{2,0,1:T(8,128)S(1)}, f32[64,4,512]{2,0,1:T(8,128)S(1)}, u32[]{:S(2)}, u32[]{:S(2)}) %collective-permute-start.14) | collective-permute-done | bytes 524320 | tf_op jit(solution)/shard_map/ppermute | solution.py:20
  134.3 0.8 copy-done.17
  135.4 1.4 pad_maximum_fusion.1
  136.9 0.9 fusion.40
  137.8 0.9 fusion.8
  139.6 1.0 pad_slice_fusion.74
  140.6 1.4 reshape.302
  142.0 2.6 %reshape.301 = f32[32,2,12,256]{3,1,0,2:T(2,128)} reshape(f32[64,12,256]{2,0,1:T(8,128)} %pad_slice_fusion.74) | data formatting | bytes 1572864 | tf_op jit(solution)/shard_map/reshape | solution.py:127
  144.6 1.9 fusion.95
  146.6 1.9 collective-permute-start.16
  148.5 1.9 collective-permute-start.17
  150.5 0.9 compare_and_fusion.5
  151.4 6.6 %collective-permute-start.18 = (f32[32,2,512]{2,0,1:T(8,128)S(1)}, f32[32,2,512]{2,0,1:T(8,128)S(1)}, u32[]{:S(2)}, u32[]{:S(2)}) collective-permute-start(f32[32,2,512]{2,0,1:T(8,128)S(1)} %pad_maximum_fusion.11), channel_id=1, source_target_pairs={{1,0},{2,1},{3,2},{4,3},{5,4},{6,5},{7,6},{8,7},{9,8},{10,9},{11,1... | collective-permute-start | bytes 393224 | tf_op jit(solution)/shard_map/ppermute | solution.py:20
  158.0 4.8 %collective-permute-start.19 = (f32[32,2,512]{2,0,1:T(8,128)S(1)}, f32[32,2,512]{2,0,1:T(8,128)S(1)}, u32[]{:S(2)}, u32[]{:S(2)}) collective-permute-start(f32[32,2,512]{2,0,1:T(8,128)S(1)} %pad_maximum_fusion.11), channel_id=1, source_target_pairs={{2,0},{3,1},{4,2},{5,3},{6,4},{7,5},{8,6},{9,7},{10,8},{11,9},{12,... | collective-permute-start | bytes 393224 | tf_op jit(solution)/shard_map/ppermute | solution.py:20
  163.0 4.2 %collective-permute-done.19 = f32[32,2,512]{2,0,1:T(8,128)S(1)} collective-permute-done((f32[32,2,512]{2,0,1:T(8,128)S(1)}, f32[32,2,512]{2,0,1:T(8,128)S(1)}, u32[]{:S(2)}, u32[]{:S(2)}) %collective-permute-start.19) | collective-permute-done | bytes 131104 | tf_op jit(solution)/shard_map/ppermute | solution.py:20
  169.3 1.9 collective-permute-start.20
  171.2 2.2 %collective-permute-start.21 = (f32[32,2,256]{2,0,1:T(8,128)S(1)}, f32[32,2,256]{2,0,1:T(8,128)S(1)}, u32[]{:S(2)}, u32[]{:S(2)}) collective-permute-start(f32[32,2,256]{2,0,1:T(8,128)S(1)} %slice_select_fusion.3), channel_id=1, source_target_pairs={{0,1},{1,2},{2,3},{3,4},{4,5},{5,6},{6,7},{7,8},{8,9},{9,10},{10,1... | collective-permute-start | bytes 196616 | tf_op jit(solution)/shard_map/ppermute | solution.py:20
  173.4 5.8 %collective-permute-start.22 = (f32[32,2,256]{2,0,1:T(8,128)S(1)}, f32[32,2,256]{2,0,1:T(8,128)S(1)}, u32[]{:S(2)}, u32[]{:S(2)}) collective-permute-start(f32[32,2,256]{2,0,1:T(8,128)S(1)} %slice_select_fusion.3), channel_id=1, source_target_pairs={{1,0},{2,1},{3,2},{4,3},{5,4},{6,5},{7,6},{8,7},{9,8},{10,9},{11,1... | collective-permute-start | bytes 196616 | tf_op jit(solution)/shard_map/ppermute | solution.py:20
  179.2 5.2 %collective-permute-start.23 = (f32[32,2,256]{2,0,1:T(8,128)S(1)}, f32[32,2,256]{2,0,1:T(8,128)S(1)}, u32[]{:S(2)}, u32[]{:S(2)}) collective-permute-start(f32[32,2,256]{2,0,1:T(8,128)S(1)} %slice_select_fusion.3), channel_id=1, source_target_pairs={{2,0},{3,1},{4,2},{5,3},{6,4},{7,5},{8,6},{9,7},{10,8},{11,9},{12,... | collective-permute-start | bytes 196616 | tf_op jit(solution)/shard_map/ppermute | solution.py:20
  184.5 2.2 %collective-permute-done.23 = f32[32,2,256]{2,0,1:T(8,128)S(1)} collective-permute-done((f32[32,2,256]{2,0,1:T(8,128)S(1)}, f32[32,2,256]{2,0,1:T(8,128)S(1)}, u32[]{:S(2)}, u32[]{:S(2)}) %collective-permute-start.23) | collective-permute-done | bytes 65568 | tf_op jit(solution)/shard_map/ppermute | solution.py:20
  186.7 1.1 fusion.113
  187.8 1.1 fusion.117
  189.3 0.9 broadcast_in_dim.36
  190.2 2.0 reshape.306
  192.3 1.1 bitcast_add_fusion
  193.4 0.9 fusion.24
  194.3 0.9 fusion.32
  195.3 2.1 collective-permute-start.24
  197.3 6.3 %collective-permute-start.25 = (f32[64,2,256]{2,0,1:T(8,128)S(1)}, f32[64,2,256]{2,0,1:T(8,128)S(1)}, u32[]{:S(2)}, u32[]{:S(2)}) collective-permute-start(f32[64,2,256]{2,0,1:T(8,128)S(1)} %get-tuple-element.19), channel_id=1, source_target_pairs={{1,0},{2,1},{3,2},{4,3},{5,4},{6,5},{7,6},{8,7},{9,8},{10,9},{11,1... | collective-permute-start | bytes 393224 | tf_op jit(solution)/shard_map/ppermute | solution.py:20
  204.4 1.5 collective-permute-done.25
  208.5 1.8 fusion.71
  210.8 2.0 slice_select_fusion
  (163 shorter events, 12.0 us)
Async XLA Ops:
  2.6 11.1 %copy-start.1 = (f32[16,16,1024]{2,1,0:T(8,128)S(1)}, f32[16,16,1024]{2,1,0:T(8,128)}, u32[]{:S(2)}) copy-start(f32[16,16,1024]{2,1,0:T(8,128)} %shard_map.46) | copy-start | bytes 3145732
  3.7 3.1 %collective-permute-start = (f32[4,16,1024]{2,1,0:T(8,128)S(1)}, f32[4,16,1024]{2,1,0:T(8,128)S(1)}, u32[]{:S(2)}, u32[]{:S(2)}) collective-permute-start(f32[4,16,1024]{2,1,0:T(8,128)S(1)} %get-tuple-element.17), channel_id=1, source_target_pairs={{0,64},{64,128},{128,192},{192,256},{256,320},{320,384},{384,448},... | collective-permute-start | bytes 786440 | tf_op jit(solution)/shard_map/ppermute | solution.py:20
  5.5 8.1 %collective-permute-start.1 = (f32[4,16,1024]{2,1,0:T(8,128)S(1)}, f32[4,16,1024]{2,1,0:T(8,128)S(1)}, u32[]{:S(2)}, u32[]{:S(2)}) collective-permute-start(f32[4,16,1024]{2,1,0:T(8,128)S(1)} %get-tuple-element.18), channel_id=1, source_target_pairs={{64,0},{128,64},{192,128},{256,192},{320,256},{384,320},{448,384},... | collective-permute-start | bytes 786440 | tf_op jit(solution)/shard_map/ppermute | solution.py:20
  6.8 65.1 %copy-start.19 = (s32[16,16]{0,1:T(8,128)}, s32[16,16]{0,1:T(8,128)S(1)}, u32[]{:S(2)}) copy-start(s32[16,16]{0,1:T(8,128)S(1)} %iota_add_fusion.4) | copy-start | bytes 3076
  6.9 35.2 %copy-start.21 = (s32[24,24]{1,0:T(8,128)}, s32[24,24]{1,0:T(8,128)S(1)}, u32[]{:S(2)}) copy-start(s32[24,24]{1,0:T(8,128)S(1)} %iota_add_fusion.1) | copy-start | bytes 6916
  13.8 24.8 %collective-permute-start.2 = (f32[24,4,1024]{2,1,0:T(4,128)S(1)}, f32[24,4,1024]{2,1,0:T(4,128)S(1)}, u32[]{:S(2)}, u32[]{:S(2)}) collective-permute-start(f32[24,4,1024]{2,1,0:T(4,128)S(1)} %get-tuple-element.15), channel_id=1, source_target_pairs={{0,1},{1,2},{2,3},{3,4},{4,5},{5,6},{6,7},{7,8},{8,9},{9,10},{10,1... | collective-permute-start | bytes 1179656 | tf_op jit(solution)/shard_map/ppermute | solution.py:20
  18.1 21.9 %collective-permute-start.3 = (f32[24,4,1024]{2,1,0:T(4,128)S(1)}, f32[24,4,1024]{2,1,0:T(4,128)S(1)}, u32[]{:S(2)}, u32[]{:S(2)}) collective-permute-start(f32[24,4,1024]{2,1,0:T(4,128)S(1)} %get-tuple-element.16), channel_id=1, source_target_pairs={{1,0},{2,1},{3,2},{4,3},{5,4},{6,5},{7,6},{8,7},{9,8},{10,9},{11,1... | collective-permute-start | bytes 1179656 | tf_op jit(solution)/shard_map/ppermute | solution.py:20
  34.8 37.4 %copy-start.23 = (pred[16,16]{0,1:T(8,128)(4,1)}, pred[16,16]{0,1:T(8,128)(4,1)S(1)}, u32[]{:S(2)}) copy-start(pred[16,16]{0,1:T(8,128)(4,1)S(1)} %broadcast_and_fusion.1) | copy-start | bytes 772
  40.4 3.2 %copy-start = (f32[24,24,1024]{2,1,0:T(8,128)}, f32[24,24,1024]{2,1,0:T(8,128)S(1)}, u32[]{:S(2)}) copy-start(f32[24,24,1024]{2,1,0:T(8,128)S(1)} %pad_maximum_fusion) | copy-start | bytes 7077892
  42.1 2.8 %copy-start.6 = (pred[24,24,256]{2,1,0:T(8,128)(4,1)}, pred[24,24,256]{2,1,0:T(8,128)(4,1)S(1)}, u32[]{:S(2)}) copy-start(pred[24,24,256]{2,1,0:T(8,128)(4,1)S(1)} %get-tuple-element.9) | copy-start | bytes 442372
  43.6 1.3 copy-start.4
  45.5 12.3 %collective-permute-start.4 = (f32[4,8,512]{2,0,1:T(4,128)S(1)}, f32[4,8,512]{2,0,1:T(4,128)S(1)}, u32[]{:S(2)}, u32[]{:S(2)}) collective-permute-start(f32[4,8,512]{2,0,1:T(4,128)S(1)} %get-tuple-element.68), channel_id=1, source_target_pairs={{0,64},{64,128},{128,192},{192,256},{256,320},{320,384},{384,448},... | collective-permute-start | bytes 196616 | tf_op jit(solution)/shard_map/ppermute | solution.py:20
  56.5 3.2 %collective-permute-start.5 = (f32[4,8,512]{2,0,1:T(4,128)S(1)}, f32[4,8,512]{2,0,1:T(4,128)S(1)}, u32[]{:S(2)}, u32[]{:S(2)}) collective-permute-start(f32[4,8,512]{2,0,1:T(4,128)S(1)} %get-tuple-element.69), channel_id=1, source_target_pairs={{64,0},{128,64},{192,128},{256,192},{320,256},{384,320},{448,384},... | collective-permute-start | bytes 196616 | tf_op jit(solution)/shard_map/ppermute | solution.py:20
  59.8 10.1 %collective-permute-start.6 = (f32[16,4,512]{2,0,1:T(8,128)S(1)}, f32[16,4,512]{2,0,1:T(8,128)S(1)}, u32[]{:S(2)}, u32[]{:S(2)}) collective-permute-start(f32[16,4,512]{2,0,1:T(8,128)S(1)} %get-tuple-element.56), channel_id=1, source_target_pairs={{0,1},{1,2},{2,3},{3,4},{4,5},{5,6},{6,7},{7,8},{8,9},{9,10},{10,1... | collective-permute-start | bytes 393224 | tf_op jit(solution)/shard_map/ppermute | solution.py:20
  61.7 9.0 %collective-permute-start.7 = (f32[16,4,512]{2,0,1:T(8,128)S(1)}, f32[16,4,512]{2,0,1:T(8,128)S(1)}, u32[]{:S(2)}, u32[]{:S(2)}) collective-permute-start(f32[16,4,512]{2,0,1:T(8,128)S(1)} %get-tuple-element.57), channel_id=1, source_target_pairs={{1,0},{2,1},{3,2},{4,3},{5,4},{6,5},{7,6},{8,7},{9,8},{10,9},{11,1... | collective-permute-start | bytes 393224 | tf_op jit(solution)/shard_map/ppermute | solution.py:20
  72.2 0.7 copy-start.9
  73.5 20.6 %collective-permute-start.8 = (f32[4,4,512]{2,0,1:T(4,128)S(1)}, f32[4,4,512]{2,0,1:T(4,128)S(1)}, u32[]{:S(2)}, u32[]{:S(2)}) collective-permute-start(f32[4,4,512]{2,0,1:T(4,128)S(1)} %get-tuple-element.73), channel_id=1, source_target_pairs={{0,64},{64,0},{128,192},{192,128},{256,320},{320,256},{384,448},{4... | collective-permute-start | bytes 98312 | tf_op jit(solution)/shard_map/ppermute | solution.py:55
  81.9 12.4 %collective-permute-start.9 = (f32[4,4,512]{2,0,1:T(4,128)S(1)}, f32[4,4,512]{2,0,1:T(4,128)S(1)}, u32[]{:S(2)}, u32[]{:S(2)}) collective-permute-start(f32[4,4,512]{2,0,1:T(4,128)S(1)} %get-tuple-element.73), channel_id=1, source_target_pairs={{0,128},{64,192},{128,0},{192,64},{256,384},{320,448},{384,256},{4... | collective-permute-start | bytes 98312 | tf_op jit(solution)/shard_map/ppermute | solution.py:55
  92.1 9.4 %collective-permute-start.10 = (f32[4,4,512]{2,0,1:T(4,128)S(1)}, f32[4,4,512]{2,0,1:T(4,128)S(1)}, u32[]{:S(2)}, u32[]{:S(2)}) collective-permute-start(f32[4,4,512]{2,0,1:T(4,128)S(1)} %get-tuple-element.73), channel_id=1, source_target_pairs={{0,192},{64,128},{128,64},{192,0},{256,448},{320,384},{384,320},{4... | collective-permute-start | bytes 98312 | tf_op jit(solution)/shard_map/ppermute | solution.py:55
  101.6 11.0 %collective-permute-start.11 = (f32[16,4,512]{2,0,1:T(8,128)S(1)}, f32[16,4,512]{2,0,1:T(8,128)S(1)}, u32[]{:S(2)}, u32[]{:S(2)}) collective-permute-start(f32[16,4,512]{2,0,1:T(8,128)S(1)} %get-tuple-element.63), channel_id=1, source_target_pairs={{0,256},{64,320},{128,384},{192,448},{256,0},{320,64},{384,128},{4... | collective-permute-start | bytes 393224 | tf_op jit(solution)/shard_map/ppermute | solution.py:55
  104.7 8.6 %collective-permute-start.12 = (f32[16,4,512]{2,0,1:T(8,128)S(1)}, f32[16,4,512]{2,0,1:T(8,128)S(1)}, u32[]{:S(2)}, u32[]{:S(2)}) collective-permute-start(f32[16,4,512]{2,0,1:T(8,128)S(1)} %get-tuple-element.63), channel_id=1, source_target_pairs={{0,512},{64,576},{128,640},{192,704},{256,768},{320,832},{384,896}... | collective-permute-start | bytes 393224 | tf_op jit(solution)/shard_map/ppermute | solution.py:55
  106.6 9.4 %collective-permute-start.13 = (f32[16,4,512]{2,0,1:T(8,128)S(1)}, f32[16,4,512]{2,0,1:T(8,128)S(1)}, u32[]{:S(2)}, u32[]{:S(2)}) collective-permute-start(f32[16,4,512]{2,0,1:T(8,128)S(1)} %get-tuple-element.63), channel_id=1, source_target_pairs={{0,768},{64,832},{128,896},{192,960},{256,512},{320,576},{384,640}... | collective-permute-start | bytes 393224 | tf_op jit(solution)/shard_map/ppermute | solution.py:55
  116.2 18.0 %collective-permute-start.14 = (f32[64,4,512]{2,0,1:T(8,128)S(1)}, f32[64,4,512]{2,0,1:T(8,128)S(1)}, u32[]{:S(2)}, u32[]{:S(2)}) collective-permute-start(f32[64,4,512]{2,0,1:T(8,128)S(1)} %pad_maximum_fusion.4), channel_id=1, source_target_pairs={{0,1},{1,2},{2,3},{3,4},{4,5},{5,6},{6,7},{7,8},{8,9},{9,10},{10,1... | collective-permute-start | bytes 1572872 | tf_op jit(solution)/shard_map/ppermute | solution.py:20
  118.1 17.3 %collective-permute-start.15 = (f32[64,4,512]{2,0,1:T(8,128)S(1)}, f32[64,4,512]{2,0,1:T(8,128)}, u32[]{:S(2)}, u32[]{:S(2)}) collective-permute-start(f32[64,4,512]{2,0,1:T(8,128)S(1)} %pad_maximum_fusion.4), channel_id=1, source_target_pairs={{1,0},{2,1},{3,2},{4,3},{5,4},{6,5},{7,6},{8,7},{9,8},{10,9},{11,1... | collective-permute-start | bytes 1572872 | tf_op jit(solution)/shard_map/ppermute | solution.py:20
  125.5 11.4 %copy-start.26 = (pred[12]{0:T(512)(128)(4,1)S(1)}, pred[12]{0:T(512)(128)(4,1)}, u32[]{:S(2)}) copy-start(pred[12]{0:T(512)(128)(4,1)} %compare_and_fusion.9) | copy-start | bytes 40
  134.3 0.8 copy-start.17
  138.7 0.9 copy-start.2
  142.0 2.6 %copy-start.8 = (f32[32,2,12,256]{3,1,0,2:T(2,128)S(1)}, f32[32,2,12,256]{3,1,0,2:T(2,128)}, u32[]{:S(2)}) copy-start(f32[32,2,12,256]{3,1,0,2:T(2,128)} %reshape.302) | copy-start | bytes 2359300
  144.5 5.9 %copy-start.25 = (pred[10]{0:T(512)(128)(4,1)S(1)}, pred[10]{0:T(512)(128)(4,1)}, u32[]{:S(2)}) copy-start(pred[10]{0:T(512)(128)(4,1)} %compare_and_fusion.8) | copy-start | bytes 34
  146.6 16.2 %collective-permute-start.16 = (f32[32,2,512]{2,0,1:T(8,128)S(1)}, f32[32,2,512]{2,0,1:T(8,128)S(1)}, u32[]{:S(2)}, u32[]{:S(2)}) collective-permute-start(f32[32,2,512]{2,0,1:T(8,128)S(1)} %pad_maximum_fusion.11), channel_id=1, source_target_pairs={{0,2},{1,3},{2,4},{3,5},{4,6},{5,7},{6,8},{7,9},{8,10},{9,11},{10,... | collective-permute-start | bytes 393224 | tf_op jit(solution)/shard_map/ppermute | solution.py:20
  148.5 14.3 %collective-permute-start.17 = (f32[32,2,512]{2,0,1:T(8,128)S(1)}, f32[32,2,512]{2,0,1:T(8,128)S(1)}, u32[]{:S(2)}, u32[]{:S(2)}) collective-permute-start(f32[32,2,512]{2,0,1:T(8,128)S(1)} %pad_maximum_fusion.11), channel_id=1, source_target_pairs={{0,1},{1,2},{2,3},{3,4},{4,5},{5,6},{6,7},{7,8},{8,9},{9,10},{10,1... | collective-permute-start | bytes 393224 | tf_op jit(solution)/shard_map/ppermute | solution.py:20
  151.4 11.5 %collective-permute-start.18 = (f32[32,2,512]{2,0,1:T(8,128)S(1)}, f32[32,2,512]{2,0,1:T(8,128)S(1)}, u32[]{:S(2)}, u32[]{:S(2)}) collective-permute-start(f32[32,2,512]{2,0,1:T(8,128)S(1)} %pad_maximum_fusion.11), channel_id=1, source_target_pairs={{1,0},{2,1},{3,2},{4,3},{5,4},{6,5},{7,6},{8,7},{9,8},{10,9},{11,1... | collective-permute-start | bytes 393224 | tf_op jit(solution)/shard_map/ppermute | solution.py:20
  158.0 9.2 %collective-permute-start.19 = (f32[32,2,512]{2,0,1:T(8,128)S(1)}, f32[32,2,512]{2,0,1:T(8,128)S(1)}, u32[]{:S(2)}, u32[]{:S(2)}) collective-permute-start(f32[32,2,512]{2,0,1:T(8,128)S(1)} %pad_maximum_fusion.11), channel_id=1, source_target_pairs={{2,0},{3,1},{4,2},{5,3},{6,4},{7,5},{8,6},{9,7},{10,8},{11,9},{12,... | collective-permute-start | bytes 393224 | tf_op jit(solution)/shard_map/ppermute | solution.py:20
  167.7 1.5 copy-start.11
  167.7 1.5 copy-start.13
  169.3 15.2 %collective-permute-start.20 = (f32[32,2,256]{2,0,1:T(8,128)S(1)}, f32[32,2,256]{2,0,1:T(8,128)S(1)}, u32[]{:S(2)}, u32[]{:S(2)}) collective-permute-start(f32[32,2,256]{2,0,1:T(8,128)S(1)} %slice_select_fusion.3), channel_id=1, source_target_pairs={{0,2},{1,3},{2,4},{3,5},{4,6},{5,7},{6,8},{7,9},{8,10},{9,11},{10,... | collective-permute-start | bytes 196616 | tf_op jit(solution)/shard_map/ppermute | solution.py:20
  171.2 13.3 %collective-permute-start.21 = (f32[32,2,256]{2,0,1:T(8,128)S(1)}, f32[32,2,256]{2,0,1:T(8,128)S(1)}, u32[]{:S(2)}, u32[]{:S(2)}) collective-permute-start(f32[32,2,256]{2,0,1:T(8,128)S(1)} %slice_select_fusion.3), channel_id=1, source_target_pairs={{0,1},{1,2},{2,3},{3,4},{4,5},{5,6},{6,7},{7,8},{8,9},{9,10},{10,1... | collective-permute-start | bytes 196616 | tf_op jit(solution)/shard_map/ppermute | solution.py:20
  173.4 11.1 %collective-permute-start.22 = (f32[32,2,256]{2,0,1:T(8,128)S(1)}, f32[32,2,256]{2,0,1:T(8,128)S(1)}, u32[]{:S(2)}, u32[]{:S(2)}) collective-permute-start(f32[32,2,256]{2,0,1:T(8,128)S(1)} %slice_select_fusion.3), channel_id=1, source_target_pairs={{1,0},{2,1},{3,2},{4,3},{5,4},{6,5},{7,6},{8,7},{9,8},{10,9},{11,1... | collective-permute-start | bytes 196616 | tf_op jit(solution)/shard_map/ppermute | solution.py:20
  179.2 7.5 %collective-permute-start.23 = (f32[32,2,256]{2,0,1:T(8,128)S(1)}, f32[32,2,256]{2,0,1:T(8,128)S(1)}, u32[]{:S(2)}, u32[]{:S(2)}) collective-permute-start(f32[32,2,256]{2,0,1:T(8,128)S(1)} %slice_select_fusion.3), channel_id=1, source_target_pairs={{2,0},{3,1},{4,2},{5,3},{6,4},{7,5},{8,6},{9,7},{10,8},{11,9},{12,... | collective-permute-start | bytes 196616 | tf_op jit(solution)/shard_map/ppermute | solution.py:20
  187.7 1.4 copy-start.12
  187.8 1.4 copy-start.14
  187.8 1.4 copy-start.18
  189.2 3.1 %copy-start.3 = (f32[64,12,256]{2,0,1:T(8,128)S(1)}, f32[64,12,256]{2,0,1:T(8,128)}, u32[]{:S(2)}) copy-start(f32[64,12,256]{2,0,1:T(8,128)} %copy-done.2) | copy-start | bytes 2359300
  189.3 4.0 %copy-start.27 = (pred[12]{0:T(512)(128)(4,1)S(1)}, pred[12]{0:T(512)(128)(4,1)}, u32[]{:S(2)}) copy-start(pred[12]{0:T(512)(128)(4,1)} %compare_and_fusion.9) | copy-start | bytes 40
  194.3 9.3 %copy-start.20 = (s32[16,16]{0,1:T(8,128)S(1)}, s32[16,16]{0,1:T(8,128)}, u32[]{:S(2)}) copy-start(s32[16,16]{0,1:T(8,128)} %copy-done.19) | copy-start | bytes 3076
  194.3 9.3 %copy-start.24 = (pred[16,16]{0,1:T(8,128)(4,1)S(1)}, pred[16,16]{0,1:T(8,128)(4,1)}, u32[]{:S(2)}) copy-start(pred[16,16]{0,1:T(8,128)(4,1)} %copy-done.23) | copy-start | bytes 772
  195.2 10.8 %copy-start.10 = (f32[16,16,256]{2,0,1:T(8,128)S(1)}, f32[16,16,256]{2,0,1:T(8,128)}, u32[]{:S(2)}) copy-start(f32[16,16,256]{2,0,1:T(8,128)} %copy-done.9) | copy-start | bytes 786436
  195.3 9.1 %collective-permute-start.24 = (f32[64,2,256]{2,0,1:T(8,128)S(1)}, f32[64,2,256]{2,0,1:T(8,128)S(1)}, u32[]{:S(2)}, u32[]{:S(2)}) collective-permute-start(f32[64,2,256]{2,0,1:T(8,128)S(1)} %get-tuple-element.20), channel_id=1, source_target_pairs={{0,1},{1,2},{2,3},{3,4},{4,5},{5,6},{6,7},{7,8},{8,9},{9,10},{10,1... | collective-permute-start | bytes 393224 | tf_op jit(solution)/shard_map/ppermute | solution.py:20
  197.3 8.5 %collective-permute-start.25 = (f32[64,2,256]{2,0,1:T(8,128)S(1)}, f32[64,2,256]{2,0,1:T(8,128)S(1)}, u32[]{:S(2)}, u32[]{:S(2)}) collective-permute-start(f32[64,2,256]{2,0,1:T(8,128)S(1)} %get-tuple-element.19), channel_id=1, source_target_pairs={{1,0},{2,1},{3,2},{4,3},{5,4},{6,5},{7,6},{8,7},{9,8},{10,9},{11,1... | collective-permute-start | bytes 393224 | tf_op jit(solution)/shard_map/ppermute | solution.py:20
  206.1 1.0 copy-start.15
  206.1 1.0 copy-start.16
  207.3 1.1 copy-start.5
  207.3 1.1 copy-start.7
  207.7 0.8 copy-start.22

commit v6 on v5

--- a/solution.py
+++ b/solution.py
@@ -10,6 +10,7 @@
 HALO_FINE = 4
 HALO_MID = 4
 HALO_COARSE = 4
+HALO_1_Y = 12
 
 
 def shifted(block, axis, distance):
@@ -70,12 +71,14 @@
     return [packed[:, :, i * depth:(i + 1) * depth] for i in range(len(arrays))]
 
 
-def inside(span_x, span_y, width, whole_x=False):
-    index_y = lax.axis_index("gy") * span_y - width + jnp.arange(span_y + 2 * width)
+def inside(span_x, span_y, width, whole_x=False, width_y=None):
+    if width_y is None:
+        width_y = width
+    index_y = lax.axis_index("gy") * span_y - width_y + jnp.arange(span_y + 2 * width_y)
     total_y = span_y * lax.axis_size("gy")
     keep_y = (index_y >= 0) & (index_y < total_y)
     if whole_x:
-        return jnp.broadcast_to(keep_y[None, :, None], (span_x, span_y + 2 * width, 1))
+        return jnp.broadcast_to(keep_y[None, :, None], (span_x, span_y + 2 * width_y, 1))
     index_x = lax.axis_index("gx") * span_x - width + jnp.arange(span_x + 2 * width)
     total_x = span_x * lax.axis_size("gx")
     keep_x = (index_x >= 0) & (index_x < total_x)
@@ -122,14 +125,15 @@
     return jnp.where(allowed, residual, 0.0)
 
 
-def restrict(values, width_x, width_y, span_x, span_y):
+def restrict(values, width_x, width_y, span_x, span_y, rim_y=0):
     rows = values[width_x - 1:width_x + span_x]
     before = rows[:-1].reshape(span_x // 2, 2, *rows.shape[1:])[:, 0]
     paired = rows[1:].reshape(span_x // 2, 2, *rows.shape[1:])
     across = 0.25 * before + 0.5 * paired[:, 0] + 0.25 * paired[:, 1]
-    cols = across[:, width_y - 1:width_y + span_y]
-    before = cols[:, :-1].reshape(cols.shape[0], span_y // 2, 2, cols.shape[2])[:, :, 0]
-    paired = cols[:, 1:].reshape(cols.shape[0], span_y // 2, 2, cols.shape[2])
+    cols = across[:, width_y - 2 * rim_y - 1:width_y + span_y + 2 * rim_y]
+    count = span_y // 2 + 2 * rim_y
+    before = cols[:, :-1].reshape(cols.shape[0], count, 2, cols.shape[2])[:, :, 0]
+    paired = cols[:, 1:].reshape(cols.shape[0], count, 2, cols.shape[2])
     return 0.25 * before + 0.5 * paired[:, :, 0] + 0.25 * paired[:, :, 1]
 
 
@@ -148,23 +152,25 @@
     return values[width:values.shape[0] - width, width:values.shape[1] - width]
 
 
-def descend(grid_level, source, coefficient, width):
+def descend(grid_level, source, coefficient, width, width_y, rim_y):
     span_x, span_y = source.shape[0], source.shape[1]
-    source, coefficient_ext = exchange_many([source, coefficient], width)
+    exchanger = lambda block, rim: along(along(block, width, "gx", 0), width_y, "gy", 1)
+    source, coefficient_ext = exchange_many([source, coefficient], width, exchanger)
     weight = 0.25**grid_level
     divisor = 4.0 * weight + 2.0 + coefficient_ext
-    allowed = inside(span_x, span_y, width)
+    allowed = inside(span_x, span_y, width, width_y=width_y)
     iterate = sweeps(jnp.zeros_like(source), source, divisor, weight, allowed, 1)
     residual = residual_of(iterate, source, divisor, weight, allowed)
-    coarse_source = restrict(residual, width, width, span_x, span_y)
-    coarse_coefficient = coarsen(interior(coefficient_ext, width))
+    coarse_source = restrict(residual, width, width_y, span_x, span_y, rim_y)
+    low = width_y - 2 * rim_y
+    coarse_coefficient = coarsen(
+        coefficient_ext[width:width + span_x, low:width_y + span_y + 2 * rim_y]
+    )
     return iterate, source, divisor, weight, allowed, coarse_source, coarse_coefficient
 
 
 def descend_whole_x(grid_level, source, coefficient, width):
-    span_y = source.shape[1]
-    source, coefficient = exchange_many([source, coefficient], width, exchange_y)
-    span_x = source.shape[0]
+    span_x, span_y = source.shape[0], source.shape[1] - 2 * width
     weight = 0.25**grid_level
     divisor = 4.0 * weight + 2.0 + coefficient
     allowed = inside(span_x, span_y, width, whole_x=True)
@@ -242,7 +248,7 @@
     source_1 = restrict(residual, width, width, span_x, span_y)
     coefficient_1 = coarsen(interior(coefficient, width))
 
-    level_1 = descend(1, source_1, coefficient_1, HALO_MID)
+    level_1 = descend(1, source_1, coefficient_1, HALO_MID, HALO_1_Y, HALO_MID)
     source_2, coefficient_2 = level_1[5], level_1[6]
     span_x2 = source_2.shape[0]
     whole = gather_x(jnp.concatenate([source_2, coefficient_2], axis=2))
@@ -255,7 +261,11 @@
     iterate_2 = exchange_y(iterate_2[:, HALO_MID:HALO_MID + source_2.shape[1] - 2 * HALO_MID], rim)
     iterate_2 = x_window(iterate_2, lax.axis_index("gx") * span_x2, span_x2 + 2 * rim, rim)
 
-    iterate_1, source_1, divisor_1, weight_1, allowed_1 = level_1[:5]
+    cut = HALO_1_Y - HALO_MID
+    iterate_1, source_1, divisor_1, allowed_1 = [
+        values[:, cut:values.shape[1] - cut] for values in (level_1[0], level_1[1], level_1[2], level_1[4])
+    ]
+    weight_1 = level_1[3]
     iterate_1 = sweeps(iterate_1 + lift(iterate_2), source_1, divisor_1, weight_1, allowed_1, 1)
     lifted = lift(interior(iterate_1, HALO_MID // 2))
 

time: 214 us -> 223 us (1.042)
  starting transfers between devices: 122 us -> 130 us
  waiting for transfers between devices: 44.7 us -> 41.4 us
  other arithmetic: 28.2 us -> 30.6 us
  local copies, waits for them, and re-layouts: 13.5 us -> 15.8 us
    ppermute x20, waiting for transfers between devices: 33.8 us -> 23.5 us  [shifted(): return lax.ppermute(block, axis, route)]
    ppermute x6, waiting for transfers between devices: 10.9 us -> 17.8 us  [gather_x(): lax.ppermute(block, 'gx', [(i, i ^ m * group) for i in range(count)])]
    ppermute x6, starting transfers between devices: 30.9 us -> 36.3 us  [gather_x(): lax.ppermute(block, 'gx', [(i, i ^ m * group) for i in range(count)])]
    ppermute x20, starting transfers between devices: 91.6 us -> 94 us  [shifted(): return lax.ppermute(block, axis, route)]
  transfers between devices with their start and end apart: 26 -> 26, of which waited for: 16 -> 12; matrix products, arithmetic and copies ran while one was open for 1% -> 2% of each run, Pallas kernels for 0% -> 0%
where the time goes in v6:
time: 223 us; the launch traced here: 222 us
  starting transfers between devices  130 us (58%)
  waiting for transfers between devices  41.4 us (19%)
  other arithmetic  30.6 us (14%)
  local copies, waits for them, and re-layouts  15.8 us (7%)
  Pallas kernels  2.52 us (1%)
    ppermute x20, starting transfers between devices, shifted(): return lax.ppermute(block, axis, route)  94 us
    ppermute x6, starting transfers between devices, gather_x(): lax.ppermute(block, 'gx', [(i, i ^ m * group) for i in range(count)])  36.3 us
    ppermute x20, waiting for transfers between devices, shifted(): return lax.ppermute(block, axis, route)  23.5 us
    ppermute x6, waiting for transfers between devices, gather_x(): lax.ppermute(block, 'gx', [(i, i ^ m * group) for i in range(count)])  17.8 us
    select_n x18, other arithmetic, half_sweep(): return jnp.where(update, renewed, iterate)  14.6 us
  transfers between devices with their start and end apart: 26, of which 12 were waited for; matrix products, arithmetic and copies ran while one was open for 2% of the time, Pallas kernels for 0%

profile of v6, /device:TPU:8, one launch (start us, length us, event | category | flops | bytes accessed | tf_op | source)
XLA Modules:
  0.0 222.2 jit_solution(853093863219554594)
XLA Ops:
  0.0 2.5 %shard_map.46 = f32[16,16,1024]{2,1,0:T(8,128)} custom-call(f32[16]{0:T(128)} %volts_ref.1, f32[16,16,256]{2,1,0:T(8,128)} %potential_ref.1, f32[16,16,256]{2,1,0:T(8,128)} %charge_ref.1, s32[16,16,256]{2,1,0:T(8,128)} %region_ref.1), custom_call_target="tpu_custom_call" | custom-call | tf_op jit(solution)/shard_map/pallas_call | solution.py:224
  2.5 1.2 fusion.260
  3.7 1.3 collective-permute-start.1
  5.0 3.0 %collective-permute-start = (f32[4,16,1024]{2,1,0:T(8,128)S(1)}, f32[4,16,1024]{2,1,0:T(8,128)S(1)}, u32[]{:S(2)}, u32[]{:S(2)}) collective-permute-start(f32[4,16,1024]{2,1,0:T(8,128)S(1)} %get-tuple-element.25), channel_id=1, source_target_pairs={{0,64},{64,128},{128,192},{192,256},{256,320},{320,384},{384,448},... | collective-permute-start | bytes 786440 | tf_op jit(solution)/shard_map/ppermute | solution.py:21
  8.1 1.0 collective-permute-done
  9.3 18.1 %collective-permute-start.3 = (f32[24,4,1024]{2,1,0:T(4,128)S(1)}, f32[24,4,1024]{2,1,0:T(4,128)S(1)}, u32[]{:S(2)}, u32[]{:S(2)}) collective-permute-start(f32[24,4,1024]{2,1,0:T(4,128)S(1)} %get-tuple-element.22), channel_id=1, source_target_pairs={{1,0},{2,1},{3,2},{4,3},{5,4},{6,5},{7,6},{8,7},{9,8},{10,9},{11,1... | collective-permute-start | bytes 1179656 | tf_op jit(solution)/shard_map/ppermute | solution.py:21
  27.5 1.9 collective-permute-start.2
  29.5 4.4 %collective-permute-done.3 = f32[24,4,1024]{2,1,0:T(4,128)S(1)} collective-permute-done((f32[24,4,1024]{2,1,0:T(4,128)S(1)}, f32[24,4,1024]{2,1,0:T(4,128)S(1)}, u32[]{:S(2)}, u32[]{:S(2)}) %collective-permute-start.3) | collective-permute-done | bytes 393248 | tf_op jit(solution)/shard_map/ppermute | solution.py:21
  33.9 5.3 %collective-permute-done.2 = f32[24,4,1024]{2,1,0:T(4,128)S(1)} collective-permute-done((f32[24,4,1024]{2,1,0:T(4,128)S(1)}, f32[24,4,1024]{2,1,0:T(4,128)S(1)}, u32[]{:S(2)}, u32[]{:S(2)}) %collective-permute-start.2) | collective-permute-done | bytes 393248 | tf_op jit(solution)/shard_map/ppermute | solution.py:21
  39.8 1.5 fusion.58
  41.3 1.5 fusion.62
  42.8 1.2 broadcast_add_fusion
  44.7 1.3 collective-permute-start.5
  46.0 14.0 %collective-permute-start.4 = (f32[4,8,512]{2,0,1:T(4,128)S(1)}, f32[4,8,512]{2,0,1:T(4,128)S(1)}, u32[]{:S(2)}, u32[]{:S(2)}) collective-permute-start(f32[4,8,512]{2,0,1:T(4,128)S(1)} %get-tuple-element.72), channel_id=1, source_target_pairs={{0,64},{64,128},{128,192},{192,256},{256,320},{320,384},{384,448},... | collective-permute-start | bytes 196616 | tf_op jit(solution)/shard_map/ppermute | solution.py:21
  60.0 0.8 collective-permute-done.4
  60.9 1.9 collective-permute-start.6
  62.8 1.9 collective-permute-start.8
  64.8 6.0 %collective-permute-start.7 = (f32[16,8,512]{2,0,1:T(8,128)S(1)}, f32[16,8,512]{2,0,1:T(8,128)S(1)}, u32[]{:S(2)}, u32[]{:S(2)}) collective-permute-start(f32[16,8,512]{2,0,1:T(8,128)S(1)} %pad_maximum_fusion.9), channel_id=1, source_target_pairs={{1,0},{2,1},{3,2},{4,3},{5,4},{6,5},{7,6},{8,7},{9,8},{10,9},{11,1... | collective-permute-start | bytes 786440 | tf_op jit(solution)/shard_map/ppermute | solution.py:21
  70.9 4.8 %collective-permute-start.9 = (f32[16,4,512]{2,0,1:T(8,128)S(1)}, f32[16,4,512]{2,0,1:T(8,128)S(1)}, u32[]{:S(2)}, u32[]{:S(2)}) collective-permute-start(f32[16,4,512]{2,0,1:T(8,128)S(1)} %get-tuple-element.64), channel_id=1, source_target_pairs={{2,0},{3,1},{4,2},{5,3},{6,4},{7,5},{8,6},{9,7},{10,8},{11,9},{12,... | collective-permute-start | bytes 393224 | tf_op jit(solution)/shard_map/ppermute | solution.py:21
  75.9 3.7 %collective-permute-done.9 = f32[16,4,512]{2,0,1:T(8,128)S(1)} collective-permute-done((f32[16,4,512]{2,0,1:T(8,128)S(1)}, f32[16,4,512]{2,0,1:T(8,128)S(1)}, u32[]{:S(2)}, u32[]{:S(2)}) %collective-permute-start.9) | collective-permute-done | bytes 131104 | tf_op jit(solution)/shard_map/ppermute | solution.py:21
  80.3 1.4 slice_add_fusion.1
  83.1 17.8 %collective-permute-start.12 = (f32[4,12,512]{2,0,1:T(4,128)S(1)}, f32[4,12,512]{2,0,1:T(4,128)S(1)}, u32[]{:S(2)}, u32[]{:S(2)}) collective-permute-start(f32[4,12,512]{2,0,1:T(4,128)S(1)} %get-tuple-element.75), channel_id=1, source_target_pairs={{0,192},{64,128},{128,64},{192,0},{256,448},{320,384},{384,320},{4... | collective-permute-start | bytes 294920 | tf_op jit(solution)/shard_map/ppermute | solution.py:56
  100.9 4.6 %collective-permute-start.11 = (f32[4,12,512]{2,0,1:T(4,128)S(1)}, f32[4,12,512]{2,0,1:T(4,128)S(1)}, u32[]{:S(2)}, u32[]{:S(2)}) collective-permute-start(f32[4,12,512]{2,0,1:T(4,128)S(1)} %get-tuple-element.75), channel_id=1, source_target_pairs={{0,128},{64,192},{128,0},{192,64},{256,384},{320,448},{384,256},{4... | collective-permute-start | bytes 294920 | tf_op jit(solution)/shard_map/ppermute | solution.py:56
  105.5 2.0 collective-permute-start.10
  107.6 4.8 %collective-permute-done.11 = f32[4,12,512]{2,0,1:T(4,128)S(1)} collective-permute-done((f32[4,12,512]{2,0,1:T(4,128)S(1)}, f32[4,12,512]{2,0,1:T(4,128)S(1)}, u32[]{:S(2)}, u32[]{:S(2)}) %collective-permute-start.11) | collective-permute-done | bytes 98336 | tf_op jit(solution)/shard_map/ppermute | solution.py:56
  112.7 5.1 %collective-permute-start.15 = (f32[16,12,512]{2,0,1:T(8,128)S(1)}, f32[16,12,512]{2,0,1:T(8,128)S(1)}, u32[]{:S(2)}, u32[]{:S(2)}) collective-permute-start(f32[16,12,512]{2,0,1:T(8,128)S(1)} %get-tuple-element.45), channel_id=1, source_target_pairs={{0,768},{64,832},{128,896},{192,960},{256,512},{320,576},{384,640}... | collective-permute-start | bytes 1179656 | tf_op jit(solution)/shard_map/ppermute | solution.py:56
  117.8 4.6 %collective-permute-start.14 = (f32[16,12,512]{2,0,1:T(8,128)S(1)}, f32[16,12,512]{2,0,1:T(8,128)S(1)}, u32[]{:S(2)}, u32[]{:S(2)}) collective-permute-start(f32[16,12,512]{2,0,1:T(8,128)S(1)} %get-tuple-element.45), channel_id=1, source_target_pairs={{0,512},{64,576},{128,640},{192,704},{256,768},{320,832},{384,896}... | collective-permute-start | bytes 1179656 | tf_op jit(solution)/shard_map/ppermute | solution.py:56
  122.4 2.1 collective-permute-start.13
  125.3 1.0 compare_and_fusion.5
  126.3 9.8 %collective-permute-done.15 = f32[16,12,512]{2,0,1:T(8,128)S(1)} collective-permute-done((f32[16,12,512]{2,0,1:T(8,128)S(1)}, f32[16,12,512]{2,0,1:T(8,128)S(1)}, u32[]{:S(2)}, u32[]{:S(2)}) %collective-permute-start.15) | collective-permute-done | bytes 393248 | tf_op jit(solution)/shard_map/ppermute | solution.py:56
  136.1 3.2 %collective-permute-done.13 = f32[16,12,512]{2,0,1:T(8,128)S(1)} collective-permute-done((f32[16,12,512]{2,0,1:T(8,128)S(1)}, f32[16,12,512]{2,0,1:T(8,128)S(1)}, u32[]{:S(2)}, u32[]{:S(2)}) %collective-permute-start.13) | collective-permute-done | bytes 393248 | tf_op jit(solution)/shard_map/ppermute | solution.py:56
  140.5 0.9 fusion.40
  141.5 0.9 fusion.8
  142.4 0.9 copy-done.2
  143.2 1.1 fusion.16
  144.3 1.3 reshape.337
  145.7 1.0 pad_slice_fusion.84
  146.7 1.9 reshape.340
  148.6 1.2 fusion.215
  150.5 2.5 %reshape.336 = f32[32,2,12,256]{3,1,0,2:T(2,128)} reshape(f32[64,12,256]{2,0,1:T(8,128)} %pad_slice_fusion.84) | data formatting | bytes 1572864 | tf_op jit(solution)/shard_map/reshape | solution.py:130
  153.0 2.0 fusion.126
  155.1 1.9 collective-permute-start.16
  157.0 1.9 collective-permute-start.17
  159.7 6.0 %collective-permute-start.18 = (f32[32,2,512]{2,0,1:T(8,128)S(1)}, f32[32,2,512]{2,0,1:T(8,128)S(1)}, u32[]{:S(2)}, u32[]{:S(2)}) collective-permute-start(f32[32,2,512]{2,0,1:T(8,128)S(1)} %pad_maximum_fusion.20), channel_id=1, source_target_pairs={{1,0},{2,1},{3,2},{4,3},{5,4},{6,5},{7,6},{8,7},{9,8},{10,9},{11,1... | collective-permute-start | bytes 393224 | tf_op jit(solution)/shard_map/ppermute | solution.py:21
  165.7 6.4 %collective-permute-start.19 = (f32[32,2,512]{2,0,1:T(8,128)S(1)}, f32[32,2,512]{2,0,1:T(8,128)S(1)}, u32[]{:S(2)}, u32[]{:S(2)}) collective-permute-start(f32[32,2,512]{2,0,1:T(8,128)S(1)} %pad_maximum_fusion.20), channel_id=1, source_target_pairs={{2,0},{3,1},{4,2},{5,3},{6,4},{7,5},{8,6},{9,7},{10,8},{11,9},{12,... | collective-permute-start | bytes 393224 | tf_op jit(solution)/shard_map/ppermute | solution.py:21
  172.2 4.1 %collective-permute-done.19 = f32[32,2,512]{2,0,1:T(8,128)S(1)} collective-permute-done((f32[32,2,512]{2,0,1:T(8,128)S(1)}, f32[32,2,512]{2,0,1:T(8,128)S(1)}, u32[]{:S(2)}, u32[]{:S(2)}) %collective-permute-start.19) | collective-permute-done | bytes 131104 | tf_op jit(solution)/shard_map/ppermute | solution.py:21
  176.4 1.0 fusion.262
  178.9 0.8 slice_select_fusion.3
  179.7 1.9 collective-permute-start.20
  182.2 1.9 collective-permute-start.21
  184.1 6.0 %collective-permute-start.22 = (f32[32,2,256]{2,0,1:T(8,128)S(1)}, f32[32,2,256]{2,0,1:T(8,128)S(1)}, u32[]{:S(2)}, u32[]{:S(2)}) collective-permute-start(f32[32,2,256]{2,0,1:T(8,128)S(1)} %slice_select_fusion.3), channel_id=1, source_target_pairs={{1,0},{2,1},{3,2},{4,3},{5,4},{6,5},{7,6},{8,7},{9,8},{10,9},{11,1... | collective-permute-start | bytes 196616 | tf_op jit(solution)/shard_map/ppermute | solution.py:21
  190.1 5.5 %collective-permute-start.23 = (f32[32,2,256]{2,0,1:T(8,128)S(1)}, f32[32,2,256]{2,0,1:T(8,128)S(1)}, u32[]{:S(2)}, u32[]{:S(2)}) collective-permute-start(f32[32,2,256]{2,0,1:T(8,128)S(1)} %slice_select_fusion.3), channel_id=1, source_target_pairs={{2,0},{3,1},{4,2},{5,3},{6,4},{7,5},{8,6},{9,7},{10,8},{11,9},{12,... | collective-permute-start | bytes 196616 | tf_op jit(solution)/shard_map/ppermute | solution.py:21
  195.8 1.9 collective-permute-done.23
  199.0 0.9 broadcast_in_dim.36
  199.9 2.0 reshape.341
  201.9 1.1 bitcast_add_fusion
  203.1 0.9 fusion.24
  204.0 0.9 fusion.32
  205.0 2.1 collective-permute-start.24
  207.1 6.0 %collective-permute-start.25 = (f32[64,2,256]{2,0,1:T(8,128)S(1)}, f32[64,2,256]{2,0,1:T(8,128)S(1)}, u32[]{:S(2)}, u32[]{:S(2)}) collective-permute-start(f32[64,2,256]{2,0,1:T(8,128)S(1)} %get-tuple-element.27), channel_id=1, source_target_pairs={{1,0},{2,1},{3,2},{4,3},{5,4},{6,5},{7,6},{8,7},{9,8},{10,9},{11,1... | collective-permute-start | bytes 393224 | tf_op jit(solution)/shard_map/ppermute | solution.py:21
  213.3 0.8 collective-permute-done.24
  214.1 1.5 collective-permute-done.25
  217.9 1.8 fusion.71
  220.2 2.0 slice_select_fusion
  (194 shorter events, 13.6 us)
Async XLA Ops:
  2.5 6.6 %copy-start.1 = (f32[16,16,1024]{2,1,0:T(8,128)S(1)}, f32[16,16,1024]{2,1,0:T(8,128)}, u32[]{:S(2)}) copy-start(f32[16,16,1024]{2,1,0:T(8,128)} %shard_map.46) | copy-start | bytes 3145732
  3.7 4.4 %collective-permute-start.1 = (f32[4,16,1024]{2,1,0:T(8,128)S(1)}, f32[4,16,1024]{2,1,0:T(8,128)S(1)}, u32[]{:S(2)}, u32[]{:S(2)}) collective-permute-start(f32[4,16,1024]{2,1,0:T(8,128)S(1)} %get-tuple-element.26), channel_id=1, source_target_pairs={{64,0},{128,64},{192,128},{256,192},{320,256},{384,320},{448,384},... | collective-permute-start | bytes 786440 | tf_op jit(solution)/shard_map/ppermute | solution.py:21
  5.0 4.2 %collective-permute-start = (f32[4,16,1024]{2,1,0:T(8,128)S(1)}, f32[4,16,1024]{2,1,0:T(8,128)S(1)}, u32[]{:S(2)}, u32[]{:S(2)}) collective-permute-start(f32[4,16,1024]{2,1,0:T(8,128)S(1)} %get-tuple-element.25), channel_id=1, source_target_pairs={{0,64},{64,128},{128,192},{192,256},{256,320},{320,384},{384,448},... | collective-permute-start | bytes 786440 | tf_op jit(solution)/shard_map/ppermute | solution.py:21
  8.1 31.2 %copy-start.36 = (pred[16]{0:T(512)(128)(4,1)}, pred[16]{0:T(512)(128)(4,1)S(1)}, u32[]{:S(2)}) copy-start(pred[16]{0:T(512)(128)(4,1)S(1)} %compare_and_fusion.9) | copy-start | bytes 52
  8.1 33.2 %copy-start.25 = (s32[24,24]{1,0:T(8,128)}, s32[24,24]{1,0:T(8,128)S(1)}, u32[]{:S(2)}) copy-start(s32[24,24]{1,0:T(8,128)S(1)} %iota_add_fusion.2) | copy-start | bytes 6916
  9.3 24.6 %collective-permute-start.3 = (f32[24,4,1024]{2,1,0:T(4,128)S(1)}, f32[24,4,1024]{2,1,0:T(4,128)S(1)}, u32[]{:S(2)}, u32[]{:S(2)}) collective-permute-start(f32[24,4,1024]{2,1,0:T(4,128)S(1)} %get-tuple-element.22), channel_id=1, source_target_pairs={{1,0},{2,1},{3,2},{4,3},{5,4},{6,5},{7,6},{8,7},{9,8},{10,9},{11,1... | collective-permute-start | bytes 1179656 | tf_op jit(solution)/shard_map/ppermute | solution.py:21
  27.5 11.8 %collective-permute-start.2 = (f32[24,4,1024]{2,1,0:T(4,128)S(1)}, f32[24,4,1024]{2,1,0:T(4,128)S(1)}, u32[]{:S(2)}, u32[]{:S(2)}) collective-permute-start(f32[24,4,1024]{2,1,0:T(4,128)S(1)} %get-tuple-element.21), channel_id=1, source_target_pairs={{0,1},{1,2},{2,3},{3,4},{4,5},{5,6},{6,7},{7,8},{8,9},{9,10},{10,1... | collective-permute-start | bytes 1179656 | tf_op jit(solution)/shard_map/ppermute | solution.py:21
  39.7 3.1 %copy-start = (f32[24,24,1024]{2,1,0:T(8,128)}, f32[24,24,1024]{2,1,0:T(8,128)S(1)}, u32[]{:S(2)}) copy-start(f32[24,24,1024]{2,1,0:T(8,128)S(1)} %pad_maximum_fusion) | copy-start | bytes 7077892
  41.3 2.7 %copy-start.4 = (pred[24,24,256]{2,1,0:T(8,128)(4,1)}, pred[24,24,256]{2,1,0:T(8,128)(4,1)S(1)}, u32[]{:S(2)}) copy-start(pred[24,24,256]{2,1,0:T(8,128)(4,1)S(1)} %get-tuple-element.11) | copy-start | bytes 442372
  44.6 37.2 %copy-start.13 = (f32[8,8,256]{2,0,1:T(8,128)}, f32[8,8,256]{2,0,1:T(8,128)S(1)}, u32[]{:S(2)}) copy-start(f32[8,8,256]{2,0,1:T(8,128)S(1)} %fusion.243) | copy-start | bytes 196612
  44.6 37.1 %copy-start.15 = (f32[8,8,256]{2,0,1:T(8,128)}, f32[8,8,256]{2,0,1:T(8,128)S(1)}, u32[]{:S(2)}) copy-start(f32[8,8,256]{2,0,1:T(8,128)S(1)} %fusion.245) | copy-start | bytes 196612
  44.7 15.3 %collective-permute-start.5 = (f32[4,8,512]{2,0,1:T(4,128)S(1)}, f32[4,8,512]{2,0,1:T(4,128)S(1)}, u32[]{:S(2)}, u32[]{:S(2)}) collective-permute-start(f32[4,8,512]{2,0,1:T(4,128)S(1)} %get-tuple-element.73), channel_id=1, source_target_pairs={{64,0},{128,64},{192,128},{256,192},{320,256},{384,320},{448,384},... | collective-permute-start | bytes 196616 | tf_op jit(solution)/shard_map/ppermute | solution.py:21
  46.0 14.9 %collective-permute-start.4 = (f32[4,8,512]{2,0,1:T(4,128)S(1)}, f32[4,8,512]{2,0,1:T(4,128)S(1)}, u32[]{:S(2)}, u32[]{:S(2)}) collective-permute-start(f32[4,8,512]{2,0,1:T(4,128)S(1)} %get-tuple-element.72), channel_id=1, source_target_pairs={{0,64},{64,128},{128,192},{192,256},{256,320},{320,384},{384,448},... | collective-permute-start | bytes 196616 | tf_op jit(solution)/shard_map/ppermute | solution.py:21
  60.0 21.8 %copy-start.18 = (f32[4,8,512]{2,0,1:T(4,128)}, f32[4,8,512]{2,0,1:T(4,128)S(1)}, u32[]{:S(2)}) copy-start(f32[4,8,512]{2,0,1:T(4,128)S(1)} %collective-permute-done.5) | copy-start | bytes 196612
  60.8 20.9 %copy-start.20 = (f32[4,8,512]{2,0,1:T(4,128)}, f32[4,8,512]{2,0,1:T(4,128)S(1)}, u32[]{:S(2)}) copy-start(f32[4,8,512]{2,0,1:T(4,128)S(1)} %collective-permute-done.4) | copy-start | bytes 196612
  60.9 14.8 %collective-permute-start.6 = (f32[16,8,512]{2,0,1:T(8,128)S(1)}, f32[16,8,512]{2,0,1:T(8,128)S(1)}, u32[]{:S(2)}, u32[]{:S(2)}) collective-permute-start(f32[16,8,512]{2,0,1:T(8,128)S(1)} %pad_maximum_fusion.9), channel_id=1, source_target_pairs={{0,1},{1,2},{2,3},{3,4},{4,5},{5,6},{6,7},{7,8},{8,9},{9,10},{10,1... | collective-permute-start | bytes 786440 | tf_op jit(solution)/shard_map/ppermute | solution.py:21
  62.8 12.9 %collective-permute-start.8 = (f32[16,4,512]{2,0,1:T(8,128)S(1)}, f32[16,4,512]{2,0,1:T(8,128)S(1)}, u32[]{:S(2)}, u32[]{:S(2)}) collective-permute-start(f32[16,4,512]{2,0,1:T(8,128)S(1)} %get-tuple-element.65), channel_id=1, source_target_pairs={{0,2},{1,3},{2,4},{3,5},{4,6},{5,7},{6,8},{7,9},{8,10},{9,11},{10,... | collective-permute-start | bytes 393224 | tf_op jit(solution)/shard_map/ppermute | solution.py:21
  64.8 11.0 %collective-permute-start.7 = (f32[16,8,512]{2,0,1:T(8,128)S(1)}, f32[16,8,512]{2,0,1:T(8,128)S(1)}, u32[]{:S(2)}, u32[]{:S(2)}) collective-permute-start(f32[16,8,512]{2,0,1:T(8,128)S(1)} %pad_maximum_fusion.9), channel_id=1, source_target_pairs={{1,0},{2,1},{3,2},{4,3},{5,4},{6,5},{7,6},{8,7},{9,8},{10,9},{11,1... | collective-permute-start | bytes 786440 | tf_op jit(solution)/shard_map/ppermute | solution.py:21
  70.9 8.7 %collective-permute-start.9 = (f32[16,4,512]{2,0,1:T(8,128)S(1)}, f32[16,4,512]{2,0,1:T(8,128)S(1)}, u32[]{:S(2)}, u32[]{:S(2)}) collective-permute-start(f32[16,4,512]{2,0,1:T(8,128)S(1)} %get-tuple-element.64), channel_id=1, source_target_pairs={{2,0},{3,1},{4,2},{5,3},{6,4},{7,5},{8,6},{9,7},{10,8},{11,9},{12,... | collective-permute-start | bytes 393224 | tf_op jit(solution)/shard_map/ppermute | solution.py:21
  75.7 6.0 %copy-start.9 = (f32[16,8,512]{2,0,1:T(8,128)}, f32[16,8,512]{2,0,1:T(8,128)S(1)}, u32[]{:S(2)}) copy-start(f32[16,8,512]{2,0,1:T(8,128)S(1)} %collective-permute-done.6) | copy-start | bytes 786436
  75.8 5.9 %copy-start.11 = (f32[16,8,512]{2,0,1:T(8,128)}, f32[16,8,512]{2,0,1:T(8,128)S(1)}, u32[]{:S(2)}) copy-start(f32[16,8,512]{2,0,1:T(8,128)S(1)} %collective-permute-done.7) | copy-start | bytes 786436
  81.8 0.8 copy-start.6
  83.1 24.5 %collective-permute-start.12 = (f32[4,12,512]{2,0,1:T(4,128)S(1)}, f32[4,12,512]{2,0,1:T(4,128)S(1)}, u32[]{:S(2)}, u32[]{:S(2)}) collective-permute-start(f32[4,12,512]{2,0,1:T(4,128)S(1)} %get-tuple-element.75), channel_id=1, source_target_pairs={{0,192},{64,128},{128,64},{192,0},{256,448},{320,384},{384,320},{4... | collective-permute-start | bytes 294920 | tf_op jit(solution)/shard_map/ppermute | solution.py:56
  100.9 11.5 %collective-permute-start.11 = (f32[4,12,512]{2,0,1:T(4,128)S(1)}, f32[4,12,512]{2,0,1:T(4,128)S(1)}, u32[]{:S(2)}, u32[]{:S(2)}) collective-permute-start(f32[4,12,512]{2,0,1:T(4,128)S(1)} %get-tuple-element.75), channel_id=1, source_target_pairs={{0,128},{64,192},{128,0},{192,64},{256,384},{320,448},{384,256},{4... | collective-permute-start | bytes 294920 | tf_op jit(solution)/shard_map/ppermute | solution.py:56
  105.5 6.9 %collective-permute-start.10 = (f32[4,12,512]{2,0,1:T(4,128)S(1)}, f32[4,12,512]{2,0,1:T(4,128)S(1)}, u32[]{:S(2)}, u32[]{:S(2)}) collective-permute-start(f32[4,12,512]{2,0,1:T(4,128)S(1)} %get-tuple-element.75), channel_id=1, source_target_pairs={{0,64},{64,0},{128,192},{192,128},{256,320},{320,256},{384,448},{4... | collective-permute-start | bytes 294920 | tf_op jit(solution)/shard_map/ppermute | solution.py:56
  107.6 33.9 %copy-start.32 = (pred[12]{0:T(512)(128)(4,1)}, pred[12]{0:T(512)(128)(4,1)S(1)}, u32[]{:S(2)}) copy-start(pred[12]{0:T(512)(128)(4,1)S(1)} %compare_and_fusion.7) | copy-start | bytes 40
  112.7 23.4 %collective-permute-start.15 = (f32[16,12,512]{2,0,1:T(8,128)S(1)}, f32[16,12,512]{2,0,1:T(8,128)S(1)}, u32[]{:S(2)}, u32[]{:S(2)}) collective-permute-start(f32[16,12,512]{2,0,1:T(8,128)S(1)} %get-tuple-element.45), channel_id=1, source_target_pairs={{0,768},{64,832},{128,896},{192,960},{256,512},{320,576},{384,640}... | collective-permute-start | bytes 1179656 | tf_op jit(solution)/shard_map/ppermute | solution.py:56
  117.8 18.2 %collective-permute-start.14 = (f32[16,12,512]{2,0,1:T(8,128)S(1)}, f32[16,12,512]{2,0,1:T(8,128)S(1)}, u32[]{:S(2)}, u32[]{:S(2)}) collective-permute-start(f32[16,12,512]{2,0,1:T(8,128)S(1)} %get-tuple-element.45), channel_id=1, source_target_pairs={{0,512},{64,576},{128,640},{192,704},{256,768},{320,832},{384,896}... | collective-permute-start | bytes 1179656 | tf_op jit(solution)/shard_map/ppermute | solution.py:56
  122.4 16.8 %collective-permute-start.13 = (f32[16,12,512]{2,0,1:T(8,128)S(1)}, f32[16,12,512]{2,0,1:T(8,128)S(1)}, u32[]{:S(2)}, u32[]{:S(2)}) collective-permute-start(f32[16,12,512]{2,0,1:T(8,128)S(1)} %get-tuple-element.45), channel_id=1, source_target_pairs={{0,256},{64,320},{128,384},{192,448},{256,0},{320,64},{384,128},{4... | collective-permute-start | bytes 1179656 | tf_op jit(solution)/shard_map/ppermute | solution.py:56
  124.5 14.9 %copy-start.28 = (pred[10]{0:T(512)(128)(4,1)}, pred[10]{0:T(512)(128)(4,1)S(1)}, u32[]{:S(2)}) copy-start(pred[10]{0:T(512)(128)(4,1)S(1)} %compare_and_fusion.6) | copy-start | bytes 34
  142.4 0.9 copy-start.2
  146.7 6.3 %copy-start.8 = (f32[32,2,12,256]{3,1,0,2:T(2,128)S(1)}, f32[32,2,12,256]{3,1,0,2:T(2,128)}, u32[]{:S(2)}) copy-start(f32[32,2,12,256]{3,1,0,2:T(2,128)} %reshape.337) | copy-start | bytes 2359300
  152.9 2.1 copy-start.22
  153.0 6.0 %copy-start.37 = (pred[16]{0:T(512)(128)(4,1)S(1)}, pred[16]{0:T(512)(128)(4,1)}, u32[]{:S(2)}) copy-start(pred[16]{0:T(512)(128)(4,1)} %copy-done.36) | copy-start | bytes 52
  153.0 6.0 %copy-start.38 = (pred[16]{0:T(512)(128)(4,1)S(1)}, pred[16]{0:T(512)(128)(4,1)}, u32[]{:S(2)}) copy-start(pred[16]{0:T(512)(128)(4,1)} %slice.921) | copy-start | bytes 52
  154.9 17.2 %copy-start.23 = (f32[32,2,256]{2,0,1:T(8,128)S(1)}, f32[32,2,256]{2,0,1:T(8,128)}, u32[]{:S(2)}) copy-start(f32[32,2,256]{2,0,1:T(8,128)} %fusion.234) | copy-start | bytes 196612
  155.1 17.0 %collective-permute-start.16 = (f32[32,2,512]{2,0,1:T(8,128)S(1)}, f32[32,2,512]{2,0,1:T(8,128)S(1)}, u32[]{:S(2)}, u32[]{:S(2)}) collective-permute-start(f32[32,2,512]{2,0,1:T(8,128)S(1)} %pad_maximum_fusion.20), channel_id=1, source_target_pairs={{0,2},{1,3},{2,4},{3,5},{4,6},{5,7},{6,8},{7,9},{8,10},{9,11},{10,... | collective-permute-start | bytes 393224 | tf_op jit(solution)/shard_map/ppermute | solution.py:21
  157.0 15.1 %collective-permute-start.17 = (f32[32,2,512]{2,0,1:T(8,128)S(1)}, f32[32,2,512]{2,0,1:T(8,128)S(1)}, u32[]{:S(2)}, u32[]{:S(2)}) collective-permute-start(f32[32,2,512]{2,0,1:T(8,128)S(1)} %pad_maximum_fusion.20), channel_id=1, source_target_pairs={{0,1},{1,2},{2,3},{3,4},{4,5},{5,6},{6,7},{7,8},{8,9},{9,10},{10,1... | collective-permute-start | bytes 393224 | tf_op jit(solution)/shard_map/ppermute | solution.py:21
  159.7 12.5 %collective-permute-start.18 = (f32[32,2,512]{2,0,1:T(8,128)S(1)}, f32[32,2,512]{2,0,1:T(8,128)S(1)}, u32[]{:S(2)}, u32[]{:S(2)}) collective-permute-start(f32[32,2,512]{2,0,1:T(8,128)S(1)} %pad_maximum_fusion.20), channel_id=1, source_target_pairs={{1,0},{2,1},{3,2},{4,3},{5,4},{6,5},{7,6},{8,7},{9,8},{10,9},{11,1... | collective-permute-start | bytes 393224 | tf_op jit(solution)/shard_map/ppermute | solution.py:21
  165.7 10.6 %collective-permute-start.19 = (f32[32,2,512]{2,0,1:T(8,128)S(1)}, f32[32,2,512]{2,0,1:T(8,128)S(1)}, u32[]{:S(2)}, u32[]{:S(2)}) collective-permute-start(f32[32,2,512]{2,0,1:T(8,128)S(1)} %pad_maximum_fusion.20), channel_id=1, source_target_pairs={{2,0},{3,1},{4,2},{5,3},{6,4},{7,5},{8,6},{9,7},{10,8},{11,9},{12,... | collective-permute-start | bytes 393224 | tf_op jit(solution)/shard_map/ppermute | solution.py:21
  172.2 5.2 %copy-start.29 = (pred[10]{0:T(512)(128)(4,1)S(1)}, pred[10]{0:T(512)(128)(4,1)}, u32[]{:S(2)}) copy-start(pred[10]{0:T(512)(128)(4,1)} %copy-done.28) | copy-start | bytes 34
  179.7 16.0 %collective-permute-start.20 = (f32[32,2,256]{2,0,1:T(8,128)S(1)}, f32[32,2,256]{2,0,1:T(8,128)S(1)}, u32[]{:S(2)}, u32[]{:S(2)}) collective-permute-start(f32[32,2,256]{2,0,1:T(8,128)S(1)} %slice_select_fusion.3), channel_id=1, source_target_pairs={{0,2},{1,3},{2,4},{3,5},{4,6},{5,7},{6,8},{7,9},{8,10},{9,11},{10,... | collective-permute-start | bytes 196616 | tf_op jit(solution)/shard_map/ppermute | solution.py:21
  182.2 13.5 %collective-permute-start.21 = (f32[32,2,256]{2,0,1:T(8,128)S(1)}, f32[32,2,256]{2,0,1:T(8,128)S(1)}, u32[]{:S(2)}, u32[]{:S(2)}) collective-permute-start(f32[32,2,256]{2,0,1:T(8,128)S(1)} %slice_select_fusion.3), channel_id=1, source_target_pairs={{0,1},{1,2},{2,3},{3,4},{4,5},{5,6},{6,7},{7,8},{8,9},{9,10},{10,1... | collective-permute-start | bytes 196616 | tf_op jit(solution)/shard_map/ppermute | solution.py:21
  184.1 11.6 %collective-permute-start.22 = (f32[32,2,256]{2,0,1:T(8,128)S(1)}, f32[32,2,256]{2,0,1:T(8,128)S(1)}, u32[]{:S(2)}, u32[]{:S(2)}) collective-permute-start(f32[32,2,256]{2,0,1:T(8,128)S(1)} %slice_select_fusion.3), channel_id=1, source_target_pairs={{1,0},{2,1},{3,2},{4,3},{5,4},{6,5},{7,6},{8,7},{9,8},{10,9},{11,1... | collective-permute-start | bytes 196616 | tf_op jit(solution)/shard_map/ppermute | solution.py:21
  190.1 7.5 %collective-permute-start.23 = (f32[32,2,256]{2,0,1:T(8,128)S(1)}, f32[32,2,256]{2,0,1:T(8,128)S(1)}, u32[]{:S(2)}, u32[]{:S(2)}) collective-permute-start(f32[32,2,256]{2,0,1:T(8,128)S(1)} %slice_select_fusion.3), channel_id=1, source_target_pairs={{2,0},{3,1},{4,2},{5,3},{6,4},{7,5},{8,6},{9,7},{10,8},{11,9},{12,... | collective-permute-start | bytes 196616 | tf_op jit(solution)/shard_map/ppermute | solution.py:21
  198.0 0.9 copy-start.24
  198.7 3.2 %copy-start.3 = (f32[64,12,256]{2,0,1:T(8,128)S(1)}, f32[64,12,256]{2,0,1:T(8,128)}, u32[]{:S(2)}) copy-start(f32[64,12,256]{2,0,1:T(8,128)} %copy-done.2) | copy-start | bytes 2359300
  199.0 4.0 %copy-start.33 = (pred[12]{0:T(512)(128)(4,1)S(1)}, pred[12]{0:T(512)(128)(4,1)}, u32[]{:S(2)}) copy-start(pred[12]{0:T(512)(128)(4,1)} %copy-done.32) | copy-start | bytes 40
  203.0 0.9 copy-start.34
  204.0 9.1 %copy-start.27 = (s32[16,16]{0,1:T(8,128)S(1)}, s32[16,16]{0,1:T(8,128)}, u32[]{:S(2)}) copy-start(s32[16,16]{0,1:T(8,128)} %iota_add_fusion.5) | copy-start | bytes 3076
  204.9 10.9 %copy-start.7 = (f32[16,32,256]{2,0,1:T(8,128)S(1)}, f32[16,32,256]{2,0,1:T(8,128)}, u32[]{:S(2)}) copy-start(f32[16,32,256]{2,0,1:T(8,128)} %copy-done.6) | copy-start | bytes 1572868
  204.9 10.9 %copy-start.10 = (f32[16,8,512]{2,0,1:T(8,128)S(1)}, f32[16,8,512]{2,0,1:T(8,128)}, u32[]{:S(2)}) copy-start(f32[16,8,512]{2,0,1:T(8,128)} %copy-done.9) | copy-start | bytes 786436
  204.9 10.9 %copy-start.12 = (f32[16,8,512]{2,0,1:T(8,128)S(1)}, f32[16,8,512]{2,0,1:T(8,128)}, u32[]{:S(2)}) copy-start(f32[16,8,512]{2,0,1:T(8,128)} %copy-done.11) | copy-start | bytes 786436
  204.9 10.9 %copy-start.14 = (f32[8,8,256]{2,0,1:T(8,128)S(1)}, f32[8,8,256]{2,0,1:T(8,128)}, u32[]{:S(2)}) copy-start(f32[8,8,256]{2,0,1:T(8,128)} %copy-done.13) | copy-start | bytes 196612
  205.0 10.9 %copy-start.16 = (f32[8,8,256]{2,0,1:T(8,128)S(1)}, f32[8,8,256]{2,0,1:T(8,128)}, u32[]{:S(2)}) copy-start(f32[8,8,256]{2,0,1:T(8,128)} %copy-done.15) | copy-start | bytes 196612
  205.0 10.9 %copy-start.17 = (f32[16,32,256]{2,0,1:T(8,128)S(1)}, f32[16,32,256]{2,0,1:T(8,128)}, u32[]{:S(2)}) copy-start(f32[16,32,256]{2,0,1:T(8,128)} %get-tuple-element.23) | copy-start | bytes 1572868
  205.0 10.9 %copy-start.19 = (f32[4,8,512]{2,0,1:T(4,128)S(1)}, f32[4,8,512]{2,0,1:T(4,128)}, u32[]{:S(2)}) copy-start(f32[4,8,512]{2,0,1:T(4,128)} %copy-done.18) | copy-start | bytes 196612
  205.0 10.9 %copy-start.21 = (f32[4,8,512]{2,0,1:T(4,128)S(1)}, f32[4,8,512]{2,0,1:T(4,128)}, u32[]{:S(2)}) copy-start(f32[4,8,512]{2,0,1:T(4,128)} %copy-done.20) | copy-start | bytes 196612
  205.0 10.9 %copy-start.31 = (pred[16,16]{0,1:T(8,128)(4,1)S(1)}, pred[16,16]{0,1:T(8,128)(4,1)}, u32[]{:S(2)}) copy-start(pred[16,16]{0,1:T(8,128)(4,1)} %copy-done.30) | copy-start | bytes 772
  205.0 9.1 %collective-permute-start.24 = (f32[64,2,256]{2,0,1:T(8,128)S(1)}, f32[64,2,256]{2,0,1:T(8,128)S(1)}, u32[]{:S(2)}, u32[]{:S(2)}) collective-permute-start(f32[64,2,256]{2,0,1:T(8,128)S(1)} %get-tuple-element.28), channel_id=1, source_target_pairs={{0,1},{1,2},{2,3},{3,4},{4,5},{5,6},{6,7},{7,8},{8,9},{9,10},{10,1... | collective-permute-start | bytes 393224 | tf_op jit(solution)/shard_map/ppermute | solution.py:21
  207.1 8.5 %collective-permute-start.25 = (f32[64,2,256]{2,0,1:T(8,128)S(1)}, f32[64,2,256]{2,0,1:T(8,128)S(1)}, u32[]{:S(2)}, u32[]{:S(2)}) collective-permute-start(f32[64,2,256]{2,0,1:T(8,128)S(1)} %get-tuple-element.27), channel_id=1, source_target_pairs={{1,0},{2,1},{3,2},{4,3},{5,4},{6,5},{7,6},{8,7},{9,8},{10,9},{11,1... | collective-permute-start | bytes 393224 | tf_op jit(solution)/shard_map/ppermute | solution.py:21
  215.9 0.7 copy-start.35
  216.8 0.9 copy-start.5
  217.2 0.7 copy-start.26
  (1 other events, 0.6 us)

commit v7 on v5

--- a/solution.py
+++ b/solution.py
@@ -124,20 +124,14 @@
 
 def restrict(values, width_x, width_y, span_x, span_y):
     rows = values[width_x - 1:width_x + span_x]
-    before = rows[:-1].reshape(span_x // 2, 2, *rows.shape[1:])[:, 0]
-    paired = rows[1:].reshape(span_x // 2, 2, *rows.shape[1:])
-    across = 0.25 * before + 0.5 * paired[:, 0] + 0.25 * paired[:, 1]
+    across = 0.25 * rows[0:-1:2] + 0.5 * rows[1::2] + 0.25 * rows[2::2]
     cols = across[:, width_y - 1:width_y + span_y]
-    before = cols[:, :-1].reshape(cols.shape[0], span_y // 2, 2, cols.shape[2])[:, :, 0]
-    paired = cols[:, 1:].reshape(cols.shape[0], span_y // 2, 2, cols.shape[2])
-    return 0.25 * before + 0.5 * paired[:, :, 0] + 0.25 * paired[:, :, 1]
+    return 0.25 * cols[:, 0:-1:2] + 0.5 * cols[:, 1::2] + 0.25 * cols[:, 2::2]
 
 
 def coarsen(values):
-    paired = values.reshape(values.shape[0] // 2, 2, values.shape[1], values.shape[2])
-    across = 0.5 * (paired[:, 0] + paired[:, 1])
-    paired = across.reshape(across.shape[0], across.shape[1] // 2, 2, across.shape[2])
-    return 0.5 * (paired[:, :, 0] + paired[:, :, 1])
+    across = 0.5 * (values[0::2] + values[1::2])
+    return 0.5 * (across[:, 0::2] + across[:, 1::2])
 
 
 def lift(coarse):

time: 214 us -> 214 us (level)
  local copies, waits for them, and re-layouts: 13.5 us -> 16.8 us
    slice x13 -> x18, local copies, waits for them, and re-layouts: 1.31 us -> 7.17 us  [the longest x5 6.82 us: restrict(): across = 0.25 * rows[0:-1:2] + 0.5 * rows[1::2] + 0.25 * rows[2::2]]
    reshape x3 -> x0, local copies, waits for them, and re-layouts: 4.08 us -> none  [the longest x1 2.57 us: restrict(): before = rows[:-1].reshape(span_x // 2, 2, *rows.shape[1:])[:, 0]]
  transfers between devices with their start and end apart: 26 -> 26, of which waited for: 16 -> 16; matrix products, arithmetic and copies ran while one was open for 1% -> 2% of each run, Pallas kernels for 0% -> 0%
where the time goes in v7:
time: 214 us; the launch traced here: 212 us
  starting transfers between devices  121 us (57%)
  waiting for transfers between devices  44.1 us (21%)
  other arithmetic  26.1 us (12%)
  local copies, waits for them, and re-layouts  16.8 us (8%)
  Pallas kernels  2.55 us (1%)
    ppermute x20, starting transfers between devices, shifted(): return lax.ppermute(block, axis, route)  91.4 us
    ppermute x20, waiting for transfers between devices, shifted(): return lax.ppermute(block, axis, route)  32.3 us
    ppermute x6, starting transfers between devices, gather_x(): lax.ppermute(block, 'gx', [(i, i ^ m * group) for i in range(count)])  30.1 us
    select_n x18, other arithmetic, half_sweep(): return jnp.where(update, renewed, iterate)  14.8 us
    ppermute x6, waiting for transfers between devices, gather_x(): lax.ppermute(block, 'gx', [(i, i ^ m * group) for i in range(count)])  11.8 us
    slice x5, local copies, waits for them, and re-layouts, restrict(): across = 0.25 * rows[0:-1:2] + 0.5 * rows[1::2] + 0.25 * rows[2::2]  6.82 us
  transfers between devices with their start and end apart: 26, of which 16 were waited for; matrix products, arithmetic and copies ran while one was open for 2% of the time, Pallas kernels for 0%

profile of v7, /device:TPU:8, one launch (start us, length us, event | category | flops | bytes accessed | tf_op | source)
XLA Modules:
  0.0 212.3 jit_solution(15743634226716227974)
XLA Ops:
  0.0 2.6 %shard_map.46 = f32[16,16,1024]{2,1,0:T(8,128)} custom-call(f32[16]{0:T(128)} %volts_ref.1, f32[16,16,256]{2,1,0:T(8,128)} %potential_ref.1, f32[16,16,256]{2,1,0:T(8,128)} %charge_ref.1, s32[16,16,256]{2,1,0:T(8,128)} %region_ref.1), custom_call_target="tpu_custom_call" | custom-call | tf_op jit(solution)/shard_map/pallas_call | solution.py:212
  2.6 1.2 fusion.219
  3.7 1.8 collective-permute-start
  5.5 1.3 collective-permute-start.1
  6.9 6.7 %collective-permute-done.1 = f32[4,16,1024]{2,1,0:T(8,128)S(1)} collective-permute-done((f32[4,16,1024]{2,1,0:T(8,128)S(1)}, f32[4,16,1024]{2,1,0:T(8,128)S(1)}, u32[]{:S(2)}, u32[]{:S(2)}) %collective-permute-start.1) | collective-permute-done | bytes 262176 | tf_op jit(solution)/shard_map/ppermute | solution.py:20
  13.8 4.3 %collective-permute-start.2 = (f32[24,4,1024]{2,1,0:T(4,128)S(1)}, f32[24,4,1024]{2,1,0:T(4,128)S(1)}, u32[]{:S(2)}, u32[]{:S(2)}) collective-permute-start(f32[24,4,1024]{2,1,0:T(4,128)S(1)} %get-tuple-element.14), channel_id=1, source_target_pairs={{0,1},{1,2},{2,3},{3,4},{4,5},{5,6},{6,7},{7,8},{8,9},{9,10},{10,1... | collective-permute-start | bytes 1179656 | tf_op jit(solution)/shard_map/ppermute | solution.py:20
  18.1 16.6 %collective-permute-start.3 = (f32[24,4,1024]{2,1,0:T(4,128)S(1)}, f32[24,4,1024]{2,1,0:T(4,128)S(1)}, u32[]{:S(2)}, u32[]{:S(2)}) collective-permute-start(f32[24,4,1024]{2,1,0:T(4,128)S(1)} %get-tuple-element.15), channel_id=1, source_target_pairs={{1,0},{2,1},{3,2},{4,3},{5,4},{6,5},{7,6},{8,7},{9,8},{10,9},{11,1... | collective-permute-start | bytes 1179656 | tf_op jit(solution)/shard_map/ppermute | solution.py:20
  34.8 3.7 %collective-permute-done.2 = f32[24,4,1024]{2,1,0:T(4,128)S(1)} collective-permute-done((f32[24,4,1024]{2,1,0:T(4,128)S(1)}, f32[24,4,1024]{2,1,0:T(4,128)S(1)}, u32[]{:S(2)}, u32[]{:S(2)}) %collective-permute-start.2) | collective-permute-done | bytes 393248 | tf_op jit(solution)/shard_map/ppermute | solution.py:20
  38.5 1.5 collective-permute-done.3
  40.6 1.6 fusion.58
  42.1 1.4 fusion.62
  45.2 10.9 %collective-permute-start.4 = (f32[4,8,512]{2,1,0:T(8,128)S(1)}, f32[4,8,512]{2,1,0:T(8,128)S(1)}, u32[]{:S(2)}, u32[]{:S(2)}) collective-permute-start(f32[4,8,512]{2,1,0:T(8,128)S(1)} %get-tuple-element.70), channel_id=1, source_target_pairs={{0,64},{64,128},{128,192},{192,256},{256,320},{320,384},{384,448},... | collective-permute-start | bytes 196616 | tf_op jit(solution)/shard_map/ppermute | solution.py:20
  56.1 1.3 collective-permute-start.5
  57.5 1.9 collective-permute-done.5
  59.4 1.9 collective-permute-start.6
  61.4 6.5 %collective-permute-start.7 = (f32[16,4,512]{2,1,0:T(4,128)S(1)}, f32[16,4,512]{2,1,0:T(4,128)S(1)}, u32[]{:S(2)}, u32[]{:S(2)}) collective-permute-start(f32[16,4,512]{2,1,0:T(4,128)S(1)} %get-tuple-element.60), channel_id=1, source_target_pairs={{1,0},{2,1},{3,2},{4,3},{5,4},{6,5},{7,6},{8,7},{9,8},{10,9},{11,1... | collective-permute-start | bytes 393224 | tf_op jit(solution)/shard_map/ppermute | solution.py:20
  67.9 1.7 collective-permute-done.6
  69.6 0.8 collective-permute-done.7
  72.2 8.4 %collective-permute-start.8 = (f32[4,4,512]{2,1,0:T(4,128)S(1)}, f32[4,4,512]{2,1,0:T(4,128)S(1)}, u32[]{:S(2)}, u32[]{:S(2)}) collective-permute-start(f32[4,4,512]{2,1,0:T(4,128)S(1)} %get-tuple-element.73), channel_id=1, source_target_pairs={{0,64},{64,0},{128,192},{192,128},{256,320},{320,256},{384,448},{4... | collective-permute-start | bytes 98312 | tf_op jit(solution)/shard_map/ppermute | solution.py:55
  80.6 10.2 %collective-permute-start.9 = (f32[4,4,512]{2,1,0:T(4,128)S(1)}, f32[4,4,512]{2,1,0:T(4,128)S(1)}, u32[]{:S(2)}, u32[]{:S(2)}) collective-permute-start(f32[4,4,512]{2,1,0:T(4,128)S(1)} %get-tuple-element.73), channel_id=1, source_target_pairs={{0,128},{64,192},{128,0},{192,64},{256,384},{320,448},{384,256},{4... | collective-permute-start | bytes 98312 | tf_op jit(solution)/shard_map/ppermute | solution.py:55
  90.8 1.9 collective-permute-start.10
  93.0 7.2 %collective-permute-done.10 = f32[4,4,512]{2,1,0:T(4,128)S(1)} collective-permute-done((f32[4,4,512]{2,1,0:T(4,128)S(1)}, f32[4,4,512]{2,1,0:T(4,128)S(1)}, u32[]{:S(2)}, u32[]{:S(2)}) %collective-permute-start.10) | collective-permute-done | bytes 32800 | tf_op jit(solution)/shard_map/ppermute | solution.py:55
  100.3 1.9 collective-permute-start.12
  102.2 5.8 %collective-permute-start.13 = (f32[16,4,512]{2,1,0:T(4,128)S(1)}, f32[16,4,512]{2,1,0:T(4,128)S(1)}, u32[]{:S(2)}, u32[]{:S(2)}) collective-permute-start(f32[16,4,512]{2,1,0:T(4,128)S(1)} %get-tuple-element.65), channel_id=1, source_target_pairs={{0,768},{64,832},{128,896},{192,960},{256,512},{320,576},{384,640}... | collective-permute-start | bytes 393224 | tf_op jit(solution)/shard_map/ppermute | solution.py:55
  108.0 1.9 collective-permute-start.11
  109.9 0.6 compare_and_fusion.9
  110.5 1.4 collective-permute-done.13
  111.9 2.9 %collective-permute-done.11 = f32[16,4,512]{2,1,0:T(4,128)S(1)} collective-permute-done((f32[16,4,512]{2,1,0:T(4,128)S(1)}, f32[16,4,512]{2,1,0:T(4,128)S(1)}, u32[]{:S(2)}, u32[]{:S(2)}) %collective-permute-start.11) | collective-permute-done | bytes 131104 | tf_op jit(solution)/shard_map/ppermute | solution.py:55
  115.3 1.9 collective-permute-start.14
  117.2 6.2 %collective-permute-start.15 = (f32[64,4,512]{2,0,1:T(8,128)S(1)}, f32[64,4,512]{2,0,1:T(8,128)}, u32[]{:S(2)}, u32[]{:S(2)}) collective-permute-start(f32[64,4,512]{2,0,1:T(8,128)S(1)} %pad_maximum_fusion.4), channel_id=1, source_target_pairs={{1,0},{2,1},{3,2},{4,3},{5,4},{6,5},{7,6},{8,7},{9,8},{10,9},{11,1... | collective-permute-start | bytes 1572872 | tf_op jit(solution)/shard_map/ppermute | solution.py:20
  124.1 7.7 %collective-permute-done.14 = f32[64,4,512]{2,0,1:T(8,128)S(1)} collective-permute-done((f32[64,4,512]{2,0,1:T(8,128)S(1)}, f32[64,4,512]{2,0,1:T(8,128)S(1)}, u32[]{:S(2)}, u32[]{:S(2)}) %collective-permute-start.14) | collective-permute-done | bytes 524320 | tf_op jit(solution)/shard_map/ppermute | solution.py:20
  131.9 0.8 copy-done.19
  133.1 1.4 pad_maximum_fusion.1
  134.5 0.9 fusion.40
  135.4 0.9 fusion.8
  137.2 1.0 pad.180
  138.2 2.0 slice.754
  140.2 2.0 slice.755
  142.2 2.8 %slice.756 = f32[32,12,256]{2,0,1:T(8,128)} slice(f32[65,12,256]{2,0,1:T(8,128)} %pad.180), slice={[2:65:2], [0:12:1], [0:256:1]} | slice | bytes 786432 | tf_op jit(solution)/shard_map/slice | solution.py:127
  145.0 1.0 fusion.195
  146.0 1.9 collective-permute-start.16
  147.9 2.4 %collective-permute-start.17 = (f32[32,2,512]{2,0,1:T(8,128)S(1)}, f32[32,2,512]{2,0,1:T(8,128)S(1)}, u32[]{:S(2)}, u32[]{:S(2)}) collective-permute-start(f32[32,2,512]{2,0,1:T(8,128)S(1)} %pad_maximum_fusion.11), channel_id=1, source_target_pairs={{0,1},{1,2},{2,3},{3,4},{4,5},{5,6},{6,7},{7,8},{8,9},{9,10},{10,1... | collective-permute-start | bytes 393224 | tf_op jit(solution)/shard_map/ppermute | solution.py:20
  150.3 1.5 compare_and_fusion.5
  151.8 6.1 %collective-permute-start.18 = (f32[32,2,512]{2,0,1:T(8,128)S(1)}, f32[32,2,512]{2,0,1:T(8,128)S(1)}, u32[]{:S(2)}, u32[]{:S(2)}) collective-permute-start(f32[32,2,512]{2,0,1:T(8,128)S(1)} %pad_maximum_fusion.11), channel_id=1, source_target_pairs={{1,0},{2,1},{3,2},{4,3},{5,4},{6,5},{7,6},{8,7},{9,8},{10,9},{11,1... | collective-permute-start | bytes 393224 | tf_op jit(solution)/shard_map/ppermute | solution.py:20
  158.0 5.0 %collective-permute-start.19 = (f32[32,2,512]{2,0,1:T(8,128)S(1)}, f32[32,2,512]{2,0,1:T(8,128)S(1)}, u32[]{:S(2)}, u32[]{:S(2)}) collective-permute-start(f32[32,2,512]{2,0,1:T(8,128)S(1)} %pad_maximum_fusion.11), channel_id=1, source_target_pairs={{2,0},{3,1},{4,2},{5,3},{6,4},{7,5},{8,6},{9,7},{10,8},{11,9},{12,... | collective-permute-start | bytes 393224 | tf_op jit(solution)/shard_map/ppermute | solution.py:20
  163.1 3.6 %collective-permute-done.19 = f32[32,2,512]{2,0,1:T(8,128)S(1)} collective-permute-done((f32[32,2,512]{2,0,1:T(8,128)S(1)}, f32[32,2,512]{2,0,1:T(8,128)S(1)}, u32[]{:S(2)}, u32[]{:S(2)}) %collective-permute-start.19) | collective-permute-done | bytes 131104 | tf_op jit(solution)/shard_map/ppermute | solution.py:20
  168.8 1.9 collective-permute-start.20
  170.7 3.1 %collective-permute-start.21 = (f32[32,2,256]{2,0,1:T(8,128)S(1)}, f32[32,2,256]{2,0,1:T(8,128)S(1)}, u32[]{:S(2)}, u32[]{:S(2)}) collective-permute-start(f32[32,2,256]{2,0,1:T(8,128)S(1)} %slice_select_fusion.3), channel_id=1, source_target_pairs={{0,1},{1,2},{2,3},{3,4},{4,5},{5,6},{6,7},{7,8},{8,9},{9,10},{10,1... | collective-permute-start | bytes 196616 | tf_op jit(solution)/shard_map/ppermute | solution.py:20
  173.8 4.9 %collective-permute-start.22 = (f32[32,2,256]{2,0,1:T(8,128)S(1)}, f32[32,2,256]{2,0,1:T(8,128)S(1)}, u32[]{:S(2)}, u32[]{:S(2)}) collective-permute-start(f32[32,2,256]{2,0,1:T(8,128)S(1)} %slice_select_fusion.3), channel_id=1, source_target_pairs={{1,0},{2,1},{3,2},{4,3},{5,4},{6,5},{7,6},{8,7},{9,8},{10,9},{11,1... | collective-permute-start | bytes 196616 | tf_op jit(solution)/shard_map/ppermute | solution.py:20
  178.7 5.3 %collective-permute-start.23 = (f32[32,2,256]{2,0,1:T(8,128)S(1)}, f32[32,2,256]{2,0,1:T(8,128)S(1)}, u32[]{:S(2)}, u32[]{:S(2)}) collective-permute-start(f32[32,2,256]{2,0,1:T(8,128)S(1)} %slice_select_fusion.3), channel_id=1, source_target_pairs={{2,0},{3,1},{4,2},{5,3},{6,4},{7,5},{8,6},{9,7},{10,8},{11,9},{12,... | collective-permute-start | bytes 196616 | tf_op jit(solution)/shard_map/ppermute | solution.py:20
  184.0 2.1 collective-permute-done.23
  186.2 1.0 fusion.107
  187.2 1.1 fusion.111
  188.7 0.9 broadcast_in_dim.36
  189.6 2.0 reshape.169
  191.6 1.1 bitcast_add_fusion
  192.7 0.9 fusion.24
  193.6 0.9 fusion.32
  194.6 2.1 collective-permute-start.24
  196.7 6.0 %collective-permute-start.25 = (f32[64,2,256]{2,0,1:T(8,128)S(1)}, f32[64,2,256]{2,0,1:T(8,128)S(1)}, u32[]{:S(2)}, u32[]{:S(2)}) collective-permute-start(f32[64,2,256]{2,0,1:T(8,128)S(1)} %get-tuple-element.18), channel_id=1, source_target_pairs={{1,0},{2,1},{3,2},{4,3},{5,4},{6,5},{7,6},{8,7},{9,8},{10,9},{11,1... | collective-permute-start | bytes 393224 | tf_op jit(solution)/shard_map/ppermute | solution.py:20
  203.0 0.7 collective-permute-done.24
  203.7 1.5 collective-permute-done.25
  208.0 1.8 fusion.66
  210.3 2.0 slice_select_fusion
  (172 shorter events, 12.9 us)
Async XLA Ops:
  2.6 11.1 %copy-start.1 = (f32[16,16,1024]{2,1,0:T(8,128)S(1)}, f32[16,16,1024]{2,1,0:T(8,128)}, u32[]{:S(2)}) copy-start(f32[16,16,1024]{2,1,0:T(8,128)} %shard_map.46) | copy-start | bytes 3145732
  3.7 3.2 %collective-permute-start = (f32[4,16,1024]{2,1,0:T(8,128)S(1)}, f32[4,16,1024]{2,1,0:T(8,128)S(1)}, u32[]{:S(2)}, u32[]{:S(2)}) collective-permute-start(f32[4,16,1024]{2,1,0:T(8,128)S(1)} %get-tuple-element.16), channel_id=1, source_target_pairs={{0,64},{64,128},{128,192},{192,256},{256,320},{320,384},{384,448},... | collective-permute-start | bytes 786440 | tf_op jit(solution)/shard_map/ppermute | solution.py:20
  5.5 8.1 %collective-permute-start.1 = (f32[4,16,1024]{2,1,0:T(8,128)S(1)}, f32[4,16,1024]{2,1,0:T(8,128)S(1)}, u32[]{:S(2)}, u32[]{:S(2)}) collective-permute-start(f32[4,16,1024]{2,1,0:T(8,128)S(1)} %get-tuple-element.17), channel_id=1, source_target_pairs={{64,0},{128,64},{192,128},{256,192},{320,256},{384,320},{448,384},... | collective-permute-start | bytes 786440 | tf_op jit(solution)/shard_map/ppermute | solution.py:20
  6.9 64.0 %copy-start.25 = (pred[16,16]{1,0:T(8,128)(4,1)}, pred[16,16]{1,0:T(8,128)(4,1)S(1)}, u32[]{:S(2)}) copy-start(pred[16,16]{1,0:T(8,128)(4,1)S(1)} %broadcast_and_fusion.1) | copy-start | bytes 772
  6.9 64.0 %copy-start.21 = (s32[16,16]{1,0:T(8,128)}, s32[16,16]{1,0:T(8,128)S(1)}, u32[]{:S(2)}) copy-start(s32[16,16]{1,0:T(8,128)S(1)} %iota_add_fusion.4) | copy-start | bytes 3076
  13.8 24.8 %collective-permute-start.2 = (f32[24,4,1024]{2,1,0:T(4,128)S(1)}, f32[24,4,1024]{2,1,0:T(4,128)S(1)}, u32[]{:S(2)}, u32[]{:S(2)}) collective-permute-start(f32[24,4,1024]{2,1,0:T(4,128)S(1)} %get-tuple-element.14), channel_id=1, source_target_pairs={{0,1},{1,2},{2,3},{3,4},{4,5},{5,6},{6,7},{7,8},{8,9},{9,10},{10,1... | collective-permute-start | bytes 1179656 | tf_op jit(solution)/shard_map/ppermute | solution.py:20
  18.1 21.9 %collective-permute-start.3 = (f32[24,4,1024]{2,1,0:T(4,128)S(1)}, f32[24,4,1024]{2,1,0:T(4,128)S(1)}, u32[]{:S(2)}, u32[]{:S(2)}) collective-permute-start(f32[24,4,1024]{2,1,0:T(4,128)S(1)} %get-tuple-element.15), channel_id=1, source_target_pairs={{1,0},{2,1},{3,2},{4,3},{5,4},{6,5},{7,6},{8,7},{9,8},{10,9},{11,1... | collective-permute-start | bytes 1179656 | tf_op jit(solution)/shard_map/ppermute | solution.py:20
  34.7 7.4 %copy-start.23 = (s32[24,24]{1,0:T(8,128)}, s32[24,24]{1,0:T(8,128)S(1)}, u32[]{:S(2)}) copy-start(s32[24,24]{1,0:T(8,128)S(1)} %iota_add_fusion.1) | copy-start | bytes 6916
  40.5 1.7 copy-start
  42.1 2.0 copy-start.8
  43.6 0.8 copy-start.2
  43.6 1.0 copy-start.10
  45.2 12.3 %collective-permute-start.4 = (f32[4,8,512]{2,1,0:T(8,128)S(1)}, f32[4,8,512]{2,1,0:T(8,128)S(1)}, u32[]{:S(2)}, u32[]{:S(2)}) collective-permute-start(f32[4,8,512]{2,1,0:T(8,128)S(1)} %get-tuple-element.70), channel_id=1, source_target_pairs={{0,64},{64,128},{128,192},{192,256},{256,320},{320,384},{384,448},... | collective-permute-start | bytes 196616 | tf_op jit(solution)/shard_map/ppermute | solution.py:20
  56.1 3.2 %collective-permute-start.5 = (f32[4,8,512]{2,1,0:T(8,128)S(1)}, f32[4,8,512]{2,1,0:T(8,128)S(1)}, u32[]{:S(2)}, u32[]{:S(2)}) collective-permute-start(f32[4,8,512]{2,1,0:T(8,128)S(1)} %get-tuple-element.71), channel_id=1, source_target_pairs={{64,0},{128,64},{192,128},{256,192},{320,256},{384,320},{448,384},... | collective-permute-start | bytes 196616 | tf_op jit(solution)/shard_map/ppermute | solution.py:20
  59.4 10.1 %collective-permute-start.6 = (f32[16,4,512]{2,1,0:T(4,128)S(1)}, f32[16,4,512]{2,1,0:T(4,128)S(1)}, u32[]{:S(2)}, u32[]{:S(2)}) collective-permute-start(f32[16,4,512]{2,1,0:T(4,128)S(1)} %get-tuple-element.59), channel_id=1, source_target_pairs={{0,1},{1,2},{2,3},{3,4},{4,5},{5,6},{6,7},{7,8},{8,9},{9,10},{10,1... | collective-permute-start | bytes 393224 | tf_op jit(solution)/shard_map/ppermute | solution.py:20
  61.4 9.0 %collective-permute-start.7 = (f32[16,4,512]{2,1,0:T(4,128)S(1)}, f32[16,4,512]{2,1,0:T(4,128)S(1)}, u32[]{:S(2)}, u32[]{:S(2)}) collective-permute-start(f32[16,4,512]{2,1,0:T(4,128)S(1)} %get-tuple-element.60), channel_id=1, source_target_pairs={{1,0},{2,1},{3,2},{4,3},{5,4},{6,5},{7,6},{8,7},{9,8},{10,9},{11,1... | collective-permute-start | bytes 393224 | tf_op jit(solution)/shard_map/ppermute | solution.py:20
  70.8 1.2 copy-start.11
  70.9 1.2 copy-start.13
  71.2 0.7 copy-start.6
  72.2 20.6 %collective-permute-start.8 = (f32[4,4,512]{2,1,0:T(4,128)S(1)}, f32[4,4,512]{2,1,0:T(4,128)S(1)}, u32[]{:S(2)}, u32[]{:S(2)}) collective-permute-start(f32[4,4,512]{2,1,0:T(4,128)S(1)} %get-tuple-element.73), channel_id=1, source_target_pairs={{0,64},{64,0},{128,192},{192,128},{256,320},{320,256},{384,448},{4... | collective-permute-start | bytes 98312 | tf_op jit(solution)/shard_map/ppermute | solution.py:55
  80.6 12.4 %collective-permute-start.9 = (f32[4,4,512]{2,1,0:T(4,128)S(1)}, f32[4,4,512]{2,1,0:T(4,128)S(1)}, u32[]{:S(2)}, u32[]{:S(2)}) collective-permute-start(f32[4,4,512]{2,1,0:T(4,128)S(1)} %get-tuple-element.73), channel_id=1, source_target_pairs={{0,128},{64,192},{128,0},{192,64},{256,384},{320,448},{384,256},{4... | collective-permute-start | bytes 98312 | tf_op jit(solution)/shard_map/ppermute | solution.py:55
  90.8 9.4 %collective-permute-start.10 = (f32[4,4,512]{2,1,0:T(4,128)S(1)}, f32[4,4,512]{2,1,0:T(4,128)S(1)}, u32[]{:S(2)}, u32[]{:S(2)}) collective-permute-start(f32[4,4,512]{2,1,0:T(4,128)S(1)} %get-tuple-element.73), channel_id=1, source_target_pairs={{0,192},{64,128},{128,64},{192,0},{256,448},{320,384},{384,320},{4... | collective-permute-start | bytes 98312 | tf_op jit(solution)/shard_map/ppermute | solution.py:55
  100.3 10.2 %collective-permute-start.12 = (f32[16,4,512]{2,1,0:T(4,128)S(1)}, f32[16,4,512]{2,1,0:T(4,128)S(1)}, u32[]{:S(2)}, u32[]{:S(2)}) collective-permute-start(f32[16,4,512]{2,1,0:T(4,128)S(1)} %get-tuple-element.65), channel_id=1, source_target_pairs={{0,512},{64,576},{128,640},{192,704},{256,768},{320,832},{384,896}... | collective-permute-start | bytes 393224 | tf_op jit(solution)/shard_map/ppermute | solution.py:55
  102.2 9.7 %collective-permute-start.13 = (f32[16,4,512]{2,1,0:T(4,128)S(1)}, f32[16,4,512]{2,1,0:T(4,128)S(1)}, u32[]{:S(2)}, u32[]{:S(2)}) collective-permute-start(f32[16,4,512]{2,1,0:T(4,128)S(1)} %get-tuple-element.65), channel_id=1, source_target_pairs={{0,768},{64,832},{128,896},{192,960},{256,512},{320,576},{384,640}... | collective-permute-start | bytes 393224 | tf_op jit(solution)/shard_map/ppermute | solution.py:55
  108.0 6.9 %collective-permute-start.11 = (f32[16,4,512]{2,1,0:T(4,128)S(1)}, f32[16,4,512]{2,1,0:T(4,128)S(1)}, u32[]{:S(2)}, u32[]{:S(2)}) collective-permute-start(f32[16,4,512]{2,1,0:T(4,128)S(1)} %get-tuple-element.65), channel_id=1, source_target_pairs={{0,256},{64,320},{128,384},{192,448},{256,0},{320,64},{384,128},{4... | collective-permute-start | bytes 393224 | tf_op jit(solution)/shard_map/ppermute | solution.py:55
  115.3 16.6 %collective-permute-start.14 = (f32[64,4,512]{2,0,1:T(8,128)S(1)}, f32[64,4,512]{2,0,1:T(8,128)S(1)}, u32[]{:S(2)}, u32[]{:S(2)}) collective-permute-start(f32[64,4,512]{2,0,1:T(8,128)S(1)} %pad_maximum_fusion.4), channel_id=1, source_target_pairs={{0,1},{1,2},{2,3},{3,4},{4,5},{5,6},{6,7},{7,8},{8,9},{9,10},{10,1... | collective-permute-start | bytes 1572872 | tf_op jit(solution)/shard_map/ppermute | solution.py:20
  117.2 15.8 %collective-permute-start.15 = (f32[64,4,512]{2,0,1:T(8,128)S(1)}, f32[64,4,512]{2,0,1:T(8,128)}, u32[]{:S(2)}, u32[]{:S(2)}) collective-permute-start(f32[64,4,512]{2,0,1:T(8,128)S(1)} %pad_maximum_fusion.4), channel_id=1, source_target_pairs={{1,0},{2,1},{3,2},{4,3},{5,4},{6,5},{7,6},{8,7},{9,8},{10,9},{11,1... | collective-permute-start | bytes 1572872 | tf_op jit(solution)/shard_map/ppermute | solution.py:20
  124.1 10.4 %copy-start.28 = (pred[12]{0:T(512)(128)(4,1)S(1)}, pred[12]{0:T(512)(128)(4,1)}, u32[]{:S(2)}) copy-start(pred[12]{0:T(512)(128)(4,1)} %compare_and_fusion.9) | copy-start | bytes 40
  131.9 0.8 copy-start.19
  136.3 0.9 copy-start.4
  145.0 21.8 %copy-start.27 = (pred[10]{0:T(512)(128)(4,1)S(1)}, pred[10]{0:T(512)(128)(4,1)}, u32[]{:S(2)}) copy-start(pred[10]{0:T(512)(128)(4,1)} %compare_and_fusion.8) | copy-start | bytes 34
  146.0 17.0 %collective-permute-start.16 = (f32[32,2,512]{2,0,1:T(8,128)S(1)}, f32[32,2,512]{2,0,1:T(8,128)S(1)}, u32[]{:S(2)}, u32[]{:S(2)}) collective-permute-start(f32[32,2,512]{2,0,1:T(8,128)S(1)} %pad_maximum_fusion.11), channel_id=1, source_target_pairs={{0,2},{1,3},{2,4},{3,5},{4,6},{5,7},{6,8},{7,9},{8,10},{9,11},{10,... | collective-permute-start | bytes 393224 | tf_op jit(solution)/shard_map/ppermute | solution.py:20
  147.9 15.1 %collective-permute-start.17 = (f32[32,2,512]{2,0,1:T(8,128)S(1)}, f32[32,2,512]{2,0,1:T(8,128)S(1)}, u32[]{:S(2)}, u32[]{:S(2)}) collective-permute-start(f32[32,2,512]{2,0,1:T(8,128)S(1)} %pad_maximum_fusion.11), channel_id=1, source_target_pairs={{0,1},{1,2},{2,3},{3,4},{4,5},{5,6},{6,7},{7,8},{8,9},{9,10},{10,1... | collective-permute-start | bytes 393224 | tf_op jit(solution)/shard_map/ppermute | solution.py:20
  151.8 11.2 %collective-permute-start.18 = (f32[32,2,512]{2,0,1:T(8,128)S(1)}, f32[32,2,512]{2,0,1:T(8,128)S(1)}, u32[]{:S(2)}, u32[]{:S(2)}) collective-permute-start(f32[32,2,512]{2,0,1:T(8,128)S(1)} %pad_maximum_fusion.11), channel_id=1, source_target_pairs={{1,0},{2,1},{3,2},{4,3},{5,4},{6,5},{7,6},{8,7},{9,8},{10,9},{11,1... | collective-permute-start | bytes 393224 | tf_op jit(solution)/shard_map/ppermute | solution.py:20
  158.0 8.7 %collective-permute-start.19 = (f32[32,2,512]{2,0,1:T(8,128)S(1)}, f32[32,2,512]{2,0,1:T(8,128)S(1)}, u32[]{:S(2)}, u32[]{:S(2)}) collective-permute-start(f32[32,2,512]{2,0,1:T(8,128)S(1)} %pad_maximum_fusion.11), channel_id=1, source_target_pairs={{2,0},{3,1},{4,2},{5,3},{6,4},{7,5},{8,6},{9,7},{10,8},{11,9},{12,... | collective-permute-start | bytes 393224 | tf_op jit(solution)/shard_map/ppermute | solution.py:20
  167.2 1.5 copy-start.15
  167.2 1.5 copy-start.17
  168.8 15.2 %collective-permute-start.20 = (f32[32,2,256]{2,0,1:T(8,128)S(1)}, f32[32,2,256]{2,0,1:T(8,128)S(1)}, u32[]{:S(2)}, u32[]{:S(2)}) collective-permute-start(f32[32,2,256]{2,0,1:T(8,128)S(1)} %slice_select_fusion.3), channel_id=1, source_target_pairs={{0,2},{1,3},{2,4},{3,5},{4,6},{5,7},{6,8},{7,9},{8,10},{9,11},{10,... | collective-permute-start | bytes 196616 | tf_op jit(solution)/shard_map/ppermute | solution.py:20
  170.7 13.3 %collective-permute-start.21 = (f32[32,2,256]{2,0,1:T(8,128)S(1)}, f32[32,2,256]{2,0,1:T(8,128)S(1)}, u32[]{:S(2)}, u32[]{:S(2)}) collective-permute-start(f32[32,2,256]{2,0,1:T(8,128)S(1)} %slice_select_fusion.3), channel_id=1, source_target_pairs={{0,1},{1,2},{2,3},{3,4},{4,5},{5,6},{6,7},{7,8},{8,9},{9,10},{10,1... | collective-permute-start | bytes 196616 | tf_op jit(solution)/shard_map/ppermute | solution.py:20
  173.8 10.2 %collective-permute-start.22 = (f32[32,2,256]{2,0,1:T(8,128)S(1)}, f32[32,2,256]{2,0,1:T(8,128)S(1)}, u32[]{:S(2)}, u32[]{:S(2)}) collective-permute-start(f32[32,2,256]{2,0,1:T(8,128)S(1)} %slice_select_fusion.3), channel_id=1, source_target_pairs={{1,0},{2,1},{3,2},{4,3},{5,4},{6,5},{7,6},{8,7},{9,8},{10,9},{11,1... | collective-permute-start | bytes 196616 | tf_op jit(solution)/shard_map/ppermute | solution.py:20
  178.7 7.5 %collective-permute-start.23 = (f32[32,2,256]{2,0,1:T(8,128)S(1)}, f32[32,2,256]{2,0,1:T(8,128)S(1)}, u32[]{:S(2)}, u32[]{:S(2)}) collective-permute-start(f32[32,2,256]{2,0,1:T(8,128)S(1)} %slice_select_fusion.3), channel_id=1, source_target_pairs={{2,0},{3,1},{4,2},{5,3},{6,4},{7,5},{8,6},{9,7},{10,8},{11,9},{12,... | collective-permute-start | bytes 196616 | tf_op jit(solution)/shard_map/ppermute | solution.py:20
  187.2 1.4 copy-start.16
  187.2 1.4 copy-start.18
  187.2 1.4 copy-start.20
  188.6 3.0 %copy-start.5 = (f32[64,12,256]{2,0,1:T(8,128)S(1)}, f32[64,12,256]{2,0,1:T(8,128)}, u32[]{:S(2)}) copy-start(f32[64,12,256]{2,0,1:T(8,128)} %copy-done.4) | copy-start | bytes 2359300
  188.7 4.0 %copy-start.29 = (pred[12]{0:T(512)(128)(4,1)S(1)}, pred[12]{0:T(512)(128)(4,1)}, u32[]{:S(2)}) copy-start(pred[12]{0:T(512)(128)(4,1)} %compare_and_fusion.9) | copy-start | bytes 40
  193.6 9.1 %copy-start.22 = (s32[16,16]{1,0:T(8,128)S(1)}, s32[16,16]{1,0:T(8,128)}, u32[]{:S(2)}) copy-start(s32[16,16]{1,0:T(8,128)} %copy-done.21) | copy-start | bytes 3076
  193.6 9.1 %copy-start.26 = (pred[16,16]{1,0:T(8,128)(4,1)S(1)}, pred[16,16]{1,0:T(8,128)(4,1)}, u32[]{:S(2)}) copy-start(pred[16,16]{1,0:T(8,128)(4,1)} %copy-done.25) | copy-start | bytes 772
  194.6 11.1 %copy-start.7 = (f32[16,16,256]{2,1,0:T(8,128)S(1)}, f32[16,16,256]{2,1,0:T(8,128)}, u32[]{:S(2)}) copy-start(f32[16,16,256]{2,1,0:T(8,128)} %copy-done.6) | copy-start | bytes 786436
  194.6 9.1 %collective-permute-start.24 = (f32[64,2,256]{2,0,1:T(8,128)S(1)}, f32[64,2,256]{2,0,1:T(8,128)S(1)}, u32[]{:S(2)}, u32[]{:S(2)}) collective-permute-start(f32[64,2,256]{2,0,1:T(8,128)S(1)} %get-tuple-element.19), channel_id=1, source_target_pairs={{0,1},{1,2},{2,3},{3,4},{4,5},{5,6},{6,7},{7,8},{8,9},{9,10},{10,1... | collective-permute-start | bytes 393224 | tf_op jit(solution)/shard_map/ppermute | solution.py:20
  196.7 8.5 %collective-permute-start.25 = (f32[64,2,256]{2,0,1:T(8,128)S(1)}, f32[64,2,256]{2,0,1:T(8,128)S(1)}, u32[]{:S(2)}, u32[]{:S(2)}) collective-permute-start(f32[64,2,256]{2,0,1:T(8,128)S(1)} %get-tuple-element.18), channel_id=1, source_target_pairs={{1,0},{2,1},{3,2},{4,3},{5,4},{6,5},{7,6},{8,7},{9,8},{10,9},{11,1... | collective-permute-start | bytes 393224 | tf_op jit(solution)/shard_map/ppermute | solution.py:20
  205.6 1.0 copy-start.12
  205.6 1.0 copy-start.14
  206.8 1.1 copy-start.3
  206.8 1.1 copy-start.9
  207.1 0.9 copy-start.24

commit v8 on v7

--- a/solution.py
+++ b/solution.py
@@ -123,9 +123,8 @@
 
 
 def restrict(values, width_x, width_y, span_x, span_y):
-    rows = values[width_x - 1:width_x + span_x]
-    across = 0.25 * rows[0:-1:2] + 0.5 * rows[1::2] + 0.25 * rows[2::2]
-    cols = across[:, width_y - 1:width_y + span_y]
+    rows = values[width_x - 1:width_x + span_x, width_y - 1:width_y + span_y]
+    cols = 0.25 * rows[0:-1:2] + 0.5 * rows[1::2] + 0.25 * rows[2::2]
     return 0.25 * cols[:, 0:-1:2] + 0.5 * cols[:, 1::2] + 0.25 * cols[:, 2::2]
 
 

time: 214 us -> 206 us (0.963)
  local copies, waits for them, and re-layouts: 16.8 us -> 10.3 us
    slice x6 -> x5, local copies, waits for them, and re-layouts: 6.83 us -> 0.9 us  [the longest x3 0.8 us: restrict(): cols = 0.25 * rows[0:-1:2] + 0.5 * rows[1::2] + 0.25 * rows[2::2]]
where the time goes in v8:
time: 206 us; the launch traced here: 205 us
  starting transfers between devices  121 us (59%)
  waiting for transfers between devices  43.9 us (21%)
  other arithmetic  24.8 us (12%)
  local copies, waits for them, and re-layouts  10.3 us (5%)
  Pallas kernels  2.56 us (1%)
    ppermute x20, starting transfers between devices, shifted(): return lax.ppermute(block, axis, route)  91.4 us
    ppermute x20, waiting for transfers between devices, shifted(): return lax.ppermute(block, axis, route)  31.7 us
    ppermute x6, starting transfers between devices, gather_x(): lax.ppermute(block, 'gx', [(i, i ^ m * group) for i in range(count)])  30.1 us
    select_n x18, other arithmetic, half_sweep(): return jnp.where(update, renewed, iterate)  13.5 us
    ppermute x6, waiting for transfers between devices, gather_x(): lax.ppermute(block, 'gx', [(i, i ^ m * group) for i in range(count)])  12.2 us
  transfers between devices with their start and end apart: 26, of which 16 were waited for; matrix products, arithmetic and copies ran while one was open for 2% of the time, Pallas kernels for 0%

profile of v8, /device:TPU:8, one launch (start us, length us, event | category | flops | bytes accessed | tf_op | source)
XLA Modules:
  0.0 204.5 jit_solution(16740438656717676482)
XLA Ops:
  0.0 2.6 %shard_map.46 = f32[16,16,1024]{2,1,0:T(8,128)} custom-call(f32[16]{0:T(128)} %volts_ref.1, f32[16,16,256]{2,1,0:T(8,128)} %potential_ref.1, f32[16,16,256]{2,1,0:T(8,128)} %charge_ref.1, s32[16,16,256]{2,1,0:T(8,128)} %region_ref.1), custom_call_target="tpu_custom_call" | custom-call | tf_op jit(solution)/shard_map/pallas_call | solution.py:211
  2.6 1.2 fusion.213
  3.7 1.8 collective-permute-start
  5.5 1.3 collective-permute-start.1
  7.0 6.6 %collective-permute-done.1 = f32[4,16,1024]{2,1,0:T(8,128)S(1)} collective-permute-done((f32[4,16,1024]{2,1,0:T(8,128)S(1)}, f32[4,16,1024]{2,1,0:T(8,128)S(1)}, u32[]{:S(2)}, u32[]{:S(2)}) %collective-permute-start.1) | collective-permute-done | bytes 262176 | tf_op jit(solution)/shard_map/ppermute | solution.py:20
  13.8 4.3 %collective-permute-start.2 = (f32[24,4,1024]{2,1,0:T(4,128)S(1)}, f32[24,4,1024]{2,1,0:T(4,128)S(1)}, u32[]{:S(2)}, u32[]{:S(2)}) collective-permute-start(f32[24,4,1024]{2,1,0:T(4,128)S(1)} %get-tuple-element.14), channel_id=1, source_target_pairs={{0,1},{1,2},{2,3},{3,4},{4,5},{5,6},{6,7},{7,8},{8,9},{9,10},{10,1... | collective-permute-start | bytes 1179656 | tf_op jit(solution)/shard_map/ppermute | solution.py:20
  18.1 16.6 %collective-permute-start.3 = (f32[24,4,1024]{2,1,0:T(4,128)S(1)}, f32[24,4,1024]{2,1,0:T(4,128)S(1)}, u32[]{:S(2)}, u32[]{:S(2)}) collective-permute-start(f32[24,4,1024]{2,1,0:T(4,128)S(1)} %get-tuple-element.15), channel_id=1, source_target_pairs={{1,0},{2,1},{3,2},{4,3},{5,4},{6,5},{7,6},{8,7},{9,8},{10,9},{11,1... | collective-permute-start | bytes 1179656 | tf_op jit(solution)/shard_map/ppermute | solution.py:20
  34.8 3.7 %collective-permute-done.2 = f32[24,4,1024]{2,1,0:T(4,128)S(1)} collective-permute-done((f32[24,4,1024]{2,1,0:T(4,128)S(1)}, f32[24,4,1024]{2,1,0:T(4,128)S(1)}, u32[]{:S(2)}, u32[]{:S(2)}) %collective-permute-start.2) | collective-permute-done | bytes 393248 | tf_op jit(solution)/shard_map/ppermute | solution.py:20
  38.5 1.5 collective-permute-done.3
  40.0 0.5 pad_maximum_fusion
  40.6 1.6 fusion.58
  42.2 1.4 fusion.62
  43.7 0.4 fusion.78
  45.2 10.9 %collective-permute-start.4 = (f32[4,8,512]{2,1,0:T(8,128)S(1)}, f32[4,8,512]{2,1,0:T(8,128)S(1)}, u32[]{:S(2)}, u32[]{:S(2)}) collective-permute-start(f32[4,8,512]{2,1,0:T(8,128)S(1)} %get-tuple-element.64), channel_id=1, source_target_pairs={{0,64},{64,128},{128,192},{192,256},{256,320},{320,384},{384,448},... | collective-permute-start | bytes 196616 | tf_op jit(solution)/shard_map/ppermute | solution.py:20
  56.2 1.3 collective-permute-start.5
  57.6 1.9 collective-permute-done.5
  59.5 1.9 collective-permute-start.6
  61.4 6.5 %collective-permute-start.7 = (f32[16,4,512]{2,1,0:T(4,128)S(1)}, f32[16,4,512]{2,1,0:T(4,128)S(1)}, u32[]{:S(2)}, u32[]{:S(2)}) collective-permute-start(f32[16,4,512]{2,1,0:T(4,128)S(1)} %get-tuple-element.57), channel_id=1, source_target_pairs={{1,0},{2,1},{3,2},{4,3},{5,4},{6,5},{7,6},{8,7},{9,8},{10,9},{11,1... | collective-permute-start | bytes 393224 | tf_op jit(solution)/shard_map/ppermute | solution.py:20
  68.0 1.7 collective-permute-done.6
  69.7 0.8 collective-permute-done.7
  71.5 0.5 copy-done.6
  72.3 8.4 %collective-permute-start.8 = (f32[4,4,512]{2,1,0:T(4,128)S(1)}, f32[4,4,512]{2,1,0:T(4,128)S(1)}, u32[]{:S(2)}, u32[]{:S(2)}) collective-permute-start(f32[4,4,512]{2,1,0:T(4,128)S(1)} %get-tuple-element.67), channel_id=1, source_target_pairs={{0,64},{64,0},{128,192},{192,128},{256,320},{320,256},{384,448},{4... | collective-permute-start | bytes 98312 | tf_op jit(solution)/shard_map/ppermute | solution.py:55
  80.7 10.2 %collective-permute-start.9 = (f32[4,4,512]{2,1,0:T(4,128)S(1)}, f32[4,4,512]{2,1,0:T(4,128)S(1)}, u32[]{:S(2)}, u32[]{:S(2)}) collective-permute-start(f32[4,4,512]{2,1,0:T(4,128)S(1)} %get-tuple-element.67), channel_id=1, source_target_pairs={{0,128},{64,192},{128,0},{192,64},{256,384},{320,448},{384,256},{4... | collective-permute-start | bytes 98312 | tf_op jit(solution)/shard_map/ppermute | solution.py:55
  90.9 1.9 collective-permute-start.10
  93.1 7.2 %collective-permute-done.10 = f32[4,4,512]{2,1,0:T(4,128)S(1)} collective-permute-done((f32[4,4,512]{2,1,0:T(4,128)S(1)}, f32[4,4,512]{2,1,0:T(4,128)S(1)}, u32[]{:S(2)}, u32[]{:S(2)}) %collective-permute-start.10) | collective-permute-done | bytes 32800 | tf_op jit(solution)/shard_map/ppermute | solution.py:55
  100.4 1.9 collective-permute-start.12
  102.3 5.8 %collective-permute-start.13 = (f32[16,4,512]{2,1,0:T(4,128)S(1)}, f32[16,4,512]{2,1,0:T(4,128)S(1)}, u32[]{:S(2)}, u32[]{:S(2)}) collective-permute-start(f32[16,4,512]{2,1,0:T(4,128)S(1)} %get-tuple-element.59), channel_id=1, source_target_pairs={{0,768},{64,832},{128,896},{192,960},{256,512},{320,576},{384,640}... | collective-permute-start | bytes 393224 | tf_op jit(solution)/shard_map/ppermute | solution.py:55
  108.1 1.9 collective-permute-start.11
  110.1 1.9 collective-permute-done.13
  112.0 2.9 %collective-permute-done.11 = f32[16,4,512]{2,1,0:T(4,128)S(1)} collective-permute-done((f32[16,4,512]{2,1,0:T(4,128)S(1)}, f32[16,4,512]{2,1,0:T(4,128)S(1)}, u32[]{:S(2)}, u32[]{:S(2)}) %collective-permute-start.11) | collective-permute-done | bytes 131104 | tf_op jit(solution)/shard_map/ppermute | solution.py:55
  115.4 1.9 collective-permute-start.14
  117.3 6.2 %collective-permute-start.15 = (f32[64,4,512]{2,0,1:T(8,128)S(1)}, f32[64,4,512]{2,0,1:T(8,128)}, u32[]{:S(2)}, u32[]{:S(2)}) collective-permute-start(f32[64,4,512]{2,0,1:T(8,128)S(1)} %pad_maximum_fusion.4), channel_id=1, source_target_pairs={{1,0},{2,1},{3,2},{4,3},{5,4},{6,5},{7,6},{8,7},{9,8},{10,9},{11,1... | collective-permute-start | bytes 1572872 | tf_op jit(solution)/shard_map/ppermute | solution.py:20
  123.5 0.5 compare_and_fusion.8
  124.1 0.6 add_multiply_fusion.2
  124.8 7.2 %collective-permute-done.14 = f32[64,4,512]{2,0,1:T(8,128)S(1)} collective-permute-done((f32[64,4,512]{2,0,1:T(8,128)S(1)}, f32[64,4,512]{2,0,1:T(8,128)S(1)}, u32[]{:S(2)}, u32[]{:S(2)}) %collective-permute-start.14) | collective-permute-done | bytes 524320 | tf_op jit(solution)/shard_map/ppermute | solution.py:20
  131.9 0.8 copy-done.20
  133.1 1.4 pad_maximum_fusion.1
  134.5 0.9 fusion.40
  135.5 0.9 fusion.8
  136.4 0.5 fusion.16
  138.2 0.9 pad_maximum_fusion.11
  139.1 1.9 collective-permute-start.16
  141.0 2.4 %collective-permute-start.17 = (f32[32,2,512]{2,0,1:T(8,128)S(1)}, f32[32,2,512]{2,0,1:T(8,128)S(1)}, u32[]{:S(2)}, u32[]{:S(2)}) collective-permute-start(f32[32,2,512]{2,0,1:T(8,128)S(1)} %pad_maximum_fusion.11), channel_id=1, source_target_pairs={{0,1},{1,2},{2,3},{3,4},{4,5},{5,6},{6,7},{7,8},{8,9},{9,10},{10,1... | collective-permute-start | bytes 393224 | tf_op jit(solution)/shard_map/ppermute | solution.py:20
  143.4 1.5 compare_and_fusion.5
  144.9 6.1 %collective-permute-start.18 = (f32[32,2,512]{2,0,1:T(8,128)S(1)}, f32[32,2,512]{2,0,1:T(8,128)S(1)}, u32[]{:S(2)}, u32[]{:S(2)}) collective-permute-start(f32[32,2,512]{2,0,1:T(8,128)S(1)} %pad_maximum_fusion.11), channel_id=1, source_target_pairs={{1,0},{2,1},{3,2},{4,3},{5,4},{6,5},{7,6},{8,7},{9,8},{10,9},{11,1... | collective-permute-start | bytes 393224 | tf_op jit(solution)/shard_map/ppermute | solution.py:20
  151.0 5.0 %collective-permute-start.19 = (f32[32,2,512]{2,0,1:T(8,128)S(1)}, f32[32,2,512]{2,0,1:T(8,128)S(1)}, u32[]{:S(2)}, u32[]{:S(2)}) collective-permute-start(f32[32,2,512]{2,0,1:T(8,128)S(1)} %pad_maximum_fusion.11), channel_id=1, source_target_pairs={{2,0},{3,1},{4,2},{5,3},{6,4},{7,5},{8,6},{9,7},{10,8},{11,9},{12,... | collective-permute-start | bytes 393224 | tf_op jit(solution)/shard_map/ppermute | solution.py:20
  156.2 3.6 %collective-permute-done.19 = f32[32,2,512]{2,0,1:T(8,128)S(1)} collective-permute-done((f32[32,2,512]{2,0,1:T(8,128)S(1)}, f32[32,2,512]{2,0,1:T(8,128)S(1)}, u32[]{:S(2)}, u32[]{:S(2)}) %collective-permute-start.19) | collective-permute-done | bytes 131104 | tf_op jit(solution)/shard_map/ppermute | solution.py:20
  161.8 1.9 collective-permute-start.20
  163.8 3.1 %collective-permute-start.21 = (f32[32,2,256]{2,0,1:T(8,128)S(1)}, f32[32,2,256]{2,0,1:T(8,128)S(1)}, u32[]{:S(2)}, u32[]{:S(2)}) collective-permute-start(f32[32,2,256]{2,0,1:T(8,128)S(1)} %slice_select_fusion.3), channel_id=1, source_target_pairs={{0,1},{1,2},{2,3},{3,4},{4,5},{5,6},{6,7},{7,8},{8,9},{9,10},{10,1... | collective-permute-start | bytes 196616 | tf_op jit(solution)/shard_map/ppermute | solution.py:20
  166.9 4.9 %collective-permute-start.22 = (f32[32,2,256]{2,0,1:T(8,128)S(1)}, f32[32,2,256]{2,0,1:T(8,128)S(1)}, u32[]{:S(2)}, u32[]{:S(2)}) collective-permute-start(f32[32,2,256]{2,0,1:T(8,128)S(1)} %slice_select_fusion.3), channel_id=1, source_target_pairs={{1,0},{2,1},{3,2},{4,3},{5,4},{6,5},{7,6},{8,7},{9,8},{10,9},{11,1... | collective-permute-start | bytes 196616 | tf_op jit(solution)/shard_map/ppermute | solution.py:20
  171.7 5.3 %collective-permute-start.23 = (f32[32,2,256]{2,0,1:T(8,128)S(1)}, f32[32,2,256]{2,0,1:T(8,128)S(1)}, u32[]{:S(2)}, u32[]{:S(2)}) collective-permute-start(f32[32,2,256]{2,0,1:T(8,128)S(1)} %slice_select_fusion.3), channel_id=1, source_target_pairs={{2,0},{3,1},{4,2},{5,3},{6,4},{7,5},{8,6},{9,7},{10,8},{11,9},{12,... | collective-permute-start | bytes 196616 | tf_op jit(solution)/shard_map/ppermute | solution.py:20
  177.1 2.1 %collective-permute-done.23 = f32[32,2,256]{2,0,1:T(8,128)S(1)} collective-permute-done((f32[32,2,256]{2,0,1:T(8,128)S(1)}, f32[32,2,256]{2,0,1:T(8,128)S(1)}, u32[]{:S(2)}, u32[]{:S(2)}) %collective-permute-start.23) | collective-permute-done | bytes 65568 | tf_op jit(solution)/shard_map/ppermute | solution.py:20
  180.9 0.9 broadcast_in_dim.36
  181.8 2.0 reshape.169
  183.8 1.1 bitcast_add_fusion
  184.9 0.9 fusion.24
  185.8 0.9 fusion.32
  186.8 2.1 %collective-permute-start.24 = (f32[64,2,256]{2,0,1:T(8,128)S(1)}, f32[64,2,256]{2,0,1:T(8,128)S(1)}, u32[]{:S(2)}, u32[]{:S(2)}) collective-permute-start(f32[64,2,256]{2,0,1:T(8,128)S(1)} %get-tuple-element.19), channel_id=1, source_target_pairs={{0,1},{1,2},{2,3},{3,4},{4,5},{5,6},{6,7},{7,8},{8,9},{9,10},{10,1... | collective-permute-start | bytes 393224 | tf_op jit(solution)/shard_map/ppermute | solution.py:20
  188.8 6.0 %collective-permute-start.25 = (f32[64,2,256]{2,0,1:T(8,128)S(1)}, f32[64,2,256]{2,0,1:T(8,128)S(1)}, u32[]{:S(2)}, u32[]{:S(2)}) collective-permute-start(f32[64,2,256]{2,0,1:T(8,128)S(1)} %get-tuple-element.18), channel_id=1, source_target_pairs={{1,0},{2,1},{3,2},{4,3},{5,4},{6,5},{7,6},{8,7},{9,8},{10,9},{11,1... | collective-permute-start | bytes 393224 | tf_op jit(solution)/shard_map/ppermute | solution.py:20
  195.1 0.7 collective-permute-done.24
  195.9 1.5 collective-permute-done.25
  200.2 1.8 fusion.66
  202.1 0.4 fusion.83
  202.5 2.0 slice_select_fusion
  (178 shorter events, 12.2 us)
Async XLA Ops:
  2.6 11.1 %copy-start.1 = (f32[16,16,1024]{2,1,0:T(8,128)S(1)}, f32[16,16,1024]{2,1,0:T(8,128)}, u32[]{:S(2)}) copy-start(f32[16,16,1024]{2,1,0:T(8,128)} %shard_map.46) | copy-start | bytes 3145732
  3.7 3.3 %collective-permute-start = (f32[4,16,1024]{2,1,0:T(8,128)S(1)}, f32[4,16,1024]{2,1,0:T(8,128)S(1)}, u32[]{:S(2)}, u32[]{:S(2)}) collective-permute-start(f32[4,16,1024]{2,1,0:T(8,128)S(1)} %get-tuple-element.16), channel_id=1, source_target_pairs={{0,64},{64,128},{128,192},{192,256},{256,320},{320,384},{384,448},... | collective-permute-start | bytes 786440 | tf_op jit(solution)/shard_map/ppermute | solution.py:20
  5.5 8.1 %collective-permute-start.1 = (f32[4,16,1024]{2,1,0:T(8,128)S(1)}, f32[4,16,1024]{2,1,0:T(8,128)S(1)}, u32[]{:S(2)}, u32[]{:S(2)}) collective-permute-start(f32[4,16,1024]{2,1,0:T(8,128)S(1)} %get-tuple-element.17), channel_id=1, source_target_pairs={{64,0},{128,64},{192,128},{256,192},{320,256},{384,320},{448,384},... | collective-permute-start | bytes 786440 | tf_op jit(solution)/shard_map/ppermute | solution.py:20
  6.9 64.1 %copy-start.28 = (pred[16,16]{1,0:T(8,128)(4,1)}, pred[16,16]{1,0:T(8,128)(4,1)S(1)}, u32[]{:S(2)}) copy-start(pred[16,16]{1,0:T(8,128)(4,1)S(1)} %broadcast_and_fusion.1) | copy-start | bytes 772
  7.0 64.0 %copy-start.24 = (s32[16,16]{1,0:T(8,128)}, s32[16,16]{1,0:T(8,128)S(1)}, u32[]{:S(2)}) copy-start(s32[16,16]{1,0:T(8,128)S(1)} %iota_add_fusion.4) | copy-start | bytes 3076
  13.8 24.8 %collective-permute-start.2 = (f32[24,4,1024]{2,1,0:T(4,128)S(1)}, f32[24,4,1024]{2,1,0:T(4,128)S(1)}, u32[]{:S(2)}, u32[]{:S(2)}) collective-permute-start(f32[24,4,1024]{2,1,0:T(4,128)S(1)} %get-tuple-element.14), channel_id=1, source_target_pairs={{0,1},{1,2},{2,3},{3,4},{4,5},{5,6},{6,7},{7,8},{8,9},{9,10},{10,1... | collective-permute-start | bytes 1179656 | tf_op jit(solution)/shard_map/ppermute | solution.py:20
  18.1 21.9 %collective-permute-start.3 = (f32[24,4,1024]{2,1,0:T(4,128)S(1)}, f32[24,4,1024]{2,1,0:T(4,128)S(1)}, u32[]{:S(2)}, u32[]{:S(2)}) collective-permute-start(f32[24,4,1024]{2,1,0:T(4,128)S(1)} %get-tuple-element.15), channel_id=1, source_target_pairs={{1,0},{2,1},{3,2},{4,3},{5,4},{6,5},{7,6},{8,7},{9,8},{10,9},{11,1... | collective-permute-start | bytes 1179656 | tf_op jit(solution)/shard_map/ppermute | solution.py:20
  34.8 7.4 %copy-start.26 = (s32[24,24]{1,0:T(8,128)}, s32[24,24]{1,0:T(8,128)S(1)}, u32[]{:S(2)}) copy-start(s32[24,24]{1,0:T(8,128)S(1)} %iota_add_fusion.1) | copy-start | bytes 6916
  40.5 1.7 copy-start
  42.1 2.0 copy-start.8
  43.6 0.8 copy-start.2
  43.6 1.0 copy-start.10
  45.2 12.3 %collective-permute-start.4 = (f32[4,8,512]{2,1,0:T(8,128)S(1)}, f32[4,8,512]{2,1,0:T(8,128)S(1)}, u32[]{:S(2)}, u32[]{:S(2)}) collective-permute-start(f32[4,8,512]{2,1,0:T(8,128)S(1)} %get-tuple-element.64), channel_id=1, source_target_pairs={{0,64},{64,128},{128,192},{192,256},{256,320},{320,384},{384,448},... | collective-permute-start | bytes 196616 | tf_op jit(solution)/shard_map/ppermute | solution.py:20
  56.2 3.2 %collective-permute-start.5 = (f32[4,8,512]{2,1,0:T(8,128)S(1)}, f32[4,8,512]{2,1,0:T(8,128)S(1)}, u32[]{:S(2)}, u32[]{:S(2)}) collective-permute-start(f32[4,8,512]{2,1,0:T(8,128)S(1)} %get-tuple-element.65), channel_id=1, source_target_pairs={{64,0},{128,64},{192,128},{256,192},{320,256},{384,320},{448,384},... | collective-permute-start | bytes 196616 | tf_op jit(solution)/shard_map/ppermute | solution.py:20
  59.5 10.1 %collective-permute-start.6 = (f32[16,4,512]{2,1,0:T(4,128)S(1)}, f32[16,4,512]{2,1,0:T(4,128)S(1)}, u32[]{:S(2)}, u32[]{:S(2)}) collective-permute-start(f32[16,4,512]{2,1,0:T(4,128)S(1)} %get-tuple-element.56), channel_id=1, source_target_pairs={{0,1},{1,2},{2,3},{3,4},{4,5},{5,6},{6,7},{7,8},{8,9},{9,10},{10,1... | collective-permute-start | bytes 393224 | tf_op jit(solution)/shard_map/ppermute | solution.py:20
  61.4 9.0 %collective-permute-start.7 = (f32[16,4,512]{2,1,0:T(4,128)S(1)}, f32[16,4,512]{2,1,0:T(4,128)S(1)}, u32[]{:S(2)}, u32[]{:S(2)}) collective-permute-start(f32[16,4,512]{2,1,0:T(4,128)S(1)} %get-tuple-element.57), channel_id=1, source_target_pairs={{1,0},{2,1},{3,2},{4,3},{5,4},{6,5},{7,6},{8,7},{9,8},{10,9},{11,1... | collective-permute-start | bytes 393224 | tf_op jit(solution)/shard_map/ppermute | solution.py:20
  70.9 1.2 copy-start.11
  70.9 1.2 copy-start.13
  71.3 0.7 copy-start.6
  72.3 20.6 %collective-permute-start.8 = (f32[4,4,512]{2,1,0:T(4,128)S(1)}, f32[4,4,512]{2,1,0:T(4,128)S(1)}, u32[]{:S(2)}, u32[]{:S(2)}) collective-permute-start(f32[4,4,512]{2,1,0:T(4,128)S(1)} %get-tuple-element.67), channel_id=1, source_target_pairs={{0,64},{64,0},{128,192},{192,128},{256,320},{320,256},{384,448},{4... | collective-permute-start | bytes 98312 | tf_op jit(solution)/shard_map/ppermute | solution.py:55
  80.7 12.4 %collective-permute-start.9 = (f32[4,4,512]{2,1,0:T(4,128)S(1)}, f32[4,4,512]{2,1,0:T(4,128)S(1)}, u32[]{:S(2)}, u32[]{:S(2)}) collective-permute-start(f32[4,4,512]{2,1,0:T(4,128)S(1)} %get-tuple-element.67), channel_id=1, source_target_pairs={{0,128},{64,192},{128,0},{192,64},{256,384},{320,448},{384,256},{4... | collective-permute-start | bytes 98312 | tf_op jit(solution)/shard_map/ppermute | solution.py:55
  90.9 9.4 %collective-permute-start.10 = (f32[4,4,512]{2,1,0:T(4,128)S(1)}, f32[4,4,512]{2,1,0:T(4,128)S(1)}, u32[]{:S(2)}, u32[]{:S(2)}) collective-permute-start(f32[4,4,512]{2,1,0:T(4,128)S(1)} %get-tuple-element.67), channel_id=1, source_target_pairs={{0,192},{64,128},{128,64},{192,0},{256,448},{320,384},{384,320},{4... | collective-permute-start | bytes 98312 | tf_op jit(solution)/shard_map/ppermute | solution.py:55
  92.8 42.7 %copy-start.22 = (s32[64,12]{0,1:T(8,128)}, s32[64,12]{0,1:T(8,128)S(1)}, u32[]{:S(2)}) copy-start(s32[64,12]{0,1:T(8,128)S(1)} %iota_add_fusion.3) | copy-start | bytes 9220
  100.4 9.7 %collective-permute-start.12 = (f32[16,4,512]{2,1,0:T(4,128)S(1)}, f32[16,4,512]{2,1,0:T(4,128)S(1)}, u32[]{:S(2)}, u32[]{:S(2)}) collective-permute-start(f32[16,4,512]{2,1,0:T(4,128)S(1)} %get-tuple-element.59), channel_id=1, source_target_pairs={{0,512},{64,576},{128,640},{192,704},{256,768},{320,832},{384,896}... | collective-permute-start | bytes 393224 | tf_op jit(solution)/shard_map/ppermute | solution.py:55
  102.3 9.7 %collective-permute-start.13 = (f32[16,4,512]{2,1,0:T(4,128)S(1)}, f32[16,4,512]{2,1,0:T(4,128)S(1)}, u32[]{:S(2)}, u32[]{:S(2)}) collective-permute-start(f32[16,4,512]{2,1,0:T(4,128)S(1)} %get-tuple-element.59), channel_id=1, source_target_pairs={{0,768},{64,832},{128,896},{192,960},{256,512},{320,576},{384,640}... | collective-permute-start | bytes 393224 | tf_op jit(solution)/shard_map/ppermute | solution.py:55
  108.1 6.9 %collective-permute-start.11 = (f32[16,4,512]{2,1,0:T(4,128)S(1)}, f32[16,4,512]{2,1,0:T(4,128)S(1)}, u32[]{:S(2)}, u32[]{:S(2)}) collective-permute-start(f32[16,4,512]{2,1,0:T(4,128)S(1)} %get-tuple-element.59), channel_id=1, source_target_pairs={{0,256},{64,320},{128,384},{192,448},{256,0},{320,64},{384,128},{4... | collective-permute-start | bytes 393224 | tf_op jit(solution)/shard_map/ppermute | solution.py:55
  110.0 26.4 %copy-start.32 = (pred[12]{0:T(512)(128)(4,1)}, pred[12]{0:T(512)(128)(4,1)S(1)}, u32[]{:S(2)}) copy-start(pred[12]{0:T(512)(128)(4,1)S(1)} %compare_and_fusion.9) | copy-start | bytes 40
  115.4 16.6 %collective-permute-start.14 = (f32[64,4,512]{2,0,1:T(8,128)S(1)}, f32[64,4,512]{2,0,1:T(8,128)S(1)}, u32[]{:S(2)}, u32[]{:S(2)}) collective-permute-start(f32[64,4,512]{2,0,1:T(8,128)S(1)} %pad_maximum_fusion.4), channel_id=1, source_target_pairs={{0,1},{1,2},{2,3},{3,4},{4,5},{5,6},{6,7},{7,8},{8,9},{9,10},{10,1... | collective-permute-start | bytes 1572872 | tf_op jit(solution)/shard_map/ppermute | solution.py:20
  117.3 15.8 %collective-permute-start.15 = (f32[64,4,512]{2,0,1:T(8,128)S(1)}, f32[64,4,512]{2,0,1:T(8,128)}, u32[]{:S(2)}, u32[]{:S(2)}) collective-permute-start(f32[64,4,512]{2,0,1:T(8,128)S(1)} %pad_maximum_fusion.4), channel_id=1, source_target_pairs={{1,0},{2,1},{3,2},{4,3},{5,4},{6,5},{7,6},{8,7},{9,8},{10,9},{11,1... | collective-permute-start | bytes 1572872 | tf_op jit(solution)/shard_map/ppermute | solution.py:20
  131.9 0.8 copy-start.20
  136.4 0.9 copy-start.4
  138.1 18.0 %copy-start.19 = (f32[32,2,256]{2,0,1:T(8,128)S(1)}, f32[32,2,256]{2,0,1:T(8,128)}, u32[]{:S(2)}) copy-start(f32[32,2,256]{2,0,1:T(8,128)} %add_multiply_fusion.2) | copy-start | bytes 196612
  138.1 21.7 %copy-start.30 = (pred[10]{0:T(512)(128)(4,1)S(1)}, pred[10]{0:T(512)(128)(4,1)}, u32[]{:S(2)}) copy-start(pred[10]{0:T(512)(128)(4,1)} %compare_and_fusion.8) | copy-start | bytes 34
  139.1 17.0 %collective-permute-start.16 = (f32[32,2,512]{2,0,1:T(8,128)S(1)}, f32[32,2,512]{2,0,1:T(8,128)S(1)}, u32[]{:S(2)}, u32[]{:S(2)}) collective-permute-start(f32[32,2,512]{2,0,1:T(8,128)S(1)} %pad_maximum_fusion.11), channel_id=1, source_target_pairs={{0,2},{1,3},{2,4},{3,5},{4,6},{5,7},{6,8},{7,9},{8,10},{9,11},{10,... | collective-permute-start | bytes 393224 | tf_op jit(solution)/shard_map/ppermute | solution.py:20
  141.0 15.1 %collective-permute-start.17 = (f32[32,2,512]{2,0,1:T(8,128)S(1)}, f32[32,2,512]{2,0,1:T(8,128)S(1)}, u32[]{:S(2)}, u32[]{:S(2)}) collective-permute-start(f32[32,2,512]{2,0,1:T(8,128)S(1)} %pad_maximum_fusion.11), channel_id=1, source_target_pairs={{0,1},{1,2},{2,3},{3,4},{4,5},{5,6},{6,7},{7,8},{8,9},{9,10},{10,1... | collective-permute-start | bytes 393224 | tf_op jit(solution)/shard_map/ppermute | solution.py:20
  144.9 11.3 %collective-permute-start.18 = (f32[32,2,512]{2,0,1:T(8,128)S(1)}, f32[32,2,512]{2,0,1:T(8,128)S(1)}, u32[]{:S(2)}, u32[]{:S(2)}) collective-permute-start(f32[32,2,512]{2,0,1:T(8,128)S(1)} %pad_maximum_fusion.11), channel_id=1, source_target_pairs={{1,0},{2,1},{3,2},{4,3},{5,4},{6,5},{7,6},{8,7},{9,8},{10,9},{11,1... | collective-permute-start | bytes 393224 | tf_op jit(solution)/shard_map/ppermute | solution.py:20
  151.0 8.7 %collective-permute-start.19 = (f32[32,2,512]{2,0,1:T(8,128)S(1)}, f32[32,2,512]{2,0,1:T(8,128)S(1)}, u32[]{:S(2)}, u32[]{:S(2)}) collective-permute-start(f32[32,2,512]{2,0,1:T(8,128)S(1)} %pad_maximum_fusion.11), channel_id=1, source_target_pairs={{2,0},{3,1},{4,2},{5,3},{6,4},{7,5},{8,6},{9,7},{10,8},{11,9},{12,... | collective-permute-start | bytes 393224 | tf_op jit(solution)/shard_map/ppermute | solution.py:20
  160.3 1.5 copy-start.15
  160.3 1.5 copy-start.17
  161.5 17.7 %copy-start.31 = (pred[10]{0:T(512)(128)(4,1)S(1)}, pred[10]{0:T(512)(128)(4,1)}, u32[]{:S(2)}) copy-start(pred[10]{0:T(512)(128)(4,1)} %compare_and_fusion.8) | copy-start | bytes 34
  161.8 15.2 %collective-permute-start.20 = (f32[32,2,256]{2,0,1:T(8,128)S(1)}, f32[32,2,256]{2,0,1:T(8,128)S(1)}, u32[]{:S(2)}, u32[]{:S(2)}) collective-permute-start(f32[32,2,256]{2,0,1:T(8,128)S(1)} %slice_select_fusion.3), channel_id=1, source_target_pairs={{0,2},{1,3},{2,4},{3,5},{4,6},{5,7},{6,8},{7,9},{8,10},{9,11},{10,... | collective-permute-start | bytes 196616 | tf_op jit(solution)/shard_map/ppermute | solution.py:20
  163.8 13.3 %collective-permute-start.21 = (f32[32,2,256]{2,0,1:T(8,128)S(1)}, f32[32,2,256]{2,0,1:T(8,128)S(1)}, u32[]{:S(2)}, u32[]{:S(2)}) collective-permute-start(f32[32,2,256]{2,0,1:T(8,128)S(1)} %slice_select_fusion.3), channel_id=1, source_target_pairs={{0,1},{1,2},{2,3},{3,4},{4,5},{5,6},{6,7},{7,8},{8,9},{9,10},{10,1... | collective-permute-start | bytes 196616 | tf_op jit(solution)/shard_map/ppermute | solution.py:20
  166.9 10.2 %collective-permute-start.22 = (f32[32,2,256]{2,0,1:T(8,128)S(1)}, f32[32,2,256]{2,0,1:T(8,128)S(1)}, u32[]{:S(2)}, u32[]{:S(2)}) collective-permute-start(f32[32,2,256]{2,0,1:T(8,128)S(1)} %slice_select_fusion.3), channel_id=1, source_target_pairs={{1,0},{2,1},{3,2},{4,3},{5,4},{6,5},{7,6},{8,7},{9,8},{10,9},{11,1... | collective-permute-start | bytes 196616 | tf_op jit(solution)/shard_map/ppermute | solution.py:20
  171.7 7.5 %collective-permute-start.23 = (f32[32,2,256]{2,0,1:T(8,128)S(1)}, f32[32,2,256]{2,0,1:T(8,128)S(1)}, u32[]{:S(2)}, u32[]{:S(2)}) collective-permute-start(f32[32,2,256]{2,0,1:T(8,128)S(1)} %slice_select_fusion.3), channel_id=1, source_target_pairs={{2,0},{3,1},{4,2},{5,3},{6,4},{7,5},{8,6},{9,7},{10,8},{11,9},{12,... | collective-permute-start | bytes 196616 | tf_op jit(solution)/shard_map/ppermute | solution.py:20
  179.6 1.0 copy-start.16
  179.7 1.1 copy-start.18
  179.7 1.1 copy-start.21
  180.3 3.4 %copy-start.5 = (f32[64,12,256]{2,0,1:T(8,128)S(1)}, f32[64,12,256]{2,0,1:T(8,128)}, u32[]{:S(2)}) copy-start(f32[64,12,256]{2,0,1:T(8,128)} %copy-done.4) | copy-start | bytes 2359300
  180.8 4.0 %copy-start.23 = (s32[64,12]{0,1:T(8,128)S(1)}, s32[64,12]{0,1:T(8,128)}, u32[]{:S(2)}) copy-start(s32[64,12]{0,1:T(8,128)} %copy-done.22) | copy-start | bytes 9220
  180.9 4.0 %copy-start.33 = (pred[12]{0:T(512)(128)(4,1)S(1)}, pred[12]{0:T(512)(128)(4,1)}, u32[]{:S(2)}) copy-start(pred[12]{0:T(512)(128)(4,1)} %copy-done.32) | copy-start | bytes 40
  185.8 9.1 %copy-start.25 = (s32[16,16]{1,0:T(8,128)S(1)}, s32[16,16]{1,0:T(8,128)}, u32[]{:S(2)}) copy-start(s32[16,16]{1,0:T(8,128)} %copy-done.24) | copy-start | bytes 3076
  185.8 9.1 %copy-start.29 = (pred[16,16]{1,0:T(8,128)(4,1)S(1)}, pred[16,16]{1,0:T(8,128)(4,1)}, u32[]{:S(2)}) copy-start(pred[16,16]{1,0:T(8,128)(4,1)} %copy-done.28) | copy-start | bytes 772
  186.7 11.1 %copy-start.7 = (f32[16,16,256]{2,1,0:T(8,128)S(1)}, f32[16,16,256]{2,1,0:T(8,128)}, u32[]{:S(2)}) copy-start(f32[16,16,256]{2,1,0:T(8,128)} %copy-done.6) | copy-start | bytes 786436
  186.8 9.1 %collective-permute-start.24 = (f32[64,2,256]{2,0,1:T(8,128)S(1)}, f32[64,2,256]{2,0,1:T(8,128)S(1)}, u32[]{:S(2)}, u32[]{:S(2)}) collective-permute-start(f32[64,2,256]{2,0,1:T(8,128)S(1)} %get-tuple-element.19), channel_id=1, source_target_pairs={{0,1},{1,2},{2,3},{3,4},{4,5},{5,6},{6,7},{7,8},{8,9},{9,10},{10,1... | collective-permute-start | bytes 393224 | tf_op jit(solution)/shard_map/ppermute | solution.py:20
  188.8 8.5 %collective-permute-start.25 = (f32[64,2,256]{2,0,1:T(8,128)S(1)}, f32[64,2,256]{2,0,1:T(8,128)S(1)}, u32[]{:S(2)}, u32[]{:S(2)}) collective-permute-start(f32[64,2,256]{2,0,1:T(8,128)S(1)} %get-tuple-element.18), channel_id=1, source_target_pairs={{1,0},{2,1},{3,2},{4,3},{5,4},{6,5},{7,6},{8,7},{9,8},{10,9},{11,1... | collective-permute-start | bytes 393224 | tf_op jit(solution)/shard_map/ppermute | solution.py:20
  197.8 1.0 copy-start.12
  197.8 1.0 copy-start.14
  199.0 1.1 copy-start.3
  199.0 1.1 copy-start.9
  199.3 0.9 copy-start.27

commit v9 on v8

--- a/solution.py
+++ b/solution.py
@@ -250,11 +250,12 @@
 
     iterate_1, source_1, divisor_1, weight_1, allowed_1 = level_1[:5]
     iterate_1 = sweeps(iterate_1 + lift(iterate_2), source_1, divisor_1, weight_1, allowed_1, 1)
-    lifted = lift(interior(iterate_1, HALO_MID // 2))
-
-    iterate = iterate + jnp.where(movable, lifted, 0.0)
-    iterate = sweeps(iterate, source, divisor, 1.0, movable, 1)
-    return interior(iterate, width)
+    cut = width - 2
+    lifted = lift(interior(iterate_1, HALO_MID - 1))
+    movable = interior(movable, cut)
+    iterate = interior(iterate, cut) + jnp.where(movable, lifted, 0.0)
+    iterate = sweeps(iterate, interior(source, cut), interior(divisor, cut), 1.0, movable, 1)
+    return interior(iterate, 2)
 
 
 def solution(mesh):

time: 206 us -> 204 us (level)
    select_n x18 -> x17, other arithmetic: 13.5 us -> 10 us  [half_sweep(): return jnp.where(update, renewed, iterate)]
where the time goes in v9:
time: 204 us; the launch traced here: 203 us
  starting transfers between devices  121 us (59%)
  waiting for transfers between devices  43.7 us (21%)
  other arithmetic  23.2 us (11%)
  local copies, waits for them, and re-layouts  10.9 us (5%)
  Pallas kernels  2.56 us (1%)
    ppermute x20, starting transfers between devices, shifted(): return lax.ppermute(block, axis, route)  91.4 us
    ppermute x20, waiting for transfers between devices, shifted(): return lax.ppermute(block, axis, route)  31.5 us
    ppermute x6, starting transfers between devices, gather_x(): lax.ppermute(block, 'gx', [(i, i ^ m * group) for i in range(count)])  30.1 us
    ppermute x6, waiting for transfers between devices, gather_x(): lax.ppermute(block, 'gx', [(i, i ^ m * group) for i in range(count)])  12.2 us
    select_n x17, other arithmetic, half_sweep(): return jnp.where(update, renewed, iterate)  10 us
    unnamed x73, local copies, waits for them, and re-layouts  4.11 us
  transfers between devices with their start and end apart: 26, of which 16 were waited for; matrix products, arithmetic and copies ran while one was open for 2% of the time, Pallas kernels for 0%

profile of v9, /device:TPU:8, one launch (start us, length us, event | category | flops | bytes accessed | tf_op | source)
XLA Modules:
  0.0 203.4 jit_solution(2448374028660423897)
XLA Ops:
  0.0 2.6 %shard_map.46 = f32[16,16,1024]{2,1,0:T(8,128)} custom-call(f32[16]{0:T(128)} %volts_ref.1, f32[16,16,256]{2,1,0:T(8,128)} %potential_ref.1, f32[16,16,256]{2,1,0:T(8,128)} %charge_ref.1, s32[16,16,256]{2,1,0:T(8,128)} %region_ref.1), custom_call_target="tpu_custom_call" | custom-call | tf_op jit(solution)/shard_map/pallas_call | solution.py:211
  2.6 1.2 fusion.218
  3.7 1.8 collective-permute-start
  5.5 1.3 collective-permute-start.1
  7.0 6.6 %collective-permute-done.1 = f32[4,16,1024]{2,1,0:T(8,128)S(1)} collective-permute-done((f32[4,16,1024]{2,1,0:T(8,128)S(1)}, f32[4,16,1024]{2,1,0:T(8,128)S(1)}, u32[]{:S(2)}, u32[]{:S(2)}) %collective-permute-start.1) | collective-permute-done | bytes 262176 | tf_op jit(solution)/shard_map/ppermute | solution.py:20
  13.8 4.3 %collective-permute-start.2 = (f32[24,4,1024]{2,1,0:T(4,128)S(1)}, f32[24,4,1024]{2,1,0:T(4,128)S(1)}, u32[]{:S(2)}, u32[]{:S(2)}) collective-permute-start(f32[24,4,1024]{2,1,0:T(4,128)S(1)} %get-tuple-element.12), channel_id=1, source_target_pairs={{0,1},{1,2},{2,3},{3,4},{4,5},{5,6},{6,7},{7,8},{8,9},{9,10},{10,1... | collective-permute-start | bytes 1179656 | tf_op jit(solution)/shard_map/ppermute | solution.py:20
  18.1 16.6 %collective-permute-start.3 = (f32[24,4,1024]{2,1,0:T(4,128)S(1)}, f32[24,4,1024]{2,1,0:T(4,128)S(1)}, u32[]{:S(2)}, u32[]{:S(2)}) collective-permute-start(f32[24,4,1024]{2,1,0:T(4,128)S(1)} %get-tuple-element.13), channel_id=1, source_target_pairs={{1,0},{2,1},{3,2},{4,3},{5,4},{6,5},{7,6},{8,7},{9,8},{10,9},{11,1... | collective-permute-start | bytes 1179656 | tf_op jit(solution)/shard_map/ppermute | solution.py:20
  34.8 3.7 %collective-permute-done.2 = f32[24,4,1024]{2,1,0:T(4,128)S(1)} collective-permute-done((f32[24,4,1024]{2,1,0:T(4,128)S(1)}, f32[24,4,1024]{2,1,0:T(4,128)S(1)}, u32[]{:S(2)}, u32[]{:S(2)}) %collective-permute-start.2) | collective-permute-done | bytes 393248 | tf_op jit(solution)/shard_map/ppermute | solution.py:20
  38.5 1.5 collective-permute-done.3
  40.5 1.6 fusion.58
  42.2 0.8 fusion.62
  42.9 0.4 fusion.74
  44.5 10.9 %collective-permute-start.4 = (f32[4,8,512]{2,1,0:T(8,128)S(1)}, f32[4,8,512]{2,1,0:T(8,128)S(1)}, u32[]{:S(2)}, u32[]{:S(2)}) collective-permute-start(f32[4,8,512]{2,1,0:T(8,128)S(1)} %get-tuple-element.65), channel_id=1, source_target_pairs={{0,64},{64,128},{128,192},{192,256},{256,320},{320,384},{384,448},... | collective-permute-start | bytes 196616 | tf_op jit(solution)/shard_map/ppermute | solution.py:20
  55.5 1.3 collective-permute-start.5
  56.8 1.9 collective-permute-done.5
  58.8 1.9 collective-permute-start.6
  60.7 6.5 %collective-permute-start.7 = (f32[16,4,512]{2,1,0:T(4,128)S(1)}, f32[16,4,512]{2,1,0:T(4,128)S(1)}, u32[]{:S(2)}, u32[]{:S(2)}) collective-permute-start(f32[16,4,512]{2,1,0:T(4,128)S(1)} %get-tuple-element.58), channel_id=1, source_target_pairs={{1,0},{2,1},{3,2},{4,3},{5,4},{6,5},{7,6},{8,7},{9,8},{10,9},{11,1... | collective-permute-start | bytes 393224 | tf_op jit(solution)/shard_map/ppermute | solution.py:20
  67.2 1.7 collective-permute-done.6
  68.9 0.8 collective-permute-done.7
  70.8 0.5 copy-done.9
  71.6 8.4 %collective-permute-start.8 = (f32[4,4,512]{2,1,0:T(4,128)S(1)}, f32[4,4,512]{2,1,0:T(4,128)S(1)}, u32[]{:S(2)}, u32[]{:S(2)}) collective-permute-start(f32[4,4,512]{2,1,0:T(4,128)S(1)} %get-tuple-element.68), channel_id=1, source_target_pairs={{0,64},{64,0},{128,192},{192,128},{256,320},{320,256},{384,448},{4... | collective-permute-start | bytes 98312 | tf_op jit(solution)/shard_map/ppermute | solution.py:55
  80.0 10.2 %collective-permute-start.9 = (f32[4,4,512]{2,1,0:T(4,128)S(1)}, f32[4,4,512]{2,1,0:T(4,128)S(1)}, u32[]{:S(2)}, u32[]{:S(2)}) collective-permute-start(f32[4,4,512]{2,1,0:T(4,128)S(1)} %get-tuple-element.68), channel_id=1, source_target_pairs={{0,128},{64,192},{128,0},{192,64},{256,384},{320,448},{384,256},{4... | collective-permute-start | bytes 98312 | tf_op jit(solution)/shard_map/ppermute | solution.py:55
  90.1 1.9 collective-permute-start.10
  92.4 7.2 %collective-permute-done.10 = f32[4,4,512]{2,1,0:T(4,128)S(1)} collective-permute-done((f32[4,4,512]{2,1,0:T(4,128)S(1)}, f32[4,4,512]{2,1,0:T(4,128)S(1)}, u32[]{:S(2)}, u32[]{:S(2)}) %collective-permute-start.10) | collective-permute-done | bytes 32800 | tf_op jit(solution)/shard_map/ppermute | solution.py:55
  99.6 1.9 collective-permute-start.12
  101.6 5.8 %collective-permute-start.13 = (f32[16,4,512]{2,1,0:T(4,128)S(1)}, f32[16,4,512]{2,1,0:T(4,128)S(1)}, u32[]{:S(2)}, u32[]{:S(2)}) collective-permute-start(f32[16,4,512]{2,1,0:T(4,128)S(1)} %get-tuple-element.60), channel_id=1, source_target_pairs={{0,768},{64,832},{128,896},{192,960},{256,512},{320,576},{384,640}... | collective-permute-start | bytes 393224 | tf_op jit(solution)/shard_map/ppermute | solution.py:55
  107.3 1.9 collective-permute-start.11
  109.4 1.9 collective-permute-done.13
  111.3 2.9 %collective-permute-done.11 = f32[16,4,512]{2,1,0:T(4,128)S(1)} collective-permute-done((f32[16,4,512]{2,1,0:T(4,128)S(1)}, f32[16,4,512]{2,1,0:T(4,128)S(1)}, u32[]{:S(2)}, u32[]{:S(2)}) %collective-permute-start.11) | collective-permute-done | bytes 131104 | tf_op jit(solution)/shard_map/ppermute | solution.py:55
  114.6 1.9 collective-permute-start.14
  116.6 6.2 %collective-permute-start.15 = (f32[64,4,512]{2,0,1:T(8,128)S(1)}, f32[64,4,512]{2,0,1:T(8,128)}, u32[]{:S(2)}, u32[]{:S(2)}) collective-permute-start(f32[64,4,512]{2,0,1:T(8,128)S(1)} %pad_maximum_fusion.4), channel_id=1, source_target_pairs={{1,0},{2,1},{3,2},{4,3},{5,4},{6,5},{7,6},{8,7},{9,8},{10,9},{11,1... | collective-permute-start | bytes 1572872 | tf_op jit(solution)/shard_map/ppermute | solution.py:20
  122.7 0.6 compare_and_fusion.6
  123.5 0.6 add_multiply_fusion.2
  124.1 7.1 %collective-permute-done.14 = f32[64,4,512]{2,0,1:T(8,128)S(1)} collective-permute-done((f32[64,4,512]{2,0,1:T(8,128)S(1)}, f32[64,4,512]{2,0,1:T(8,128)S(1)}, u32[]{:S(2)}, u32[]{:S(2)}) %collective-permute-start.14) | collective-permute-done | bytes 524320 | tf_op jit(solution)/shard_map/ppermute | solution.py:20
  131.2 0.8 copy-done.21
  132.4 1.4 pad_maximum_fusion.1
  133.8 0.9 fusion.40
  134.7 0.9 fusion.8
  135.7 0.5 fusion.16
  137.5 0.9 pad_maximum_fusion.11
  138.4 1.9 collective-permute-start.16
  140.3 1.6 compare_and_fusion.3
  141.9 2.4 %collective-permute-start.17 = (f32[32,2,512]{2,0,1:T(8,128)S(1)}, f32[32,2,512]{2,0,1:T(8,128)S(1)}, u32[]{:S(2)}, u32[]{:S(2)}) collective-permute-start(f32[32,2,512]{2,0,1:T(8,128)S(1)} %pad_maximum_fusion.11), channel_id=1, source_target_pairs={{0,1},{1,2},{2,3},{3,4},{4,5},{5,6},{6,7},{7,8},{8,9},{9,10},{10,1... | collective-permute-start | bytes 393224 | tf_op jit(solution)/shard_map/ppermute | solution.py:20
  144.3 6.2 %collective-permute-start.18 = (f32[32,2,512]{2,0,1:T(8,128)S(1)}, f32[32,2,512]{2,0,1:T(8,128)S(1)}, u32[]{:S(2)}, u32[]{:S(2)}) collective-permute-start(f32[32,2,512]{2,0,1:T(8,128)S(1)} %pad_maximum_fusion.11), channel_id=1, source_target_pairs={{1,0},{2,1},{3,2},{4,3},{5,4},{6,5},{7,6},{8,7},{9,8},{10,9},{11,1... | collective-permute-start | bytes 393224 | tf_op jit(solution)/shard_map/ppermute | solution.py:20
  150.5 5.0 %collective-permute-start.19 = (f32[32,2,512]{2,0,1:T(8,128)S(1)}, f32[32,2,512]{2,0,1:T(8,128)S(1)}, u32[]{:S(2)}, u32[]{:S(2)}) collective-permute-start(f32[32,2,512]{2,0,1:T(8,128)S(1)} %pad_maximum_fusion.11), channel_id=1, source_target_pairs={{2,0},{3,1},{4,2},{5,3},{6,4},{7,5},{8,6},{9,7},{10,8},{11,9},{12,... | collective-permute-start | bytes 393224 | tf_op jit(solution)/shard_map/ppermute | solution.py:20
  155.6 3.6 %collective-permute-done.19 = f32[32,2,512]{2,0,1:T(8,128)S(1)} collective-permute-done((f32[32,2,512]{2,0,1:T(8,128)S(1)}, f32[32,2,512]{2,0,1:T(8,128)S(1)}, u32[]{:S(2)}, u32[]{:S(2)}) %collective-permute-start.19) | collective-permute-done | bytes 131104 | tf_op jit(solution)/shard_map/ppermute | solution.py:20
  161.3 1.9 collective-permute-start.20
  163.2 1.0 add_select_fusion.2
  164.2 3.1 %collective-permute-start.21 = (f32[32,2,256]{2,0,1:T(8,128)S(1)}, f32[32,2,256]{2,0,1:T(8,128)S(1)}, u32[]{:S(2)}, u32[]{:S(2)}) collective-permute-start(f32[32,2,256]{2,0,1:T(8,128)S(1)} %slice_select_fusion.3), channel_id=1, source_target_pairs={{0,1},{1,2},{2,3},{3,4},{4,5},{5,6},{6,7},{7,8},{8,9},{9,10},{10,1... | collective-permute-start | bytes 196616 | tf_op jit(solution)/shard_map/ppermute | solution.py:20
  167.3 4.9 %collective-permute-start.22 = (f32[32,2,256]{2,0,1:T(8,128)S(1)}, f32[32,2,256]{2,0,1:T(8,128)S(1)}, u32[]{:S(2)}, u32[]{:S(2)}) collective-permute-start(f32[32,2,256]{2,0,1:T(8,128)S(1)} %slice_select_fusion.3), channel_id=1, source_target_pairs={{1,0},{2,1},{3,2},{4,3},{5,4},{6,5},{7,6},{8,7},{9,8},{10,9},{11,1... | collective-permute-start | bytes 196616 | tf_op jit(solution)/shard_map/ppermute | solution.py:20
  172.2 5.3 %collective-permute-start.23 = (f32[32,2,256]{2,0,1:T(8,128)S(1)}, f32[32,2,256]{2,0,1:T(8,128)S(1)}, u32[]{:S(2)}, u32[]{:S(2)}) collective-permute-start(f32[32,2,256]{2,0,1:T(8,128)S(1)} %slice_select_fusion.3), channel_id=1, source_target_pairs={{2,0},{3,1},{4,2},{5,3},{6,4},{7,5},{8,6},{9,7},{10,8},{11,9},{12,... | collective-permute-start | bytes 196616 | tf_op jit(solution)/shard_map/ppermute | solution.py:20
  177.5 2.1 %collective-permute-done.23 = f32[32,2,256]{2,0,1:T(8,128)S(1)} collective-permute-done((f32[32,2,256]{2,0,1:T(8,128)S(1)}, f32[32,2,256]{2,0,1:T(8,128)S(1)}, u32[]{:S(2)}, u32[]{:S(2)}) %collective-permute-start.23) | collective-permute-done | bytes 65568 | tf_op jit(solution)/shard_map/ppermute | solution.py:20
  181.3 0.9 broadcast_in_dim.38
  182.2 2.0 reshape.184
  184.2 1.1 bitcast_add_fusion
  185.3 0.9 fusion.24
  186.3 0.9 fusion.32
  187.2 2.1 %collective-permute-start.24 = (f32[64,2,256]{2,0,1:T(8,128)S(1)}, f32[64,2,256]{2,0,1:T(8,128)S(1)}, u32[]{:S(2)}, u32[]{:S(2)}) collective-permute-start(f32[64,2,256]{2,0,1:T(8,128)S(1)} %get-tuple-element.17), channel_id=1, source_target_pairs={{0,1},{1,2},{2,3},{3,4},{4,5},{5,6},{6,7},{7,8},{8,9},{9,10},{10,1... | collective-permute-start | bytes 393224 | tf_op jit(solution)/shard_map/ppermute | solution.py:20
  189.3 6.0 %collective-permute-start.25 = (f32[64,2,256]{2,0,1:T(8,128)S(1)}, f32[64,2,256]{2,0,1:T(8,128)S(1)}, u32[]{:S(2)}, u32[]{:S(2)}) collective-permute-start(f32[64,2,256]{2,0,1:T(8,128)S(1)} %get-tuple-element.16), channel_id=1, source_target_pairs={{1,0},{2,1},{3,2},{4,3},{5,4},{6,5},{7,6},{8,7},{9,8},{10,9},{11,1... | collective-permute-start | bytes 393224 | tf_op jit(solution)/shard_map/ppermute | solution.py:20
  195.7 0.6 collective-permute-done.24
  196.3 1.5 collective-permute-done.25
  200.6 0.7 fusion.221
  201.7 0.6 copy-done.15
  202.3 1.0 slice_select_fusion
  (179 shorter events, 12.9 us)
Async XLA Ops:
  2.6 11.1 %copy-start = (f32[16,16,1024]{2,1,0:T(8,128)S(1)}, f32[16,16,1024]{2,1,0:T(8,128)}, u32[]{:S(2)}) copy-start(f32[16,16,1024]{2,1,0:T(8,128)} %shard_map.46) | copy-start | bytes 3145732
  3.7 3.3 %collective-permute-start = (f32[4,16,1024]{2,1,0:T(8,128)S(1)}, f32[4,16,1024]{2,1,0:T(8,128)S(1)}, u32[]{:S(2)}, u32[]{:S(2)}) collective-permute-start(f32[4,16,1024]{2,1,0:T(8,128)S(1)} %get-tuple-element.14), channel_id=1, source_target_pairs={{0,64},{64,128},{128,192},{192,256},{256,320},{320,384},{384,448},... | collective-permute-start | bytes 786440 | tf_op jit(solution)/shard_map/ppermute | solution.py:20
  5.5 8.1 %collective-permute-start.1 = (f32[4,16,1024]{2,1,0:T(8,128)S(1)}, f32[4,16,1024]{2,1,0:T(8,128)S(1)}, u32[]{:S(2)}, u32[]{:S(2)}) collective-permute-start(f32[4,16,1024]{2,1,0:T(8,128)S(1)} %get-tuple-element.15), channel_id=1, source_target_pairs={{64,0},{128,64},{192,128},{256,192},{320,256},{384,320},{448,384},... | collective-permute-start | bytes 786440 | tf_op jit(solution)/shard_map/ppermute | solution.py:20
  6.9 63.3 %copy-start.27 = (pred[16,16]{1,0:T(8,128)(4,1)}, pred[16,16]{1,0:T(8,128)(4,1)S(1)}, u32[]{:S(2)}) copy-start(pred[16,16]{1,0:T(8,128)(4,1)S(1)} %broadcast_and_fusion.1) | copy-start | bytes 772
  7.0 63.2 %copy-start.25 = (s32[16,16]{1,0:T(8,128)}, s32[16,16]{1,0:T(8,128)S(1)}, u32[]{:S(2)}) copy-start(s32[16,16]{1,0:T(8,128)S(1)} %iota_add_fusion.5) | copy-start | bytes 3076
  13.8 24.8 %collective-permute-start.2 = (f32[24,4,1024]{2,1,0:T(4,128)S(1)}, f32[24,4,1024]{2,1,0:T(4,128)S(1)}, u32[]{:S(2)}, u32[]{:S(2)}) collective-permute-start(f32[24,4,1024]{2,1,0:T(4,128)S(1)} %get-tuple-element.12), channel_id=1, source_target_pairs={{0,1},{1,2},{2,3},{3,4},{4,5},{5,6},{6,7},{7,8},{8,9},{9,10},{10,1... | collective-permute-start | bytes 1179656 | tf_op jit(solution)/shard_map/ppermute | solution.py:20
  18.1 21.9 %collective-permute-start.3 = (f32[24,4,1024]{2,1,0:T(4,128)S(1)}, f32[24,4,1024]{2,1,0:T(4,128)S(1)}, u32[]{:S(2)}, u32[]{:S(2)}) collective-permute-start(f32[24,4,1024]{2,1,0:T(4,128)S(1)} %get-tuple-element.13), channel_id=1, source_target_pairs={{1,0},{2,1},{3,2},{4,3},{5,4},{6,5},{7,6},{8,7},{9,8},{10,9},{11,1... | collective-permute-start | bytes 1179656 | tf_op jit(solution)/shard_map/ppermute | solution.py:20
  42.1 1.3 copy-start.5
  42.1 1.3 copy-start.7
  42.9 0.8 copy-start.1
  44.5 12.3 %collective-permute-start.4 = (f32[4,8,512]{2,1,0:T(8,128)S(1)}, f32[4,8,512]{2,1,0:T(8,128)S(1)}, u32[]{:S(2)}, u32[]{:S(2)}) collective-permute-start(f32[4,8,512]{2,1,0:T(8,128)S(1)} %get-tuple-element.65), channel_id=1, source_target_pairs={{0,64},{64,128},{128,192},{192,256},{256,320},{320,384},{384,448},... | collective-permute-start | bytes 196616 | tf_op jit(solution)/shard_map/ppermute | solution.py:20
  55.5 3.2 %collective-permute-start.5 = (f32[4,8,512]{2,1,0:T(8,128)S(1)}, f32[4,8,512]{2,1,0:T(8,128)S(1)}, u32[]{:S(2)}, u32[]{:S(2)}) collective-permute-start(f32[4,8,512]{2,1,0:T(8,128)S(1)} %get-tuple-element.66), channel_id=1, source_target_pairs={{64,0},{128,64},{192,128},{256,192},{320,256},{384,320},{448,384},... | collective-permute-start | bytes 196616 | tf_op jit(solution)/shard_map/ppermute | solution.py:20
  58.8 10.1 %collective-permute-start.6 = (f32[16,4,512]{2,1,0:T(4,128)S(1)}, f32[16,4,512]{2,1,0:T(4,128)S(1)}, u32[]{:S(2)}, u32[]{:S(2)}) collective-permute-start(f32[16,4,512]{2,1,0:T(4,128)S(1)} %get-tuple-element.57), channel_id=1, source_target_pairs={{0,1},{1,2},{2,3},{3,4},{4,5},{5,6},{6,7},{7,8},{8,9},{9,10},{10,1... | collective-permute-start | bytes 393224 | tf_op jit(solution)/shard_map/ppermute | solution.py:20
  60.7 9.0 %collective-permute-start.7 = (f32[16,4,512]{2,1,0:T(4,128)S(1)}, f32[16,4,512]{2,1,0:T(4,128)S(1)}, u32[]{:S(2)}, u32[]{:S(2)}) collective-permute-start(f32[16,4,512]{2,1,0:T(4,128)S(1)} %get-tuple-element.58), channel_id=1, source_target_pairs={{1,0},{2,1},{3,2},{4,3},{5,4},{6,5},{7,6},{8,7},{9,8},{10,9},{11,1... | collective-permute-start | bytes 393224 | tf_op jit(solution)/shard_map/ppermute | solution.py:20
  70.2 1.2 copy-start.11
  70.2 1.2 copy-start.13
  70.6 0.7 copy-start.9
  71.6 20.6 %collective-permute-start.8 = (f32[4,4,512]{2,1,0:T(4,128)S(1)}, f32[4,4,512]{2,1,0:T(4,128)S(1)}, u32[]{:S(2)}, u32[]{:S(2)}) collective-permute-start(f32[4,4,512]{2,1,0:T(4,128)S(1)} %get-tuple-element.68), channel_id=1, source_target_pairs={{0,64},{64,0},{128,192},{192,128},{256,320},{320,256},{384,448},{4... | collective-permute-start | bytes 98312 | tf_op jit(solution)/shard_map/ppermute | solution.py:55
  80.0 12.4 %collective-permute-start.9 = (f32[4,4,512]{2,1,0:T(4,128)S(1)}, f32[4,4,512]{2,1,0:T(4,128)S(1)}, u32[]{:S(2)}, u32[]{:S(2)}) collective-permute-start(f32[4,4,512]{2,1,0:T(4,128)S(1)} %get-tuple-element.68), channel_id=1, source_target_pairs={{0,128},{64,192},{128,0},{192,64},{256,384},{320,448},{384,256},{4... | collective-permute-start | bytes 98312 | tf_op jit(solution)/shard_map/ppermute | solution.py:55
  90.1 9.4 %collective-permute-start.10 = (f32[4,4,512]{2,1,0:T(4,128)S(1)}, f32[4,4,512]{2,1,0:T(4,128)S(1)}, u32[]{:S(2)}, u32[]{:S(2)}) collective-permute-start(f32[4,4,512]{2,1,0:T(4,128)S(1)} %get-tuple-element.68), channel_id=1, source_target_pairs={{0,192},{64,128},{128,64},{192,0},{256,448},{320,384},{384,320},{4... | collective-permute-start | bytes 98312 | tf_op jit(solution)/shard_map/ppermute | solution.py:55
  92.1 42.7 %copy-start.23 = (s32[64,12]{0,1:T(8,128)}, s32[64,12]{0,1:T(8,128)S(1)}, u32[]{:S(2)}) copy-start(s32[64,12]{0,1:T(8,128)S(1)} %iota_add_fusion.4) | copy-start | bytes 9220
  99.6 9.7 %collective-permute-start.12 = (f32[16,4,512]{2,1,0:T(4,128)S(1)}, f32[16,4,512]{2,1,0:T(4,128)S(1)}, u32[]{:S(2)}, u32[]{:S(2)}) collective-permute-start(f32[16,4,512]{2,1,0:T(4,128)S(1)} %get-tuple-element.60), channel_id=1, source_target_pairs={{0,512},{64,576},{128,640},{192,704},{256,768},{320,832},{384,896}... | collective-permute-start | bytes 393224 | tf_op jit(solution)/shard_map/ppermute | solution.py:55
  101.6 9.7 %collective-permute-start.13 = (f32[16,4,512]{2,1,0:T(4,128)S(1)}, f32[16,4,512]{2,1,0:T(4,128)S(1)}, u32[]{:S(2)}, u32[]{:S(2)}) collective-permute-start(f32[16,4,512]{2,1,0:T(4,128)S(1)} %get-tuple-element.60), channel_id=1, source_target_pairs={{0,768},{64,832},{128,896},{192,960},{256,512},{320,576},{384,640}... | collective-permute-start | bytes 393224 | tf_op jit(solution)/shard_map/ppermute | solution.py:55
  107.3 6.9 %collective-permute-start.11 = (f32[16,4,512]{2,1,0:T(4,128)S(1)}, f32[16,4,512]{2,1,0:T(4,128)S(1)}, u32[]{:S(2)}, u32[]{:S(2)}) collective-permute-start(f32[16,4,512]{2,1,0:T(4,128)S(1)} %get-tuple-element.60), channel_id=1, source_target_pairs={{0,256},{64,320},{128,384},{192,448},{256,0},{320,64},{384,128},{4... | collective-permute-start | bytes 393224 | tf_op jit(solution)/shard_map/ppermute | solution.py:55
  109.3 26.4 %copy-start.31 = (pred[12]{0:T(512)(128)(4,1)}, pred[12]{0:T(512)(128)(4,1)S(1)}, u32[]{:S(2)}) copy-start(pred[12]{0:T(512)(128)(4,1)S(1)} %compare_and_fusion.7) | copy-start | bytes 40
  114.6 16.6 %collective-permute-start.14 = (f32[64,4,512]{2,0,1:T(8,128)S(1)}, f32[64,4,512]{2,0,1:T(8,128)S(1)}, u32[]{:S(2)}, u32[]{:S(2)}) collective-permute-start(f32[64,4,512]{2,0,1:T(8,128)S(1)} %pad_maximum_fusion.4), channel_id=1, source_target_pairs={{0,1},{1,2},{2,3},{3,4},{4,5},{5,6},{6,7},{7,8},{8,9},{9,10},{10,1... | collective-permute-start | bytes 1572872 | tf_op jit(solution)/shard_map/ppermute | solution.py:20
  116.6 15.8 %collective-permute-start.15 = (f32[64,4,512]{2,0,1:T(8,128)S(1)}, f32[64,4,512]{2,0,1:T(8,128)}, u32[]{:S(2)}, u32[]{:S(2)}) collective-permute-start(f32[64,4,512]{2,0,1:T(8,128)S(1)} %pad_maximum_fusion.4), channel_id=1, source_target_pairs={{1,0},{2,1},{3,2},{4,3},{5,4},{6,5},{7,6},{8,7},{9,8},{10,9},{11,1... | collective-permute-start | bytes 1572872 | tf_op jit(solution)/shard_map/ppermute | solution.py:20
  131.2 0.8 copy-start.21
  135.7 0.9 copy-start.3
  137.4 18.1 %copy-start.20 = (f32[32,2,256]{2,0,1:T(8,128)S(1)}, f32[32,2,256]{2,0,1:T(8,128)}, u32[]{:S(2)}) copy-start(f32[32,2,256]{2,0,1:T(8,128)} %add_multiply_fusion.2) | copy-start | bytes 196612
  137.5 21.8 %copy-start.29 = (pred[10]{0:T(512)(128)(4,1)S(1)}, pred[10]{0:T(512)(128)(4,1)}, u32[]{:S(2)}) copy-start(pred[10]{0:T(512)(128)(4,1)} %compare_and_fusion.6) | copy-start | bytes 34
  138.4 17.1 %collective-permute-start.16 = (f32[32,2,512]{2,0,1:T(8,128)S(1)}, f32[32,2,512]{2,0,1:T(8,128)S(1)}, u32[]{:S(2)}, u32[]{:S(2)}) collective-permute-start(f32[32,2,512]{2,0,1:T(8,128)S(1)} %pad_maximum_fusion.11), channel_id=1, source_target_pairs={{0,2},{1,3},{2,4},{3,5},{4,6},{5,7},{6,8},{7,9},{8,10},{9,11},{10,... | collective-permute-start | bytes 393224 | tf_op jit(solution)/shard_map/ppermute | solution.py:20
  141.9 13.6 %collective-permute-start.17 = (f32[32,2,512]{2,0,1:T(8,128)S(1)}, f32[32,2,512]{2,0,1:T(8,128)S(1)}, u32[]{:S(2)}, u32[]{:S(2)}) collective-permute-start(f32[32,2,512]{2,0,1:T(8,128)S(1)} %pad_maximum_fusion.11), channel_id=1, source_target_pairs={{0,1},{1,2},{2,3},{3,4},{4,5},{5,6},{6,7},{7,8},{8,9},{9,10},{10,1... | collective-permute-start | bytes 393224 | tf_op jit(solution)/shard_map/ppermute | solution.py:20
  144.3 11.3 %collective-permute-start.18 = (f32[32,2,512]{2,0,1:T(8,128)S(1)}, f32[32,2,512]{2,0,1:T(8,128)S(1)}, u32[]{:S(2)}, u32[]{:S(2)}) collective-permute-start(f32[32,2,512]{2,0,1:T(8,128)S(1)} %pad_maximum_fusion.11), channel_id=1, source_target_pairs={{1,0},{2,1},{3,2},{4,3},{5,4},{6,5},{7,6},{8,7},{9,8},{10,9},{11,1... | collective-permute-start | bytes 393224 | tf_op jit(solution)/shard_map/ppermute | solution.py:20
  150.5 8.7 %collective-permute-start.19 = (f32[32,2,512]{2,0,1:T(8,128)S(1)}, f32[32,2,512]{2,0,1:T(8,128)S(1)}, u32[]{:S(2)}, u32[]{:S(2)}) collective-permute-start(f32[32,2,512]{2,0,1:T(8,128)S(1)} %pad_maximum_fusion.11), channel_id=1, source_target_pairs={{2,0},{3,1},{4,2},{5,3},{6,4},{7,5},{8,6},{9,7},{10,8},{11,9},{12,... | collective-permute-start | bytes 393224 | tf_op jit(solution)/shard_map/ppermute | solution.py:20
  159.7 1.5 copy-start.16
  159.7 1.5 copy-start.18
  160.9 18.7 %copy-start.30 = (pred[10]{0:T(512)(128)(4,1)S(1)}, pred[10]{0:T(512)(128)(4,1)}, u32[]{:S(2)}) copy-start(pred[10]{0:T(512)(128)(4,1)} %compare_and_fusion.6) | copy-start | bytes 34
  161.3 16.2 %collective-permute-start.20 = (f32[32,2,256]{2,0,1:T(8,128)S(1)}, f32[32,2,256]{2,0,1:T(8,128)S(1)}, u32[]{:S(2)}, u32[]{:S(2)}) collective-permute-start(f32[32,2,256]{2,0,1:T(8,128)S(1)} %slice_select_fusion.3), channel_id=1, source_target_pairs={{0,2},{1,3},{2,4},{3,5},{4,6},{5,7},{6,8},{7,9},{8,10},{9,11},{10,... | collective-permute-start | bytes 196616 | tf_op jit(solution)/shard_map/ppermute | solution.py:20
  164.2 13.2 %collective-permute-start.21 = (f32[32,2,256]{2,0,1:T(8,128)S(1)}, f32[32,2,256]{2,0,1:T(8,128)S(1)}, u32[]{:S(2)}, u32[]{:S(2)}) collective-permute-start(f32[32,2,256]{2,0,1:T(8,128)S(1)} %slice_select_fusion.3), channel_id=1, source_target_pairs={{0,1},{1,2},{2,3},{3,4},{4,5},{5,6},{6,7},{7,8},{8,9},{9,10},{10,1... | collective-permute-start | bytes 196616 | tf_op jit(solution)/shard_map/ppermute | solution.py:20
  167.3 10.2 %collective-permute-start.22 = (f32[32,2,256]{2,0,1:T(8,128)S(1)}, f32[32,2,256]{2,0,1:T(8,128)S(1)}, u32[]{:S(2)}, u32[]{:S(2)}) collective-permute-start(f32[32,2,256]{2,0,1:T(8,128)S(1)} %slice_select_fusion.3), channel_id=1, source_target_pairs={{1,0},{2,1},{3,2},{4,3},{5,4},{6,5},{7,6},{8,7},{9,8},{10,9},{11,1... | collective-permute-start | bytes 196616 | tf_op jit(solution)/shard_map/ppermute | solution.py:20
  172.2 7.5 %collective-permute-start.23 = (f32[32,2,256]{2,0,1:T(8,128)S(1)}, f32[32,2,256]{2,0,1:T(8,128)S(1)}, u32[]{:S(2)}, u32[]{:S(2)}) collective-permute-start(f32[32,2,256]{2,0,1:T(8,128)S(1)} %slice_select_fusion.3), channel_id=1, source_target_pairs={{2,0},{3,1},{4,2},{5,3},{6,4},{7,5},{8,6},{9,7},{10,8},{11,9},{12,... | collective-permute-start | bytes 196616 | tf_op jit(solution)/shard_map/ppermute | solution.py:20
  180.1 1.0 copy-start.17
  180.1 1.1 copy-start.19
  180.1 1.1 copy-start.22
  180.8 3.4 %copy-start.4 = (f32[64,12,256]{2,0,1:T(8,128)S(1)}, f32[64,12,256]{2,0,1:T(8,128)}, u32[]{:S(2)}) copy-start(f32[64,12,256]{2,0,1:T(8,128)} %copy-done.3) | copy-start | bytes 2359300
  181.3 4.0 %copy-start.24 = (s32[64,12]{0,1:T(8,128)S(1)}, s32[64,12]{0,1:T(8,128)}, u32[]{:S(2)}) copy-start(s32[64,12]{0,1:T(8,128)} %copy-done.23) | copy-start | bytes 9220
  181.3 4.0 %copy-start.32 = (pred[12]{0:T(512)(128)(4,1)S(1)}, pred[12]{0:T(512)(128)(4,1)}, u32[]{:S(2)}) copy-start(pred[12]{0:T(512)(128)(4,1)} %copy-done.31) | copy-start | bytes 40
  186.3 9.1 %copy-start.26 = (s32[16,16]{1,0:T(8,128)S(1)}, s32[16,16]{1,0:T(8,128)}, u32[]{:S(2)}) copy-start(s32[16,16]{1,0:T(8,128)} %copy-done.25) | copy-start | bytes 3076
  186.3 9.1 %copy-start.28 = (pred[16,16]{1,0:T(8,128)(4,1)S(1)}, pred[16,16]{1,0:T(8,128)(4,1)}, u32[]{:S(2)}) copy-start(pred[16,16]{1,0:T(8,128)(4,1)} %copy-done.27) | copy-start | bytes 772
  186.3 9.3 %copy-start.6 = (pred[24,24,256]{2,1,0:T(8,128)(4,1)S(1)}, pred[24,24,256]{2,1,0:T(8,128)(4,1)}, u32[]{:S(2)}) copy-start(pred[24,24,256]{2,1,0:T(8,128)(4,1)} %copy-done.5) | copy-start | bytes 442372
  187.2 11.1 %copy-start.10 = (f32[16,16,256]{2,1,0:T(8,128)S(1)}, f32[16,16,256]{2,1,0:T(8,128)}, u32[]{:S(2)}) copy-start(f32[16,16,256]{2,1,0:T(8,128)} %copy-done.9) | copy-start | bytes 786436
  187.2 9.1 %collective-permute-start.24 = (f32[64,2,256]{2,0,1:T(8,128)S(1)}, f32[64,2,256]{2,0,1:T(8,128)S(1)}, u32[]{:S(2)}, u32[]{:S(2)}) collective-permute-start(f32[64,2,256]{2,0,1:T(8,128)S(1)} %get-tuple-element.17), channel_id=1, source_target_pairs={{0,1},{1,2},{2,3},{3,4},{4,5},{5,6},{6,7},{7,8},{8,9},{9,10},{10,1... | collective-permute-start | bytes 393224 | tf_op jit(solution)/shard_map/ppermute | solution.py:20
  189.3 8.5 %collective-permute-start.25 = (f32[64,2,256]{2,0,1:T(8,128)S(1)}, f32[64,2,256]{2,0,1:T(8,128)S(1)}, u32[]{:S(2)}, u32[]{:S(2)}) collective-permute-start(f32[64,2,256]{2,0,1:T(8,128)S(1)} %get-tuple-element.16), channel_id=1, source_target_pairs={{1,0},{2,1},{3,2},{4,3},{5,4},{6,5},{7,6},{8,7},{9,8},{10,9},{11,1... | collective-permute-start | bytes 393224 | tf_op jit(solution)/shard_map/ppermute | solution.py:20
  198.3 1.0 copy-start.12
  198.3 1.0 copy-start.14
  199.3 1.1 copy-start.2
  199.5 1.1 copy-start.8
  201.3 1.0 copy-start.15

commit v10 on v9

--- a/solution.py
+++ b/solution.py
@@ -231,8 +231,9 @@
     coefficient = screen * jnp.exp(potential)
     divisor = 4.0 * 1.0 + 2.0 + coefficient
     iterate = sweeps(dirichlet, source, divisor, 1.0, movable, 1)
-    residual = residual_of(iterate, source, divisor, 1.0, movable)
-    source_1 = restrict(residual, width, width, span_x, span_y)
+    near = [interior(values, width - 2) for values in (iterate, source, divisor, movable)]
+    residual = residual_of(near[0], near[1], near[2], 1.0, near[3])
+    source_1 = restrict(residual, 2, 2, span_x, span_y)
     coefficient_1 = coarsen(interior(coefficient, width))
 
     level_1 = descend(1, source_1, coefficient_1, HALO_MID)
@@ -242,10 +243,14 @@
     level_2 = descend_whole_x(2, whole[:, :, :depth], whole[:, :, depth:], HALO_MID)
     iterate_3 = coarsest_whole_x(level_2[5], level_2[6], HALO_COARSE)
 
-    iterate_2, source_2, divisor_2, weight_2, allowed_2 = level_2[:5]
+    rim = HALO_MID // 2
+    iterate_2, source_2, divisor_2, allowed_2 = [
+        values[:, rim:values.shape[1] - rim] for values in (level_2[0], level_2[1], level_2[2], level_2[4])
+    ]
+    weight_2 = level_2[3]
+    iterate_3 = iterate_3[:, 1:iterate_3.shape[1] - 1]
     iterate_2 = sweeps(iterate_2 + lift(iterate_3), source_2, divisor_2, weight_2, allowed_2, 1)
-    rim = HALO_MID // 2
-    iterate_2 = exchange_y(iterate_2[:, HALO_MID:HALO_MID + source_2.shape[1] - 2 * HALO_MID], rim)
+    iterate_2 = exchange_y(iterate_2[:, rim:source_2.shape[1] - rim], rim)
     iterate_2 = x_window(iterate_2, lax.axis_index("gx") * span_x2, span_x2 + 2 * rim, rim)
 
     iterate_1, source_1, divisor_1, weight_1, allowed_1 = level_1[:5]

time: 204 us -> 215 us (1.054)
  local copies, waits for them, and re-layouts: 10.9 us -> 20.3 us
  other arithmetic: 23.2 us -> 32.3 us
  waiting for transfers between devices: 43.7 us -> 35.7 us
    ppermute x20, waiting for transfers between devices: 31.5 us -> 24.1 us  [shifted(): return lax.ppermute(block, axis, route)]
    select_n x17 -> x16, other arithmetic: 10 us -> 16.9 us  [half_sweep(): return jnp.where(update, renewed, iterate)]
    concatenate x2, local copies, waits for them, and re-layouts: 0.02 us -> 5.75 us  [along(): return jnp.concatenate(low + [block] + high, axis=dim)]
    slice x4 -> x6, local copies, waits for them, and re-layouts: 0.09 us -> 2.72 us  [coarsen(): return 0.5 * (across[:, 0::2] + across[:, 1::2])]
    add x0 -> x1, other arithmetic: none -> 2.35 us  [descend_whole_x(): divisor = 4.0 * weight + 2.0 + coefficient]
  transfers between devices with their start and end apart: 26 -> 26, of which waited for: 16 -> 16; matrix products, arithmetic and copies ran while one was open for 2% -> 4% of each run, Pallas kernels for 0% -> 0%
where the time goes in v10:
time: 215 us; the launch traced here: 214 us
  starting transfers between devices  122 us (57%)
  waiting for transfers between devices  35.7 us (17%)
  other arithmetic  32.3 us (15%)
  local copies, waits for them, and re-layouts  20.3 us (9%)
  Pallas kernels  2.52 us (1%)
    ppermute x20, starting transfers between devices, shifted(): return lax.ppermute(block, axis, route)  91.5 us
    ppermute x6, starting transfers between devices, gather_x(): lax.ppermute(block, 'gx', [(i, i ^ m * group) for i in range(count)])  30.1 us
    ppermute x20, waiting for transfers between devices, shifted(): return lax.ppermute(block, axis, route)  24.1 us
    select_n x16, other arithmetic, half_sweep(): return jnp.where(update, renewed, iterate)  16.9 us
    ppermute x6, waiting for transfers between devices, gather_x(): lax.ppermute(block, 'gx', [(i, i ^ m * group) for i in range(count)])  11.6 us
    concatenate x2, local copies, waits for them, and re-layouts, along(): return jnp.concatenate(low + [block] + high, axis=dim)  5.75 us
  transfers between devices with their start and end apart: 26, of which 16 were waited for; matrix products, arithmetic and copies ran while one was open for 4% of the time, Pallas kernels for 0%

profile of v10, /device:TPU:8, one launch (start us, length us, event | category | flops | bytes accessed | tf_op | source)
XLA Modules:
  0.0 214.0 jit_solution(4948217445534183410)
XLA Ops:
  0.0 2.5 %shard_map.46 = f32[16,16,1024]{2,1,0:T(8,128)} custom-call(f32[16]{0:T(128)} %volts_ref.1, f32[16,16,256]{2,1,0:T(8,128)} %potential_ref.1, f32[16,16,256]{2,1,0:T(8,128)} %charge_ref.1, s32[16,16,256]{2,1,0:T(8,128)} %region_ref.1), custom_call_target="tpu_custom_call" | custom-call | tf_op jit(solution)/shard_map/pallas_call | solution.py:211
  2.5 1.2 fusion.187
  3.7 1.8 collective-permute-start
  5.4 1.3 collective-permute-start.1
  6.9 1.1 add_select_fusion.4
  8.0 5.6 %collective-permute-done.1 = f32[4,16,1024]{2,1,0:T(8,128)S(1)} collective-permute-done((f32[4,16,1024]{2,1,0:T(8,128)S(1)}, f32[4,16,1024]{2,1,0:T(8,128)S(1)}, u32[]{:S(2)}, u32[]{:S(2)}) %collective-permute-start.1) | collective-permute-done | bytes 262176 | tf_op jit(solution)/shard_map/ppermute | solution.py:20
  13.7 4.3 %collective-permute-start.2 = (f32[24,4,1024]{2,1,0:T(4,128)S(1)}, f32[24,4,1024]{2,1,0:T(4,128)S(1)}, u32[]{:S(2)}, u32[]{:S(2)}) collective-permute-start(f32[24,4,1024]{2,1,0:T(4,128)S(1)} %get-tuple-element.14), channel_id=1, source_target_pairs={{0,1},{1,2},{2,3},{3,4},{4,5},{5,6},{6,7},{7,8},{8,9},{9,10},{10,1... | collective-permute-start | bytes 1179656 | tf_op jit(solution)/shard_map/ppermute | solution.py:20
  18.0 16.6 %collective-permute-start.3 = (f32[24,4,1024]{2,1,0:T(4,128)S(1)}, f32[24,4,1024]{2,1,0:T(4,128)S(1)}, u32[]{:S(2)}, u32[]{:S(2)}) collective-permute-start(f32[24,4,1024]{2,1,0:T(4,128)S(1)} %get-tuple-element.15), channel_id=1, source_target_pairs={{1,0},{2,1},{3,2},{4,3},{5,4},{6,5},{7,6},{8,7},{9,8},{10,9},{11,1... | collective-permute-start | bytes 1179656 | tf_op jit(solution)/shard_map/ppermute | solution.py:20
  35.1 3.4 %collective-permute-done.2 = f32[24,4,1024]{2,1,0:T(4,128)S(1)} collective-permute-done((f32[24,4,1024]{2,1,0:T(4,128)S(1)}, f32[24,4,1024]{2,1,0:T(4,128)S(1)}, u32[]{:S(2)}, u32[]{:S(2)}) %collective-permute-start.2) | collective-permute-done | bytes 393248 | tf_op jit(solution)/shard_map/ppermute | solution.py:20
  38.5 1.5 collective-permute-done.3
  40.5 1.6 fusion.32
  44.6 10.9 %collective-permute-start.4 = (f32[4,8,512]{2,1,0:T(8,128)S(1)}, f32[4,8,512]{2,1,0:T(8,128)S(1)}, u32[]{:S(2)}, u32[]{:S(2)}) collective-permute-start(f32[4,8,512]{2,1,0:T(8,128)S(1)} %get-tuple-element.72), channel_id=1, source_target_pairs={{0,64},{64,128},{128,192},{192,256},{256,320},{320,384},{384,448},... | collective-permute-start | bytes 196616 | tf_op jit(solution)/shard_map/ppermute | solution.py:20
  55.5 1.3 collective-permute-start.5
  56.9 1.9 collective-permute-done.5
  58.9 1.9 collective-permute-start.6
  60.8 6.5 %collective-permute-start.7 = (f32[16,4,512]{2,1,0:T(4,128)S(1)}, f32[16,4,512]{2,1,0:T(4,128)S(1)}, u32[]{:S(2)}, u32[]{:S(2)}) collective-permute-start(f32[16,4,512]{2,1,0:T(4,128)S(1)} %get-tuple-element.65), channel_id=1, source_target_pairs={{1,0},{2,1},{3,2},{4,3},{5,4},{6,5},{7,6},{8,7},{9,8},{10,9},{11,1... | collective-permute-start | bytes 393224 | tf_op jit(solution)/shard_map/ppermute | solution.py:20
  67.3 1.7 collective-permute-done.6
  69.0 0.8 collective-permute-done.7
  71.2 8.4 %collective-permute-start.8 = (f32[4,4,512]{2,1,0:T(4,128)S(1)}, f32[4,4,512]{2,1,0:T(4,128)S(1)}, u32[]{:S(2)}, u32[]{:S(2)}) collective-permute-start(f32[4,4,512]{2,1,0:T(4,128)S(1)} %get-tuple-element.75), channel_id=1, source_target_pairs={{0,64},{64,0},{128,192},{192,128},{256,320},{320,256},{384,448},{4... | collective-permute-start | bytes 98312 | tf_op jit(solution)/shard_map/ppermute | solution.py:55
  79.6 10.2 %collective-permute-start.9 = (f32[4,4,512]{2,1,0:T(4,128)S(1)}, f32[4,4,512]{2,1,0:T(4,128)S(1)}, u32[]{:S(2)}, u32[]{:S(2)}) collective-permute-start(f32[4,4,512]{2,1,0:T(4,128)S(1)} %get-tuple-element.75), channel_id=1, source_target_pairs={{0,128},{64,192},{128,0},{192,64},{256,384},{320,448},{384,256},{4... | collective-permute-start | bytes 98312 | tf_op jit(solution)/shard_map/ppermute | solution.py:55
  89.8 1.9 collective-permute-start.10
  92.0 7.2 %collective-permute-done.10 = f32[4,4,512]{2,1,0:T(4,128)S(1)} collective-permute-done((f32[4,4,512]{2,1,0:T(4,128)S(1)}, f32[4,4,512]{2,1,0:T(4,128)S(1)}, u32[]{:S(2)}, u32[]{:S(2)}) %collective-permute-start.10) | collective-permute-done | bytes 32800 | tf_op jit(solution)/shard_map/ppermute | solution.py:55
  99.3 1.9 collective-permute-start.12
  101.3 5.8 %collective-permute-start.13 = (f32[16,4,512]{2,1,0:T(4,128)S(1)}, f32[16,4,512]{2,1,0:T(4,128)S(1)}, u32[]{:S(2)}, u32[]{:S(2)}) collective-permute-start(f32[16,4,512]{2,1,0:T(4,128)S(1)} %get-tuple-element.67), channel_id=1, source_target_pairs={{0,768},{64,832},{128,896},{192,960},{256,512},{320,576},{384,640}... | collective-permute-start | bytes 393224 | tf_op jit(solution)/shard_map/ppermute | solution.py:55
  107.0 1.9 collective-permute-start.11
  109.7 1.3 collective-permute-done.13
  111.0 2.9 %collective-permute-done.11 = f32[16,4,512]{2,1,0:T(4,128)S(1)} collective-permute-done((f32[16,4,512]{2,1,0:T(4,128)S(1)}, f32[16,4,512]{2,1,0:T(4,128)S(1)}, u32[]{:S(2)}, u32[]{:S(2)}) %collective-permute-start.11) | collective-permute-done | bytes 131104 | tf_op jit(solution)/shard_map/ppermute | solution.py:55
  114.2 1.9 collective-permute-start.14
  116.2 6.2 %collective-permute-start.15 = (f32[64,4,512]{2,1,0:T(4,128)S(1)}, f32[64,4,512]{2,1,0:T(4,128)S(1)}, u32[]{:S(2)}, u32[]{:S(2)}) collective-permute-start(f32[64,4,512]{2,1,0:T(4,128)S(1)} %pad_maximum_fusion.5), channel_id=1, source_target_pairs={{1,0},{2,1},{3,2},{4,3},{5,4},{6,5},{7,6},{8,7},{9,8},{10,9},{11,1... | collective-permute-start | bytes 1572872 | tf_op jit(solution)/shard_map/ppermute | solution.py:20
  123.0 1.3 slice.795
  124.3 1.3 slice.796
  125.6 0.9 add_multiply_fusion.2
  126.5 4.3 %collective-permute-done.14 = f32[64,4,512]{2,1,0:T(4,128)S(1)} collective-permute-done((f32[64,4,512]{2,1,0:T(4,128)S(1)}, f32[64,4,512]{2,1,0:T(4,128)S(1)}, u32[]{:S(2)}, u32[]{:S(2)}) %collective-permute-start.14) | collective-permute-done | bytes 524320 | tf_op jit(solution)/shard_map/ppermute | solution.py:20
  130.8 1.2 collective-permute-done.15
  132.8 1.6 fusion.13
  134.3 2.3 %slice_add_fusion = (f32[64,12,256]{2,1,0:T(8,128)}, f32[64,12,256]{2,1,0:T(8,128)S(1)}) fusion(f32[64,12,512]{2,1,0:T(8,128)S(1)} %pad_maximum_fusion.1, f32[64,12,256]{2,1,0:T(8,128)S(1)} %fusion.13, pred[12]{0:T(512)(128)(4,1)S(1)} %copy-done.48, s32[64,12]{1,0:T(8,128)S(1)} %iota_add_fusion.1), kind=kLoop, calls=%fused_computation.61 | loop fusion | flops 4718592 | bytes 3935244 | tf_op jit(solution)/shard_map/add | solution.py:162
  136.7 0.7 fusion.9
  138.8 1.9 collective-permute-start.16
  140.7 2.3 %collective-permute-start.17 = (f32[32,2,512]{2,1,0:T(2,128)S(1)}, f32[32,2,512]{2,1,0:T(2,128)S(1)}, u32[]{:S(2)}, u32[]{:S(2)}) collective-permute-start(f32[32,2,512]{2,1,0:T(2,128)S(1)} %pad_maximum_fusion.12), channel_id=1, source_target_pairs={{0,1},{1,2},{2,3},{3,4},{4,5},{5,6},{6,7},{7,8},{8,9},{9,10},{10,1... | collective-permute-start | bytes 393224 | tf_op jit(solution)/shard_map/ppermute | solution.py:20
  143.0 6.2 %collective-permute-start.18 = (f32[32,2,512]{2,1,0:T(2,128)S(1)}, f32[32,2,512]{2,1,0:T(2,128)S(1)}, u32[]{:S(2)}, u32[]{:S(2)}) collective-permute-start(f32[32,2,512]{2,1,0:T(2,128)S(1)} %pad_maximum_fusion.12), channel_id=1, source_target_pairs={{1,0},{2,1},{3,2},{4,3},{5,4},{6,5},{7,6},{8,7},{9,8},{10,9},{11,1... | collective-permute-start | bytes 393224 | tf_op jit(solution)/shard_map/ppermute | solution.py:20
  149.1 5.0 %collective-permute-start.19 = (f32[32,2,512]{2,1,0:T(2,128)S(1)}, f32[32,2,512]{2,1,0:T(2,128)}, u32[]{:S(2)}, u32[]{:S(2)}) collective-permute-start(f32[32,2,512]{2,1,0:T(2,128)S(1)} %pad_maximum_fusion.12), channel_id=1, source_target_pairs={{2,0},{3,1},{4,2},{5,3},{6,4},{7,5},{8,6},{9,7},{10,8},{11,9},{12,... | collective-permute-start | bytes 393224 | tf_op jit(solution)/shard_map/ppermute | solution.py:20
  154.1 1.3 compare_and_fusion.1
  156.2 0.7 copy-done.37
  156.8 1.0 collective-permute-done.19
  157.9 2.3 %concatenate.50 = f32[32,10,512]{2,1,0:T(8,128)S(1)} concatenate(f32[32,2,512]{2,1,0:T(2,128)} %copy-done.35, f32[32,2,512]{2,1,0:T(2,128)} %copy-done.36, f32[32,2,512]{2,1,0:T(2,128)} %copy-done.31, f32[32,2,512]{2,1,0:T(2,128)} %copy-done.37, f32[32,2,512]{2,1,0:T(2,128)} %collective-permute-done.19), dimensions={1} | concatenate | bytes 1310720 | tf_op jit(solution)/shard_map/concatenate | solution.py:40
  163.3 1.1 slice_select_fusion.4
  164.4 1.9 collective-permute-start.20
  166.3 3.2 %collective-permute-start.21 = (f32[32,2,256]{2,1,0:T(2,128)S(1)}, f32[32,2,256]{2,1,0:T(2,128)S(1)}, u32[]{:S(2)}, u32[]{:S(2)}) collective-permute-start(f32[32,2,256]{2,1,0:T(2,128)S(1)} %slice_select_fusion.4), channel_id=1, source_target_pairs={{0,1},{1,2},{2,3},{3,4},{4,5},{5,6},{6,7},{7,8},{8,9},{9,10},{10,1... | collective-permute-start | bytes 196616 | tf_op jit(solution)/shard_map/ppermute | solution.py:20
  169.6 4.8 %collective-permute-start.22 = (f32[32,2,256]{2,1,0:T(2,128)S(1)}, f32[32,2,256]{2,1,0:T(2,128)S(1)}, u32[]{:S(2)}, u32[]{:S(2)}) collective-permute-start(f32[32,2,256]{2,1,0:T(2,128)S(1)} %slice_select_fusion.4), channel_id=1, source_target_pairs={{1,0},{2,1},{3,2},{4,3},{5,4},{6,5},{7,6},{8,7},{9,8},{10,9},{11,1... | collective-permute-start | bytes 196616 | tf_op jit(solution)/shard_map/ppermute | solution.py:20
  174.4 5.3 %collective-permute-start.23 = (f32[32,2,256]{2,1,0:T(2,128)S(1)}, f32[32,2,256]{2,1,0:T(2,128)}, u32[]{:S(2)}, u32[]{:S(2)}) collective-permute-start(f32[32,2,256]{2,1,0:T(2,128)S(1)} %slice_select_fusion.4), channel_id=1, source_target_pairs={{2,0},{3,1},{4,2},{5,3},{6,4},{7,5},{8,6},{9,7},{10,8},{11,9},{12,... | collective-permute-start | bytes 196616 | tf_op jit(solution)/shard_map/ppermute | solution.py:20
  181.0 0.9 collective-permute-done.23
  181.9 3.4 %concatenate.51 = f32[32,10,256]{2,1,0:T(8,128)} concatenate(f32[32,2,256]{2,1,0:T(2,128)} %copy-done.42, f32[32,2,256]{2,1,0:T(2,128)} %copy-done.43, f32[32,2,256]{2,1,0:T(2,128)} %copy-done.32, f32[32,2,256]{2,1,0:T(2,128)} %copy-done.44, f32[32,2,256]{2,1,0:T(2,128)} %collective-permute-done.23), dimensions={1} | concatenate | bytes 655360 | tf_op jit(solution)/shard_map/concatenate | solution.py:40
  185.3 3.3 %fusion.62 = f32[32,10,256]{2,1,0:T(8,128)S(1)} fusion(f32[32,10,256]{2,1,0:T(8,128)} %concatenate.51, f32[32,10,512]{2,1,0:T(8,128)S(1)} %concatenate.50, pred[10]{0:T(512)(128)(4,1)} %compare_and_fusion.4, s32[32,10]{1,0:T(8,128)S(1)} %iota_add_fusion.3), kind=kLoop, calls=%fused_computation.176 | loop fusion | flops 1966080 | bytes 1312010 | tf_op jit(solution)/shard_map/jit(_where)/select_n | solution.py:109
  189.7 1.3 slice_select_fusion.3
  191.1 1.0 broadcast_in_dim.40
  192.0 2.2 %reshape.202 = f32[64,8,256]{2,1,0:T(8,128)} reshape(f32[64,4,2,256]{3,2,1,0:T(2,128)} %broadcast_in_dim.40) | data formatting | bytes 1048576 | tf_op jit(solution)/shard_map/reshape | solution.py:137
  194.3 1.3 slice_add_fusion.2
  195.6 2.1 fusion.70
  197.7 0.8 fusion.74
  198.6 1.9 collective-permute-start.24
  200.6 6.3 %collective-permute-start.25 = (f32[64,2,256]{2,1,0:T(2,128)S(1)}, f32[64,2,256]{2,1,0:T(2,128)S(1)}, u32[]{:S(2)}, u32[]{:S(2)}) collective-permute-start(f32[64,2,256]{2,1,0:T(2,128)S(1)} %get-tuple-element.29), channel_id=1, source_target_pairs={{1,0},{2,1},{3,2},{4,3},{5,4},{6,5},{7,6},{8,7},{9,8},{10,9},{11,1... | collective-permute-start | bytes 393224 | tf_op jit(solution)/shard_map/ppermute | solution.py:20
  207.6 1.5 collective-permute-done.25
  211.6 0.7 fusion.112
  212.9 1.0 slice_select_fusion.1
  (205 shorter events, 18.9 us)
Async XLA Ops:
  2.5 11.1 %copy-start = (f32[16,16,1024]{2,1,0:T(8,128)S(1)}, f32[16,16,1024]{2,1,0:T(8,128)}, u32[]{:S(2)}) copy-start(f32[16,16,1024]{2,1,0:T(8,128)} %shard_map.46) | copy-start | bytes 3145732
  3.7 4.3 %collective-permute-start = (f32[4,16,1024]{2,1,0:T(8,128)S(1)}, f32[4,16,1024]{2,1,0:T(8,128)S(1)}, u32[]{:S(2)}, u32[]{:S(2)}) collective-permute-start(f32[4,16,1024]{2,1,0:T(8,128)S(1)} %get-tuple-element.19), channel_id=1, source_target_pairs={{0,64},{64,128},{128,192},{192,256},{256,320},{320,384},{384,448},... | collective-permute-start | bytes 786440 | tf_op jit(solution)/shard_map/ppermute | solution.py:20
  5.4 8.1 %collective-permute-start.1 = (f32[4,16,1024]{2,1,0:T(8,128)S(1)}, f32[4,16,1024]{2,1,0:T(8,128)S(1)}, u32[]{:S(2)}, u32[]{:S(2)}) collective-permute-start(f32[4,16,1024]{2,1,0:T(8,128)S(1)} %get-tuple-element.20), channel_id=1, source_target_pairs={{64,0},{128,64},{192,128},{256,192},{320,256},{384,320},{448,384},... | collective-permute-start | bytes 786440 | tf_op jit(solution)/shard_map/ppermute | solution.py:20
  6.9 63.4 %copy-start.40 = (pred[16,16]{1,0:T(8,128)(4,1)}, pred[16,16]{1,0:T(8,128)(4,1)S(1)}, u32[]{:S(2)}) copy-start(pred[16,16]{1,0:T(8,128)(4,1)S(1)} %broadcast_and_fusion.1) | copy-start | bytes 772
  6.9 33.0 %copy-start.38 = (s32[20,20]{1,0:T(8,128)}, s32[20,20]{1,0:T(8,128)S(1)}, u32[]{:S(2)}) copy-start(s32[20,20]{1,0:T(8,128)S(1)} %iota_add_fusion.5) | copy-start | bytes 4804
  13.7 24.8 %collective-permute-start.2 = (f32[24,4,1024]{2,1,0:T(4,128)S(1)}, f32[24,4,1024]{2,1,0:T(4,128)S(1)}, u32[]{:S(2)}, u32[]{:S(2)}) collective-permute-start(f32[24,4,1024]{2,1,0:T(4,128)S(1)} %get-tuple-element.14), channel_id=1, source_target_pairs={{0,1},{1,2},{2,3},{3,4},{4,5},{5,6},{6,7},{7,8},{8,9},{9,10},{10,1... | collective-permute-start | bytes 1179656 | tf_op jit(solution)/shard_map/ppermute | solution.py:20
  18.0 21.9 %collective-permute-start.3 = (f32[24,4,1024]{2,1,0:T(4,128)S(1)}, f32[24,4,1024]{2,1,0:T(4,128)S(1)}, u32[]{:S(2)}, u32[]{:S(2)}) collective-permute-start(f32[24,4,1024]{2,1,0:T(4,128)S(1)} %get-tuple-element.15), channel_id=1, source_target_pairs={{1,0},{2,1},{3,2},{4,3},{5,4},{6,5},{7,6},{8,7},{9,8},{10,9},{11,1... | collective-permute-start | bytes 1179656 | tf_op jit(solution)/shard_map/ppermute | solution.py:20
  34.7 35.6 %copy-start.33 = (s32[16,16]{1,0:T(8,128)}, s32[16,16]{1,0:T(8,128)S(1)}, u32[]{:S(2)}) copy-start(s32[16,16]{1,0:T(8,128)S(1)} %iota_add_fusion.6) | copy-start | bytes 3076
  40.5 2.2 %copy-start.7 = (f32[24,24,256]{2,1,0:T(8,128)}, f32[24,24,256]{2,1,0:T(8,128)S(1)}, u32[]{:S(2)}) copy-start(f32[24,24,256]{2,1,0:T(8,128)S(1)} %get-tuple-element.11) | copy-start | bytes 1769476
  42.1 1.2 copy-start.5
  42.2 1.2 copy-start.20
  42.7 1.0 copy-start.29
  44.6 12.3 %collective-permute-start.4 = (f32[4,8,512]{2,1,0:T(8,128)S(1)}, f32[4,8,512]{2,1,0:T(8,128)S(1)}, u32[]{:S(2)}, u32[]{:S(2)}) collective-permute-start(f32[4,8,512]{2,1,0:T(8,128)S(1)} %get-tuple-element.72), channel_id=1, source_target_pairs={{0,64},{64,128},{128,192},{192,256},{256,320},{320,384},{384,448},... | collective-permute-start | bytes 196616 | tf_op jit(solution)/shard_map/ppermute | solution.py:20
  55.5 3.2 %collective-permute-start.5 = (f32[4,8,512]{2,1,0:T(8,128)S(1)}, f32[4,8,512]{2,1,0:T(8,128)S(1)}, u32[]{:S(2)}, u32[]{:S(2)}) collective-permute-start(f32[4,8,512]{2,1,0:T(8,128)S(1)} %get-tuple-element.73), channel_id=1, source_target_pairs={{64,0},{128,64},{192,128},{256,192},{320,256},{384,320},{448,384},... | collective-permute-start | bytes 196616 | tf_op jit(solution)/shard_map/ppermute | solution.py:20
  58.9 10.1 %collective-permute-start.6 = (f32[16,4,512]{2,1,0:T(4,128)S(1)}, f32[16,4,512]{2,1,0:T(4,128)S(1)}, u32[]{:S(2)}, u32[]{:S(2)}) collective-permute-start(f32[16,4,512]{2,1,0:T(4,128)S(1)} %get-tuple-element.64), channel_id=1, source_target_pairs={{0,1},{1,2},{2,3},{3,4},{4,5},{5,6},{6,7},{7,8},{8,9},{9,10},{10,1... | collective-permute-start | bytes 393224 | tf_op jit(solution)/shard_map/ppermute | solution.py:20
  60.8 9.0 %collective-permute-start.7 = (f32[16,4,512]{2,1,0:T(4,128)S(1)}, f32[16,4,512]{2,1,0:T(4,128)S(1)}, u32[]{:S(2)}, u32[]{:S(2)}) collective-permute-start(f32[16,4,512]{2,1,0:T(4,128)S(1)} %get-tuple-element.65), channel_id=1, source_target_pairs={{1,0},{2,1},{3,2},{4,3},{5,4},{6,5},{7,6},{8,7},{9,8},{10,9},{11,1... | collective-permute-start | bytes 393224 | tf_op jit(solution)/shard_map/ppermute | solution.py:20
  71.2 20.6 %collective-permute-start.8 = (f32[4,4,512]{2,1,0:T(4,128)S(1)}, f32[4,4,512]{2,1,0:T(4,128)S(1)}, u32[]{:S(2)}, u32[]{:S(2)}) collective-permute-start(f32[4,4,512]{2,1,0:T(4,128)S(1)} %get-tuple-element.75), channel_id=1, source_target_pairs={{0,64},{64,0},{128,192},{192,128},{256,320},{320,256},{384,448},{4... | collective-permute-start | bytes 98312 | tf_op jit(solution)/shard_map/ppermute | solution.py:55
  79.6 12.4 %collective-permute-start.9 = (f32[4,4,512]{2,1,0:T(4,128)S(1)}, f32[4,4,512]{2,1,0:T(4,128)S(1)}, u32[]{:S(2)}, u32[]{:S(2)}) collective-permute-start(f32[4,4,512]{2,1,0:T(4,128)S(1)} %get-tuple-element.75), channel_id=1, source_target_pairs={{0,128},{64,192},{128,0},{192,64},{256,384},{320,448},{384,256},{4... | collective-permute-start | bytes 98312 | tf_op jit(solution)/shard_map/ppermute | solution.py:55
  89.8 9.4 %collective-permute-start.10 = (f32[4,4,512]{2,1,0:T(4,128)S(1)}, f32[4,4,512]{2,1,0:T(4,128)S(1)}, u32[]{:S(2)}, u32[]{:S(2)}) collective-permute-start(f32[4,4,512]{2,1,0:T(4,128)S(1)} %get-tuple-element.75), channel_id=1, source_target_pairs={{0,192},{64,128},{128,64},{192,0},{256,448},{320,384},{384,320},{4... | collective-permute-start | bytes 98312 | tf_op jit(solution)/shard_map/ppermute | solution.py:55
  99.3 10.3 %collective-permute-start.12 = (f32[16,4,512]{2,1,0:T(4,128)S(1)}, f32[16,4,512]{2,1,0:T(4,128)S(1)}, u32[]{:S(2)}, u32[]{:S(2)}) collective-permute-start(f32[16,4,512]{2,1,0:T(4,128)S(1)} %get-tuple-element.67), channel_id=1, source_target_pairs={{0,512},{64,576},{128,640},{192,704},{256,768},{320,832},{384,896}... | collective-permute-start | bytes 393224 | tf_op jit(solution)/shard_map/ppermute | solution.py:55
  101.3 9.7 %collective-permute-start.13 = (f32[16,4,512]{2,1,0:T(4,128)S(1)}, f32[16,4,512]{2,1,0:T(4,128)S(1)}, u32[]{:S(2)}, u32[]{:S(2)}) collective-permute-start(f32[16,4,512]{2,1,0:T(4,128)S(1)} %get-tuple-element.67), channel_id=1, source_target_pairs={{0,768},{64,832},{128,896},{192,960},{256,512},{320,576},{384,640}... | collective-permute-start | bytes 393224 | tf_op jit(solution)/shard_map/ppermute | solution.py:55
  107.0 6.9 %collective-permute-start.11 = (f32[16,4,512]{2,1,0:T(4,128)S(1)}, f32[16,4,512]{2,1,0:T(4,128)S(1)}, u32[]{:S(2)}, u32[]{:S(2)}) collective-permute-start(f32[16,4,512]{2,1,0:T(4,128)S(1)} %get-tuple-element.67), channel_id=1, source_target_pairs={{0,256},{64,320},{128,384},{192,448},{256,0},{320,64},{384,128},{4... | collective-permute-start | bytes 393224 | tf_op jit(solution)/shard_map/ppermute | solution.py:55
  109.0 4.9 %copy-start.47 = (pred[12]{0:T(512)(128)(4,1)}, pred[12]{0:T(512)(128)(4,1)S(1)}, u32[]{:S(2)}) copy-start(pred[12]{0:T(512)(128)(4,1)S(1)} %compare_and_fusion.5) | copy-start | bytes 40
  114.1 18.3 %copy-start.10 = (f32[16,4,512]{2,1,0:T(4,128)}, f32[16,4,512]{2,1,0:T(4,128)S(1)}, u32[]{:S(2)}) copy-start(f32[16,4,512]{2,1,0:T(4,128)S(1)} %get-tuple-element.40) | copy-start | bytes 393220
  114.1 18.3 %copy-start.12 = (f32[16,4,512]{2,1,0:T(4,128)}, f32[16,4,512]{2,1,0:T(4,128)S(1)}, u32[]{:S(2)}) copy-start(f32[16,4,512]{2,1,0:T(4,128)S(1)} %get-tuple-element.41) | copy-start | bytes 393220
  114.1 18.3 %copy-start.14 = (f32[16,4,512]{2,1,0:T(4,128)}, f32[16,4,512]{2,1,0:T(4,128)S(1)}, u32[]{:S(2)}) copy-start(f32[16,4,512]{2,1,0:T(4,128)S(1)} %get-tuple-element.42) | copy-start | bytes 393220
  114.2 16.6 %collective-permute-start.14 = (f32[64,4,512]{2,1,0:T(4,128)S(1)}, f32[64,4,512]{2,1,0:T(4,128)S(1)}, u32[]{:S(2)}, u32[]{:S(2)}) collective-permute-start(f32[64,4,512]{2,1,0:T(4,128)S(1)} %pad_maximum_fusion.5), channel_id=1, source_target_pairs={{0,1},{1,2},{2,3},{3,4},{4,5},{5,6},{6,7},{7,8},{8,9},{9,10},{10,1... | collective-permute-start | bytes 1572872 | tf_op jit(solution)/shard_map/ppermute | solution.py:20
  116.2 15.8 %collective-permute-start.15 = (f32[64,4,512]{2,1,0:T(4,128)S(1)}, f32[64,4,512]{2,1,0:T(4,128)S(1)}, u32[]{:S(2)}, u32[]{:S(2)}) collective-permute-start(f32[64,4,512]{2,1,0:T(4,128)S(1)} %pad_maximum_fusion.5), channel_id=1, source_target_pairs={{1,0},{2,1},{3,2},{4,3},{5,4},{6,5},{7,6},{8,7},{9,8},{10,9},{11,1... | collective-permute-start | bytes 1572872 | tf_op jit(solution)/shard_map/ppermute | solution.py:20
  126.5 6.2 %copy-start.48 = (pred[12]{0:T(512)(128)(4,1)S(1)}, pred[12]{0:T(512)(128)(4,1)}, u32[]{:S(2)}) copy-start(pred[12]{0:T(512)(128)(4,1)} %copy-done.47) | copy-start | bytes 40
  130.8 1.7 copy-start.1
  137.4 16.7 %copy-start.45 = (pred[10]{0:T(512)(128)(4,1)S(1)}, pred[10]{0:T(512)(128)(4,1)}, u32[]{:S(2)}) copy-start(pred[10]{0:T(512)(128)(4,1)} %compare_and_fusion.4) | copy-start | bytes 34
  138.8 16.7 %copy-start.31 = (f32[32,2,512]{2,1,0:T(2,128)}, f32[32,2,512]{2,1,0:T(2,128)S(1)}, u32[]{:S(2)}) copy-start(f32[32,2,512]{2,1,0:T(2,128)S(1)} %pad_maximum_fusion.12) | copy-start | bytes 393220
  138.8 16.7 %collective-permute-start.16 = (f32[32,2,512]{2,1,0:T(2,128)S(1)}, f32[32,2,512]{2,1,0:T(2,128)S(1)}, u32[]{:S(2)}, u32[]{:S(2)}) collective-permute-start(f32[32,2,512]{2,1,0:T(2,128)S(1)} %pad_maximum_fusion.12), channel_id=1, source_target_pairs={{0,2},{1,3},{2,4},{3,5},{4,6},{5,7},{6,8},{7,9},{8,10},{9,11},{10,... | collective-permute-start | bytes 393224 | tf_op jit(solution)/shard_map/ppermute | solution.py:20
  140.7 14.8 %collective-permute-start.17 = (f32[32,2,512]{2,1,0:T(2,128)S(1)}, f32[32,2,512]{2,1,0:T(2,128)S(1)}, u32[]{:S(2)}, u32[]{:S(2)}) collective-permute-start(f32[32,2,512]{2,1,0:T(2,128)S(1)} %pad_maximum_fusion.12), channel_id=1, source_target_pairs={{0,1},{1,2},{2,3},{3,4},{4,5},{5,6},{6,7},{7,8},{8,9},{9,10},{10,1... | collective-permute-start | bytes 393224 | tf_op jit(solution)/shard_map/ppermute | solution.py:20
  143.0 12.5 %collective-permute-start.18 = (f32[32,2,512]{2,1,0:T(2,128)S(1)}, f32[32,2,512]{2,1,0:T(2,128)S(1)}, u32[]{:S(2)}, u32[]{:S(2)}) collective-permute-start(f32[32,2,512]{2,1,0:T(2,128)S(1)} %pad_maximum_fusion.12), channel_id=1, source_target_pairs={{1,0},{2,1},{3,2},{4,3},{5,4},{6,5},{7,6},{8,7},{9,8},{10,9},{11,1... | collective-permute-start | bytes 393224 | tf_op jit(solution)/shard_map/ppermute | solution.py:20
  149.1 8.7 %collective-permute-start.19 = (f32[32,2,512]{2,1,0:T(2,128)S(1)}, f32[32,2,512]{2,1,0:T(2,128)}, u32[]{:S(2)}, u32[]{:S(2)}) collective-permute-start(f32[32,2,512]{2,1,0:T(2,128)S(1)} %pad_maximum_fusion.12), channel_id=1, source_target_pairs={{2,0},{3,1},{4,2},{5,3},{6,4},{7,5},{8,6},{9,7},{10,8},{11,9},{12,... | collective-permute-start | bytes 393224 | tf_op jit(solution)/shard_map/ppermute | solution.py:20
  160.9 2.4 %copy-start.27 = (f32[32,10,256]{2,1,0:T(8,128)}, f32[32,10,256]{2,1,0:T(8,128)S(1)}, u32[]{:S(2)}) copy-start(f32[32,10,256]{2,1,0:T(8,128)S(1)} %get-tuple-element.16) | copy-start | bytes 983044
  160.9 2.4 %copy-start.28 = (f32[32,10,256]{2,1,0:T(8,128)}, f32[32,10,256]{2,1,0:T(8,128)S(1)}, u32[]{:S(2)}) copy-start(f32[32,10,256]{2,1,0:T(8,128)S(1)} %get-tuple-element.18) | copy-start | bytes 983044
  164.4 10.0 %copy-start.32 = (f32[32,2,256]{2,1,0:T(2,128)}, f32[32,2,256]{2,1,0:T(2,128)S(1)}, u32[]{:S(2)}) copy-start(f32[32,2,256]{2,1,0:T(2,128)S(1)} %slice_select_fusion.4) | copy-start | bytes 196612
  164.4 15.3 %collective-permute-start.20 = (f32[32,2,256]{2,1,0:T(2,128)S(1)}, f32[32,2,256]{2,1,0:T(2,128)S(1)}, u32[]{:S(2)}, u32[]{:S(2)}) collective-permute-start(f32[32,2,256]{2,1,0:T(2,128)S(1)} %slice_select_fusion.4), channel_id=1, source_target_pairs={{0,2},{1,3},{2,4},{3,5},{4,6},{5,7},{6,8},{7,9},{8,10},{9,11},{10,... | collective-permute-start | bytes 196616 | tf_op jit(solution)/shard_map/ppermute | solution.py:20
  166.3 13.4 %collective-permute-start.21 = (f32[32,2,256]{2,1,0:T(2,128)S(1)}, f32[32,2,256]{2,1,0:T(2,128)S(1)}, u32[]{:S(2)}, u32[]{:S(2)}) collective-permute-start(f32[32,2,256]{2,1,0:T(2,128)S(1)} %slice_select_fusion.4), channel_id=1, source_target_pairs={{0,1},{1,2},{2,3},{3,4},{4,5},{5,6},{6,7},{7,8},{8,9},{9,10},{10,1... | collective-permute-start | bytes 196616 | tf_op jit(solution)/shard_map/ppermute | solution.py:20
  169.6 10.2 %collective-permute-start.22 = (f32[32,2,256]{2,1,0:T(2,128)S(1)}, f32[32,2,256]{2,1,0:T(2,128)S(1)}, u32[]{:S(2)}, u32[]{:S(2)}) collective-permute-start(f32[32,2,256]{2,1,0:T(2,128)S(1)} %slice_select_fusion.4), channel_id=1, source_target_pairs={{1,0},{2,1},{3,2},{4,3},{5,4},{6,5},{7,6},{8,7},{9,8},{10,9},{11,1... | collective-permute-start | bytes 196616 | tf_op jit(solution)/shard_map/ppermute | solution.py:20
  174.4 7.5 %collective-permute-start.23 = (f32[32,2,256]{2,1,0:T(2,128)S(1)}, f32[32,2,256]{2,1,0:T(2,128)}, u32[]{:S(2)}, u32[]{:S(2)}) collective-permute-start(f32[32,2,256]{2,1,0:T(2,128)S(1)} %slice_select_fusion.4), channel_id=1, source_target_pairs={{2,0},{3,1},{4,2},{5,3},{6,4},{7,5},{8,6},{9,7},{10,8},{11,9},{12,... | collective-permute-start | bytes 196616 | tf_op jit(solution)/shard_map/ppermute | solution.py:20
  185.3 3.3 %copy-start.46 = (pred[10]{0:T(512)(128)(4,1)S(1)}, pred[10]{0:T(512)(128)(4,1)}, u32[]{:S(2)}) copy-start(pred[10]{0:T(512)(128)(4,1)} %compare_and_fusion.4) | copy-start | bytes 34
  191.0 4.6 %copy-start.2 = (f32[64,4,512]{2,1,0:T(4,128)S(1)}, f32[64,4,512]{2,1,0:T(4,128)}, u32[]{:S(2)}) copy-start(f32[64,4,512]{2,1,0:T(4,128)} %copy-done.1) | copy-start | bytes 1572868
  191.0 4.6 %copy-start.4 = (f32[64,4,512]{2,1,0:T(4,128)S(1)}, f32[64,4,512]{2,1,0:T(4,128)}, u32[]{:S(2)}) copy-start(f32[64,4,512]{2,1,0:T(4,128)} %copy-done.3) | copy-start | bytes 1572868
  191.0 4.6 %copy-start.49 = (pred[8]{0:T(512)(128)(4,1)S(1)}, pred[8]{0:T(512)(128)(4,1)}, u32[]{:S(2)}) copy-start(pred[8]{0:T(512)(128)(4,1)} %slice.745) | copy-start | bytes 28
  194.3 3.4 %copy-start.9 = (f32[64,12,256]{2,1,0:T(8,128)S(1)}, f32[64,12,256]{2,1,0:T(8,128)}, u32[]{:S(2)}) copy-start(f32[64,12,256]{2,1,0:T(8,128)} %get-tuple-element.12) | copy-start | bytes 2359300
  194.3 3.4 %copy-start.11 = (f32[16,4,512]{2,1,0:T(4,128)S(1)}, f32[16,4,512]{2,1,0:T(4,128)}, u32[]{:S(2)}) copy-start(f32[16,4,512]{2,1,0:T(4,128)} %copy-done.10) | copy-start | bytes 393220
  194.3 3.4 %copy-start.13 = (f32[16,4,512]{2,1,0:T(4,128)S(1)}, f32[16,4,512]{2,1,0:T(4,128)}, u32[]{:S(2)}) copy-start(f32[16,4,512]{2,1,0:T(4,128)} %copy-done.12) | copy-start | bytes 393220
  194.3 3.4 %copy-start.15 = (f32[16,4,512]{2,1,0:T(4,128)S(1)}, f32[16,4,512]{2,1,0:T(4,128)}, u32[]{:S(2)}) copy-start(f32[16,4,512]{2,1,0:T(4,128)} %copy-done.14) | copy-start | bytes 393220
  197.7 9.1 %copy-start.34 = (s32[16,16]{1,0:T(8,128)S(1)}, s32[16,16]{1,0:T(8,128)}, u32[]{:S(2)}) copy-start(s32[16,16]{1,0:T(8,128)} %copy-done.33) | copy-start | bytes 3076
  197.7 9.1 %copy-start.41 = (pred[16,16]{1,0:T(8,128)(4,1)S(1)}, pred[16,16]{1,0:T(8,128)(4,1)}, u32[]{:S(2)}) copy-start(pred[16,16]{1,0:T(8,128)(4,1)} %copy-done.40) | copy-start | bytes 772
  198.6 9.0 %collective-permute-start.24 = (f32[64,2,256]{2,1,0:T(2,128)S(1)}, f32[64,2,256]{2,1,0:T(2,128)S(1)}, u32[]{:S(2)}, u32[]{:S(2)}) collective-permute-start(f32[64,2,256]{2,1,0:T(2,128)S(1)} %get-tuple-element.30), channel_id=1, source_target_pairs={{0,1},{1,2},{2,3},{3,4},{4,5},{5,6},{6,7},{7,8},{8,9},{9,10},{10,1... | collective-permute-start | bytes 393224 | tf_op jit(solution)/shard_map/ppermute | solution.py:20
  200.6 8.5 %collective-permute-start.25 = (f32[64,2,256]{2,1,0:T(2,128)S(1)}, f32[64,2,256]{2,1,0:T(2,128)S(1)}, u32[]{:S(2)}, u32[]{:S(2)}) collective-permute-start(f32[64,2,256]{2,1,0:T(2,128)S(1)} %get-tuple-element.29), channel_id=1, source_target_pairs={{1,0},{2,1},{3,2},{4,3},{5,4},{6,5},{7,6},{8,7},{9,8},{10,9},{11,1... | collective-permute-start | bytes 393224 | tf_op jit(solution)/shard_map/ppermute | solution.py:20
  209.2 1.0 copy-start.23
  209.2 1.0 copy-start.25
  210.3 1.1 copy-start.6
  210.4 1.2 copy-start.8
  210.4 1.2 copy-start.39
  211.6 1.1 copy-start.17
  211.6 1.2 copy-start.19
  211.6 1.3 copy-start.26
  211.6 1.3 copy-start.30
  (12 other events, 8.9 us)

commit v11 on v9

--- a/solution.py
+++ b/solution.py
@@ -22,10 +22,10 @@
 
 def exchange(block, width):
     block = jnp.concatenate(
+        [shifted(block[:, -width:], "gy", 1), block, shifted(block[:, :width], "gy", -1)], axis=1
+    )
+    return jnp.concatenate(
         [shifted(block[-width:], "gx", 1), block, shifted(block[:width], "gx", -1)], axis=0
-    )
-    return jnp.concatenate(
-        [shifted(block[:, -width:], "gy", 1), block, shifted(block[:, :width], "gy", -1)], axis=1
     )
 
 

time: 204 us -> 211 us (1.034)
  starting transfers between devices: 121 us -> 126 us
    ppermute x20, starting transfers between devices: 91.4 us -> 94.9 us  [shifted(): return lax.ppermute(block, axis, route)]
  transfers between devices with their start and end apart: 26 -> 26, of which waited for: 16 -> 15; matrix products, arithmetic and copies ran while one was open for 2% -> 2% of each run, Pallas kernels for 0% -> 0%
where the time goes in v11:
time: 211 us; the launch traced here: 210 us
  starting transfers between devices  126 us (60%)
  waiting for transfers between devices  45.1 us (21%)
  other arithmetic  23.1 us (11%)
  local copies, waits for them, and re-layouts  11.1 us (5%)
  Pallas kernels  2.56 us (1%)
    ppermute x20, starting transfers between devices, shifted(): return lax.ppermute(block, axis, route)  94.9 us
    ppermute x20, waiting for transfers between devices, shifted(): return lax.ppermute(block, axis, route)  32.9 us
    ppermute x6, starting transfers between devices, gather_x(): lax.ppermute(block, 'gx', [(i, i ^ m * group) for i in range(count)])  31.5 us
    ppermute x6, waiting for transfers between devices, gather_x(): lax.ppermute(block, 'gx', [(i, i ^ m * group) for i in range(count)])  12.2 us
    select_n x17, other arithmetic, half_sweep(): return jnp.where(update, renewed, iterate)  10 us
  transfers between devices with their start and end apart: 26, of which 15 were waited for; matrix products, arithmetic and copies ran while one was open for 2% of the time, Pallas kernels for 0%

profile of v11, /device:TPU:8, one launch (start us, length us, event | category | flops | bytes accessed | tf_op | source)
XLA Modules:
  0.0 209.8 jit_solution(2047865366004585487)
XLA Ops:
  0.0 2.6 %shard_map.46 = f32[16,16,1024]{2,1,0:T(8,128)} custom-call(f32[16]{0:T(128)} %volts_ref.1, f32[16,16,256]{2,1,0:T(8,128)} %potential_ref.1, f32[16,16,256]{2,1,0:T(8,128)} %charge_ref.1, s32[16,16,256]{2,1,0:T(8,128)} %region_ref.1), custom_call_target="tpu_custom_call" | custom-call | tf_op jit(solution)/shard_map/pallas_call | solution.py:211
  2.6 1.4 fusion.218
  4.0 4.3 %collective-permute-start = (f32[16,4,1024]{2,1,0:T(4,128)S(1)}, f32[16,4,1024]{2,1,0:T(4,128)S(1)}, u32[]{:S(2)}, u32[]{:S(2)}) collective-permute-start(f32[16,4,1024]{2,1,0:T(4,128)S(1)} %get-tuple-element.14), channel_id=1, source_target_pairs={{0,1},{1,2},{2,3},{3,4},{4,5},{5,6},{6,7},{7,8},{8,9},{9,10},{10,1... | collective-permute-start | bytes 786440 | tf_op jit(solution)/shard_map/ppermute | solution.py:20
  8.3 15.8 %collective-permute-start.1 = (f32[16,4,1024]{2,1,0:T(4,128)S(1)}, f32[16,4,1024]{2,1,0:T(4,128)S(1)}, u32[]{:S(2)}, u32[]{:S(2)}) collective-permute-start(f32[16,4,1024]{2,1,0:T(4,128)S(1)} %get-tuple-element.15), channel_id=1, source_target_pairs={{1,0},{2,1},{3,2},{4,3},{5,4},{6,5},{7,6},{8,7},{9,8},{10,9},{11,1... | collective-permute-start | bytes 786440 | tf_op jit(solution)/shard_map/ppermute | solution.py:20
  24.2 4.2 %collective-permute-done = f32[16,4,1024]{2,1,0:T(4,128)S(1)} collective-permute-done((f32[16,4,1024]{2,1,0:T(4,128)S(1)}, f32[16,4,1024]{2,1,0:T(4,128)S(1)}, u32[]{:S(2)}, u32[]{:S(2)}) %collective-permute-start) | collective-permute-done | bytes 262176 | tf_op jit(solution)/shard_map/ppermute | solution.py:20
  28.4 1.1 collective-permute-done.1
  29.7 1.3 collective-permute-start.2
  31.0 1.3 collective-permute-start.3
  32.4 8.2 %collective-permute-done.3 = f32[4,24,1024]{2,1,0:T(8,128)S(1)} collective-permute-done((f32[4,24,1024]{2,1,0:T(8,128)S(1)}, f32[4,24,1024]{2,1,0:T(8,128)S(1)}, u32[]{:S(2)}, u32[]{:S(2)}) %collective-permute-start.3) | collective-permute-done | bytes 393248 | tf_op jit(solution)/shard_map/ppermute | solution.py:20
  41.1 1.6 fusion.58
  42.7 0.8 fusion.62
  43.5 0.4 fusion.74
  45.1 1.9 collective-permute-start.4
  47.0 6.5 %collective-permute-start.5 = (f32[8,4,512]{2,1,0:T(4,128)S(1)}, f32[8,4,512]{2,1,0:T(4,128)S(1)}, u32[]{:S(2)}, u32[]{:S(2)}) collective-permute-start(f32[8,4,512]{2,1,0:T(4,128)S(1)} %get-tuple-element.66), channel_id=1, source_target_pairs={{1,0},{2,1},{3,2},{4,3},{5,4},{6,5},{7,6},{8,7},{9,8},{10,9},{11,1... | collective-permute-start | bytes 196616 | tf_op jit(solution)/shard_map/ppermute | solution.py:20
  53.9 1.6 collective-permute-done.5
  55.5 16.0 %collective-permute-start.6 = (f32[4,16,512]{2,1,0:T(8,128)S(1)}, f32[4,16,512]{2,1,0:T(8,128)S(1)}, u32[]{:S(2)}, u32[]{:S(2)}) collective-permute-start(f32[4,16,512]{2,1,0:T(8,128)S(1)} %get-tuple-element.57), channel_id=1, source_target_pairs={{0,64},{64,128},{128,192},{192,256},{256,320},{320,384},{384,448},... | collective-permute-start | bytes 393224 | tf_op jit(solution)/shard_map/ppermute | solution.py:20
  71.5 1.3 collective-permute-start.7
  72.8 2.4 %collective-permute-done.7 = f32[4,16,512]{2,1,0:T(8,128)S(1)} collective-permute-done((f32[4,16,512]{2,1,0:T(8,128)S(1)}, f32[4,16,512]{2,1,0:T(8,128)S(1)}, u32[]{:S(2)}, u32[]{:S(2)}) %collective-permute-start.7) | collective-permute-done | bytes 131104 | tf_op jit(solution)/shard_map/ppermute | solution.py:20
  76.3 0.5 copy-done.9
  77.0 10.1 %collective-permute-start.8 = (f32[4,4,512]{2,1,0:T(4,128)S(1)}, f32[4,4,512]{2,1,0:T(4,128)S(1)}, u32[]{:S(2)}, u32[]{:S(2)}) collective-permute-start(f32[4,4,512]{2,1,0:T(4,128)S(1)} %get-tuple-element.68), channel_id=1, source_target_pairs={{0,64},{64,0},{128,192},{192,128},{256,320},{320,256},{384,448},{4... | collective-permute-start | bytes 98312 | tf_op jit(solution)/shard_map/ppermute | solution.py:55
  87.1 8.1 %collective-permute-start.9 = (f32[4,4,512]{2,1,0:T(4,128)S(1)}, f32[4,4,512]{2,1,0:T(4,128)S(1)}, u32[]{:S(2)}, u32[]{:S(2)}) collective-permute-start(f32[4,4,512]{2,1,0:T(4,128)S(1)} %get-tuple-element.68), channel_id=1, source_target_pairs={{0,128},{64,192},{128,0},{192,64},{256,384},{320,448},{384,256},{4... | collective-permute-start | bytes 98312 | tf_op jit(solution)/shard_map/ppermute | solution.py:55
  95.2 1.9 collective-permute-start.10
  97.2 7.4 %collective-permute-done.10 = f32[4,4,512]{2,1,0:T(4,128)S(1)} collective-permute-done((f32[4,4,512]{2,1,0:T(4,128)S(1)}, f32[4,4,512]{2,1,0:T(4,128)S(1)}, u32[]{:S(2)}, u32[]{:S(2)}) %collective-permute-start.10) | collective-permute-done | bytes 32800 | tf_op jit(solution)/shard_map/ppermute | solution.py:55
  104.8 5.7 %collective-permute-start.12 = (f32[16,4,512]{2,1,0:T(4,128)S(1)}, f32[16,4,512]{2,1,0:T(4,128)S(1)}, u32[]{:S(2)}, u32[]{:S(2)}) collective-permute-start(f32[16,4,512]{2,1,0:T(4,128)S(1)} %get-tuple-element.60), channel_id=1, source_target_pairs={{0,512},{64,576},{128,640},{192,704},{256,768},{320,832},{384,896}... | collective-permute-start | bytes 393224 | tf_op jit(solution)/shard_map/ppermute | solution.py:55
  110.5 3.8 %collective-permute-start.13 = (f32[16,4,512]{2,1,0:T(4,128)S(1)}, f32[16,4,512]{2,1,0:T(4,128)S(1)}, u32[]{:S(2)}, u32[]{:S(2)}) collective-permute-start(f32[16,4,512]{2,1,0:T(4,128)S(1)} %get-tuple-element.60), channel_id=1, source_target_pairs={{0,768},{64,832},{128,896},{192,960},{256,512},{320,576},{384,640}... | collective-permute-start | bytes 393224 | tf_op jit(solution)/shard_map/ppermute | solution.py:55
  114.2 1.9 collective-permute-start.11
  116.2 2.5 %collective-permute-done.13 = f32[16,4,512]{2,1,0:T(4,128)S(1)} collective-permute-done((f32[16,4,512]{2,1,0:T(4,128)S(1)}, f32[16,4,512]{2,1,0:T(4,128)S(1)}, u32[]{:S(2)}, u32[]{:S(2)}) %collective-permute-start.13) | collective-permute-done | bytes 131104 | tf_op jit(solution)/shard_map/ppermute | solution.py:55
  118.8 2.3 %collective-permute-done.11 = f32[16,4,512]{2,1,0:T(4,128)S(1)} collective-permute-done((f32[16,4,512]{2,1,0:T(4,128)S(1)}, f32[16,4,512]{2,1,0:T(4,128)S(1)}, u32[]{:S(2)}, u32[]{:S(2)}) %collective-permute-start.11) | collective-permute-done | bytes 131104 | tf_op jit(solution)/shard_map/ppermute | solution.py:55
  121.5 1.9 collective-permute-start.14
  123.4 6.0 %collective-permute-start.15 = (f32[64,4,512]{2,0,1:T(8,128)S(1)}, f32[64,4,512]{2,0,1:T(8,128)}, u32[]{:S(2)}, u32[]{:S(2)}) collective-permute-start(f32[64,4,512]{2,0,1:T(8,128)S(1)} %pad_maximum_fusion.4), channel_id=1, source_target_pairs={{1,0},{2,1},{3,2},{4,3},{5,4},{6,5},{7,6},{8,7},{9,8},{10,9},{11,1... | collective-permute-start | bytes 1572872 | tf_op jit(solution)/shard_map/ppermute | solution.py:20
  129.5 0.6 compare_and_fusion.6
  130.2 0.6 add_multiply_fusion.2
  130.9 6.8 %collective-permute-done.14 = f32[64,4,512]{2,0,1:T(8,128)S(1)} collective-permute-done((f32[64,4,512]{2,0,1:T(8,128)S(1)}, f32[64,4,512]{2,0,1:T(8,128)S(1)}, u32[]{:S(2)}, u32[]{:S(2)}) %collective-permute-start.14) | collective-permute-done | bytes 524320 | tf_op jit(solution)/shard_map/ppermute | solution.py:20
  137.7 0.8 copy-done.21
  138.8 1.4 pad_maximum_fusion.1
  140.3 0.9 fusion.40
  141.2 0.9 fusion.8
  142.1 0.5 fusion.16
  144.0 0.9 pad_maximum_fusion.11
  144.8 1.9 collective-permute-start.16
  146.8 1.6 compare_and_fusion.3
  148.4 1.9 collective-permute-start.17
  150.3 6.6 %collective-permute-start.18 = (f32[32,2,512]{2,0,1:T(8,128)S(1)}, f32[32,2,512]{2,0,1:T(8,128)S(1)}, u32[]{:S(2)}, u32[]{:S(2)}) collective-permute-start(f32[32,2,512]{2,0,1:T(8,128)S(1)} %pad_maximum_fusion.11), channel_id=1, source_target_pairs={{1,0},{2,1},{3,2},{4,3},{5,4},{6,5},{7,6},{8,7},{9,8},{10,9},{11,1... | collective-permute-start | bytes 393224 | tf_op jit(solution)/shard_map/ppermute | solution.py:20
  156.9 5.0 %collective-permute-start.19 = (f32[32,2,512]{2,0,1:T(8,128)S(1)}, f32[32,2,512]{2,0,1:T(8,128)S(1)}, u32[]{:S(2)}, u32[]{:S(2)}) collective-permute-start(f32[32,2,512]{2,0,1:T(8,128)S(1)} %pad_maximum_fusion.11), channel_id=1, source_target_pairs={{2,0},{3,1},{4,2},{5,3},{6,4},{7,5},{8,6},{9,7},{10,8},{11,9},{12,... | collective-permute-start | bytes 393224 | tf_op jit(solution)/shard_map/ppermute | solution.py:20
  162.0 3.6 %collective-permute-done.19 = f32[32,2,512]{2,0,1:T(8,128)S(1)} collective-permute-done((f32[32,2,512]{2,0,1:T(8,128)S(1)}, f32[32,2,512]{2,0,1:T(8,128)S(1)}, u32[]{:S(2)}, u32[]{:S(2)}) %collective-permute-start.19) | collective-permute-done | bytes 131104 | tf_op jit(solution)/shard_map/ppermute | solution.py:20
  167.7 1.9 collective-permute-start.20
  169.7 1.0 add_select_fusion.2
  170.7 2.0 collective-permute-start.21
  172.7 5.9 %collective-permute-start.22 = (f32[32,2,256]{2,0,1:T(8,128)S(1)}, f32[32,2,256]{2,0,1:T(8,128)S(1)}, u32[]{:S(2)}, u32[]{:S(2)}) collective-permute-start(f32[32,2,256]{2,0,1:T(8,128)S(1)} %slice_select_fusion.3), channel_id=1, source_target_pairs={{1,0},{2,1},{3,2},{4,3},{5,4},{6,5},{7,6},{8,7},{9,8},{10,9},{11,1... | collective-permute-start | bytes 196616 | tf_op jit(solution)/shard_map/ppermute | solution.py:20
  178.6 5.3 %collective-permute-start.23 = (f32[32,2,256]{2,0,1:T(8,128)S(1)}, f32[32,2,256]{2,0,1:T(8,128)S(1)}, u32[]{:S(2)}, u32[]{:S(2)}) collective-permute-start(f32[32,2,256]{2,0,1:T(8,128)S(1)} %slice_select_fusion.3), channel_id=1, source_target_pairs={{2,0},{3,1},{4,2},{5,3},{6,4},{7,5},{8,6},{9,7},{10,8},{11,9},{12,... | collective-permute-start | bytes 196616 | tf_op jit(solution)/shard_map/ppermute | solution.py:20
  184.0 2.1 %collective-permute-done.23 = f32[32,2,256]{2,0,1:T(8,128)S(1)} collective-permute-done((f32[32,2,256]{2,0,1:T(8,128)S(1)}, f32[32,2,256]{2,0,1:T(8,128)S(1)}, u32[]{:S(2)}, u32[]{:S(2)}) %collective-permute-start.23) | collective-permute-done | bytes 65568 | tf_op jit(solution)/shard_map/ppermute | solution.py:20
  187.8 0.9 broadcast_in_dim.38
  188.7 2.0 reshape.184
  190.7 1.1 bitcast_add_fusion
  191.8 0.9 fusion.24
  192.7 0.9 fusion.32
  193.7 2.1 collective-permute-start.24
  195.8 6.0 %collective-permute-start.25 = (f32[64,2,256]{2,0,1:T(8,128)S(1)}, f32[64,2,256]{2,0,1:T(8,128)S(1)}, u32[]{:S(2)}, u32[]{:S(2)}) collective-permute-start(f32[64,2,256]{2,0,1:T(8,128)S(1)} %get-tuple-element.16), channel_id=1, source_target_pairs={{1,0},{2,1},{3,2},{4,3},{5,4},{6,5},{7,6},{8,7},{9,8},{10,9},{11,1... | collective-permute-start | bytes 393224 | tf_op jit(solution)/shard_map/ppermute | solution.py:20
  202.2 0.6 collective-permute-done.24
  202.8 1.5 collective-permute-done.25
  206.4 0.4 copy-done.2
  207.0 0.7 fusion.221
  208.1 0.6 copy-done.15
  208.8 1.0 slice_select_fusion
  (179 shorter events, 12.4 us)
Async XLA Ops:
  2.6 27.0 %copy-start = (f32[16,16,1024]{2,1,0:T(8,128)S(1)}, f32[16,16,1024]{2,1,0:T(8,128)}, u32[]{:S(2)}) copy-start(f32[16,16,1024]{2,1,0:T(8,128)} %shard_map.46) | copy-start | bytes 3145732
  4.0 24.5 %collective-permute-start = (f32[16,4,1024]{2,1,0:T(4,128)S(1)}, f32[16,4,1024]{2,1,0:T(4,128)S(1)}, u32[]{:S(2)}, u32[]{:S(2)}) collective-permute-start(f32[16,4,1024]{2,1,0:T(4,128)S(1)} %get-tuple-element.14), channel_id=1, source_target_pairs={{0,1},{1,2},{2,3},{3,4},{4,5},{5,6},{6,7},{7,8},{8,9},{9,10},{10,1... | collective-permute-start | bytes 786440 | tf_op jit(solution)/shard_map/ppermute | solution.py:20
  8.3 21.3 %collective-permute-start.1 = (f32[16,4,1024]{2,1,0:T(4,128)S(1)}, f32[16,4,1024]{2,1,0:T(4,128)S(1)}, u32[]{:S(2)}, u32[]{:S(2)}) collective-permute-start(f32[16,4,1024]{2,1,0:T(4,128)S(1)} %get-tuple-element.15), channel_id=1, source_target_pairs={{1,0},{2,1},{3,2},{4,3},{5,4},{6,5},{7,6},{8,7},{9,8},{10,9},{11,1... | collective-permute-start | bytes 786440 | tf_op jit(solution)/shard_map/ppermute | solution.py:20
  24.1 51.6 %copy-start.27 = (pred[16,16]{1,0:T(8,128)(4,1)}, pred[16,16]{1,0:T(8,128)(4,1)S(1)}, u32[]{:S(2)}) copy-start(pred[16,16]{1,0:T(8,128)(4,1)S(1)} %broadcast_and_fusion.1) | copy-start | bytes 772
  24.2 51.5 %copy-start.25 = (s32[16,16]{1,0:T(8,128)}, s32[16,16]{1,0:T(8,128)S(1)}, u32[]{:S(2)}) copy-start(s32[16,16]{1,0:T(8,128)S(1)} %iota_add_fusion.5) | copy-start | bytes 3076
  29.7 2.7 %collective-permute-start.2 = (f32[4,24,1024]{2,1,0:T(8,128)S(1)}, f32[4,24,1024]{2,1,0:T(8,128)S(1)}, u32[]{:S(2)}, u32[]{:S(2)}) collective-permute-start(f32[4,24,1024]{2,1,0:T(8,128)S(1)} %get-tuple-element.12), channel_id=1, source_target_pairs={{0,64},{64,128},{128,192},{192,256},{256,320},{320,384},{384,448},... | collective-permute-start | bytes 1179656 | tf_op jit(solution)/shard_map/ppermute | solution.py:20
  31.0 9.7 %collective-permute-start.3 = (f32[4,24,1024]{2,1,0:T(8,128)S(1)}, f32[4,24,1024]{2,1,0:T(8,128)S(1)}, u32[]{:S(2)}, u32[]{:S(2)}) collective-permute-start(f32[4,24,1024]{2,1,0:T(8,128)S(1)} %get-tuple-element.13), channel_id=1, source_target_pairs={{64,0},{128,64},{192,128},{256,192},{320,256},{384,320},{448,384},... | collective-permute-start | bytes 1179656 | tf_op jit(solution)/shard_map/ppermute | solution.py:20
  42.7 1.3 copy-start.5
  42.7 1.3 copy-start.7
  43.5 0.8 copy-start.1
  45.1 8.7 %collective-permute-start.4 = (f32[8,4,512]{2,1,0:T(4,128)S(1)}, f32[8,4,512]{2,1,0:T(4,128)S(1)}, u32[]{:S(2)}, u32[]{:S(2)}) collective-permute-start(f32[8,4,512]{2,1,0:T(4,128)S(1)} %get-tuple-element.65), channel_id=1, source_target_pairs={{0,1},{1,2},{2,3},{3,4},{4,5},{5,6},{6,7},{7,8},{8,9},{9,10},{10,1... | collective-permute-start | bytes 196616 | tf_op jit(solution)/shard_map/ppermute | solution.py:20
  47.0 8.4 %collective-permute-start.5 = (f32[8,4,512]{2,1,0:T(4,128)S(1)}, f32[8,4,512]{2,1,0:T(4,128)S(1)}, u32[]{:S(2)}, u32[]{:S(2)}) collective-permute-start(f32[8,4,512]{2,1,0:T(4,128)S(1)} %get-tuple-element.66), channel_id=1, source_target_pairs={{1,0},{2,1},{3,2},{4,3},{5,4},{6,5},{7,6},{8,7},{9,8},{10,9},{11,1... | collective-permute-start | bytes 196616 | tf_op jit(solution)/shard_map/ppermute | solution.py:20
  55.5 17.3 %collective-permute-start.6 = (f32[4,16,512]{2,1,0:T(8,128)S(1)}, f32[4,16,512]{2,1,0:T(8,128)S(1)}, u32[]{:S(2)}, u32[]{:S(2)}) collective-permute-start(f32[4,16,512]{2,1,0:T(8,128)S(1)} %get-tuple-element.57), channel_id=1, source_target_pairs={{0,64},{64,128},{128,192},{192,256},{256,320},{320,384},{384,448},... | collective-permute-start | bytes 393224 | tf_op jit(solution)/shard_map/ppermute | solution.py:20
  71.5 3.7 %collective-permute-start.7 = (f32[4,16,512]{2,1,0:T(8,128)S(1)}, f32[4,16,512]{2,1,0:T(8,128)S(1)}, u32[]{:S(2)}, u32[]{:S(2)}) collective-permute-start(f32[4,16,512]{2,1,0:T(8,128)S(1)} %get-tuple-element.58), channel_id=1, source_target_pairs={{64,0},{128,64},{192,128},{256,192},{320,256},{384,320},{448,384},... | collective-permute-start | bytes 393224 | tf_op jit(solution)/shard_map/ppermute | solution.py:20
  75.6 1.2 copy-start.11
  75.7 1.2 copy-start.13
  76.0 0.7 copy-start.9
  77.0 20.2 %collective-permute-start.8 = (f32[4,4,512]{2,1,0:T(4,128)S(1)}, f32[4,4,512]{2,1,0:T(4,128)S(1)}, u32[]{:S(2)}, u32[]{:S(2)}) collective-permute-start(f32[4,4,512]{2,1,0:T(4,128)S(1)} %get-tuple-element.68), channel_id=1, source_target_pairs={{0,64},{64,0},{128,192},{192,128},{256,320},{320,256},{384,448},{4... | collective-permute-start | bytes 98312 | tf_op jit(solution)/shard_map/ppermute | solution.py:55
  87.1 10.1 %collective-permute-start.9 = (f32[4,4,512]{2,1,0:T(4,128)S(1)}, f32[4,4,512]{2,1,0:T(4,128)S(1)}, u32[]{:S(2)}, u32[]{:S(2)}) collective-permute-start(f32[4,4,512]{2,1,0:T(4,128)S(1)} %get-tuple-element.68), channel_id=1, source_target_pairs={{0,128},{64,192},{128,0},{192,64},{256,384},{320,448},{384,256},{4... | collective-permute-start | bytes 98312 | tf_op jit(solution)/shard_map/ppermute | solution.py:55
  95.2 9.4 %collective-permute-start.10 = (f32[4,4,512]{2,1,0:T(4,128)S(1)}, f32[4,4,512]{2,1,0:T(4,128)S(1)}, u32[]{:S(2)}, u32[]{:S(2)}) collective-permute-start(f32[4,4,512]{2,1,0:T(4,128)S(1)} %get-tuple-element.68), channel_id=1, source_target_pairs={{0,192},{64,128},{128,64},{192,0},{256,448},{320,384},{384,320},{4... | collective-permute-start | bytes 98312 | tf_op jit(solution)/shard_map/ppermute | solution.py:55
  97.2 44.0 %copy-start.23 = (s32[64,12]{0,1:T(8,128)}, s32[64,12]{0,1:T(8,128)S(1)}, u32[]{:S(2)}) copy-start(s32[64,12]{0,1:T(8,128)S(1)} %iota_add_fusion.4) | copy-start | bytes 9220
  104.8 11.5 %collective-permute-start.12 = (f32[16,4,512]{2,1,0:T(4,128)S(1)}, f32[16,4,512]{2,1,0:T(4,128)S(1)}, u32[]{:S(2)}, u32[]{:S(2)}) collective-permute-start(f32[16,4,512]{2,1,0:T(4,128)S(1)} %get-tuple-element.60), channel_id=1, source_target_pairs={{0,512},{64,576},{128,640},{192,704},{256,768},{320,832},{384,896}... | collective-permute-start | bytes 393224 | tf_op jit(solution)/shard_map/ppermute | solution.py:55
  110.5 8.3 %collective-permute-start.13 = (f32[16,4,512]{2,1,0:T(4,128)S(1)}, f32[16,4,512]{2,1,0:T(4,128)S(1)}, u32[]{:S(2)}, u32[]{:S(2)}) collective-permute-start(f32[16,4,512]{2,1,0:T(4,128)S(1)} %get-tuple-element.60), channel_id=1, source_target_pairs={{0,768},{64,832},{128,896},{192,960},{256,512},{320,576},{384,640}... | collective-permute-start | bytes 393224 | tf_op jit(solution)/shard_map/ppermute | solution.py:55
  114.2 6.9 %collective-permute-start.11 = (f32[16,4,512]{2,1,0:T(4,128)S(1)}, f32[16,4,512]{2,1,0:T(4,128)S(1)}, u32[]{:S(2)}, u32[]{:S(2)}) collective-permute-start(f32[16,4,512]{2,1,0:T(4,128)S(1)} %get-tuple-element.60), channel_id=1, source_target_pairs={{0,256},{64,320},{128,384},{192,448},{256,0},{320,64},{384,128},{4... | collective-permute-start | bytes 393224 | tf_op jit(solution)/shard_map/ppermute | solution.py:55
  116.2 25.9 %copy-start.31 = (pred[12]{0:T(512)(128)(4,1)}, pred[12]{0:T(512)(128)(4,1)S(1)}, u32[]{:S(2)}) copy-start(pred[12]{0:T(512)(128)(4,1)S(1)} %compare_and_fusion.7) | copy-start | bytes 40
  121.5 16.1 %collective-permute-start.14 = (f32[64,4,512]{2,0,1:T(8,128)S(1)}, f32[64,4,512]{2,0,1:T(8,128)S(1)}, u32[]{:S(2)}, u32[]{:S(2)}) collective-permute-start(f32[64,4,512]{2,0,1:T(8,128)S(1)} %pad_maximum_fusion.4), channel_id=1, source_target_pairs={{0,1},{1,2},{2,3},{3,4},{4,5},{5,6},{6,7},{7,8},{8,9},{9,10},{10,1... | collective-permute-start | bytes 1572872 | tf_op jit(solution)/shard_map/ppermute | solution.py:20
  123.4 15.4 %collective-permute-start.15 = (f32[64,4,512]{2,0,1:T(8,128)S(1)}, f32[64,4,512]{2,0,1:T(8,128)}, u32[]{:S(2)}, u32[]{:S(2)}) collective-permute-start(f32[64,4,512]{2,0,1:T(8,128)S(1)} %pad_maximum_fusion.4), channel_id=1, source_target_pairs={{1,0},{2,1},{3,2},{4,3},{5,4},{6,5},{7,6},{8,7},{9,8},{10,9},{11,1... | collective-permute-start | bytes 1572872 | tf_op jit(solution)/shard_map/ppermute | solution.py:20
  137.7 0.8 copy-start.21
  142.1 0.9 copy-start.3
  143.9 18.1 %copy-start.20 = (f32[32,2,256]{2,0,1:T(8,128)S(1)}, f32[32,2,256]{2,0,1:T(8,128)}, u32[]{:S(2)}) copy-start(f32[32,2,256]{2,0,1:T(8,128)} %add_multiply_fusion.2) | copy-start | bytes 196612
  143.9 21.8 %copy-start.29 = (pred[10]{0:T(512)(128)(4,1)S(1)}, pred[10]{0:T(512)(128)(4,1)}, u32[]{:S(2)}) copy-start(pred[10]{0:T(512)(128)(4,1)} %compare_and_fusion.6) | copy-start | bytes 34
  144.8 17.1 %collective-permute-start.16 = (f32[32,2,512]{2,0,1:T(8,128)S(1)}, f32[32,2,512]{2,0,1:T(8,128)S(1)}, u32[]{:S(2)}, u32[]{:S(2)}) collective-permute-start(f32[32,2,512]{2,0,1:T(8,128)S(1)} %pad_maximum_fusion.11), channel_id=1, source_target_pairs={{0,2},{1,3},{2,4},{3,5},{4,6},{5,7},{6,8},{7,9},{8,10},{9,11},{10,... | collective-permute-start | bytes 393224 | tf_op jit(solution)/shard_map/ppermute | solution.py:20
  148.4 13.6 %collective-permute-start.17 = (f32[32,2,512]{2,0,1:T(8,128)S(1)}, f32[32,2,512]{2,0,1:T(8,128)S(1)}, u32[]{:S(2)}, u32[]{:S(2)}) collective-permute-start(f32[32,2,512]{2,0,1:T(8,128)S(1)} %pad_maximum_fusion.11), channel_id=1, source_target_pairs={{0,1},{1,2},{2,3},{3,4},{4,5},{5,6},{6,7},{7,8},{8,9},{9,10},{10,1... | collective-permute-start | bytes 393224 | tf_op jit(solution)/shard_map/ppermute | solution.py:20
  150.3 11.7 %collective-permute-start.18 = (f32[32,2,512]{2,0,1:T(8,128)S(1)}, f32[32,2,512]{2,0,1:T(8,128)S(1)}, u32[]{:S(2)}, u32[]{:S(2)}) collective-permute-start(f32[32,2,512]{2,0,1:T(8,128)S(1)} %pad_maximum_fusion.11), channel_id=1, source_target_pairs={{1,0},{2,1},{3,2},{4,3},{5,4},{6,5},{7,6},{8,7},{9,8},{10,9},{11,1... | collective-permute-start | bytes 393224 | tf_op jit(solution)/shard_map/ppermute | solution.py:20
  156.9 8.7 %collective-permute-start.19 = (f32[32,2,512]{2,0,1:T(8,128)S(1)}, f32[32,2,512]{2,0,1:T(8,128)S(1)}, u32[]{:S(2)}, u32[]{:S(2)}) collective-permute-start(f32[32,2,512]{2,0,1:T(8,128)S(1)} %pad_maximum_fusion.11), channel_id=1, source_target_pairs={{2,0},{3,1},{4,2},{5,3},{6,4},{7,5},{8,6},{9,7},{10,8},{11,9},{12,... | collective-permute-start | bytes 393224 | tf_op jit(solution)/shard_map/ppermute | solution.py:20
  166.1 1.5 copy-start.16
  166.1 1.5 copy-start.18
  167.4 18.7 %copy-start.30 = (pred[10]{0:T(512)(128)(4,1)S(1)}, pred[10]{0:T(512)(128)(4,1)}, u32[]{:S(2)}) copy-start(pred[10]{0:T(512)(128)(4,1)} %compare_and_fusion.6) | copy-start | bytes 34
  167.7 16.2 %collective-permute-start.20 = (f32[32,2,256]{2,0,1:T(8,128)S(1)}, f32[32,2,256]{2,0,1:T(8,128)S(1)}, u32[]{:S(2)}, u32[]{:S(2)}) collective-permute-start(f32[32,2,256]{2,0,1:T(8,128)S(1)} %slice_select_fusion.3), channel_id=1, source_target_pairs={{0,2},{1,3},{2,4},{3,5},{4,6},{5,7},{6,8},{7,9},{8,10},{9,11},{10,... | collective-permute-start | bytes 196616 | tf_op jit(solution)/shard_map/ppermute | solution.py:20
  170.7 13.2 %collective-permute-start.21 = (f32[32,2,256]{2,0,1:T(8,128)S(1)}, f32[32,2,256]{2,0,1:T(8,128)S(1)}, u32[]{:S(2)}, u32[]{:S(2)}) collective-permute-start(f32[32,2,256]{2,0,1:T(8,128)S(1)} %slice_select_fusion.3), channel_id=1, source_target_pairs={{0,1},{1,2},{2,3},{3,4},{4,5},{5,6},{6,7},{7,8},{8,9},{9,10},{10,1... | collective-permute-start | bytes 196616 | tf_op jit(solution)/shard_map/ppermute | solution.py:20
  172.7 11.3 %collective-permute-start.22 = (f32[32,2,256]{2,0,1:T(8,128)S(1)}, f32[32,2,256]{2,0,1:T(8,128)S(1)}, u32[]{:S(2)}, u32[]{:S(2)}) collective-permute-start(f32[32,2,256]{2,0,1:T(8,128)S(1)} %slice_select_fusion.3), channel_id=1, source_target_pairs={{1,0},{2,1},{3,2},{4,3},{5,4},{6,5},{7,6},{8,7},{9,8},{10,9},{11,1... | collective-permute-start | bytes 196616 | tf_op jit(solution)/shard_map/ppermute | solution.py:20
  178.6 7.5 %collective-permute-start.23 = (f32[32,2,256]{2,0,1:T(8,128)S(1)}, f32[32,2,256]{2,0,1:T(8,128)S(1)}, u32[]{:S(2)}, u32[]{:S(2)}) collective-permute-start(f32[32,2,256]{2,0,1:T(8,128)S(1)} %slice_select_fusion.3), channel_id=1, source_target_pairs={{2,0},{3,1},{4,2},{5,3},{6,4},{7,5},{8,6},{9,7},{10,8},{11,9},{12,... | collective-permute-start | bytes 196616 | tf_op jit(solution)/shard_map/ppermute | solution.py:20
  186.6 1.0 copy-start.17
  186.6 1.1 copy-start.19
  186.6 1.1 copy-start.22
  187.3 3.4 %copy-start.4 = (f32[64,12,256]{2,0,1:T(8,128)S(1)}, f32[64,12,256]{2,0,1:T(8,128)}, u32[]{:S(2)}) copy-start(f32[64,12,256]{2,0,1:T(8,128)} %copy-done.3) | copy-start | bytes 2359300
  187.7 4.0 %copy-start.24 = (s32[64,12]{0,1:T(8,128)S(1)}, s32[64,12]{0,1:T(8,128)}, u32[]{:S(2)}) copy-start(s32[64,12]{0,1:T(8,128)} %copy-done.23) | copy-start | bytes 9220
  187.8 4.0 %copy-start.32 = (pred[12]{0:T(512)(128)(4,1)S(1)}, pred[12]{0:T(512)(128)(4,1)}, u32[]{:S(2)}) copy-start(pred[12]{0:T(512)(128)(4,1)} %copy-done.31) | copy-start | bytes 40
  192.7 9.1 %copy-start.26 = (s32[16,16]{1,0:T(8,128)S(1)}, s32[16,16]{1,0:T(8,128)}, u32[]{:S(2)}) copy-start(s32[16,16]{1,0:T(8,128)} %copy-done.25) | copy-start | bytes 3076
  192.7 9.1 %copy-start.28 = (pred[16,16]{1,0:T(8,128)(4,1)S(1)}, pred[16,16]{1,0:T(8,128)(4,1)}, u32[]{:S(2)}) copy-start(pred[16,16]{1,0:T(8,128)(4,1)} %copy-done.27) | copy-start | bytes 772
  192.7 9.3 %copy-start.6 = (pred[24,24,256]{2,1,0:T(8,128)(4,1)S(1)}, pred[24,24,256]{2,1,0:T(8,128)(4,1)}, u32[]{:S(2)}) copy-start(pred[24,24,256]{2,1,0:T(8,128)(4,1)} %copy-done.5) | copy-start | bytes 442372
  193.7 11.1 %copy-start.10 = (f32[16,16,256]{2,1,0:T(8,128)S(1)}, f32[16,16,256]{2,1,0:T(8,128)}, u32[]{:S(2)}) copy-start(f32[16,16,256]{2,1,0:T(8,128)} %copy-done.9) | copy-start | bytes 786436
  193.7 9.1 %collective-permute-start.24 = (f32[64,2,256]{2,0,1:T(8,128)S(1)}, f32[64,2,256]{2,0,1:T(8,128)S(1)}, u32[]{:S(2)}, u32[]{:S(2)}) collective-permute-start(f32[64,2,256]{2,0,1:T(8,128)S(1)} %get-tuple-element.17), channel_id=1, source_target_pairs={{0,1},{1,2},{2,3},{3,4},{4,5},{5,6},{6,7},{7,8},{8,9},{9,10},{10,1... | collective-permute-start | bytes 393224 | tf_op jit(solution)/shard_map/ppermute | solution.py:20
  195.8 8.5 %collective-permute-start.25 = (f32[64,2,256]{2,0,1:T(8,128)S(1)}, f32[64,2,256]{2,0,1:T(8,128)S(1)}, u32[]{:S(2)}, u32[]{:S(2)}) collective-permute-start(f32[64,2,256]{2,0,1:T(8,128)S(1)} %get-tuple-element.16), channel_id=1, source_target_pairs={{1,0},{2,1},{3,2},{4,3},{5,4},{6,5},{7,6},{8,7},{9,8},{10,9},{11,1... | collective-permute-start | bytes 393224 | tf_op jit(solution)/shard_map/ppermute | solution.py:20
  204.7 1.0 copy-start.12
  204.7 1.0 copy-start.14
  205.7 1.1 copy-start.2
  205.9 1.1 copy-start.8
  207.8 1.0 copy-start.15

commit v12 on v9

--- a/solution.py
+++ b/solution.py
@@ -231,8 +231,9 @@
     coefficient = screen * jnp.exp(potential)
     divisor = 4.0 * 1.0 + 2.0 + coefficient
     iterate = sweeps(dirichlet, source, divisor, 1.0, movable, 1)
-    residual = residual_of(iterate, source, divisor, 1.0, movable)
-    source_1 = restrict(residual, width, width, span_x, span_y)
+    near = [interior(values, width - 2) for values in (iterate, source, divisor, movable)]
+    residual = residual_of(near[0], near[1], near[2], 1.0, near[3])
+    source_1 = restrict(residual, 2, 2, span_x, span_y)
     coefficient_1 = coarsen(interior(coefficient, width))
 
     level_1 = descend(1, source_1, coefficient_1, HALO_MID)

time: 204 us -> 206 us (level)
    unnamed x73 -> x63, local copies, waits for them, and re-layouts: 4.11 us -> 5.36 us
where the time goes in v12:
time: 206 us; the launch traced here: 205 us
  starting transfers between devices  121 us (59%)
  waiting for transfers between devices  43.9 us (21%)
  other arithmetic  22.6 us (11%)
  local copies, waits for them, and re-layouts  12.6 us (6%)
  Pallas kernels  2.57 us (1%)
    ppermute x20, starting transfers between devices, shifted(): return lax.ppermute(block, axis, route)  91.4 us
    ppermute x20, waiting for transfers between devices, shifted(): return lax.ppermute(block, axis, route)  31.7 us
    ppermute x6, starting transfers between devices, gather_x(): lax.ppermute(block, 'gx', [(i, i ^ m * group) for i in range(count)])  30.1 us
    ppermute x6, waiting for transfers between devices, gather_x(): lax.ppermute(block, 'gx', [(i, i ^ m * group) for i in range(count)])  12.3 us
    select_n x17, other arithmetic, half_sweep(): return jnp.where(update, renewed, iterate)  10.6 us
    unnamed x63, local copies, waits for them, and re-layouts  5.36 us
  transfers between devices with their start and end apart: 26, of which 16 were waited for; matrix products, arithmetic and copies ran while one was open for 2% of the time, Pallas kernels for 0%

profile of v12, /device:TPU:8, one launch (start us, length us, event | category | flops | bytes accessed | tf_op | source)
XLA Modules:
  0.0 204.6 jit_solution(16917237540528846678)
XLA Ops:
  0.0 2.6 %shard_map.46 = f32[16,16,1024]{2,1,0:T(8,128)} custom-call(f32[16]{0:T(128)} %volts_ref.1, f32[16,16,256]{2,1,0:T(8,128)} %potential_ref.1, f32[16,16,256]{2,1,0:T(8,128)} %charge_ref.1, s32[16,16,256]{2,1,0:T(8,128)} %region_ref.1), custom_call_target="tpu_custom_call" | custom-call | tf_op jit(solution)/shard_map/pallas_call | solution.py:211
  2.6 1.2 fusion.214
  3.7 1.8 collective-permute-start
  5.5 1.3 collective-permute-start.1
  7.0 6.6 %collective-permute-done.1 = f32[4,16,1024]{2,1,0:T(8,128)S(1)} collective-permute-done((f32[4,16,1024]{2,1,0:T(8,128)S(1)}, f32[4,16,1024]{2,1,0:T(8,128)S(1)}, u32[]{:S(2)}, u32[]{:S(2)}) %collective-permute-start.1) | collective-permute-done | bytes 262176 | tf_op jit(solution)/shard_map/ppermute | solution.py:20
  13.8 4.3 %collective-permute-start.2 = (f32[24,4,1024]{2,1,0:T(4,128)S(1)}, f32[24,4,1024]{2,1,0:T(4,128)S(1)}, u32[]{:S(2)}, u32[]{:S(2)}) collective-permute-start(f32[24,4,1024]{2,1,0:T(4,128)S(1)} %get-tuple-element.12), channel_id=1, source_target_pairs={{0,1},{1,2},{2,3},{3,4},{4,5},{5,6},{6,7},{7,8},{8,9},{9,10},{10,1... | collective-permute-start | bytes 1179656 | tf_op jit(solution)/shard_map/ppermute | solution.py:20
  18.1 16.6 %collective-permute-start.3 = (f32[24,4,1024]{2,1,0:T(4,128)S(1)}, f32[24,4,1024]{2,1,0:T(4,128)S(1)}, u32[]{:S(2)}, u32[]{:S(2)}) collective-permute-start(f32[24,4,1024]{2,1,0:T(4,128)S(1)} %get-tuple-element.13), channel_id=1, source_target_pairs={{1,0},{2,1},{3,2},{4,3},{5,4},{6,5},{7,6},{8,7},{9,8},{10,9},{11,1... | collective-permute-start | bytes 1179656 | tf_op jit(solution)/shard_map/ppermute | solution.py:20
  35.1 3.4 %collective-permute-done.2 = f32[24,4,1024]{2,1,0:T(4,128)S(1)} collective-permute-done((f32[24,4,1024]{2,1,0:T(4,128)S(1)}, f32[24,4,1024]{2,1,0:T(4,128)S(1)}, u32[]{:S(2)}, u32[]{:S(2)}) %collective-permute-start.2) | collective-permute-done | bytes 393248 | tf_op jit(solution)/shard_map/ppermute | solution.py:20
  38.6 1.5 collective-permute-done.3
  40.6 1.5 fusion.58
  42.9 0.6 fusion.217
  44.8 10.9 %collective-permute-start.4 = (f32[4,8,512]{2,1,0:T(8,128)S(1)}, f32[4,8,512]{2,1,0:T(8,128)S(1)}, u32[]{:S(2)}, u32[]{:S(2)}) collective-permute-start(f32[4,8,512]{2,1,0:T(8,128)S(1)} %get-tuple-element.70), channel_id=1, source_target_pairs={{0,64},{64,128},{128,192},{192,256},{256,320},{320,384},{384,448},... | collective-permute-start | bytes 196616 | tf_op jit(solution)/shard_map/ppermute | solution.py:20
  55.7 1.3 collective-permute-start.5
  57.1 1.9 collective-permute-done.5
  59.1 1.9 collective-permute-start.6
  61.0 6.5 %collective-permute-start.7 = (f32[16,4,512]{2,1,0:T(4,128)S(1)}, f32[16,4,512]{2,1,0:T(4,128)S(1)}, u32[]{:S(2)}, u32[]{:S(2)}) collective-permute-start(f32[16,4,512]{2,1,0:T(4,128)S(1)} %get-tuple-element.63), channel_id=1, source_target_pairs={{1,0},{2,1},{3,2},{4,3},{5,4},{6,5},{7,6},{8,7},{9,8},{10,9},{11,1... | collective-permute-start | bytes 393224 | tf_op jit(solution)/shard_map/ppermute | solution.py:20
  67.5 1.7 collective-permute-done.6
  69.2 0.8 collective-permute-done.7
  71.1 0.5 copy-done.7
  71.8 8.4 %collective-permute-start.8 = (f32[4,4,512]{2,1,0:T(4,128)S(1)}, f32[4,4,512]{2,1,0:T(4,128)S(1)}, u32[]{:S(2)}, u32[]{:S(2)}) collective-permute-start(f32[4,4,512]{2,1,0:T(4,128)S(1)} %get-tuple-element.73), channel_id=1, source_target_pairs={{0,64},{64,0},{128,192},{192,128},{256,320},{320,256},{384,448},{4... | collective-permute-start | bytes 98312 | tf_op jit(solution)/shard_map/ppermute | solution.py:55
  80.2 10.2 %collective-permute-start.9 = (f32[4,4,512]{2,1,0:T(4,128)S(1)}, f32[4,4,512]{2,1,0:T(4,128)S(1)}, u32[]{:S(2)}, u32[]{:S(2)}) collective-permute-start(f32[4,4,512]{2,1,0:T(4,128)S(1)} %get-tuple-element.73), channel_id=1, source_target_pairs={{0,128},{64,192},{128,0},{192,64},{256,384},{320,448},{384,256},{4... | collective-permute-start | bytes 98312 | tf_op jit(solution)/shard_map/ppermute | solution.py:55
  90.4 1.9 collective-permute-start.10
  92.6 7.2 %collective-permute-done.10 = f32[4,4,512]{2,1,0:T(4,128)S(1)} collective-permute-done((f32[4,4,512]{2,1,0:T(4,128)S(1)}, f32[4,4,512]{2,1,0:T(4,128)S(1)}, u32[]{:S(2)}, u32[]{:S(2)}) %collective-permute-start.10) | collective-permute-done | bytes 32800 | tf_op jit(solution)/shard_map/ppermute | solution.py:55
  99.9 1.9 collective-permute-start.12
  101.8 5.8 %collective-permute-start.13 = (f32[16,4,512]{2,1,0:T(4,128)S(1)}, f32[16,4,512]{2,1,0:T(4,128)S(1)}, u32[]{:S(2)}, u32[]{:S(2)}) collective-permute-start(f32[16,4,512]{2,1,0:T(4,128)S(1)} %get-tuple-element.65), channel_id=1, source_target_pairs={{0,768},{64,832},{128,896},{192,960},{256,512},{320,576},{384,640}... | collective-permute-start | bytes 393224 | tf_op jit(solution)/shard_map/ppermute | solution.py:55
  107.6 1.9 collective-permute-start.11
  109.6 1.9 collective-permute-done.13
  111.5 2.9 %collective-permute-done.11 = f32[16,4,512]{2,1,0:T(4,128)S(1)} collective-permute-done((f32[16,4,512]{2,1,0:T(4,128)S(1)}, f32[16,4,512]{2,1,0:T(4,128)S(1)}, u32[]{:S(2)}, u32[]{:S(2)}) %collective-permute-start.11) | collective-permute-done | bytes 131104 | tf_op jit(solution)/shard_map/ppermute | solution.py:55
  114.9 1.9 collective-permute-start.14
  116.8 6.2 %collective-permute-start.15 = (f32[64,4,512]{2,0,1:T(8,128)S(1)}, f32[64,4,512]{2,0,1:T(8,128)}, u32[]{:S(2)}, u32[]{:S(2)}) collective-permute-start(f32[64,4,512]{2,0,1:T(8,128)S(1)} %pad_maximum_fusion.4), channel_id=1, source_target_pairs={{1,0},{2,1},{3,2},{4,3},{5,4},{6,5},{7,6},{8,7},{9,8},{10,9},{11,1... | collective-permute-start | bytes 1572872 | tf_op jit(solution)/shard_map/ppermute | solution.py:20
  123.2 8.3 %collective-permute-done.14 = f32[64,4,512]{2,0,1:T(8,128)S(1)} collective-permute-done((f32[64,4,512]{2,0,1:T(8,128)S(1)}, f32[64,4,512]{2,0,1:T(8,128)S(1)}, u32[]{:S(2)}, u32[]{:S(2)}) %collective-permute-start.14) | collective-permute-done | bytes 524320 | tf_op jit(solution)/shard_map/ppermute | solution.py:20
  131.5 0.8 copy-done.24
  132.6 1.4 pad_maximum_fusion.1
  134.1 0.9 fusion.40
  135.0 0.9 fusion.8
  135.9 0.5 fusion.16
  137.3 0.9 slice.769
  138.2 1.0 multiply_add_fusion.1
  139.2 1.9 collective-permute-start.16
  141.1 0.9 compare_and_fusion.3
  142.1 2.4 %collective-permute-start.17 = (f32[32,2,512]{2,0,1:T(8,128)S(1)}, f32[32,2,512]{2,0,1:T(8,128)S(1)}, u32[]{:S(2)}, u32[]{:S(2)}) collective-permute-start(f32[32,2,512]{2,0,1:T(8,128)S(1)} %pad_maximum_fusion.11), channel_id=1, source_target_pairs={{0,1},{1,2},{2,3},{3,4},{4,5},{5,6},{6,7},{7,8},{8,9},{9,10},{10,1... | collective-permute-start | bytes 393224 | tf_op jit(solution)/shard_map/ppermute | solution.py:20
  144.4 6.2 %collective-permute-start.18 = (f32[32,2,512]{2,0,1:T(8,128)S(1)}, f32[32,2,512]{2,0,1:T(8,128)S(1)}, u32[]{:S(2)}, u32[]{:S(2)}) collective-permute-start(f32[32,2,512]{2,0,1:T(8,128)S(1)} %pad_maximum_fusion.11), channel_id=1, source_target_pairs={{1,0},{2,1},{3,2},{4,3},{5,4},{6,5},{7,6},{8,7},{9,8},{10,9},{11,1... | collective-permute-start | bytes 393224 | tf_op jit(solution)/shard_map/ppermute | solution.py:20
  150.6 5.0 %collective-permute-start.19 = (f32[32,2,512]{2,0,1:T(8,128)S(1)}, f32[32,2,512]{2,0,1:T(8,128)S(1)}, u32[]{:S(2)}, u32[]{:S(2)}) collective-permute-start(f32[32,2,512]{2,0,1:T(8,128)S(1)} %pad_maximum_fusion.11), channel_id=1, source_target_pairs={{2,0},{3,1},{4,2},{5,3},{6,4},{7,5},{8,6},{9,7},{10,8},{11,9},{12,... | collective-permute-start | bytes 393224 | tf_op jit(solution)/shard_map/ppermute | solution.py:20
  155.7 3.6 %collective-permute-done.19 = f32[32,2,512]{2,0,1:T(8,128)S(1)} collective-permute-done((f32[32,2,512]{2,0,1:T(8,128)S(1)}, f32[32,2,512]{2,0,1:T(8,128)S(1)}, u32[]{:S(2)}, u32[]{:S(2)}) %collective-permute-start.19) | collective-permute-done | bytes 131104 | tf_op jit(solution)/shard_map/ppermute | solution.py:20
  161.4 1.9 collective-permute-start.20
  163.3 1.0 add_select_fusion.2
  164.4 3.1 %collective-permute-start.21 = (f32[32,2,256]{2,0,1:T(8,128)S(1)}, f32[32,2,256]{2,0,1:T(8,128)S(1)}, u32[]{:S(2)}, u32[]{:S(2)}) collective-permute-start(f32[32,2,256]{2,0,1:T(8,128)S(1)} %slice_select_fusion.4), channel_id=1, source_target_pairs={{0,1},{1,2},{2,3},{3,4},{4,5},{5,6},{6,7},{7,8},{8,9},{9,10},{10,1... | collective-permute-start | bytes 196616 | tf_op jit(solution)/shard_map/ppermute | solution.py:20
  167.4 4.9 %collective-permute-start.22 = (f32[32,2,256]{2,0,1:T(8,128)S(1)}, f32[32,2,256]{2,0,1:T(8,128)S(1)}, u32[]{:S(2)}, u32[]{:S(2)}) collective-permute-start(f32[32,2,256]{2,0,1:T(8,128)S(1)} %slice_select_fusion.4), channel_id=1, source_target_pairs={{1,0},{2,1},{3,2},{4,3},{5,4},{6,5},{7,6},{8,7},{9,8},{10,9},{11,1... | collective-permute-start | bytes 196616 | tf_op jit(solution)/shard_map/ppermute | solution.py:20
  172.3 5.3 %collective-permute-start.23 = (f32[32,2,256]{2,0,1:T(8,128)S(1)}, f32[32,2,256]{2,0,1:T(8,128)S(1)}, u32[]{:S(2)}, u32[]{:S(2)}) collective-permute-start(f32[32,2,256]{2,0,1:T(8,128)S(1)} %slice_select_fusion.4), channel_id=1, source_target_pairs={{2,0},{3,1},{4,2},{5,3},{6,4},{7,5},{8,6},{9,7},{10,8},{11,9},{12,... | collective-permute-start | bytes 196616 | tf_op jit(solution)/shard_map/ppermute | solution.py:20
  177.6 0.8 constant_dynamic-update-slice_fusion.9
  178.5 1.3 collective-permute-done.23
  181.4 0.9 broadcast_in_dim.39
  182.3 2.0 reshape.184
  184.3 1.1 bitcast_add_fusion
  185.4 1.5 fusion.24
  187.0 0.9 fusion.32
  187.9 2.1 %collective-permute-start.24 = (f32[64,2,256]{2,0,1:T(8,128)S(1)}, f32[64,2,256]{2,0,1:T(8,128)S(1)}, u32[]{:S(2)}, u32[]{:S(2)}) collective-permute-start(f32[64,2,256]{2,0,1:T(8,128)S(1)} %get-tuple-element.17), channel_id=1, source_target_pairs={{0,1},{1,2},{2,3},{3,4},{4,5},{5,6},{6,7},{7,8},{8,9},{9,10},{10,1... | collective-permute-start | bytes 393224 | tf_op jit(solution)/shard_map/ppermute | solution.py:20
  190.0 6.0 %collective-permute-start.25 = (f32[64,2,256]{2,0,1:T(8,128)S(1)}, f32[64,2,256]{2,0,1:T(8,128)S(1)}, u32[]{:S(2)}, u32[]{:S(2)}) collective-permute-start(f32[64,2,256]{2,0,1:T(8,128)S(1)} %get-tuple-element.16), channel_id=1, source_target_pairs={{1,0},{2,1},{3,2},{4,3},{5,4},{6,5},{7,6},{8,7},{9,8},{10,9},{11,1... | collective-permute-start | bytes 393224 | tf_op jit(solution)/shard_map/ppermute | solution.py:20
  196.3 0.8 collective-permute-done.24
  197.0 1.5 collective-permute-done.25
  200.7 0.5 copy-done.4
  201.4 0.7 fusion.78
  202.6 0.6 copy-done.10
  203.5 1.0 slice_select_fusion.1
  (171 shorter events, 13.6 us)
Async XLA Ops:
  2.6 11.1 %copy-start = (f32[16,16,1024]{2,1,0:T(8,128)S(1)}, f32[16,16,1024]{2,1,0:T(8,128)}, u32[]{:S(2)}) copy-start(f32[16,16,1024]{2,1,0:T(8,128)} %shard_map.46) | copy-start | bytes 3145732
  3.7 3.3 %collective-permute-start = (f32[4,16,1024]{2,1,0:T(8,128)S(1)}, f32[4,16,1024]{2,1,0:T(8,128)S(1)}, u32[]{:S(2)}, u32[]{:S(2)}) collective-permute-start(f32[4,16,1024]{2,1,0:T(8,128)S(1)} %get-tuple-element.14), channel_id=1, source_target_pairs={{0,64},{64,128},{128,192},{192,256},{256,320},{320,384},{384,448},... | collective-permute-start | bytes 786440 | tf_op jit(solution)/shard_map/ppermute | solution.py:20
  5.5 8.1 %collective-permute-start.1 = (f32[4,16,1024]{2,1,0:T(8,128)S(1)}, f32[4,16,1024]{2,1,0:T(8,128)S(1)}, u32[]{:S(2)}, u32[]{:S(2)}) collective-permute-start(f32[4,16,1024]{2,1,0:T(8,128)S(1)} %get-tuple-element.15), channel_id=1, source_target_pairs={{64,0},{128,64},{192,128},{256,192},{320,256},{384,320},{448,384},... | collective-permute-start | bytes 786440 | tf_op jit(solution)/shard_map/ppermute | solution.py:20
  13.8 24.8 %collective-permute-start.2 = (f32[24,4,1024]{2,1,0:T(4,128)S(1)}, f32[24,4,1024]{2,1,0:T(4,128)S(1)}, u32[]{:S(2)}, u32[]{:S(2)}) collective-permute-start(f32[24,4,1024]{2,1,0:T(4,128)S(1)} %get-tuple-element.12), channel_id=1, source_target_pairs={{0,1},{1,2},{2,3},{3,4},{4,5},{5,6},{6,7},{7,8},{8,9},{9,10},{10,1... | collective-permute-start | bytes 1179656 | tf_op jit(solution)/shard_map/ppermute | solution.py:20
  18.1 21.9 %collective-permute-start.3 = (f32[24,4,1024]{2,1,0:T(4,128)S(1)}, f32[24,4,1024]{2,1,0:T(4,128)S(1)}, u32[]{:S(2)}, u32[]{:S(2)}) collective-permute-start(f32[24,4,1024]{2,1,0:T(4,128)S(1)} %get-tuple-element.13), channel_id=1, source_target_pairs={{1,0},{2,1},{3,2},{4,3},{5,4},{6,5},{7,6},{8,7},{9,8},{10,9},{11,1... | collective-permute-start | bytes 1179656 | tf_op jit(solution)/shard_map/ppermute | solution.py:20
  40.6 2.1 %copy-start.5 = (f32[24,24,256]{2,1,0:T(8,128)}, f32[24,24,256]{2,1,0:T(8,128)S(1)}, u32[]{:S(2)}) copy-start(f32[24,24,256]{2,1,0:T(8,128)S(1)} %get-tuple-element.11) | copy-start | bytes 1769476
  42.1 0.8 copy-start.3
  42.7 1.2 copy-start.22
  43.5 0.8 copy-start.9
  43.5 1.0 copy-start.11
  44.8 12.3 %collective-permute-start.4 = (f32[4,8,512]{2,1,0:T(8,128)S(1)}, f32[4,8,512]{2,1,0:T(8,128)S(1)}, u32[]{:S(2)}, u32[]{:S(2)}) collective-permute-start(f32[4,8,512]{2,1,0:T(8,128)S(1)} %get-tuple-element.70), channel_id=1, source_target_pairs={{0,64},{64,128},{128,192},{192,256},{256,320},{320,384},{384,448},... | collective-permute-start | bytes 196616 | tf_op jit(solution)/shard_map/ppermute | solution.py:20
  55.7 3.2 %collective-permute-start.5 = (f32[4,8,512]{2,1,0:T(8,128)S(1)}, f32[4,8,512]{2,1,0:T(8,128)S(1)}, u32[]{:S(2)}, u32[]{:S(2)}) collective-permute-start(f32[4,8,512]{2,1,0:T(8,128)S(1)} %get-tuple-element.71), channel_id=1, source_target_pairs={{64,0},{128,64},{192,128},{256,192},{320,256},{384,320},{448,384},... | collective-permute-start | bytes 196616 | tf_op jit(solution)/shard_map/ppermute | solution.py:20
  59.1 10.1 %collective-permute-start.6 = (f32[16,4,512]{2,1,0:T(4,128)S(1)}, f32[16,4,512]{2,1,0:T(4,128)S(1)}, u32[]{:S(2)}, u32[]{:S(2)}) collective-permute-start(f32[16,4,512]{2,1,0:T(4,128)S(1)} %get-tuple-element.62), channel_id=1, source_target_pairs={{0,1},{1,2},{2,3},{3,4},{4,5},{5,6},{6,7},{7,8},{8,9},{9,10},{10,1... | collective-permute-start | bytes 393224 | tf_op jit(solution)/shard_map/ppermute | solution.py:20
  61.0 9.0 %collective-permute-start.7 = (f32[16,4,512]{2,1,0:T(4,128)S(1)}, f32[16,4,512]{2,1,0:T(4,128)S(1)}, u32[]{:S(2)}, u32[]{:S(2)}) collective-permute-start(f32[16,4,512]{2,1,0:T(4,128)S(1)} %get-tuple-element.63), channel_id=1, source_target_pairs={{1,0},{2,1},{3,2},{4,3},{5,4},{6,5},{7,6},{8,7},{9,8},{10,9},{11,1... | collective-permute-start | bytes 393224 | tf_op jit(solution)/shard_map/ppermute | solution.py:20
  70.5 1.2 copy-start.13
  70.5 1.2 copy-start.15
  70.8 0.7 copy-start.7
  71.8 20.6 %collective-permute-start.8 = (f32[4,4,512]{2,1,0:T(4,128)S(1)}, f32[4,4,512]{2,1,0:T(4,128)S(1)}, u32[]{:S(2)}, u32[]{:S(2)}) collective-permute-start(f32[4,4,512]{2,1,0:T(4,128)S(1)} %get-tuple-element.73), channel_id=1, source_target_pairs={{0,64},{64,0},{128,192},{192,128},{256,320},{320,256},{384,448},{4... | collective-permute-start | bytes 98312 | tf_op jit(solution)/shard_map/ppermute | solution.py:55
  80.2 12.4 %collective-permute-start.9 = (f32[4,4,512]{2,1,0:T(4,128)S(1)}, f32[4,4,512]{2,1,0:T(4,128)S(1)}, u32[]{:S(2)}, u32[]{:S(2)}) collective-permute-start(f32[4,4,512]{2,1,0:T(4,128)S(1)} %get-tuple-element.73), channel_id=1, source_target_pairs={{0,128},{64,192},{128,0},{192,64},{256,384},{320,448},{384,256},{4... | collective-permute-start | bytes 98312 | tf_op jit(solution)/shard_map/ppermute | solution.py:55
  90.4 9.4 %collective-permute-start.10 = (f32[4,4,512]{2,1,0:T(4,128)S(1)}, f32[4,4,512]{2,1,0:T(4,128)S(1)}, u32[]{:S(2)}, u32[]{:S(2)}) collective-permute-start(f32[4,4,512]{2,1,0:T(4,128)S(1)} %get-tuple-element.73), channel_id=1, source_target_pairs={{0,192},{64,128},{128,64},{192,0},{256,448},{320,384},{384,320},{4... | collective-permute-start | bytes 98312 | tf_op jit(solution)/shard_map/ppermute | solution.py:55
  99.9 9.7 %collective-permute-start.12 = (f32[16,4,512]{2,1,0:T(4,128)S(1)}, f32[16,4,512]{2,1,0:T(4,128)S(1)}, u32[]{:S(2)}, u32[]{:S(2)}) collective-permute-start(f32[16,4,512]{2,1,0:T(4,128)S(1)} %get-tuple-element.65), channel_id=1, source_target_pairs={{0,512},{64,576},{128,640},{192,704},{256,768},{320,832},{384,896}... | collective-permute-start | bytes 393224 | tf_op jit(solution)/shard_map/ppermute | solution.py:55
  101.8 9.7 %collective-permute-start.13 = (f32[16,4,512]{2,1,0:T(4,128)S(1)}, f32[16,4,512]{2,1,0:T(4,128)S(1)}, u32[]{:S(2)}, u32[]{:S(2)}) collective-permute-start(f32[16,4,512]{2,1,0:T(4,128)S(1)} %get-tuple-element.65), channel_id=1, source_target_pairs={{0,768},{64,832},{128,896},{192,960},{256,512},{320,576},{384,640}... | collective-permute-start | bytes 393224 | tf_op jit(solution)/shard_map/ppermute | solution.py:55
  107.6 6.9 %collective-permute-start.11 = (f32[16,4,512]{2,1,0:T(4,128)S(1)}, f32[16,4,512]{2,1,0:T(4,128)S(1)}, u32[]{:S(2)}, u32[]{:S(2)}) collective-permute-start(f32[16,4,512]{2,1,0:T(4,128)S(1)} %get-tuple-element.65), channel_id=1, source_target_pairs={{0,256},{64,320},{128,384},{192,448},{256,0},{320,64},{384,128},{4... | collective-permute-start | bytes 393224 | tf_op jit(solution)/shard_map/ppermute | solution.py:55
  109.6 26.4 %copy-start.26 = (pred[12]{0:T(512)(128)(4,1)}, pred[12]{0:T(512)(128)(4,1)S(1)}, u32[]{:S(2)}) copy-start(pred[12]{0:T(512)(128)(4,1)S(1)} %compare_and_fusion.7) | copy-start | bytes 40
  114.9 16.6 %collective-permute-start.14 = (f32[64,4,512]{2,0,1:T(8,128)S(1)}, f32[64,4,512]{2,0,1:T(8,128)S(1)}, u32[]{:S(2)}, u32[]{:S(2)}) collective-permute-start(f32[64,4,512]{2,0,1:T(8,128)S(1)} %pad_maximum_fusion.4), channel_id=1, source_target_pairs={{0,1},{1,2},{2,3},{3,4},{4,5},{5,6},{6,7},{7,8},{8,9},{9,10},{10,1... | collective-permute-start | bytes 1572872 | tf_op jit(solution)/shard_map/ppermute | solution.py:20
  116.8 15.8 %collective-permute-start.15 = (f32[64,4,512]{2,0,1:T(8,128)S(1)}, f32[64,4,512]{2,0,1:T(8,128)}, u32[]{:S(2)}, u32[]{:S(2)}) collective-permute-start(f32[64,4,512]{2,0,1:T(8,128)S(1)} %pad_maximum_fusion.4), channel_id=1, source_target_pairs={{1,0},{2,1},{3,2},{4,3},{5,4},{6,5},{7,6},{8,7},{9,8},{10,9},{11,1... | collective-permute-start | bytes 1572872 | tf_op jit(solution)/shard_map/ppermute | solution.py:20
  131.5 0.8 copy-start.24
  135.9 0.9 copy-start.1
  139.2 16.4 %collective-permute-start.16 = (f32[32,2,512]{2,0,1:T(8,128)S(1)}, f32[32,2,512]{2,0,1:T(8,128)S(1)}, u32[]{:S(2)}, u32[]{:S(2)}) collective-permute-start(f32[32,2,512]{2,0,1:T(8,128)S(1)} %pad_maximum_fusion.11), channel_id=1, source_target_pairs={{0,2},{1,3},{2,4},{3,5},{4,6},{5,7},{6,8},{7,9},{8,10},{9,11},{10,... | collective-permute-start | bytes 393224 | tf_op jit(solution)/shard_map/ppermute | solution.py:20
  142.1 13.6 %collective-permute-start.17 = (f32[32,2,512]{2,0,1:T(8,128)S(1)}, f32[32,2,512]{2,0,1:T(8,128)S(1)}, u32[]{:S(2)}, u32[]{:S(2)}) collective-permute-start(f32[32,2,512]{2,0,1:T(8,128)S(1)} %pad_maximum_fusion.11), channel_id=1, source_target_pairs={{0,1},{1,2},{2,3},{3,4},{4,5},{5,6},{6,7},{7,8},{8,9},{9,10},{10,1... | collective-permute-start | bytes 393224 | tf_op jit(solution)/shard_map/ppermute | solution.py:20
  144.4 11.3 %collective-permute-start.18 = (f32[32,2,512]{2,0,1:T(8,128)S(1)}, f32[32,2,512]{2,0,1:T(8,128)S(1)}, u32[]{:S(2)}, u32[]{:S(2)}) collective-permute-start(f32[32,2,512]{2,0,1:T(8,128)S(1)} %pad_maximum_fusion.11), channel_id=1, source_target_pairs={{1,0},{2,1},{3,2},{4,3},{5,4},{6,5},{7,6},{8,7},{9,8},{10,9},{11,1... | collective-permute-start | bytes 393224 | tf_op jit(solution)/shard_map/ppermute | solution.py:20
  150.6 8.7 %collective-permute-start.19 = (f32[32,2,512]{2,0,1:T(8,128)S(1)}, f32[32,2,512]{2,0,1:T(8,128)S(1)}, u32[]{:S(2)}, u32[]{:S(2)}) collective-permute-start(f32[32,2,512]{2,0,1:T(8,128)S(1)} %pad_maximum_fusion.11), channel_id=1, source_target_pairs={{2,0},{3,1},{4,2},{5,3},{6,4},{7,5},{8,6},{9,7},{10,8},{11,9},{12,... | collective-permute-start | bytes 393224 | tf_op jit(solution)/shard_map/ppermute | solution.py:20
  159.8 1.5 copy-start.18
  159.8 1.5 copy-start.20
  161.4 16.2 %collective-permute-start.20 = (f32[32,2,256]{2,0,1:T(8,128)S(1)}, f32[32,2,256]{2,0,1:T(8,128)}, u32[]{:S(2)}, u32[]{:S(2)}) collective-permute-start(f32[32,2,256]{2,0,1:T(8,128)S(1)} %slice_select_fusion.4), channel_id=1, source_target_pairs={{0,2},{1,3},{2,4},{3,5},{4,6},{5,7},{6,8},{7,9},{8,10},{9,11},{10,... | collective-permute-start | bytes 196616 | tf_op jit(solution)/shard_map/ppermute | solution.py:20
  164.4 14.1 %collective-permute-start.21 = (f32[32,2,256]{2,0,1:T(8,128)S(1)}, f32[32,2,256]{2,0,1:T(8,128)S(1)}, u32[]{:S(2)}, u32[]{:S(2)}) collective-permute-start(f32[32,2,256]{2,0,1:T(8,128)S(1)} %slice_select_fusion.4), channel_id=1, source_target_pairs={{0,1},{1,2},{2,3},{3,4},{4,5},{5,6},{6,7},{7,8},{8,9},{9,10},{10,1... | collective-permute-start | bytes 196616 | tf_op jit(solution)/shard_map/ppermute | solution.py:20
  167.4 11.0 %collective-permute-start.22 = (f32[32,2,256]{2,0,1:T(8,128)S(1)}, f32[32,2,256]{2,0,1:T(8,128)S(1)}, u32[]{:S(2)}, u32[]{:S(2)}) collective-permute-start(f32[32,2,256]{2,0,1:T(8,128)S(1)} %slice_select_fusion.4), channel_id=1, source_target_pairs={{1,0},{2,1},{3,2},{4,3},{5,4},{6,5},{7,6},{8,7},{9,8},{10,9},{11,1... | collective-permute-start | bytes 196616 | tf_op jit(solution)/shard_map/ppermute | solution.py:20
  172.3 7.5 %collective-permute-start.23 = (f32[32,2,256]{2,0,1:T(8,128)S(1)}, f32[32,2,256]{2,0,1:T(8,128)S(1)}, u32[]{:S(2)}, u32[]{:S(2)}) collective-permute-start(f32[32,2,256]{2,0,1:T(8,128)S(1)} %slice_select_fusion.4), channel_id=1, source_target_pairs={{2,0},{3,1},{4,2},{5,3},{6,4},{7,5},{8,6},{9,7},{10,8},{11,9},{12,... | collective-permute-start | bytes 196616 | tf_op jit(solution)/shard_map/ppermute | solution.py:20
  180.2 1.0 copy-start.19
  180.2 1.1 copy-start.21
  180.2 1.1 copy-start.25
  180.9 3.4 %copy-start.2 = (f32[64,12,256]{2,0,1:T(8,128)S(1)}, f32[64,12,256]{2,0,1:T(8,128)}, u32[]{:S(2)}) copy-start(f32[64,12,256]{2,0,1:T(8,128)} %copy-done.1) | copy-start | bytes 2359300
  185.4 1.6 copy-start.27
  187.9 11.1 %copy-start.8 = (f32[16,16,256]{2,1,0:T(8,128)S(1)}, f32[16,16,256]{2,1,0:T(8,128)}, u32[]{:S(2)}) copy-start(f32[16,16,256]{2,1,0:T(8,128)} %copy-done.7) | copy-start | bytes 786436
  187.9 9.1 %collective-permute-start.24 = (f32[64,2,256]{2,0,1:T(8,128)S(1)}, f32[64,2,256]{2,0,1:T(8,128)S(1)}, u32[]{:S(2)}, u32[]{:S(2)}) collective-permute-start(f32[64,2,256]{2,0,1:T(8,128)S(1)} %get-tuple-element.17), channel_id=1, source_target_pairs={{0,1},{1,2},{2,3},{3,4},{4,5},{5,6},{6,7},{7,8},{8,9},{9,10},{10,1... | collective-permute-start | bytes 393224 | tf_op jit(solution)/shard_map/ppermute | solution.py:20
  190.0 8.5 %collective-permute-start.25 = (f32[64,2,256]{2,0,1:T(8,128)S(1)}, f32[64,2,256]{2,0,1:T(8,128)S(1)}, u32[]{:S(2)}, u32[]{:S(2)}) collective-permute-start(f32[64,2,256]{2,0,1:T(8,128)S(1)} %get-tuple-element.16), channel_id=1, source_target_pairs={{1,0},{2,1},{3,2},{4,3},{5,4},{6,5},{7,6},{8,7},{9,8},{10,9},{11,1... | collective-permute-start | bytes 393224 | tf_op jit(solution)/shard_map/ppermute | solution.py:20
  199.0 1.0 copy-start.14
  199.0 1.0 copy-start.16
  200.2 1.1 copy-start.4
  200.2 1.2 copy-start.6
  202.2 1.0 copy-start.10
  202.2 1.2 copy-start.12
  202.2 1.3 copy-start.17
  202.2 1.3 copy-start.23
